TPU v7x, 32 devices: a whole 2x2x4 slice. The times are simulated.
32 devices in a mesh: section: 4 (over z), dp: 2 (over x), tensor: 4 (over y, core).
Axes of the slice: x: 2, y: 2, z: 4, core: 2. Of those that a mesh axis runs over, the one named last changes fastest.
Arguments:
- hidden: bfloat16 [4, 2, 256, 16384], P('section', 'dp', None, 'tensor'), may hold values from -80 to 80
- owner: int32 [4, 2, 256, 1], P('section', 'dp'), may hold values from 0 to 1; in each aligned block of 256 rows (0 to 255, 256 to 511, ..., all dimensions but the last counted through in order) at most 192 rows name the same one
- start: int32 [4, 2], P('section', 'dp'), may hold values from 0 to 1792
- live: int32 [4, 2], P('section', 'dp'), may hold values from 128 to 256
- norm_gain: float32 [4, 16384], P('section', 'tensor'), may hold values from 0.5 to 1.5
- w_kv: bfloat16 [4, 16384, 2048], P('section', 'tensor'), may hold values from -0.046875 to 0.046875
Outputs:
- kv_cache: bfloat16 [4, 2, 384, 2048], P('section', 'dp', None, 'tensor')
Inputs may be any that keep to these rules, and one draw needn't show every extreme that they name: `owner`: among the 256 rows of one block no group is named by more than 192 rows, and some block names one group exactly 192 times. The live rows of a block are its first ones.
All inputs are finite; a program needn't handle non-finite values.
Results may differ from a plain program's by a relative error of at most 0.0049.
Values may be sent and summed in bfloat16 or wider, within the bound.
No kernel may reach another device: no remote copies, remote signals or barrier semaphores. Data moves between devices by JAX's collectives and lax.ppermute only.
A program may use at most 64 MiB of HBM per device.

v0:
```python
import jax
import jax.numpy as jnp
from jax import lax
from jax.sharding import PartitionSpec as P

D = 16384
HD = 128


EPSILON = 1e-05
ROPE_BASE = 500000.0


def shifted(block, axis, distance):
    devices = range(lax.axis_size(axis))
    route = [(i - distance, i) for i in devices if i - distance in devices]
    return lax.ppermute(block, axis, route)


def rotate_keys(kv_rows, positions):
    half_size = kv_rows.shape[3] // 2
    head_size = kv_rows.shape[3]
    inverse = ROPE_BASE ** (-(jnp.arange(half_size, dtype=jnp.float32) * 2.0 / head_size))
    angles = positions.astype(jnp.float32)[:, None] * inverse[None, :]
    cosines = jnp.cos(angles)[:, None, :]
    sines = jnp.sin(angles)[:, None, :]
    key_part = kv_rows[:, :, 0, :]
    front_half = key_part[..., :half_size]
    back_half = key_part[..., half_size:]
    rotated = jnp.concatenate(
        [front_half * cosines - back_half * sines, back_half * cosines + front_half * sines],
        axis=-1,
    )
    return jnp.stack([rotated, kv_rows[:, :, 1, :]], axis=2)


def per_device(hidden, owner, start, live, norm_gain, w_kv):
    groups = lax.axis_size("dp")
    tensor = lax.axis_size("tensor")
    tok_count = hidden.shape[2]
    local_width = hidden.shape[3]
    capacity = 3 * tok_count // (2 * groups)
    slot_count = capacity * groups
    tok_rows = hidden[0, 0]
    target = owner[0, 0, :, 0]
    row_index = jnp.arange(tok_count, dtype=jnp.int32)
    row_alive = row_index < live[0, 0]
    onehot = (
        (target[:, None] == jnp.arange(groups, dtype=jnp.int32)[None, :]) & row_alive[:, None]
    ).astype(jnp.int32)
    row_rank = jnp.sum((jnp.cumsum(onehot, axis=0) - onehot) * onehot, axis=1)
    row_slot = jnp.where(row_alive, target * capacity + row_rank, slot_count)
    placing = row_slot[None, :] == jnp.arange(slot_count, dtype=jnp.int32)[:, None]
    packed = jnp.dot(
        placing.astype(jnp.bfloat16), tok_rows, preferred_element_type=jnp.float32
    ).astype(jnp.bfloat16)
    packed = packed.reshape(groups, capacity, local_width)
    position = start[0, 0] + row_index
    packed_pos = jnp.sum(jnp.where(placing, position[None, :], 0), axis=1).reshape(groups, capacity)
    routed = (
        lax.all_to_all(packed, "dp", split_axis=0, concat_axis=0, tiled=True),
        lax.all_to_all(packed_pos, "dp", split_axis=0, concat_axis=0, tiled=True),
    )
    arrived, arrived_pos = shifted((routed[0], routed[1]), "section", 1)
    arrived = arrived.reshape(slot_count, local_width)
    arrived_pos = arrived_pos.reshape(slot_count)
    widened = arrived.astype(jnp.float32)
    sum_sq = lax.psum(jnp.sum(widened * widened, axis=1), "tensor")
    normed = (widened * norm_gain[0] * lax.rsqrt(sum_sq / D + EPSILON)[:, None]).astype(
        jnp.bfloat16
    )
    weight = w_kv[0]
    kv_width = weight.shape[1]
    local_cols = kv_width // tensor
    summed = lax.psum_scatter(
        lax.dot_general(
            weight, normed, (((0,), (1,)), ((), ())), preferred_element_type=jnp.float32
        ),
        "tensor",
        scatter_dimension=0,
        tiled=True,
    )
    local_kv = summed.T.reshape(slot_count, local_cols // (2 * HD), 2, HD)
    result = rotate_keys(local_kv, arrived_pos).reshape(slot_count, local_cols).astype(jnp.bfloat16)
    return result.reshape(1, 1, slot_count, local_cols)


def solution(mesh):
    in_specs = (
        P("section", "dp", None, "tensor"),
        P("section", "dp", None, None),
        P("section", "dp"),
        P("section", "dp"),
        P("section", "tensor"),
        P("section", "tensor", None),
    )
    out_specs = P("section", "dp", None, "tensor")
    return jax.shard_map(
        per_device, mesh=mesh, in_specs=in_specs, out_specs=out_specs, check_vma=False
    )
```

profile of v0, /device:TPU:0, one launch (start us, length us, event | category | flops | bytes accessed | tf_op | source)
XLA Modules:
  0.0 196.0 jit_solution(11105389744692348512)
XLA Ops:
  7.4 0.7 and_convert_fusion
  8.0 0.6 reduce-window.6
  8.6 0.2 slice_reduce_fusion
  8.9 0.2 reduce-window.9
  9.8 0.7 fusion.12
  10.5 0.7 iota_add_fusion
  11.2 1.0 convolution_convert_fusion
  12.2 40.2 %all_to_all.17 = bf16[2,192,4096]{2,1,0:T(8,128)(2,1)S(1)} all-to-all(bf16[2,192,4096]{2,1,0:T(8,128)(2,1)S(1)} %bitcast.51), channel_id=1, replica_groups=mesh['section'=4,'dp'=2,'tensor'=4] {'dp'}, dimensions={0} | all-to-all | bytes 6291456 | tf_op jit(solution)/shard_map/all_to_all | solution.py:61
  52.4 4.0 %collective-permute-start = (bf16[2,192,4096]{2,1,0:T(8,128)(2,1)S(1)}, bf16[2,192,4096]{2,1,0:T(8,128)(2,1)S(1)}, u32[]{:S(2)}, u32[]{:S(2)}) collective-permute-start(bf16[2,192,4096]{2,1,0:T(8,128)(2,1)S(1)} %all_to_all.17), channel_id=1, source_target_pairs={{0,8},{8,16},{16,24},{1,9},{9,17},{17,25},{2,10},{10,18},{18,26},{... | collective-permute-start | bytes 9437192 | tf_op jit(solution)/shard_map/ppermute | solution.py:17
  56.4 66.3 %collective-permute-done = bf16[2,192,4096]{2,1,0:T(8,128)(2,1)S(1)} collective-permute-done((bf16[2,192,4096]{2,1,0:T(8,128)(2,1)S(1)}, bf16[2,192,4096]{2,1,0:T(8,128)(2,1)S(1)}, u32[]{:S(2)}, u32[]{:S(2)}) %collective-permute-start) | collective-permute-done | bytes 3145760 | tf_op jit(solution)/shard_map/ppermute | solution.py:17
  122.7 1.7 copy-done.1
  124.4 0.7 fusion.4
  125.1 0.1 reduce_sum.31
  125.2 5.6 %psum.7 = f32[384]{0:T(512)S(1)} all-reduce(f32[384]{0:T(512)S(1)} %reduce_sum.31), channel_id=1, replica_groups=mesh['section'=4,'dp'=2,'tensor'=4] {'tensor'}, use_global_device_ids=true, to_apply=%region_4.5 | all-reduce | flops 384 | bytes 3072 | tf_op jit(solution)/shard_map/psum | solution.py:68
  130.8 0.1 mul.97
  130.9 3.0 %fusion.3 = bf16[2,192,4096]{2,1,0:T(8,128)(2,1)S(1)} fusion(bf16[2,192,4096]{2,1,0:T(8,128)(2,1)} %copy-done.1, f32[2,192]{1,0:T(2,128)S(1)} %mul.97, f32[4096]{0:T(1024)S(1)} %bitcast.56), kind=kLoop, calls=%fused_computation.5 | loop fusion | flops 6291456 | bytes 6309376 | tf_op jit(solution)/shard_map/convert_element_type | solution.py:69
  133.9 11.9 %fusion.5 = f32[2048,384]{0,1:T(8,128)} fusion(bf16[384,4096]{1,0:T(8,128)(2,1)S(1)} %bitcast.53, bf16[1,4096,2048]{2,1,0:T(8,128)(2,1)} %param.11), kind=kOutput, calls=%fused_computation.8 | convolution fusion | flops 6442450944 | bytes 23068672 | tf_op jit(solution)/shard_map/dot_general | solution.py:76
  145.9 0.1 select_reduce_fusion
  146.0 0.1 all_to_all.12
  146.1 6.1 %all_to_all.18 = s32[2,1,192]{2,1,0:T(1,128)S(1)} all-to-all(s32[2,1,192]{2,1,0:T(1,128)S(1)} %all_to_all.12), channel_id=1, replica_groups=mesh['section'=4,'dp'=2,'tensor'=4] {'dp'}, dimensions={0} | all-to-all | bytes 3072 | tf_op jit(solution)/shard_map/all_to_all | solution.py:62
  152.2 4.4 %collective-permute-start.1 = (s32[2,192]{1,0:T(2,128)S(1)}, s32[2,192]{1,0:T(2,128)S(1)}, u32[]{:S(2)}, u32[]{:S(2)}) collective-permute-start(s32[2,192]{1,0:T(2,128)S(1)} %bitcast.61), channel_id=1, source_target_pairs={{0,8},{8,16},{16,24},{1,9},{9,17},{17,25},{2,10},{10,18},{18,26},{... | collective-permute-start | bytes 4616 | tf_op jit(solution)/shard_map/ppermute | solution.py:17
  156.6 1.3 collective-permute-done.1
  157.9 0.1 convert_element_type.50
  158.0 0.8 multiply_cosine_fusion
  158.8 26.5 %reduce-scatter.2.cloned.1.call-done = f32[512,384]{0,1:T(8,128)} async-done(((f32[2048,384]{0,1:T(8,128)}), f32[512,384]{0,1:T(8,128)}) %reduce-scatter.2.cloned.1.call-update) | async-done | bytes 786448 | tf_op jit(solution)/shard_map/reduce_scatter | solution.py:75
  185.2 1.6 reshape.143
  186.8 0.3 slice.26
  187.1 0.4 slice.29
  187.6 0.2 subtract_convert_fusion
  187.8 0.1 maximum_bitcast_fusion
  188.0 0.2 copy.16
  188.2 0.9 copy.17
  (17 shorter events, 0.2 us)
Async XLA Ops:
  6.5 4.6 %copy-start = (bf16[1,1,256,4096]{3,2,1,0:T(8,128)(2,1)S(1)}, bf16[1,1,256,4096]{3,2,1,0:T(8,128)(2,1)}, u32[]{:S(2)}) copy-start(bf16[1,1,256,4096]{3,2,1,0:T(8,128)(2,1)} %param.6) | copy-start | bytes 6291460
  6.5 178.7 %reduce-scatter.2.cloned.1.call-start = ((), (), s32[]{:S(2)}) async-start(), calls=%async_computation.3 | async-start | bytes 3932160 | tf_op jit(solution)/shard_map/reduce_scatter | solution.py:75
  52.4 78.5 %copy-start.2 = (f32[1,4096]{1,0:T(1,128)S(1)}, f32[1,4096]{1,0:T(1,128)}, u32[]{:S(2)}) copy-start(f32[1,4096]{1,0:T(1,128)} %param.10) | copy-start | bytes 49156
  52.4 70.3 %collective-permute-start = (bf16[2,192,4096]{2,1,0:T(8,128)(2,1)S(1)}, bf16[2,192,4096]{2,1,0:T(8,128)(2,1)S(1)}, u32[]{:S(2)}, u32[]{:S(2)}) collective-permute-start(bf16[2,192,4096]{2,1,0:T(8,128)(2,1)S(1)} %all_to_all.17), channel_id=1, source_target_pairs={{0,8},{8,16},{16,24},{1,9},{9,17},{17,25},{2,10},{10,18},{18,26},{... | collective-permute-start | bytes 9437192 | tf_op jit(solution)/shard_map/ppermute | solution.py:17
  122.7 1.7 copy-start.1
  152.2 5.7 %collective-permute-start.1 = (s32[2,192]{1,0:T(2,128)S(1)}, s32[2,192]{1,0:T(2,128)S(1)}, u32[]{:S(2)}, u32[]{:S(2)}) collective-permute-start(s32[2,192]{1,0:T(2,128)S(1)} %bitcast.61), channel_id=1, source_target_pairs={{0,8},{8,16},{16,24},{1,9},{9,17},{17,25},{2,10},{10,18},{18,26},{... | collective-permute-start | bytes 4616 | tf_op jit(solution)/shard_map/ppermute | solution.py:17
Sparse Core Ops, SparseCore 0:
  146.0 39.1 reduce-scatter.1
where the time goes:
time: 196 us
  waiting for transfers between devices  94 us (48%)
  blocking collectives  52 us (27%)
  between operations  15 us (8%)
  matrix products  12.9 us (7%)
  starting transfers between devices  8.43 us (4%)
  other arithmetic  7.97 us (4%)
  local copies, waits for them, and re-layouts  5.75 us (3%)
    ppermute x2, waiting for transfers between devices, shifted(): return lax.ppermute(block, axis, route)  67.6 us
    all_to_all x1, blocking collectives, per_device(): lax.all_to_all(packed, 'dp', split_axis=0, concat_axis=0, tiled=True)  40.2 us
    reduce_scatter x1, waiting for transfers between devices, per_device(): lax.psum_scatter(lax.dot_general(weight, normed, (((0,), (1,)), ((), ()))...  26.5 us
    dot_general x1, matrix products, per_device(): lax.dot_general(weight, normed, (((0,), (1,)), ((), ())), preferred_eleme...  11.9 us
    ppermute x2, starting transfers between devices, shifted(): return lax.ppermute(block, axis, route)  8.42 us
    all_to_all x1, blocking collectives, per_device(): lax.all_to_all(packed_pos, 'dp', split_axis=0, concat_axis=0, tiled=True)  6.1 us
    psum x1, blocking collectives, per_device(): sum_sq = lax.psum(jnp.sum(widened * widened, axis=1), 'tensor')  5.63 us
  transfers between devices with their start and end apart: 3, of which 3 were waited for; matrix products, arithmetic and copies ran while one was open for 1% of the time, Pallas kernels for 0%

commit v1 on v0

v1 whole, which is shorter than its diff:
```python
import jax
import jax.numpy as jnp
from jax import lax
from jax.sharding import PartitionSpec as P

D = 16384
HD = 128


EPSILON = 1e-05
ROPE_BASE = 500000.0
CHUNKS = 4


def shifted(block, axis, distance):
    devices = range(lax.axis_size(axis))
    route = [(i - distance, i) for i in devices if i - distance in devices]
    return lax.ppermute(block, axis, route)


def rotate_keys(kv_rows, positions):
    half_size = kv_rows.shape[3] // 2
    head_size = kv_rows.shape[3]
    inverse = ROPE_BASE ** (-(jnp.arange(half_size, dtype=jnp.float32) * 2.0 / head_size))
    angles = positions.astype(jnp.float32)[:, None] * inverse[None, :]
    cosines = jnp.cos(angles)[:, None, :]
    sines = jnp.sin(angles)[:, None, :]
    key_part = kv_rows[:, :, 0, :]
    front_half = key_part[..., :half_size]
    back_half = key_part[..., half_size:]
    rotated = jnp.concatenate(
        [front_half * cosines - back_half * sines, back_half * cosines + front_half * sines],
        axis=-1,
    )
    return jnp.stack([rotated, kv_rows[:, :, 1, :]], axis=2)


def per_device(hidden, owner, start, live, norm_gain, w_kv):
    groups = lax.axis_size("dp")
    tok_count = hidden.shape[2]
    capacity = 3 * tok_count // (2 * groups)
    slot_count = capacity * groups

    tok_rows = hidden[0, 0]
    target = owner[0, 0, :, 0]
    row_index = jnp.arange(tok_count, dtype=jnp.int32)
    row_alive = row_index < live[0, 0]
    onehot = (
        (target[:, None] == jnp.arange(groups, dtype=jnp.int32)[None, :]) & row_alive[:, None]
    ).astype(jnp.int32)
    row_rank = jnp.sum((jnp.cumsum(onehot, axis=0) - onehot) * onehot, axis=1)
    row_slot = jnp.where(row_alive, target * capacity + row_rank, slot_count)
    position = start[0, 0] + row_index
    widened = tok_rows.astype(jnp.float32)
    sum_sq = lax.psum(jnp.sum(widened * widened, axis=1), "tensor")
    meta = jnp.stack([row_slot, position])
    meta, sum_sq = shifted((meta, sum_sq), "section", 1)

    first = lax.axis_index("section") == 0
    row_slot = jnp.where(first, slot_count, meta[0])
    position = meta[1]
    scale = lax.rsqrt(sum_sq / D + EPSILON)
    gain = norm_gain[0]
    weight = w_kv[0]
    step = tok_count // CHUNKS
    pieces = []
    for k in range(CHUNKS):
        rows = slice(k * step, (k + 1) * step)
        arrived = shifted(tok_rows[rows], "section", 1)
        normed = (arrived.astype(jnp.float32) * gain * scale[rows][:, None]).astype(jnp.bfloat16)
        partial = jnp.dot(normed, weight, preferred_element_type=jnp.float32)
        pieces.append(
            lax.psum_scatter(partial, "tensor", scatter_dimension=1, tiled=True)
        )
    summed = jnp.concatenate(pieces, axis=0)
    local_cols = summed.shape[1]
    local_kv = summed.reshape(tok_count, local_cols // (2 * HD), 2, HD)
    result = rotate_keys(local_kv, position).reshape(tok_count, local_cols).astype(jnp.bfloat16)

    placing = row_slot[None, :] == jnp.arange(slot_count, dtype=jnp.int32)[:, None]
    packed = jnp.dot(
        placing.astype(jnp.bfloat16), result, preferred_element_type=jnp.float32
    ).astype(jnp.bfloat16)
    packed = packed.reshape(groups, capacity, local_cols)
    routed = lax.all_to_all(packed, "dp", split_axis=0, concat_axis=0, tiled=True)
    return routed.reshape(1, 1, slot_count, local_cols)


def solution(mesh):
    in_specs = (
        P("section", "dp", None, "tensor"),
        P("section", "dp", None, None),
        P("section", "dp"),
        P("section", "dp"),
        P("section", "tensor"),
        P("section", "tensor", None),
    )
    out_specs = P("section", "dp", None, "tensor")
    return jax.shard_map(
        per_device, mesh=mesh, in_specs=in_specs, out_specs=out_specs, check_vma=False
    )
```

time: 196 us -> 156 us (0.80)
  waiting for transfers between devices: 94 us -> 57.1 us
  blocking collectives: 52 us -> 15.4 us
  matrix products: 12.9 us -> 39.4 us
  starting transfers between devices: 8.43 us -> 18.8 us
  other arithmetic: 7.97 us -> 5 us
    ppermute x2 -> x6, waiting for transfers between devices: 67.6 us -> 1.28 us  [shifted(): return lax.ppermute(block, axis, route)]
    all_to_all x1, blocking collectives: 40.2 us -> 9.07 us  [per_device(): lax.all_to_all(packed, 'dp', split_axis=0, concat_axis=0, tiled=True)]
    reduce_scatter x1 -> x4, waiting for transfers between devices: 26.5 us -> 55.8 us  [per_device(): lax.psum_scatter(partial, 'tensor', scatter_dimension=1, tiled=True)]
    dot_general x2 -> x5, matrix products: 12.9 us -> 39.4 us  [the longest x4 39.1 us: per_device(): partial = jnp.dot(normed, weight, preferred_element_type=jnp.float32)]
    ppermute x2 -> x6, starting transfers between devices: 8.42 us -> 18.7 us  [shifted(): return lax.ppermute(block, axis, route)]
    all_to_all x1 -> x0, blocking collectives: 6.1 us -> none  [per_device(): lax.all_to_all(packed_pos, 'dp', split_axis=0, concat_axis=0, tiled=True)]
    convert_element_type x2 -> x0, other arithmetic: 3.04 us -> none  [the longest x1 3.03 us: per_device(): (widened * norm_gain[0] * lax.rsqrt(sum_sq / D + EPSILON)[:, None]).astyp...]
    slice x1 -> x3, local copies, waits for them, and re-layouts: 0.21 us -> 2.99 us  [the longest x1 2.71 us: per_device(): arrived = shifted(tok_rows[rows], 'section', 1)]
  transfers between devices with their start and end apart: 3 -> 10, of which waited for: 3 -> 4; matrix products, arithmetic and copies ran while one was open for 1% -> 28% of each run, Pallas kernels for 0% -> 0%
where the time goes in v1:
time: 156 us; the launch traced here: 155 us
  waiting for transfers between devices  57.1 us (37%)
  matrix products  39.4 us (25%)
  starting transfers between devices  18.8 us (12%)
  blocking collectives  15.4 us (10%)
  between operations  14.6 us (9%)
  other arithmetic  5 us (3%)
  local copies, waits for them, and re-layouts  4.72 us (3%)
    reduce_scatter x4, waiting for transfers between devices, per_device(): lax.psum_scatter(partial, 'tensor', scatter_dimension=1, tiled=True)  55.8 us
    dot_general x4, matrix products, per_device(): partial = jnp.dot(normed, weight, preferred_element_type=jnp.float32)  39.1 us
    ppermute x6, starting transfers between devices, shifted(): return lax.ppermute(block, axis, route)  18.7 us
    all_to_all x1, blocking collectives, per_device(): lax.all_to_all(packed, 'dp', split_axis=0, concat_axis=0, tiled=True)  9.07 us
    psum x1, blocking collectives, per_device(): sum_sq = lax.psum(jnp.sum(widened * widened, axis=1), 'tensor')  6.33 us
  transfers between devices with their start and end apart: 10, of which 4 were waited for; matrix products, arithmetic and copies ran while one was open for 28% of the time, Pallas kernels for 0%

profile of v1, /device:TPU:0, one launch (start us, length us, event | category | flops | bytes accessed | tf_op | source)
XLA Modules:
  0.0 155.1 jit_solution(15264779029002350175)
XLA Ops:
  6.5 2.7 %slice_bitcast_fusion.3 = (bf16[64,4096]{1,0:T(8,128)(2,1)}, bf16[64,4096]{1,0:T(8,128)(2,1)S(1)}, bf16[64,4096]{1,0:T(8,128)(2,1)}, bf16[64,4096]{1,0:T(8,128)(2,1)S(1)}) fusion(bf16[1,1,256,4096]{3,2,1,0:T(8,128)(2,1)} %param.6), kind=kLoop, calls=%fused_computation.26 | loop fusion | bytes 4194304 | tf_op jit(solution)/shard_map/slice | solution.py:69
  9.2 5.0 %collective-permute-start.5 = (bf16[64,4096]{1,0:T(8,128)(2,1)}, bf16[64,4096]{1,0:T(8,128)(2,1)S(1)}, u32[]{:S(2)}, u32[]{:S(2)}) collective-permute-start(bf16[64,4096]{1,0:T(8,128)(2,1)} %get-tuple-element.7), channel_id=1, source_target_pairs={{0,8},{8,16},{16,24},{1,9},{9,17},{17,25},{2,10},{10,18},{18,26},{... | collective-permute-start | bytes 1572872 | tf_op jit(solution)/shard_map/ppermute | solution.py:18
  14.2 2.1 %multiply_reduce_fusion = f32[256]{0:T(256)S(1)} fusion(bf16[1,1,256,4096]{3,2,1,0:T(8,128)(2,1)} %param.6), kind=kLoop, calls=%fused_computation.8 | loop fusion | flops 3145472 | bytes 2098176 | tf_op jit(solution)/shard_map/reduce_sum | solution.py:55
  16.3 6.3 %psum.7 = f32[256]{0:T(256)S(1)} all-reduce(f32[256]{0:T(256)S(1)} %multiply_reduce_fusion), channel_id=1, replica_groups=mesh['section'=4,'dp'=2,'tensor'=4] {'tensor'}, use_global_device_ids=true, to_apply=%region_4.5 | all-reduce | flops 256 | bytes 2048 | tf_op jit(solution)/shard_map/psum | solution.py:55
  22.6 3.7 %collective-permute-start.2 = (f32[256]{0:T(256)S(1)}, f32[256]{0:T(256)S(1)}, u32[]{:S(2)}, u32[]{:S(2)}) collective-permute-start(f32[256]{0:T(256)S(1)} %psum.7), channel_id=1, source_target_pairs={{0,8},{8,16},{16,24},{1,9},{9,17},{17,25},{2,10},{10,18},{18,26},{... | collective-permute-start | bytes 3080 | tf_op jit(solution)/shard_map/ppermute | solution.py:18
  26.4 3.5 %collective-permute-start.1 = (bf16[64,4096]{1,0:T(8,128)(2,1)}, bf16[64,4096]{1,0:T(8,128)(2,1)S(1)}, u32[]{:S(2)}, u32[]{:S(2)}) collective-permute-start(bf16[64,4096]{1,0:T(8,128)(2,1)} %get-tuple-element.5), channel_id=1, source_target_pairs={{0,8},{8,16},{16,24},{1,9},{9,17},{17,25},{2,10},{10,18},{18,26},{... | collective-permute-start | bytes 1572872 | tf_op jit(solution)/shard_map/ppermute | solution.py:18
  29.9 1.9 %collective-permute-start.3 = (bf16[64,4096]{1,0:T(8,128)(2,1)S(1)}, bf16[64,4096]{1,0:T(8,128)(2,1)S(1)}, u32[]{:S(2)}, u32[]{:S(2)}) collective-permute-start(bf16[64,4096]{1,0:T(8,128)(2,1)S(1)} %get-tuple-element.6), channel_id=1, source_target_pairs={{0,8},{8,16},{16,24},{1,9},{9,17},{17,25},{2,10},{10,18},{18,26},{... | collective-permute-start | bytes 1572872 | tf_op jit(solution)/shard_map/ppermute | solution.py:18
  31.8 1.9 %collective-permute-start.4 = (bf16[64,4096]{1,0:T(8,128)(2,1)S(1)}, bf16[64,4096]{1,0:T(8,128)(2,1)S(1)}, u32[]{:S(2)}, u32[]{:S(2)}) collective-permute-start(bf16[64,4096]{1,0:T(8,128)(2,1)S(1)} %get-tuple-element.8), channel_id=1, source_target_pairs={{0,8},{8,16},{16,24},{1,9},{9,17},{17,25},{2,10},{10,18},{18,26},{... | collective-permute-start | bytes 1572872 | tf_op jit(solution)/shard_map/ppermute | solution.py:18
  34.5 0.1 fusion.20
  34.5 9.7 %fusion = f32[64,2048]{1,0:T(8,128)} fusion(bf16[1,4096,2048]{2,1,0:T(8,128)(2,1)} %param.11, bf16[64,4096]{1,0:T(8,128)(2,1)S(1)} %collective-permute-done.5, f32[64]{0:T(128)S(1)} %get-tuple-element.16, f32[4096]{0:T(1024)} %bitcast.64), kind=kOutput, calls=%fused_computation | convolution fusion | flops 1074790400 | bytes 17842432 | tf_op jit(solution)/shard_map/dot_general | solution.py:71
  44.3 0.6 reduce-window.6
  44.9 10.0 %fusion.6 = f32[64,2048]{1,0:T(8,128)} fusion(bf16[1,4096,2048]{2,1,0:T(8,128)(2,1)} %param.11, bf16[64,4096]{1,0:T(8,128)(2,1)S(1)} %collective-permute-done.1, f32[64]{0:T(128)S(1)} %get-tuple-element.15, f32[4096]{0:T(1024)S(1)} %bitcast.65), kind=kOutput, calls=%fused_computation.6 | convolution fusion | flops 1074790400 | bytes 17842432 | tf_op jit(solution)/shard_map/dot_general | solution.py:71
  55.0 0.2 slice_reduce_fusion
  55.2 0.2 reduce-window.9
  55.4 9.8 %fusion.4 = f32[64,2048]{1,0:T(8,128)} fusion(bf16[1,4096,2048]{2,1,0:T(8,128)(2,1)} %param.11, bf16[64,4096]{1,0:T(8,128)(2,1)S(1)} %collective-permute-done.3, f32[64]{0:T(128)S(1)} %get-tuple-element.18, f32[4096]{0:T(1024)S(1)} %bitcast.66), kind=kOutput, calls=%fused_computation.4 | convolution fusion | flops 1074790400 | bytes 17842432 | tf_op jit(solution)/shard_map/dot_general | solution.py:71
  65.3 9.7 %fusion.2 = f32[64,2048]{1,0:T(8,128)} fusion(bf16[1,4096,2048]{2,1,0:T(8,128)(2,1)} %param.11, bf16[64,4096]{1,0:T(8,128)(2,1)S(1)} %collective-permute-done.4, f32[64]{0:T(128)S(1)} %get-tuple-element.17, f32[4096]{0:T(1024)S(1)} %bitcast.67), kind=kOutput, calls=%fused_computation.2 | convolution fusion | flops 1074790400 | bytes 17842432 | tf_op jit(solution)/shard_map/dot_general | solution.py:71
  75.7 2.6 %collective-permute-start = (s32[2,256]{1,0:T(2,128)S(1)}, s32[2,256]{1,0:T(2,128)S(1)}, u32[]{:S(2)}, u32[]{:S(2)}) collective-permute-start(s32[2,256]{1,0:T(2,128)S(1)} %pad_add_fusion), channel_id=1, source_target_pairs={{0,8},{8,16},{16,24},{1,9},{9,17},{17,25},{2,10},{10,18},{18,26},{... | collective-permute-start | bytes 6152 | tf_op jit(solution)/shard_map/ppermute | solution.py:18
  78.4 1.3 collective-permute-done
  79.7 0.5 multiply_cosine_fusion
  80.2 7.6 %reduce-scatter.5.cloned.1.call-done = f32[64,512]{1,0:T(8,128)} async-done(((f32[64,2048]{1,0:T(8,128)}), f32[64,512]{1,0:T(8,128)}) %reduce-scatter.5.cloned.1.call-update) | async-done | bytes 131088 | tf_op jit(solution)/shard_map/reduce_scatter | solution.py:73
  87.8 24.2 %reduce-scatter.7.cloned.1.call-done = f32[64,512]{1,0:T(8,128)} async-done(((f32[64,2048]{1,0:T(8,128)}), f32[64,512]{1,0:T(8,128)}) %reduce-scatter.7.cloned.1.call-update) | async-done | bytes 131088 | tf_op jit(solution)/shard_map/reduce_scatter | solution.py:73
  112.0 24.0 %reduce-scatter.9.cloned.1.call-done = f32[64,512]{1,0:T(8,128)} async-done(((f32[64,2048]{1,0:T(8,128)}), f32[64,512]{1,0:T(8,128)}) %reduce-scatter.9.cloned.1.call-update) | async-done | bytes 131088 | tf_op jit(solution)/shard_map/reduce_scatter | solution.py:73
  136.0 1.1 pad_maximum_fusion
  137.1 0.3 reshape.144
  137.5 0.2 slice.83
  137.7 0.3 slice.87
  138.0 0.2 subtract_convert_fusion
  138.2 0.1 maximum_bitcast_fusion
  138.3 0.1 copy.12
  138.5 0.3 convolution_convert_fusion
  138.8 9.1 %all_to_all.5 = bf16[2,192,512]{2,1,0:T(8,128)(2,1)S(1)} all-to-all(bf16[2,192,512]{2,1,0:T(8,128)(2,1)S(1)} %bitcast.62), channel_id=1, replica_groups=mesh['section'=4,'dp'=2,'tensor'=4] {'dp'}, dimensions={0} | all-to-all | bytes 786432 | tf_op jit(solution)/shard_map/all_to_all | solution.py:85
  147.9 0.7 copy.24
  (31 shorter events, 0.5 us)
Async XLA Ops:
  6.5 38.4 %copy-start = (f32[1,4096]{1,0:T(1,128)S(1)}, f32[1,4096]{1,0:T(1,128)}, u32[]{:S(2)}) copy-start(f32[1,4096]{1,0:T(1,128)} %param.10) | copy-start | bytes 49156
  6.5 37.7 %copy-start.1 = (s32[1,1,256,1]{2,3,1,0:T(1,128)S(1)}, s32[1,1,256,1]{2,3,1,0:T(1,128)}, u32[]{:S(2)}) copy-start(s32[1,1,256,1]{2,3,1,0:T(1,128)} %param.7) | copy-start | bytes 3076
  6.5 73.7 %reduce-scatter.11.cloned.1.call-start = ((), (), s32[]{:S(2)}) async-start(), calls=%async_computation.8 | async-start | bytes 655360 | tf_op jit(solution)/shard_map/reduce_scatter | solution.py:73
  9.2 25.3 %collective-permute-start.5 = (bf16[64,4096]{1,0:T(8,128)(2,1)}, bf16[64,4096]{1,0:T(8,128)(2,1)S(1)}, u32[]{:S(2)}, u32[]{:S(2)}) collective-permute-start(bf16[64,4096]{1,0:T(8,128)(2,1)} %get-tuple-element.7), channel_id=1, source_target_pairs={{0,8},{8,16},{16,24},{1,9},{9,17},{17,25},{2,10},{10,18},{18,26},{... | collective-permute-start | bytes 1572872 | tf_op jit(solution)/shard_map/ppermute | solution.py:18
  22.6 11.8 %collective-permute-start.2 = (f32[256]{0:T(256)S(1)}, f32[256]{0:T(256)S(1)}, u32[]{:S(2)}, u32[]{:S(2)}) collective-permute-start(f32[256]{0:T(256)S(1)} %psum.7), channel_id=1, source_target_pairs={{0,8},{8,16},{16,24},{1,9},{9,17},{17,25},{2,10},{10,18},{18,26},{... | collective-permute-start | bytes 3080 | tf_op jit(solution)/shard_map/ppermute | solution.py:18
  26.4 18.5 %collective-permute-start.1 = (bf16[64,4096]{1,0:T(8,128)(2,1)}, bf16[64,4096]{1,0:T(8,128)(2,1)S(1)}, u32[]{:S(2)}, u32[]{:S(2)}) collective-permute-start(bf16[64,4096]{1,0:T(8,128)(2,1)} %get-tuple-element.5), channel_id=1, source_target_pairs={{0,8},{8,16},{16,24},{1,9},{9,17},{17,25},{2,10},{10,18},{18,26},{... | collective-permute-start | bytes 1572872 | tf_op jit(solution)/shard_map/ppermute | solution.py:18
  29.9 25.4 %collective-permute-start.3 = (bf16[64,4096]{1,0:T(8,128)(2,1)S(1)}, bf16[64,4096]{1,0:T(8,128)(2,1)S(1)}, u32[]{:S(2)}, u32[]{:S(2)}) collective-permute-start(bf16[64,4096]{1,0:T(8,128)(2,1)S(1)} %get-tuple-element.6), channel_id=1, source_target_pairs={{0,8},{8,16},{16,24},{1,9},{9,17},{17,25},{2,10},{10,18},{18,26},{... | collective-permute-start | bytes 1572872 | tf_op jit(solution)/shard_map/ppermute | solution.py:18
  31.8 33.5 %collective-permute-start.4 = (bf16[64,4096]{1,0:T(8,128)(2,1)S(1)}, bf16[64,4096]{1,0:T(8,128)(2,1)S(1)}, u32[]{:S(2)}, u32[]{:S(2)}) collective-permute-start(bf16[64,4096]{1,0:T(8,128)(2,1)S(1)} %get-tuple-element.8), channel_id=1, source_target_pairs={{0,8},{8,16},{16,24},{1,9},{9,17},{17,25},{2,10},{10,18},{18,26},{... | collective-permute-start | bytes 1572872 | tf_op jit(solution)/shard_map/ppermute | solution.py:18
  44.2 43.5 %reduce-scatter.5.cloned.1.call-start = ((), (), s32[]{:S(2)}) async-start(), calls=%async_computation.5 | async-start | bytes 655360 | tf_op jit(solution)/shard_map/reduce_scatter | solution.py:73
  54.9 57.0 %reduce-scatter.7.cloned.1.call-start = ((), (), s32[]{:S(2)}) async-start(), calls=%async_computation.6 | async-start | bytes 655360 | tf_op jit(solution)/shard_map/reduce_scatter | solution.py:73
  65.2 70.8 %reduce-scatter.9.cloned.1.call-start = ((), (), s32[]{:S(2)}) async-start(), calls=%async_computation.7 | async-start | bytes 655360 | tf_op jit(solution)/shard_map/reduce_scatter | solution.py:73
  75.7 3.9 %collective-permute-start = (s32[2,256]{1,0:T(2,128)S(1)}, s32[2,256]{1,0:T(2,128)S(1)}, u32[]{:S(2)}, u32[]{:S(2)}) collective-permute-start(s32[2,256]{1,0:T(2,128)S(1)} %pad_add_fusion), channel_id=1, source_target_pairs={{0,8},{8,16},{16,24},{1,9},{9,17},{17,25},{2,10},{10,18},{18,26},{... | collective-permute-start | bytes 6152 | tf_op jit(solution)/shard_map/ppermute | solution.py:18
Sparse Core Ops, SparseCore 0:
  44.4 19.2 reduce-scatter.10
  66.1 21.6 reduce-scatter.4
  90.3 21.6 reduce-scatter.6
  114.3 21.6 reduce-scatter.8

commit v2 on v1

--- a/solution.py
+++ b/solution.py
@@ -16,6 +16,24 @@
     devices = range(lax.axis_size(axis))
     route = [(i - distance, i) for i in devices if i - distance in devices]
     return lax.ppermute(block, axis, route)
+
+
+def scatter_sum(partial, axis):
+    size = lax.axis_size(axis)
+    me = lax.axis_index(axis)
+    rows, width = partial.shape
+    block = width // size
+    current = partial.reshape(rows, size, block)
+    bit = 1
+    while bit < size:
+        halves = current.reshape(rows, -1, 2, block)
+        mine_hi = (me // bit) % 2 == 1
+        keep = jnp.where(mine_hi, halves[:, :, 1], halves[:, :, 0])
+        send = jnp.where(mine_hi, halves[:, :, 0], halves[:, :, 1])
+        pairs = [(i, i ^ bit) for i in range(size)]
+        current = (keep + lax.ppermute(send, axis, pairs)).reshape(rows, -1, block)
+        bit *= 2
+    return current.reshape(rows, block)
 
 
 def rotate_keys(kv_rows, positions):
@@ -62,17 +80,16 @@
     scale = lax.rsqrt(sum_sq / D + EPSILON)
     gain = norm_gain[0]
     weight = w_kv[0]
-    step = tok_count // CHUNKS
-    pieces = []
+    local_width = tok_rows.shape[1]
+    step = local_width // CHUNKS
+    partial = None
     for k in range(CHUNKS):
-        rows = slice(k * step, (k + 1) * step)
-        arrived = shifted(tok_rows[rows], "section", 1)
-        normed = (arrived.astype(jnp.float32) * gain * scale[rows][:, None]).astype(jnp.bfloat16)
-        partial = jnp.dot(normed, weight, preferred_element_type=jnp.float32)
-        pieces.append(
-            lax.psum_scatter(partial, "tensor", scatter_dimension=1, tiled=True)
-        )
-    summed = jnp.concatenate(pieces, axis=0)
+        cols = slice(k * step, (k + 1) * step)
+        arrived = shifted(tok_rows[:, cols], "section", 1)
+        normed = (arrived.astype(jnp.float32) * gain[cols] * scale[:, None]).astype(jnp.bfloat16)
+        term = jnp.dot(normed, weight[cols], preferred_element_type=jnp.float32)
+        partial = term if partial is None else partial + term
+    summed = scatter_sum(partial, "tensor")
     local_cols = summed.shape[1]
     local_kv = summed.reshape(tok_count, local_cols // (2 * HD), 2, HD)
     result = rotate_keys(local_kv, position).reshape(tok_count, local_cols).astype(jnp.bfloat16)

time: 156 us -> 99.8 us (0.64)
  waiting for transfers between devices: 57.1 us -> 29 us
  matrix products: 39.4 us -> 16 us
  between operations: 14.6 us -> 1.62 us
  local copies, waits for them, and re-layouts: 4.72 us -> 11.8 us
  starting transfers between devices: 18.8 us -> 22.3 us
    reduce_scatter x4 -> x0, waiting for transfers between devices: 55.8 us -> none  [per_device(): lax.psum_scatter(partial, 'tensor', scatter_dimension=1, tiled=True)]
    dot_general x4, matrix products: 39.1 us -> 15.7 us  [per_device(): term = jnp.dot(normed, weight[cols], preferred_element_type=jnp.float32)]
    ppermute x6, waiting for transfers between devices: 1.28 us -> 16.8 us  [shifted(): return lax.ppermute(block, axis, route)]
    ppermute x0 -> x2, waiting for transfers between devices: none -> 12.2 us  [scatter_sum(): current = (keep + lax.ppermute(send, axis, pairs)).reshape(rows, -1, block)]
    unnamed x7 -> x9, local copies, waits for them, and re-layouts: 0.8 us -> 4.08 us
    another operation x1, local copies, waits for them, and re-layouts: 0.14 us -> 3.03 us  [scatter_sum(): halves = current.reshape(rows, -1, 2, block)]
    ppermute x6, starting transfers between devices: 18.7 us -> 20.6 us  [shifted(): return lax.ppermute(block, axis, route)]
    ppermute x0 -> x2, starting transfers between devices: none -> 1.66 us  [scatter_sum(): current = (keep + lax.ppermute(send, axis, pairs)).reshape(rows, -1, block)]
  transfers between devices with their start and end apart: 10 -> 8, of which waited for: 4 -> 4; matrix products, arithmetic and copies ran while one was open for 28% -> 14% of each run, Pallas kernels for 0% -> 0%
where the time goes in v2:
time: 99.8 us; the launch traced here: 99.3 us
  waiting for transfers between devices  29 us (29%)
  starting transfers between devices  22.3 us (22%)
  matrix products  16 us (16%)
  blocking collectives  15.1 us (15%)
  local copies, waits for them, and re-layouts  11.8 us (12%)
  other arithmetic  3.57 us (4%)
  between operations  1.62 us (2%)
    ppermute x6, starting transfers between devices, shifted(): return lax.ppermute(block, axis, route)  20.6 us
    ppermute x6, waiting for transfers between devices, shifted(): return lax.ppermute(block, axis, route)  16.8 us
    dot_general x4, matrix products, per_device(): term = jnp.dot(normed, weight[cols], preferred_element_type=jnp.float32)  15.7 us
    ppermute x2, waiting for transfers between devices, scatter_sum(): current = (keep + lax.ppermute(send, axis, pairs)).reshape(rows, -1, block)  12.2 us
    all_to_all x1, blocking collectives, per_device(): lax.all_to_all(packed, 'dp', split_axis=0, concat_axis=0, tiled=True)  8.74 us
    psum x1, blocking collectives, per_device(): sum_sq = lax.psum(jnp.sum(widened * widened, axis=1), 'tensor')  6.33 us
    unnamed x9, local copies, waits for them, and re-layouts  4.08 us
    another operation x1, local copies, waits for them, and re-layouts, scatter_sum(): halves = current.reshape(rows, -1, 2, block)  3.03 us
  transfers between devices with their start and end apart: 8, of which 4 were waited for; matrix products, arithmetic and copies ran while one was open for 14% of the time, Pallas kernels for 0%

profile of v2, /device:TPU:0, one launch (start us, length us, event | category | flops | bytes accessed | tf_op | source)
XLA Modules:
  0.0 99.3 jit_solution(7182129760131073400)
XLA Ops:
  0.0 1.8 %fusion.35 = (bf16[256,1024]{1,0:T(8,128)(2,1)S(1)}, bf16[256,1024]{1,0:T(8,128)(2,1)S(1)}, bf16[256,1024]{1,0:T(8,128)(2,1)S(1)}, bf16[256,1024]{1,0:T(8,128)(2,1)S(1)}) fusion(bf16[256,4096]{1,0:T(8,128)(2,1)} %bitcast.81), kind=kLoop, calls=%fused_computation.63 | loop fusion | bytes 4194304 | tf_op jit(solution)/shard_map/slice | solution.py:88
  1.8 5.7 %collective-permute-start.4 = (bf16[256,1024]{1,0:T(8,128)(2,1)S(1)}, bf16[256,1024]{1,0:T(8,128)(2,1)}, u32[]{:S(2)}, u32[]{:S(2)}) collective-permute-start(bf16[256,1024]{1,0:T(8,128)(2,1)S(1)} %get-tuple-element.8), channel_id=1, source_target_pairs={{0,8},{8,16},{16,24},{1,9},{9,17},{17,25},{2,10},{10,18},{18,26},{... | collective-permute-start | bytes 1572872 | tf_op jit(solution)/shard_map/ppermute | solution.py:18
  7.6 0.5 multiply_reduce_fusion
  8.1 6.3 %psum.7 = f32[256]{0:T(256)S(1)} all-reduce(f32[256]{0:T(256)S(1)} %multiply_reduce_fusion), channel_id=1, replica_groups=mesh['section'=4,'dp'=2,'tensor'=4] {'tensor'}, use_global_device_ids=true, to_apply=%region_4.5 | all-reduce | flops 256 | bytes 2048 | tf_op jit(solution)/shard_map/psum | solution.py:73
  14.4 3.1 %collective-permute-start.2 = (f32[256]{0:T(256)S(1)}, f32[256]{0:T(256)S(1)}, u32[]{:S(2)}, u32[]{:S(2)}) collective-permute-start(f32[256]{0:T(256)S(1)} %psum.7), channel_id=1, source_target_pairs={{0,8},{8,16},{16,24},{1,9},{9,17},{17,25},{2,10},{10,18},{18,26},{... | collective-permute-start | bytes 3080 | tf_op jit(solution)/shard_map/ppermute | solution.py:18
  17.5 4.3 %collective-permute-start.3 = (bf16[256,1024]{1,0:T(8,128)(2,1)S(1)}, bf16[256,1024]{1,0:T(8,128)(2,1)}, u32[]{:S(2)}, u32[]{:S(2)}) collective-permute-start(bf16[256,1024]{1,0:T(8,128)(2,1)S(1)} %get-tuple-element.9), channel_id=1, source_target_pairs={{0,8},{8,16},{16,24},{1,9},{9,17},{17,25},{2,10},{10,18},{18,26},{... | collective-permute-start | bytes 1572872 | tf_op jit(solution)/shard_map/ppermute | solution.py:18
  21.8 1.3 %collective-permute-start.1 = (bf16[256,1024]{1,0:T(8,128)(2,1)S(1)}, bf16[256,1024]{1,0:T(8,128)(2,1)S(1)}, u32[]{:S(2)}, u32[]{:S(2)}) collective-permute-start(bf16[256,1024]{1,0:T(8,128)(2,1)S(1)} %get-tuple-element.10), channel_id=1, source_target_pairs={{0,8},{8,16},{16,24},{1,9},{9,17},{17,25},{2,10},{10,18},{18,26},{... | collective-permute-start | bytes 1572872 | tf_op jit(solution)/shard_map/ppermute | solution.py:18
  23.1 1.8 %collective-permute-start.5 = (bf16[256,1024]{1,0:T(8,128)(2,1)S(1)}, bf16[256,1024]{1,0:T(8,128)(2,1)S(1)}, u32[]{:S(2)}, u32[]{:S(2)}) collective-permute-start(bf16[256,1024]{1,0:T(8,128)(2,1)S(1)} %get-tuple-element.7), channel_id=1, source_target_pairs={{0,8},{8,16},{16,24},{1,9},{9,17},{17,25},{2,10},{10,18},{18,26},{... | collective-permute-start | bytes 1572872 | tf_op jit(solution)/shard_map/ppermute | solution.py:18
  25.6 3.7 %fusion.2 = f32[256,2048]{1,0:T(8,128)S(1)} fusion(bf16[1,4096,2048]{2,1,0:T(8,128)(2,1)} %param.11, bf16[256,1024]{1,0:T(8,128)(2,1)} %collective-permute-done.4, f32[1024]{0:T(1024)S(1)} %bitcast.96, f32[256]{0:T(256)S(1)} %add_rsqrt_fusion), kind=kOutput, calls=%fused_computation.2 | convolution fusion | flops 1074790400 | bytes 6820864 | tf_op jit(solution)/shard_map/dot_general | solution.py:90
  29.3 4.0 %collective-permute-done.3 = bf16[256,1024]{1,0:T(8,128)(2,1)} collective-permute-done((bf16[256,1024]{1,0:T(8,128)(2,1)S(1)}, bf16[256,1024]{1,0:T(8,128)(2,1)}, u32[]{:S(2)}, u32[]{:S(2)}) %collective-permute-start.3) | collective-permute-done | bytes 524320 | tf_op jit(solution)/shard_map/ppermute | solution.py:18
  33.3 3.7 %fusion.4 = f32[256,2048]{1,0:T(8,128)S(1)} fusion(bf16[1,4096,2048]{2,1,0:T(8,128)(2,1)} %param.11, bf16[256,1024]{1,0:T(8,128)(2,1)} %collective-permute-done.3, f32[1024]{0:T(1024)S(1)} %bitcast.95, f32[256]{0:T(256)S(1)} %add_rsqrt_fusion), kind=kOutput, calls=%fused_computation.4 | convolution fusion | flops 1074790400 | bytes 6820864 | tf_op jit(solution)/shard_map/dot_general | solution.py:90
  37.0 7.6 %collective-permute-done.1 = bf16[256,1024]{1,0:T(8,128)(2,1)S(1)} collective-permute-done((bf16[256,1024]{1,0:T(8,128)(2,1)S(1)}, bf16[256,1024]{1,0:T(8,128)(2,1)S(1)}, u32[]{:S(2)}, u32[]{:S(2)}) %collective-permute-start.1) | collective-permute-done | bytes 524320 | tf_op jit(solution)/shard_map/ppermute | solution.py:18
  44.6 3.5 %fusion.18 = f32[256,2048]{1,0:T(8,128)S(1)} fusion(f32[256,2048]{1,0:T(8,128)S(1)} %fusion.2, f32[256,2048]{1,0:T(8,128)S(1)} %fusion.4, bf16[1,4096,2048]{2,1,0:T(8,128)(2,1)} %param.11, bf16[256,1024]{1,0:T(8,128)(2,1)S(1)} %collective-permute-done.1, f32[256]{0:T(256)S(1)} %add_rsqrt_fusion, f32[1024]{0:T(1024)S(1)} %bitcast.87), kind=kOutput, calls=%fused_computation.15 | convolution fusion | flops 1075838976 | bytes 11015168 | tf_op jit(solution)/shard_map/dot_general | solution.py:90
  48.1 5.3 %collective-permute-done.5 = bf16[256,1024]{1,0:T(8,128)(2,1)S(1)} collective-permute-done((bf16[256,1024]{1,0:T(8,128)(2,1)S(1)}, bf16[256,1024]{1,0:T(8,128)(2,1)S(1)}, u32[]{:S(2)}, u32[]{:S(2)}) %collective-permute-start.5) | collective-permute-done | bytes 524320 | tf_op jit(solution)/shard_map/ppermute | solution.py:18
  53.3 4.9 %fusion.15 = f32[256,2048]{1,0:T(8,128)} fusion(f32[256,2048]{1,0:T(8,128)S(1)} %fusion.18, bf16[1,4096,2048]{2,1,0:T(8,128)(2,1)} %param.11, bf16[256,1024]{1,0:T(8,128)(2,1)S(1)} %collective-permute-done.5, f32[1024]{0:T(1024)S(1)} %bitcast.88, f32[256]{0:T(256)S(1)} %add_rsqrt_fusion), kind=kOutput, calls=%fused_computation.14 | convolution fusion | flops 1075314688 | bytes 8918016 | tf_op jit(solution)/shard_map/dot_general | solution.py:90
  58.2 3.0 %reshape_reshape.6 = f32[256,2,2,512]{3,2,1,0:T(2,128)S(1)} reshape(f32[256,2048]{1,0:T(8,128)} %fusion.15) | data formatting | bytes 4194304 | tf_op jit(solution)/shard_map/reshape;reshape | solution.py:29
  61.2 2.6 %fusion.34 = (f32[256,2,1,512]{3,2,1,0:T(1,128)S(1)}, f32[256,2,1,512]{3,2,1,0:T(1,128)}) fusion(f32[256,2,2,512]{3,2,1,0:T(2,128)S(1)} %reshape_reshape.6), kind=kLoop, calls=%fused_computation.62 | loop fusion | bytes 4194304 | tf_op jit(solution)/shard_map/slice | solution.py:31
  63.8 2.4 %copy.31 = f32[256,2,1,512]{0,3,1,2:T(8,128)S(1)} copy(f32[256,2,1,512]{3,2,1,0:T(1,128)} %get-tuple-element.6) | data formatting | bytes 2097152
  66.2 1.0 copy.30
  67.2 0.1 select_bitcast_fusion
  67.4 0.6 reduce-window.6
  68.0 0.2 slice_reduce_fusion
  68.3 0.2 reduce-window.9
  69.2 4.4 %collective-permute-start = (s32[2,256]{1,0:T(2,128)S(1)}, s32[2,256]{1,0:T(2,128)S(1)}, u32[]{:S(2)}, u32[]{:S(2)}) collective-permute-start(s32[2,256]{1,0:T(2,128)S(1)} %pad_add_fusion), channel_id=1, source_target_pairs={{0,8},{8,16},{16,24},{1,9},{9,17},{17,25},{2,10},{10,18},{18,26},{... | collective-permute-start | bytes 6152 | tf_op jit(solution)/shard_map/ppermute | solution.py:18
  73.7 1.4 %fusion.21 = f32[256,1,2,512]{0,3,2,1:T(8,128)S(1)} fusion(f32[256,2,512]{0,2,1:T(8,128)} %collective-permute-done.6, f32[256,2,1,512]{0,3,1,2:T(8,128)S(1)} %copy.30, f32[256,2,1,512]{0,3,1,2:T(8,128)S(1)} %copy.31, pred[]{:T(512)S(6)} %eq.66), kind=kLoop, calls=%fused_computation.18 | loop fusion | flops 524288 | bytes 4194305 | tf_op jit(solution)/shard_map/reshape | solution.py:29
  75.2 1.6 %collective-permute-start.7 = (f32[256,1,512]{0,2,1:T(8,128)S(1)}, f32[256,1,512]{0,2,1:T(8,128)S(1)}, u32[]{:S(2)}, u32[]{:S(2)}) collective-permute-start(f32[256,1,512]{0,2,1:T(8,128)S(1)} %select_bitcast_fusion.1), channel_id=1, source_target_pairs={{0,2},{1,3},{2,0},{3,1},{4,6},{5,7},{6,4},{7,5},{8,10},{9,11},{10,... | collective-permute-start | bytes 1572872 | tf_op jit(solution)/shard_map/ppermute | solution.py:34
  76.8 0.3 multiply_cosine_fusion
  77.1 12.2 %collective-permute-done.7 = f32[256,1,512]{0,2,1:T(8,128)S(1)} collective-permute-done((f32[256,1,512]{0,2,1:T(8,128)S(1)}, f32[256,1,512]{0,2,1:T(8,128)S(1)}, u32[]{:S(2)}, u32[]{:S(2)}) %collective-permute-start.7) | collective-permute-done | bytes 524320 | tf_op jit(solution)/shard_map/ppermute | solution.py:34
  89.3 0.1 bitcast_add_fusion.1
  89.5 0.3 convolution_convert_fusion
  89.8 8.7 %all_to_all.5 = bf16[2,192,512]{2,1,0:T(8,128)(2,1)S(1)} all-to-all(bf16[2,192,512]{2,1,0:T(8,128)(2,1)S(1)} %bitcast.84), channel_id=1, replica_groups=mesh['section'=4,'dp'=2,'tensor'=4] {'dp'}, dimensions={0} | all-to-all | bytes 786432 | tf_op jit(solution)/shard_map/all_to_all | solution.py:102
  98.6 0.7 copy.37
  (28 shorter events, 0.4 us)
Async XLA Ops:
  0.0 7.6 %copy-start = (bf16[1,1,256,4096]{3,2,1,0:T(8,128)(2,1)S(1)}, bf16[1,1,256,4096]{3,2,1,0:T(8,128)(2,1)}, u32[]{:S(2)}) copy-start(bf16[1,1,256,4096]{3,2,1,0:T(8,128)(2,1)} %param.6) | copy-start | bytes 6291460
  0.0 25.6 %copy-start.1 = (f32[1,4096]{1,0:T(1,128)S(1)}, f32[1,4096]{1,0:T(1,128)}, u32[]{:S(2)}) copy-start(f32[1,4096]{1,0:T(1,128)} %param.10) | copy-start | bytes 49156
  1.8 23.8 %collective-permute-start.4 = (bf16[256,1024]{1,0:T(8,128)(2,1)S(1)}, bf16[256,1024]{1,0:T(8,128)(2,1)}, u32[]{:S(2)}, u32[]{:S(2)}) collective-permute-start(bf16[256,1024]{1,0:T(8,128)(2,1)S(1)} %get-tuple-element.8), channel_id=1, source_target_pairs={{0,8},{8,16},{16,24},{1,9},{9,17},{17,25},{2,10},{10,18},{18,26},{... | collective-permute-start | bytes 1572872 | tf_op jit(solution)/shard_map/ppermute | solution.py:18
  14.4 11.2 %collective-permute-start.2 = (f32[256]{0:T(256)S(1)}, f32[256]{0:T(256)S(1)}, u32[]{:S(2)}, u32[]{:S(2)}) collective-permute-start(f32[256]{0:T(256)S(1)} %psum.7), channel_id=1, source_target_pairs={{0,8},{8,16},{16,24},{1,9},{9,17},{17,25},{2,10},{10,18},{18,26},{... | collective-permute-start | bytes 3080 | tf_op jit(solution)/shard_map/ppermute | solution.py:18
  17.5 15.8 %collective-permute-start.3 = (bf16[256,1024]{1,0:T(8,128)(2,1)S(1)}, bf16[256,1024]{1,0:T(8,128)(2,1)}, u32[]{:S(2)}, u32[]{:S(2)}) collective-permute-start(bf16[256,1024]{1,0:T(8,128)(2,1)S(1)} %get-tuple-element.9), channel_id=1, source_target_pairs={{0,8},{8,16},{16,24},{1,9},{9,17},{17,25},{2,10},{10,18},{18,26},{... | collective-permute-start | bytes 1572872 | tf_op jit(solution)/shard_map/ppermute | solution.py:18
  21.8 22.7 %collective-permute-start.1 = (bf16[256,1024]{1,0:T(8,128)(2,1)S(1)}, bf16[256,1024]{1,0:T(8,128)(2,1)S(1)}, u32[]{:S(2)}, u32[]{:S(2)}) collective-permute-start(bf16[256,1024]{1,0:T(8,128)(2,1)S(1)} %get-tuple-element.10), channel_id=1, source_target_pairs={{0,8},{8,16},{16,24},{1,9},{9,17},{17,25},{2,10},{10,18},{18,26},{... | collective-permute-start | bytes 1572872 | tf_op jit(solution)/shard_map/ppermute | solution.py:18
  23.1 30.2 %collective-permute-start.5 = (bf16[256,1024]{1,0:T(8,128)(2,1)S(1)}, bf16[256,1024]{1,0:T(8,128)(2,1)S(1)}, u32[]{:S(2)}, u32[]{:S(2)}) collective-permute-start(bf16[256,1024]{1,0:T(8,128)(2,1)S(1)} %get-tuple-element.7), channel_id=1, source_target_pairs={{0,8},{8,16},{16,24},{1,9},{9,17},{17,25},{2,10},{10,18},{18,26},{... | collective-permute-start | bytes 1572872 | tf_op jit(solution)/shard_map/ppermute | solution.py:18
  63.8 3.6 %copy-start.2 = (s32[1,1,256,1]{2,3,1,0:T(1,128)S(1)}, s32[1,1,256,1]{2,3,1,0:T(1,128)}, u32[]{:S(2)}) copy-start(s32[1,1,256,1]{2,3,1,0:T(1,128)} %param.7) | copy-start | bytes 3076
  67.3 6.3 %collective-permute-start.6 = (f32[256,2,512]{0,2,1:T(8,128)S(1)}, f32[256,2,512]{0,2,1:T(8,128)}, u32[]{:S(2)}, u32[]{:S(2)}) collective-permute-start(f32[256,2,512]{0,2,1:T(8,128)S(1)} %select_bitcast_fusion), channel_id=1, source_target_pairs={{0,1},{1,0},{2,3},{3,2},{4,5},{5,4},{6,7},{7,6},{8,9},{9,8},{10,11... | collective-permute-start | bytes 3145736 | tf_op jit(solution)/shard_map/ppermute | solution.py:34
  69.2 7.6 %collective-permute-start = (s32[2,256]{1,0:T(2,128)S(1)}, s32[2,256]{1,0:T(2,128)S(1)}, u32[]{:S(2)}, u32[]{:S(2)}) collective-permute-start(s32[2,256]{1,0:T(2,128)S(1)} %pad_add_fusion), channel_id=1, source_target_pairs={{0,8},{8,16},{16,24},{1,9},{9,17},{17,25},{2,10},{10,18},{18,26},{... | collective-permute-start | bytes 6152 | tf_op jit(solution)/shard_map/ppermute | solution.py:18
  75.2 14.1 %collective-permute-start.7 = (f32[256,1,512]{0,2,1:T(8,128)S(1)}, f32[256,1,512]{0,2,1:T(8,128)S(1)}, u32[]{:S(2)}, u32[]{:S(2)}) collective-permute-start(f32[256,1,512]{0,2,1:T(8,128)S(1)} %select_bitcast_fusion.1), channel_id=1, source_target_pairs={{0,2},{1,3},{2,0},{3,1},{4,6},{5,7},{6,4},{7,5},{8,10},{9,11},{10,... | collective-permute-start | bytes 1572872 | tf_op jit(solution)/shard_map/ppermute | solution.py:34

commit v3 on v2

v3 whole, which is shorter than its diff:
```python
import jax
import jax.numpy as jnp
from jax import lax
from jax.sharding import PartitionSpec as P

D = 16384
HD = 128


EPSILON = 1e-05
ROPE_BASE = 500000.0
CHUNKS = 4


def shifted(block, axis, distance):
    devices = range(lax.axis_size(axis))
    route = [(i - distance, i) for i in devices if i - distance in devices]
    return lax.ppermute(block, axis, route)


def scatter_sum(partial, axis):
    size = lax.axis_size(axis)
    me = lax.axis_index(axis)
    levels = size.bit_length() - 1
    width, rows = partial.shape
    current = partial.reshape((2,) * levels + (width // size, rows))
    bit = 1
    while bit < size:
        mine = (me // bit) % 2
        where = current.ndim - 3
        keep = lax.dynamic_index_in_dim(current, mine, where, keepdims=False)
        send = lax.dynamic_index_in_dim(current, 1 - mine, where, keepdims=False)
        pairs = [(i, i ^ bit) for i in range(size)]
        current = keep + lax.ppermute(send, axis, pairs)
        bit *= 2
    return current


def rotate_keys(kv_cols, positions):
    head_size = kv_cols.shape[2]
    half_size = head_size // 2
    inverse = ROPE_BASE ** (-(jnp.arange(half_size, dtype=jnp.float32) * 2.0 / head_size))
    angles = inverse[:, None] * positions.astype(jnp.float32)[None, :]
    cosines = jnp.cos(angles)[None]
    sines = jnp.sin(angles)[None]
    key_part = kv_cols[:, 0]
    front_half = key_part[:, :half_size]
    back_half = key_part[:, half_size:]
    rotated = jnp.concatenate(
        [front_half * cosines - back_half * sines, back_half * cosines + front_half * sines],
        axis=1,
    )
    return jnp.stack([rotated, kv_cols[:, 1]], axis=1)


def per_device(hidden, owner, start, live, norm_gain, w_kv):
    groups = lax.axis_size("dp")
    tok_count = hidden.shape[2]
    capacity = 3 * tok_count // (2 * groups)
    slot_count = capacity * groups

    tok_rows = hidden[0, 0]
    target = owner[0, 0, :, 0]
    row_index = jnp.arange(tok_count, dtype=jnp.int32)
    row_alive = row_index < live[0, 0]
    onehot = (
        (target[:, None] == jnp.arange(groups, dtype=jnp.int32)[None, :]) & row_alive[:, None]
    ).astype(jnp.int32)
    row_rank = jnp.sum((jnp.cumsum(onehot, axis=0) - onehot) * onehot, axis=1)
    row_slot = jnp.where(row_alive, target * capacity + row_rank, slot_count)
    position = start[0, 0] + row_index
    widened = tok_rows.astype(jnp.float32)
    sum_sq = lax.psum(jnp.sum(widened * widened, axis=1), "tensor")
    meta = jnp.stack([sum_sq, row_slot.astype(jnp.float32), position.astype(jnp.float32)])
    meta = shifted(meta, "section", 1)
    sum_sq = meta[0]

    first = lax.axis_index("section") == 0
    row_slot = jnp.where(first, slot_count, meta[1].astype(jnp.int32))
    position = meta[2].astype(jnp.int32)
    scale = lax.rsqrt(sum_sq / D + EPSILON)
    gain = norm_gain[0]
    weight = w_kv[0]
    local_width = tok_rows.shape[1]
    step = local_width // CHUNKS
    partial = None
    for k in range(CHUNKS):
        cols = slice(k * step, (k + 1) * step)
        arrived = shifted(tok_rows[:, cols], "section", 1)
        normed = (arrived.astype(jnp.float32) * gain[cols] * scale[:, None]).astype(jnp.bfloat16)
        term = lax.dot_general(
            weight[cols], normed, (((0,), (1,)), ((), ())), preferred_element_type=jnp.float32
        )
        partial = term if partial is None else partial + term
    summed = scatter_sum(partial, "tensor")
    local_cols = summed.shape[0]
    local_kv = summed.reshape(local_cols // (2 * HD), 2, HD, tok_count)
    result = rotate_keys(local_kv, position).reshape(local_cols, tok_count).astype(jnp.bfloat16)

    placing = row_slot[None, :] == jnp.arange(slot_count, dtype=jnp.int32)[:, None]
    packed = lax.dot_general(
        placing.astype(jnp.bfloat16), result, (((1,), (1,)), ((), ())),
        preferred_element_type=jnp.float32,
    ).astype(jnp.bfloat16)
    packed = packed.reshape(groups, capacity, local_cols)
    me = lax.axis_index("dp")
    received = [None] * groups
    received[0] = lax.dynamic_index_in_dim(packed, me, 0, keepdims=False)
    for offset in range(1, groups):
        outgoing = lax.dynamic_index_in_dim(packed, (me + offset) % groups, 0, keepdims=False)
        pairs = [(i, (i + offset) % groups) for i in range(groups)]
        received[offset] = lax.ppermute(outgoing, "dp", pairs)
    stacked = jnp.stack(received)
    routed = jnp.take(stacked, (me - jnp.arange(groups, dtype=jnp.int32)) % groups, axis=0)
    return routed.reshape(1, 1, slot_count, local_cols)


def solution(mesh):
    in_specs = (
        P("section", "dp", None, "tensor"),
        P("section", "dp", None, None),
        P("section", "dp"),
        P("section", "dp"),
        P("section", "tensor"),
        P("section", "tensor", None),
    )
    out_specs = P("section", "dp", None, "tensor")
    return jax.shard_map(
        per_device, mesh=mesh, in_specs=in_specs, out_specs=out_specs, check_vma=False
    )
```

time: 99.8 us -> 95.9 us (0.961)
  blocking collectives: 15.1 us -> 6.33 us
  waiting for transfers between devices: 29 us -> 35.9 us
  starting transfers between devices: 22.3 us -> 19.4 us
  local copies, waits for them, and re-layouts: 11.8 us -> 13.3 us
    all_to_all x1 -> x0, blocking collectives: 8.74 us -> none  [per_device(): lax.all_to_all(packed, 'dp', split_axis=0, concat_axis=0, tiled=True)]
    ppermute x2 -> x3, waiting for transfers between devices: 12.2 us -> 18.4 us  [the longest x2 13.8 us: scatter_sum(): current = keep + lax.ppermute(send, axis, pairs)]
    ppermute x6 -> x5, starting transfers between devices: 20.6 us -> 16.2 us  [shifted(): return lax.ppermute(block, axis, route)]
    another operation x1 -> x0, local copies, waits for them, and re-layouts: 3.03 us -> none  [scatter_sum(): halves = current.reshape(rows, -1, 2, block)]
    reshape x0 -> x1, local copies, waits for them, and re-layouts: none -> 3.03 us  [scatter_sum(): current = partial.reshape((2,) * levels + (width // size, rows))]
    dynamic_slice x0 -> x2, local copies, waits for them, and re-layouts: none -> 2.82 us  [the longest x1 2.78 us: scatter_sum(): keep = lax.dynamic_index_in_dim(current, mine, where, keepdims=False)]
    slice x3 -> x2, local copies, waits for them, and re-layouts: 2.83 us -> 0.23 us  [the longest x1 2.6 us: scatter_sum(): keep = jnp.where(mine_hi, halves[:, :, 1], halves[:, :, 0])]
    ppermute x2 -> x3, starting transfers between devices: 1.66 us -> 3.15 us  [the longest x2 1.59 us: scatter_sum(): current = keep + lax.ppermute(send, axis, pairs)]
  transfers between devices with their start and end apart: 8 -> 8, of which waited for: 4 -> 6; matrix products, arithmetic and copies ran while one was open for 14% -> 15% of each run, Pallas kernels for 0% -> 0%
where the time goes in v3:
time: 95.9 us; the launch traced here: 95.5 us
  waiting for transfers between devices  35.9 us (37%)
  starting transfers between devices  19.4 us (20%)
  matrix products  16 us (17%)
  local copies, waits for them, and re-layouts  13.3 us (14%)
  blocking collectives  6.33 us (7%)
  other arithmetic  2.99 us (3%)
  between operations  1.59 us (2%)
    ppermute x5, waiting for transfers between devices, shifted(): return lax.ppermute(block, axis, route)  17.5 us
    ppermute x5, starting transfers between devices, shifted(): return lax.ppermute(block, axis, route)  16.2 us
    dot_general x4, matrix products, per_device(): lax.dot_general(weight[cols], normed, (((0,), (1,)), ((), ())), preferred...  15.7 us
    ppermute x2, waiting for transfers between devices, scatter_sum(): current = keep + lax.ppermute(send, axis, pairs)  13.8 us
    psum x1, blocking collectives, per_device(): sum_sq = lax.psum(jnp.sum(widened * widened, axis=1), 'tensor')  6.33 us
    ppermute x1, waiting for transfers between devices, per_device(): received[offset] = lax.ppermute(outgoing, 'dp', pairs)  4.57 us
    unnamed x8, local copies, waits for them, and re-layouts  4.57 us
    reshape x1, local copies, waits for them, and re-layouts, scatter_sum(): current = partial.reshape((2,) * levels + (width // size, rows))  3.03 us
  transfers between devices with their start and end apart: 8, of which 6 were waited for; matrix products, arithmetic and copies ran while one was open for 15% of the time, Pallas kernels for 0%

profile of v3, /device:TPU:0, one launch (start us, length us, event | category | flops | bytes accessed | tf_op | source)
XLA Modules:
  0.0 95.5 jit_solution(8978862750045280066)
XLA Ops:
  0.0 1.8 %fusion.43 = (bf16[256,1024]{1,0:T(8,128)(2,1)S(1)}, bf16[256,1024]{1,0:T(8,128)(2,1)S(1)}, bf16[256,1024]{1,0:T(8,128)(2,1)S(1)}, bf16[256,1024]{1,0:T(8,128)(2,1)S(1)}) fusion(bf16[256,4096]{1,0:T(8,128)(2,1)} %bitcast.89), kind=kLoop, calls=%fused_computation.86 | loop fusion | bytes 4194304 | tf_op jit(solution)/shard_map/slice | solution.py:89
  1.9 5.7 %collective-permute-start.3 = (bf16[256,1024]{1,0:T(8,128)(2,1)S(1)}, bf16[256,1024]{1,0:T(8,128)(2,1)}, u32[]{:S(2)}, u32[]{:S(2)}) collective-permute-start(bf16[256,1024]{1,0:T(8,128)(2,1)S(1)} %get-tuple-element.8), channel_id=1, source_target_pairs={{0,8},{8,16},{16,24},{1,9},{9,17},{17,25},{2,10},{10,18},{18,26},{... | collective-permute-start | bytes 1572872 | tf_op jit(solution)/shard_map/ppermute | solution.py:18
  7.6 0.5 multiply_reduce_fusion
  8.8 0.6 reduce-window.6
  9.4 0.2 slice_reduce_fusion
  9.6 0.2 reduce-window.9
  10.5 6.3 %psum.7 = f32[1,256]{1,0:T(1,128)S(1)} all-reduce(f32[1,256]{1,0:T(1,128)S(1)} %bitcast.105), channel_id=1, replica_groups=mesh['section'=4,'dp'=2,'tensor'=4] {'tensor'}, use_global_device_ids=true, to_apply=%region_1.2 | all-reduce | flops 256 | bytes 2048 | tf_op jit(solution)/shard_map/psum | solution.py:73
  16.9 3.1 %collective-permute-start = (f32[3,256]{1,0:T(4,128)S(1)}, f32[3,256]{1,0:T(4,128)S(1)}, u32[]{:S(2)}, u32[]{:S(2)}) collective-permute-start(f32[3,256]{1,0:T(4,128)S(1)} %pad_maximum_fusion.2), channel_id=1, source_target_pairs={{0,8},{8,16},{16,24},{1,9},{9,17},{17,25},{2,10},{10,18},{18,26},{... | collective-permute-start | bytes 9224 | tf_op jit(solution)/shard_map/ppermute | solution.py:18
  20.1 4.3 %collective-permute-start.2 = (bf16[256,1024]{1,0:T(8,128)(2,1)S(1)}, bf16[256,1024]{1,0:T(8,128)(2,1)}, u32[]{:S(2)}, u32[]{:S(2)}) collective-permute-start(bf16[256,1024]{1,0:T(8,128)(2,1)S(1)} %get-tuple-element.9), channel_id=1, source_target_pairs={{0,8},{8,16},{16,24},{1,9},{9,17},{17,25},{2,10},{10,18},{18,26},{... | collective-permute-start | bytes 1572872 | tf_op jit(solution)/shard_map/ppermute | solution.py:18
  24.3 1.3 %collective-permute-start.1 = (bf16[256,1024]{1,0:T(8,128)(2,1)S(1)}, bf16[256,1024]{1,0:T(8,128)(2,1)S(1)}, u32[]{:S(2)}, u32[]{:S(2)}) collective-permute-start(bf16[256,1024]{1,0:T(8,128)(2,1)S(1)} %get-tuple-element.10), channel_id=1, source_target_pairs={{0,8},{8,16},{16,24},{1,9},{9,17},{17,25},{2,10},{10,18},{18,26},{... | collective-permute-start | bytes 1572872 | tf_op jit(solution)/shard_map/ppermute | solution.py:18
  25.7 1.8 %collective-permute-start.4 = (bf16[256,1024]{1,0:T(8,128)(2,1)S(1)}, bf16[256,1024]{1,0:T(8,128)(2,1)S(1)}, u32[]{:S(2)}, u32[]{:S(2)}) collective-permute-start(bf16[256,1024]{1,0:T(8,128)(2,1)S(1)} %get-tuple-element.7), channel_id=1, source_target_pairs={{0,8},{8,16},{16,24},{1,9},{9,17},{17,25},{2,10},{10,18},{18,26},{... | collective-permute-start | bytes 1572872 | tf_op jit(solution)/shard_map/ppermute | solution.py:18
  27.5 3.7 %fusion.2 = f32[256,2048]{1,0:T(8,128)S(1)} fusion(bf16[1,4096,2048]{2,1,0:T(8,128)(2,1)} %param.11, bf16[256,1024]{1,0:T(8,128)(2,1)} %collective-permute-done.3, f32[1024]{0:T(1024)S(1)} %bitcast.110, f32[256]{0:T(256)S(1)} %bitcast.96), kind=kOutput, calls=%fused_computation.3 | convolution fusion | flops 1074790400 | bytes 6820864 | tf_op jit(solution)/shard_map/dot_general | solution.py:91
  31.2 4.6 %collective-permute-done.2 = bf16[256,1024]{1,0:T(8,128)(2,1)} collective-permute-done((bf16[256,1024]{1,0:T(8,128)(2,1)S(1)}, bf16[256,1024]{1,0:T(8,128)(2,1)}, u32[]{:S(2)}, u32[]{:S(2)}) %collective-permute-start.2) | collective-permute-done | bytes 524320 | tf_op jit(solution)/shard_map/ppermute | solution.py:18
  35.8 3.7 %fusion.4 = f32[256,2048]{1,0:T(8,128)S(1)} fusion(bf16[1,4096,2048]{2,1,0:T(8,128)(2,1)} %param.11, bf16[256,1024]{1,0:T(8,128)(2,1)} %collective-permute-done.2, f32[1024]{0:T(1024)S(1)} %bitcast.109, f32[256]{0:T(256)S(1)} %bitcast.97), kind=kOutput, calls=%fused_computation.5 | convolution fusion | flops 1074790400 | bytes 6820864 | tf_op jit(solution)/shard_map/dot_general | solution.py:91
  39.5 7.6 %collective-permute-done.1 = bf16[256,1024]{1,0:T(8,128)(2,1)S(1)} collective-permute-done((bf16[256,1024]{1,0:T(8,128)(2,1)S(1)}, bf16[256,1024]{1,0:T(8,128)(2,1)S(1)}, u32[]{:S(2)}, u32[]{:S(2)}) %collective-permute-start.1) | collective-permute-done | bytes 524320 | tf_op jit(solution)/shard_map/ppermute | solution.py:18
  47.1 3.5 %fusion.21 = f32[256,2048]{1,0:T(8,128)S(1)} fusion(f32[256,2048]{1,0:T(8,128)S(1)} %fusion.2, f32[256,2048]{1,0:T(8,128)S(1)} %fusion.4, bf16[1,4096,2048]{2,1,0:T(8,128)(2,1)} %param.11, bf16[256,1024]{1,0:T(8,128)(2,1)S(1)} %collective-permute-done.1, f32[256]{0:T(256)S(1)} %bitcast.98, f32[1024]{0:T(1024)S(1)} %bitcast.100), kind=kOutput, calls=%fused_computation.17 | convolution fusion | flops 1075838976 | bytes 11015168 | tf_op jit(solution)/shard_map/dot_general | solution.py:91
  50.6 5.3 %collective-permute-done.4 = bf16[256,1024]{1,0:T(8,128)(2,1)S(1)} collective-permute-done((bf16[256,1024]{1,0:T(8,128)(2,1)S(1)}, bf16[256,1024]{1,0:T(8,128)(2,1)S(1)}, u32[]{:S(2)}, u32[]{:S(2)}) %collective-permute-start.4) | collective-permute-done | bytes 524320 | tf_op jit(solution)/shard_map/ppermute | solution.py:18
  55.9 4.9 %fusion.18 = f32[2048,256]{0,1:T(8,128)} fusion(f32[256,2048]{1,0:T(8,128)S(1)} %fusion.21, bf16[1,4096,2048]{2,1,0:T(8,128)(2,1)} %param.11, bf16[256,1024]{1,0:T(8,128)(2,1)S(1)} %collective-permute-done.4, f32[1024]{0:T(1024)S(1)} %bitcast.101, f32[256]{0:T(256)S(1)} %bitcast.99), kind=kOutput, calls=%fused_computation.16 | convolution fusion | flops 1075314688 | bytes 8918016 | tf_op jit(solution)/shard_map/dot_general | solution.py:91
  60.7 3.0 %reshape.257 = f32[2,2,512,256]{2,1,0,3:T(2,128)S(1)} reshape(f32[2048,256]{0,1:T(8,128)} %fusion.18) | data formatting | bytes 4194304 | tf_op jit(solution)/shard_map/reshape | solution.py:26
  63.8 2.8 %constant_dynamic-slice_fusion.2 = (f32[2,1,512,256]{2,1,0,3:T(1,128)S(1)}, f32[2,1,512,256]{2,1,0,3:T(1,128)}) fusion(f32[2,2,512,256]{2,1,0,3:T(2,128)S(1)} %reshape.257, s32[]{:T(128)S(6)} %select_n.111, s32[]{:T(128)S(6)} %select_n.112), kind=kLoop, calls=%fused_computation.70 | loop fusion | bytes 4194312 | tf_op jit(solution)/shard_map/jit(dynamic_index_in_dim)/dynamic_slice | solution.py:31
  66.5 3.6 %copy.14 = f32[2,1,512,256]{3,2,0,1:T(8,128)} copy(f32[2,1,512,256]{2,1,0,3:T(1,128)} %get-tuple-element.6) | data formatting | bytes 2097152
  70.3 0.9 copy.13
  71.3 1.7 %collective-permute-done.5 = f32[2,512,256]{2,1,0:T(8,128)S(1)} collective-permute-done((f32[2,512,256]{2,1,0:T(8,128)}, f32[2,512,256]{2,1,0:T(8,128)S(1)}, u32[]{:S(2)}, u32[]{:S(2)}) %collective-permute-start.5) | collective-permute-done | bytes 1048608 | tf_op jit(solution)/shard_map/ppermute | solution.py:34
  73.0 0.1 bitcast_add_fusion
  73.2 1.6 %collective-permute-start.6 = (f32[512,256]{1,0:T(8,128)S(1)}, f32[512,256]{1,0:T(8,128)S(1)}, u32[]{:S(2)}, u32[]{:S(2)}) collective-permute-start(f32[512,256]{1,0:T(8,128)S(1)} %dynamic-slice_bitcast_fusion), channel_id=1, source_target_pairs={{0,2},{1,3},{2,0},{3,1},{4,6},{5,7},{6,4},{7,5},{8,10},{9,11},{10,... | collective-permute-start | bytes 1572872 | tf_op jit(solution)/shard_map/ppermute | solution.py:34
  74.8 0.3 multiply_cosine_fusion
  75.1 12.1 %collective-permute-done.6 = f32[512,256]{1,0:T(8,128)S(1)} collective-permute-done((f32[512,256]{1,0:T(8,128)S(1)}, f32[512,256]{1,0:T(8,128)S(1)}, u32[]{:S(2)}, u32[]{:S(2)}) %collective-permute-start.6) | collective-permute-done | bytes 524320 | tf_op jit(solution)/shard_map/ppermute | solution.py:34
  87.5 0.3 convolution_convert_fusion
  87.8 1.6 %collective-permute-start.7 = (bf16[192,512]{1,0:T(8,128)(2,1)S(1)}, bf16[192,512]{1,0:T(8,128)(2,1)S(1)}, u32[]{:S(2)}, u32[]{:S(2)}) collective-permute-start(bf16[192,512]{1,0:T(8,128)(2,1)S(1)} %get-tuple-element.12), channel_id=1, source_target_pairs={{0,4},{4,0},{1,5},{5,1},{2,6},{6,2},{3,7},{7,3},{8,12},{12,8},{9,1... | collective-permute-start | bytes 589832 | tf_op jit(solution)/shard_map/ppermute | solution.py:112
  89.4 4.6 %collective-permute-done.7 = bf16[192,512]{1,0:T(8,128)(2,1)S(1)} collective-permute-done((bf16[192,512]{1,0:T(8,128)(2,1)S(1)}, bf16[192,512]{1,0:T(8,128)(2,1)S(1)}, u32[]{:S(2)}, u32[]{:S(2)}) %collective-permute-start.7) | collective-permute-done | bytes 196640 | tf_op jit(solution)/shard_map/ppermute | solution.py:112
  94.0 0.6 gather_fusion
  94.6 0.9 broadcast_select_fusion
  (34 shorter events, 0.7 us)
Async XLA Ops:
  0.0 7.6 %copy-start = (bf16[1,1,256,4096]{3,2,1,0:T(8,128)(2,1)S(1)}, bf16[1,1,256,4096]{3,2,1,0:T(8,128)(2,1)}, u32[]{:S(2)}) copy-start(bf16[1,1,256,4096]{3,2,1,0:T(8,128)(2,1)} %param.6) | copy-start | bytes 6291460
  0.0 8.8 %copy-start.2 = (s32[1,1,256,1]{2,3,1,0:T(1,128)S(1)}, s32[1,1,256,1]{2,3,1,0:T(1,128)}, u32[]{:S(2)}) copy-start(s32[1,1,256,1]{2,3,1,0:T(1,128)} %param.7) | copy-start | bytes 3076
  0.0 27.4 %copy-start.1 = (f32[1,4096]{1,0:T(1,128)S(1)}, f32[1,4096]{1,0:T(1,128)}, u32[]{:S(2)}) copy-start(f32[1,4096]{1,0:T(1,128)} %param.10) | copy-start | bytes 49156
  1.9 25.7 %collective-permute-start.3 = (bf16[256,1024]{1,0:T(8,128)(2,1)S(1)}, bf16[256,1024]{1,0:T(8,128)(2,1)}, u32[]{:S(2)}, u32[]{:S(2)}) collective-permute-start(bf16[256,1024]{1,0:T(8,128)(2,1)S(1)} %get-tuple-element.8), channel_id=1, source_target_pairs={{0,8},{8,16},{16,24},{1,9},{9,17},{17,25},{2,10},{10,18},{18,26},{... | collective-permute-start | bytes 1572872 | tf_op jit(solution)/shard_map/ppermute | solution.py:18
  16.9 10.6 %collective-permute-start = (f32[3,256]{1,0:T(4,128)S(1)}, f32[3,256]{1,0:T(4,128)S(1)}, u32[]{:S(2)}, u32[]{:S(2)}) collective-permute-start(f32[3,256]{1,0:T(4,128)S(1)} %pad_maximum_fusion.2), channel_id=1, source_target_pairs={{0,8},{8,16},{16,24},{1,9},{9,17},{17,25},{2,10},{10,18},{18,26},{... | collective-permute-start | bytes 9224 | tf_op jit(solution)/shard_map/ppermute | solution.py:18
  20.1 15.8 %collective-permute-start.2 = (bf16[256,1024]{1,0:T(8,128)(2,1)S(1)}, bf16[256,1024]{1,0:T(8,128)(2,1)}, u32[]{:S(2)}, u32[]{:S(2)}) collective-permute-start(bf16[256,1024]{1,0:T(8,128)(2,1)S(1)} %get-tuple-element.9), channel_id=1, source_target_pairs={{0,8},{8,16},{16,24},{1,9},{9,17},{17,25},{2,10},{10,18},{18,26},{... | collective-permute-start | bytes 1572872 | tf_op jit(solution)/shard_map/ppermute | solution.py:18
  24.3 22.7 %collective-permute-start.1 = (bf16[256,1024]{1,0:T(8,128)(2,1)S(1)}, bf16[256,1024]{1,0:T(8,128)(2,1)S(1)}, u32[]{:S(2)}, u32[]{:S(2)}) collective-permute-start(bf16[256,1024]{1,0:T(8,128)(2,1)S(1)} %get-tuple-element.10), channel_id=1, source_target_pairs={{0,8},{8,16},{16,24},{1,9},{9,17},{17,25},{2,10},{10,18},{18,26},{... | collective-permute-start | bytes 1572872 | tf_op jit(solution)/shard_map/ppermute | solution.py:18
  25.7 30.2 %collective-permute-start.4 = (bf16[256,1024]{1,0:T(8,128)(2,1)S(1)}, bf16[256,1024]{1,0:T(8,128)(2,1)S(1)}, u32[]{:S(2)}, u32[]{:S(2)}) collective-permute-start(bf16[256,1024]{1,0:T(8,128)(2,1)S(1)} %get-tuple-element.7), channel_id=1, source_target_pairs={{0,8},{8,16},{16,24},{1,9},{9,17},{17,25},{2,10},{10,18},{18,26},{... | collective-permute-start | bytes 1572872 | tf_op jit(solution)/shard_map/ppermute | solution.py:18
  70.1 2.9 %collective-permute-start.5 = (f32[2,512,256]{2,1,0:T(8,128)}, f32[2,512,256]{2,1,0:T(8,128)S(1)}, u32[]{:S(2)}, u32[]{:S(2)}) collective-permute-start(f32[2,512,256]{2,1,0:T(8,128)} %bitcast.21), channel_id=1, source_target_pairs={{0,1},{1,0},{2,3},{3,2},{4,5},{5,4},{6,7},{7,6},{8,9},{9,8},{10,11... | collective-permute-start | bytes 3145736 | tf_op jit(solution)/shard_map/ppermute | solution.py:34
  73.2 14.0 %collective-permute-start.6 = (f32[512,256]{1,0:T(8,128)S(1)}, f32[512,256]{1,0:T(8,128)S(1)}, u32[]{:S(2)}, u32[]{:S(2)}) collective-permute-start(f32[512,256]{1,0:T(8,128)S(1)} %dynamic-slice_bitcast_fusion), channel_id=1, source_target_pairs={{0,2},{1,3},{2,0},{3,1},{4,6},{5,7},{6,4},{7,5},{8,10},{9,11},{10,... | collective-permute-start | bytes 1572872 | tf_op jit(solution)/shard_map/ppermute | solution.py:34
  87.8 6.2 %collective-permute-start.7 = (bf16[192,512]{1,0:T(8,128)(2,1)S(1)}, bf16[192,512]{1,0:T(8,128)(2,1)S(1)}, u32[]{:S(2)}, u32[]{:S(2)}) collective-permute-start(bf16[192,512]{1,0:T(8,128)(2,1)S(1)} %get-tuple-element.12), channel_id=1, source_target_pairs={{0,4},{4,0},{1,5},{5,1},{2,6},{6,2},{3,7},{7,3},{8,12},{12,8},{9,1... | collective-permute-start | bytes 589832 | tf_op jit(solution)/shard_map/ppermute | solution.py:112

commit v4 on v3

--- a/solution.py
+++ b/solution.py
@@ -18,22 +18,23 @@
     return lax.ppermute(block, axis, route)
 
 
-def scatter_sum(partial, axis):
+def scatter_sum(blocks, axis):
     size = lax.axis_size(axis)
-    me = lax.axis_index(axis)
-    levels = size.bit_length() - 1
-    width, rows = partial.shape
-    current = partial.reshape((2,) * levels + (width // size, rows))
+    current = blocks
     bit = 1
     while bit < size:
-        mine = (me // bit) % 2
-        where = current.ndim - 3
-        keep = lax.dynamic_index_in_dim(current, mine, where, keepdims=False)
-        send = lax.dynamic_index_in_dim(current, 1 - mine, where, keepdims=False)
+        half = current.shape[0] // 2
+        keep, send = current[:half], current[half:]
+        if bit >= 2:
+            send = send.astype(jnp.bfloat16)
         pairs = [(i, i ^ bit) for i in range(size)]
-        current = keep + lax.ppermute(send, axis, pairs)
+        current = keep + lax.ppermute(send, axis, pairs).astype(jnp.float32)
         bit *= 2
-    return current
+    return current[0]
+
+
+def bit_reversed(index, levels):
+    return int(format(index, "0%db" % levels)[::-1], 2) if levels else 0
 
 
 def rotate_keys(kv_cols, positions):
@@ -83,14 +84,25 @@
     weight = w_kv[0]
     local_width = tok_rows.shape[1]
     step = local_width // CHUNKS
+    tensor = lax.axis_size("tensor")
+    me_t = lax.axis_index("tensor")
+    levels = tensor.bit_length() - 1
+    block = weight.shape[1] // tensor
     partial = None
     for k in range(CHUNKS):
         cols = slice(k * step, (k + 1) * step)
         arrived = shifted(tok_rows[:, cols], "section", 1)
         normed = (arrived.astype(jnp.float32) * gain[cols] * scale[:, None]).astype(jnp.bfloat16)
-        term = lax.dot_general(
-            weight[cols], normed, (((0,), (1,)), ((), ())), preferred_element_type=jnp.float32
-        )
+        terms = []
+        for s in range(tensor):
+            column = jnp.bitwise_xor(me_t, bit_reversed(s, levels)) * block
+            piece = lax.dynamic_slice_in_dim(weight[cols], column, block, axis=1)
+            terms.append(
+                lax.dot_general(
+                    piece, normed, (((0,), (1,)), ((), ())), preferred_element_type=jnp.float32
+                )
+            )
+        term = jnp.stack(terms)
         partial = term if partial is None else partial + term
     summed = scatter_sum(partial, "tensor")
     local_cols = summed.shape[0]

time: 95.9 us -> 89.1 us (0.929)
  waiting for transfers between devices: 35.9 us -> 14.4 us
  matrix products: 16 us -> 26.1 us
  local copies, waits for them, and re-layouts: 13.3 us -> 16.4 us
    ppermute x5, waiting for transfers between devices: 17.5 us -> 0.01 us  [shifted(): return lax.ppermute(block, axis, route)]
    slice x1 -> x4, local copies, waits for them, and re-layouts: 0.21 us -> 13.7 us  [the longest x1 12.4 us: per_device(): piece = lax.dynamic_slice_in_dim(weight[cols], column, block, axis=1)]
    dot_general x4 -> x16, matrix products: 15.7 us -> 25.8 us  [per_device(): lax.dot_general(piece, normed, (((0,), (1,)), ((), ())), preferred_elemen...]
    unnamed x8 -> x14, local copies, waits for them, and re-layouts: 4.57 us -> 0.03 us
    ppermute x2, waiting for transfers between devices: 13.8 us -> 9.85 us  [scatter_sum(): current = keep + lax.ppermute(send, axis, pairs).astype(jnp.float32)]
    reshape x1 -> x0, local copies, waits for them, and re-layouts: 3.03 us -> none  [scatter_sum(): current = partial.reshape((2,) * levels + (width // size, rows))]
    dynamic_slice x1 -> x0, local copies, waits for them, and re-layouts: 2.78 us -> none  [scatter_sum(): keep = lax.dynamic_index_in_dim(current, mine, where, keepdims=False)]
    ppermute x5, starting transfers between devices: 16.2 us -> 17.3 us  [shifted(): return lax.ppermute(block, axis, route)]
  transfers between devices with their start and end apart: 8 -> 8, of which waited for: 6 -> 3; matrix products, arithmetic and copies ran while one was open for 15% -> 38% of each run, Pallas kernels for 0% -> 0%
where the time goes in v4:
time: 89.1 us; the launch traced here: 88.3 us
  matrix products  26.1 us (29%)
  starting transfers between devices  19.8 us (22%)
  local copies, waits for them, and re-layouts  16.4 us (18%)
  waiting for transfers between devices  14.4 us (16%)
  blocking collectives  6.33 us (7%)
  other arithmetic  3.6 us (4%)
  between operations  1.75 us (2%)
    dot_general x16, matrix products, per_device(): lax.dot_general(piece, normed, (((0,), (1,)), ((), ())), preferred_elemen...  25.8 us
    ppermute x5, starting transfers between devices, shifted(): return lax.ppermute(block, axis, route)  17.3 us
    slice x1, local copies, waits for them, and re-layouts, per_device(): piece = lax.dynamic_slice_in_dim(weight[cols], column, block, axis=1)  12.4 us
    ppermute x2, waiting for transfers between devices, scatter_sum(): current = keep + lax.ppermute(send, axis, pairs).astype(jnp.float32)  9.85 us
    psum x1, blocking collectives, per_device(): sum_sq = lax.psum(jnp.sum(widened * widened, axis=1), 'tensor')  6.33 us
    ppermute x1, waiting for transfers between devices, per_device(): received[offset] = lax.ppermute(outgoing, 'dp', pairs)  4.57 us
    slice x1, local copies, waits for them, and re-layouts, per_device(): arrived = shifted(tok_rows[:, cols], 'section', 1)  1.84 us
  transfers between devices with their start and end apart: 8, of which 3 were waited for; matrix products, arithmetic and copies ran while one was open for 38% of the time, Pallas kernels for 0%

profile of v4, /device:TPU:0, one launch (start us, length us, event | category | flops | bytes accessed | tf_op | source)
XLA Modules:
  0.0 88.3 jit_solution(14602955240559708801)
XLA Ops:
  0.0 1.8 %fusion.62 = (bf16[256,1024]{1,0:T(8,128)(2,1)S(1)}, bf16[256,1024]{1,0:T(8,128)(2,1)S(1)}, bf16[256,1024]{1,0:T(8,128)(2,1)S(1)}, bf16[256,1024]{1,0:T(8,128)(2,1)S(1)}) fusion(bf16[256,4096]{1,0:T(8,128)(2,1)} %bitcast.138), kind=kLoop, calls=%fused_computation.128 | loop fusion | bytes 4194304 | tf_op jit(solution)/shard_map/slice | solution.py:94
  1.8 5.0 %collective-permute-start.1 = (bf16[256,1024]{1,0:T(8,128)(2,1)S(1)}, bf16[256,1024]{1,0:T(8,128)(2,1)S(1)}, u32[]{:S(2)}, u32[]{:S(2)}) collective-permute-start(bf16[256,1024]{1,0:T(8,128)(2,1)S(1)} %get-tuple-element.12), channel_id=1, source_target_pairs={{0,8},{8,16},{16,24},{1,9},{9,17},{17,25},{2,10},{10,18},{18,26},{... | collective-permute-start | bytes 1572872 | tf_op jit(solution)/shard_map/ppermute | solution.py:18
  8.0 0.6 reduce-window.6
  9.8 6.3 %psum.7 = f32[1,256]{1,0:T(1,128)S(1)} all-reduce(f32[1,256]{1,0:T(1,128)S(1)} %bitcast.148), channel_id=1, replica_groups=mesh['section'=4,'dp'=2,'tensor'=4] {'tensor'}, use_global_device_ids=true, to_apply=%region_1.2 | all-reduce | flops 256 | bytes 2048 | tf_op jit(solution)/shard_map/psum | solution.py:74
  16.2 3.7 %collective-permute-start = (f32[3,256]{1,0:T(4,128)S(1)}, f32[3,256]{1,0:T(4,128)S(1)}, u32[]{:S(2)}, u32[]{:S(2)}) collective-permute-start(f32[3,256]{1,0:T(4,128)S(1)} %pad_maximum_fusion.2), channel_id=1, source_target_pairs={{0,8},{8,16},{16,24},{1,9},{9,17},{17,25},{2,10},{10,18},{18,26},{... | collective-permute-start | bytes 9224 | tf_op jit(solution)/shard_map/ppermute | solution.py:18
  19.9 4.3 %collective-permute-start.2 = (bf16[256,1024]{1,0:T(8,128)(2,1)S(1)}, bf16[256,1024]{1,0:T(8,128)(2,1)}, u32[]{:S(2)}, u32[]{:S(2)}) collective-permute-start(bf16[256,1024]{1,0:T(8,128)(2,1)S(1)} %get-tuple-element.11), channel_id=1, source_target_pairs={{0,8},{8,16},{16,24},{1,9},{9,17},{17,25},{2,10},{10,18},{18,26},{... | collective-permute-start | bytes 1572872 | tf_op jit(solution)/shard_map/ppermute | solution.py:18
  24.2 2.1 %collective-permute-start.3 = (bf16[256,1024]{1,0:T(8,128)(2,1)S(1)}, bf16[256,1024]{1,0:T(8,128)(2,1)}, u32[]{:S(2)}, u32[]{:S(2)}) collective-permute-start(bf16[256,1024]{1,0:T(8,128)(2,1)S(1)} %get-tuple-element.10), channel_id=1, source_target_pairs={{0,8},{8,16},{16,24},{1,9},{9,17},{17,25},{2,10},{10,18},{18,26},{... | collective-permute-start | bytes 1572872 | tf_op jit(solution)/shard_map/ppermute | solution.py:18
  26.3 2.2 %collective-permute-start.4 = (bf16[256,1024]{1,0:T(8,128)(2,1)S(1)}, bf16[256,1024]{1,0:T(8,128)(2,1)}, u32[]{:S(2)}, u32[]{:S(2)}) collective-permute-start(bf16[256,1024]{1,0:T(8,128)(2,1)S(1)} %get-tuple-element.9), channel_id=1, source_target_pairs={{0,8},{8,16},{16,24},{1,9},{9,17},{17,25},{2,10},{10,18},{18,26},{... | collective-permute-start | bytes 1572872 | tf_op jit(solution)/shard_map/ppermute | solution.py:18
  28.5 12.4 %fusion.61 = (bf16[1,1024,2048]{2,1,0:T(8,128)(2,1)}, bf16[1,1024,2048]{2,1,0:T(8,128)(2,1)}, bf16[1,1024,2048]{2,1,0:T(8,128)(2,1)}, bf16[1,1024,2048]{2,1,0:T(8,128)(2,1)}) fusion(bf16[1,4096,2048]{2,1,0:T(8,128)(2,1)} %param.11), kind=kLoop, calls=%fused_computation.127 | loop fusion | bytes 33554432 | tf_op jit(solution)/shard_map/slice | solution.py:99
  41.0 2.0 %convolution_bitcast_fusion.12 = f32[1,512,256]{2,1,0:T(8,128)S(1)} fusion(bf16[1,1024,2048]{2,1,0:T(8,128)(2,1)} %get-tuple-element.7, s32[]{:T(128)S(6)} %select_n.110, bf16[256,1024]{1,0:T(8,128)(2,1)S(1)} %collective-permute-done.1, f32[256]{0:T(256)S(1)} %bitcast.168, f32[1024]{0:T(1024)S(1)} %bitcast.164), kind=kOutput, calls=%fused_computation.18 | convolution fusion | flops 269484032 | bytes 2102276 | tf_op jit(solution)/shard_map/dot_general | solution.py:101
  43.0 2.6 %convolution_bitcast_fusion.13 = f32[1,512,256]{2,1,0:T(8,128)S(1)} fusion(bf16[1,1024,2048]{2,1,0:T(8,128)(2,1)} %get-tuple-element.7, s32[]{:T(128)S(6)} %select_n.109, bf16[256,1024]{1,0:T(8,128)(2,1)S(1)} %collective-permute-done.1, f32[256]{0:T(256)S(1)} %bitcast.169, f32[1024]{0:T(1024)S(1)} %bitcast.165), kind=kOutput, calls=%fused_computation.19 | convolution fusion | flops 269484032 | bytes 2102276 | tf_op jit(solution)/shard_map/dot_general | solution.py:101
  45.6 1.6 %convolution_bitcast_fusion.8 = f32[1,512,256]{2,1,0:T(8,128)S(1)} fusion(bf16[1,1024,2048]{2,1,0:T(8,128)(2,1)S(1)} %copy-done.3, s32[]{:T(128)S(6)} %select_n.110, bf16[256,1024]{1,0:T(8,128)(2,1)} %collective-permute-done.2, f32[1024]{0:T(1024)S(1)} %bitcast.160, f32[256]{0:T(256)S(1)} %bitcast.170), kind=kOutput, calls=%fused_computation.14 | convolution fusion | flops 269484032 | bytes 2102276 | tf_op jit(solution)/shard_map/dot_general | solution.py:101
  47.2 1.6 %convolution_bitcast_fusion.9 = f32[1,512,256]{2,1,0:T(8,128)S(1)} fusion(bf16[1,1024,2048]{2,1,0:T(8,128)(2,1)S(1)} %copy-done.3, s32[]{:T(128)S(6)} %select_n.109, bf16[256,1024]{1,0:T(8,128)(2,1)} %collective-permute-done.2, f32[1024]{0:T(1024)S(1)} %bitcast.161, f32[256]{0:T(256)S(1)} %bitcast.171), kind=kOutput, calls=%fused_computation.15 | convolution fusion | flops 269484032 | bytes 2102276 | tf_op jit(solution)/shard_map/dot_general | solution.py:101
  49.5 1.9 %convolution_bitcast_fusion.10 = f32[1,512,256]{2,1,0:T(8,128)S(1)} fusion(bf16[1,1024,2048]{2,1,0:T(8,128)(2,1)S(1)} %copy-done.3, s32[]{:T(128)S(6)} %select_n.108, bf16[256,1024]{1,0:T(8,128)(2,1)} %collective-permute-done.2, f32[1024]{0:T(1024)S(1)} %bitcast.162, f32[256]{0:T(256)S(1)} %bitcast.173), kind=kOutput, calls=%fused_computation.16 | convolution fusion | flops 269484032 | bytes 2102276 | tf_op jit(solution)/shard_map/dot_general | solution.py:101
  51.4 0.6 convolution_bitcast_fusion.15
  52.0 1.6 %convolution_bitcast_fusion.11 = f32[1,512,256]{2,1,0:T(8,128)S(1)} fusion(bf16[1,1024,2048]{2,1,0:T(8,128)(2,1)S(1)} %copy-done.3, s32[]{:T(128)S(6)} %select_n.107, bf16[256,1024]{1,0:T(8,128)(2,1)} %collective-permute-done.2, f32[1024]{0:T(1024)S(1)} %bitcast.163, f32[256]{0:T(256)S(1)} %bitcast.175), kind=kOutput, calls=%fused_computation.17 | convolution fusion | flops 269484032 | bytes 2102276 | tf_op jit(solution)/shard_map/dot_general | solution.py:101
  53.7 1.8 %convolution_bitcast_fusion.4 = f32[1,512,256]{2,1,0:T(8,128)S(1)} fusion(bf16[1,1024,2048]{2,1,0:T(8,128)(2,1)S(1)} %copy-done.2, s32[]{:T(128)S(6)} %select_n.110, bf16[256,1024]{1,0:T(8,128)(2,1)} %collective-permute-done.3, f32[1024]{0:T(1024)S(1)} %bitcast.156, f32[256]{0:T(256)S(1)} %bitcast.176), kind=kOutput, calls=%fused_computation.10 | convolution fusion | flops 269484032 | bytes 2102276 | tf_op jit(solution)/shard_map/dot_general | solution.py:101
  55.5 1.6 %convolution_bitcast_fusion.5 = f32[1,512,256]{2,1,0:T(8,128)S(1)} fusion(bf16[1,1024,2048]{2,1,0:T(8,128)(2,1)S(1)} %copy-done.2, s32[]{:T(128)S(6)} %select_n.109, bf16[256,1024]{1,0:T(8,128)(2,1)} %collective-permute-done.3, f32[1024]{0:T(1024)S(1)} %bitcast.157, f32[256]{0:T(256)S(1)} %bitcast.177), kind=kOutput, calls=%fused_computation.11 | convolution fusion | flops 269484032 | bytes 2102276 | tf_op jit(solution)/shard_map/dot_general | solution.py:101
  57.2 1.6 %convolution_bitcast_fusion.6 = f32[1,512,256]{2,1,0:T(8,128)S(1)} fusion(bf16[1,1024,2048]{2,1,0:T(8,128)(2,1)S(1)} %copy-done.2, s32[]{:T(128)S(6)} %select_n.108, bf16[256,1024]{1,0:T(8,128)(2,1)} %collective-permute-done.3, f32[1024]{0:T(1024)S(1)} %bitcast.158, f32[256]{0:T(256)S(1)} %bitcast.178), kind=kOutput, calls=%fused_computation.12 | convolution fusion | flops 269484032 | bytes 2102276 | tf_op jit(solution)/shard_map/dot_general | solution.py:101
  58.8 1.6 %convolution_bitcast_fusion.7 = f32[1,512,256]{2,1,0:T(8,128)S(1)} fusion(bf16[1,1024,2048]{2,1,0:T(8,128)(2,1)S(1)} %copy-done.2, s32[]{:T(128)S(6)} %select_n.107, bf16[256,1024]{1,0:T(8,128)(2,1)} %collective-permute-done.3, f32[1024]{0:T(1024)S(1)} %bitcast.159, f32[256]{0:T(256)S(1)} %bitcast.179), kind=kOutput, calls=%fused_computation.13 | convolution fusion | flops 269484032 | bytes 2102276 | tf_op jit(solution)/shard_map/dot_general | solution.py:101
  60.4 1.6 %convolution_bitcast_fusion = f32[1,512,256]{2,1,0:T(8,128)S(1)} fusion(bf16[1,1024,2048]{2,1,0:T(8,128)(2,1)S(1)} %copy-done.1, s32[]{:T(128)S(6)} %select_n.110, bf16[256,1024]{1,0:T(8,128)(2,1)} %collective-permute-done.4, f32[1024]{0:T(1024)S(1)} %bitcast.152, f32[256]{0:T(256)S(1)} %bitcast.180), kind=kOutput, calls=%fused_computation.6 | convolution fusion | flops 269484032 | bytes 2102276 | tf_op jit(solution)/shard_map/dot_general | solution.py:101
  62.1 1.6 %convolution_bitcast_fusion.1 = f32[1,512,256]{2,1,0:T(8,128)S(1)} fusion(bf16[1,1024,2048]{2,1,0:T(8,128)(2,1)S(1)} %copy-done.1, s32[]{:T(128)S(6)} %select_n.109, bf16[256,1024]{1,0:T(8,128)(2,1)} %collective-permute-done.4, f32[1024]{0:T(1024)S(1)} %bitcast.153, f32[256]{0:T(256)S(1)} %bitcast.181), kind=kOutput, calls=%fused_computation.7 | convolution fusion | flops 269484032 | bytes 2102276 | tf_op jit(solution)/shard_map/dot_general | solution.py:101
  63.7 1.6 %convolution_bitcast_fusion.2 = f32[1,512,256]{2,1,0:T(8,128)S(1)} fusion(bf16[1,1024,2048]{2,1,0:T(8,128)(2,1)S(1)} %copy-done.1, s32[]{:T(128)S(6)} %select_n.108, bf16[256,1024]{1,0:T(8,128)(2,1)} %collective-permute-done.4, f32[1024]{0:T(1024)S(1)} %bitcast.154, f32[256]{0:T(256)S(1)} %bitcast.182), kind=kOutput, calls=%fused_computation.8 | convolution fusion | flops 269484032 | bytes 2102276 | tf_op jit(solution)/shard_map/dot_general | solution.py:101
  65.4 1.6 %convolution_bitcast_fusion.3 = f32[1,512,256]{2,1,0:T(8,128)S(1)} fusion(bf16[1,1024,2048]{2,1,0:T(8,128)(2,1)S(1)} %copy-done.1, s32[]{:T(128)S(6)} %select_n.107, bf16[256,1024]{1,0:T(8,128)(2,1)} %collective-permute-done.4, f32[1024]{0:T(1024)S(1)} %bitcast.155, f32[256]{0:T(256)S(1)} %bitcast.183), kind=kOutput, calls=%fused_computation.9 | convolution fusion | flops 269484032 | bytes 2102276 | tf_op jit(solution)/shard_map/dot_general | solution.py:101
  67.0 0.6 fusion.1
  67.6 1.0 %slice.132 = f32[2,512,256]{2,1,0:T(8,128)} slice(f32[4,512,256]{2,1,0:T(8,128)S(1)} %fusion.1), slice={[2:4], [0:512], [0:256]} | slice | bytes 2097152 | tf_op jit(solution)/shard_map/slice | solution.py:27
  68.9 2.7 %collective-permute-done.5 = f32[2,512,256]{2,1,0:T(8,128)S(1)} collective-permute-done((f32[2,512,256]{2,1,0:T(8,128)}, f32[2,512,256]{2,1,0:T(8,128)S(1)}, u32[]{:S(2)}, u32[]{:S(2)}) %collective-permute-start.5) | collective-permute-done | bytes 1048608 | tf_op jit(solution)/shard_map/ppermute | solution.py:31
  71.7 0.9 %collective-permute-start.6 = (bf16[1,512,256]{2,1,0:T(8,128)(2,1)S(1)}, bf16[1,512,256]{2,1,0:T(8,128)(2,1)S(1)}, u32[]{:S(2)}, u32[]{:S(2)}) collective-permute-start(bf16[1,512,256]{2,1,0:T(8,128)(2,1)S(1)} %slice.161), channel_id=1, source_target_pairs={{0,2},{1,3},{2,0},{3,1},{4,6},{5,7},{6,4},{7,5},{8,10},{9,11},{10,... | collective-permute-start | bytes 786440 | tf_op jit(solution)/shard_map/ppermute | solution.py:31
  73.0 7.2 %collective-permute-done.6 = bf16[1,512,256]{2,1,0:T(8,128)(2,1)S(1)} collective-permute-done((bf16[1,512,256]{2,1,0:T(8,128)(2,1)S(1)}, bf16[1,512,256]{2,1,0:T(8,128)(2,1)S(1)}, u32[]{:S(2)}, u32[]{:S(2)}) %collective-permute-start.6) | collective-permute-done | bytes 262176 | tf_op jit(solution)/shard_map/ppermute | solution.py:31
  80.7 1.6 %collective-permute-start.7 = (bf16[192,512]{1,0:T(8,128)(2,1)S(1)}, bf16[192,512]{1,0:T(8,128)(2,1)S(1)}, u32[]{:S(2)}, u32[]{:S(2)}) collective-permute-start(bf16[192,512]{1,0:T(8,128)(2,1)S(1)} %get-tuple-element.14), channel_id=1, source_target_pairs={{0,4},{4,0},{1,5},{5,1},{2,6},{6,2},{3,7},{7,3},{8,12},{12,8},{9,1... | collective-permute-start | bytes 589832 | tf_op jit(solution)/shard_map/ppermute | solution.py:124
  82.3 4.6 %collective-permute-done.7 = bf16[192,512]{1,0:T(8,128)(2,1)S(1)} collective-permute-done((bf16[192,512]{1,0:T(8,128)(2,1)S(1)}, bf16[192,512]{1,0:T(8,128)(2,1)S(1)}, u32[]{:S(2)}, u32[]{:S(2)}) %collective-permute-start.7) | collective-permute-done | bytes 196640 | tf_op jit(solution)/shard_map/ppermute | solution.py:124
  87.5 0.9 broadcast_select_fusion
  (53 shorter events, 3.5 us)
Async XLA Ops:
  0.0 6.8 %copy-start = (bf16[1,1,256,4096]{3,2,1,0:T(8,128)(2,1)S(1)}, bf16[1,1,256,4096]{3,2,1,0:T(8,128)(2,1)}, u32[]{:S(2)}) copy-start(bf16[1,1,256,4096]{3,2,1,0:T(8,128)(2,1)} %param.6) | copy-start | bytes 6291460
  0.0 8.0 %copy-start.6 = (s32[1,1,256,1]{2,3,1,0:T(1,128)S(1)}, s32[1,1,256,1]{2,3,1,0:T(1,128)}, u32[]{:S(2)}) copy-start(s32[1,1,256,1]{2,3,1,0:T(1,128)} %param.7) | copy-start | bytes 3076
  1.8 39.2 %collective-permute-start.1 = (bf16[256,1024]{1,0:T(8,128)(2,1)S(1)}, bf16[256,1024]{1,0:T(8,128)(2,1)S(1)}, u32[]{:S(2)}, u32[]{:S(2)}) collective-permute-start(bf16[256,1024]{1,0:T(8,128)(2,1)S(1)} %get-tuple-element.12), channel_id=1, source_target_pairs={{0,8},{8,16},{16,24},{1,9},{9,17},{17,25},{2,10},{10,18},{18,26},{... | collective-permute-start | bytes 1572872 | tf_op jit(solution)/shard_map/ppermute | solution.py:18
  16.2 24.8 %collective-permute-start = (f32[3,256]{1,0:T(4,128)S(1)}, f32[3,256]{1,0:T(4,128)S(1)}, u32[]{:S(2)}, u32[]{:S(2)}) collective-permute-start(f32[3,256]{1,0:T(4,128)S(1)} %pad_maximum_fusion.2), channel_id=1, source_target_pairs={{0,8},{8,16},{16,24},{1,9},{9,17},{17,25},{2,10},{10,18},{18,26},{... | collective-permute-start | bytes 9224 | tf_op jit(solution)/shard_map/ppermute | solution.py:18
  19.9 25.6 %collective-permute-start.2 = (bf16[256,1024]{1,0:T(8,128)(2,1)S(1)}, bf16[256,1024]{1,0:T(8,128)(2,1)}, u32[]{:S(2)}, u32[]{:S(2)}) collective-permute-start(bf16[256,1024]{1,0:T(8,128)(2,1)S(1)} %get-tuple-element.11), channel_id=1, source_target_pairs={{0,8},{8,16},{16,24},{1,9},{9,17},{17,25},{2,10},{10,18},{18,26},{... | collective-permute-start | bytes 1572872 | tf_op jit(solution)/shard_map/ppermute | solution.py:18
  24.2 29.4 %collective-permute-start.3 = (bf16[256,1024]{1,0:T(8,128)(2,1)S(1)}, bf16[256,1024]{1,0:T(8,128)(2,1)}, u32[]{:S(2)}, u32[]{:S(2)}) collective-permute-start(bf16[256,1024]{1,0:T(8,128)(2,1)S(1)} %get-tuple-element.10), channel_id=1, source_target_pairs={{0,8},{8,16},{16,24},{1,9},{9,17},{17,25},{2,10},{10,18},{18,26},{... | collective-permute-start | bytes 1572872 | tf_op jit(solution)/shard_map/ppermute | solution.py:18
  26.3 14.6 %copy-start.5 = (f32[1,4096]{1,0:T(1,128)S(1)}, f32[1,4096]{1,0:T(1,128)}, u32[]{:S(2)}) copy-start(f32[1,4096]{1,0:T(1,128)} %param.10) | copy-start | bytes 49156
  26.3 34.1 %collective-permute-start.4 = (bf16[256,1024]{1,0:T(8,128)(2,1)S(1)}, bf16[256,1024]{1,0:T(8,128)(2,1)}, u32[]{:S(2)}, u32[]{:S(2)}) collective-permute-start(bf16[256,1024]{1,0:T(8,128)(2,1)S(1)} %get-tuple-element.9), channel_id=1, source_target_pairs={{0,8},{8,16},{16,24},{1,9},{9,17},{17,25},{2,10},{10,18},{18,26},{... | collective-permute-start | bytes 1572872 | tf_op jit(solution)/shard_map/ppermute | solution.py:18
  41.0 4.6 %copy-start.3 = (bf16[1,1024,2048]{2,1,0:T(8,128)(2,1)S(1)}, bf16[1,1024,2048]{2,1,0:T(8,128)(2,1)}, u32[]{:S(2)}) copy-start(bf16[1,1024,2048]{2,1,0:T(8,128)(2,1)} %get-tuple-element.6) | copy-start | bytes 12582916
  41.0 7.9 %copy-start.4 = (bf16[1,1024,2048]{2,1,0:T(8,128)(2,1)S(1)}, bf16[1,1024,2048]{2,1,0:T(8,128)(2,1)}, u32[]{:S(2)}) copy-start(bf16[1,1024,2048]{2,1,0:T(8,128)(2,1)} %get-tuple-element.7) | copy-start | bytes 12582916
  48.9 4.8 %copy-start.2 = (bf16[1,1024,2048]{2,1,0:T(8,128)(2,1)S(1)}, bf16[1,1024,2048]{2,1,0:T(8,128)(2,1)}, u32[]{:S(2)}) copy-start(bf16[1,1024,2048]{2,1,0:T(8,128)(2,1)} %get-tuple-element.8) | copy-start | bytes 12582916
  53.7 6.7 %copy-start.1 = (bf16[1,1024,2048]{2,1,0:T(8,128)(2,1)S(1)}, bf16[1,1024,2048]{2,1,0:T(8,128)(2,1)}, u32[]{:S(2)}) copy-start(bf16[1,1024,2048]{2,1,0:T(8,128)(2,1)} %get-tuple-element.5) | copy-start | bytes 12582916
  68.7 2.9 %collective-permute-start.5 = (f32[2,512,256]{2,1,0:T(8,128)}, f32[2,512,256]{2,1,0:T(8,128)S(1)}, u32[]{:S(2)}, u32[]{:S(2)}) collective-permute-start(f32[2,512,256]{2,1,0:T(8,128)} %slice.132), channel_id=1, source_target_pairs={{0,1},{1,0},{2,3},{3,2},{4,5},{5,4},{6,7},{7,6},{8,9},{9,8},{10,11... | collective-permute-start | bytes 3145736 | tf_op jit(solution)/shard_map/ppermute | solution.py:31
  71.7 8.4 %collective-permute-start.6 = (bf16[1,512,256]{2,1,0:T(8,128)(2,1)S(1)}, bf16[1,512,256]{2,1,0:T(8,128)(2,1)S(1)}, u32[]{:S(2)}, u32[]{:S(2)}) collective-permute-start(bf16[1,512,256]{2,1,0:T(8,128)(2,1)S(1)} %slice.161), channel_id=1, source_target_pairs={{0,2},{1,3},{2,0},{3,1},{4,6},{5,7},{6,4},{7,5},{8,10},{9,11},{10,... | collective-permute-start | bytes 786440 | tf_op jit(solution)/shard_map/ppermute | solution.py:31
  80.7 6.2 %collective-permute-start.7 = (bf16[192,512]{1,0:T(8,128)(2,1)S(1)}, bf16[192,512]{1,0:T(8,128)(2,1)S(1)}, u32[]{:S(2)}, u32[]{:S(2)}) collective-permute-start(bf16[192,512]{1,0:T(8,128)(2,1)S(1)} %get-tuple-element.14), channel_id=1, source_target_pairs={{0,4},{4,0},{1,5},{5,1},{2,6},{6,2},{3,7},{7,3},{8,12},{12,8},{9,1... | collective-permute-start | bytes 589832 | tf_op jit(solution)/shard_map/ppermute | solution.py:124

commit v5 on v4

--- a/solution.py
+++ b/solution.py
@@ -9,7 +9,7 @@
 
 EPSILON = 1e-05
 ROPE_BASE = 500000.0
-CHUNKS = 4
+CHUNK_EIGHTHS = (1, 1, 1, 1, 1, 1, 1, 1)
 
 
 def shifted(block, axis, distance):
@@ -31,6 +31,15 @@
         current = keep + lax.ppermute(send, axis, pairs).astype(jnp.float32)
         bit *= 2
     return current[0]
+
+
+def all_sum(value, axis):
+    size = lax.axis_size(axis)
+    bit = 1
+    while bit < size:
+        value = value + lax.ppermute(value, axis, [(i, i ^ bit) for i in range(size)])
+        bit *= 2
+    return value
 
 
 def bit_reversed(index, levels):
@@ -71,10 +80,10 @@
     row_slot = jnp.where(row_alive, target * capacity + row_rank, slot_count)
     position = start[0, 0] + row_index
     widened = tok_rows.astype(jnp.float32)
-    sum_sq = lax.psum(jnp.sum(widened * widened, axis=1), "tensor")
-    meta = jnp.stack([sum_sq, row_slot.astype(jnp.float32), position.astype(jnp.float32)])
+    part_sq = jnp.sum(widened * widened, axis=1)
+    meta = jnp.stack([part_sq, row_slot.astype(jnp.float32), position.astype(jnp.float32)])
     meta = shifted(meta, "section", 1)
-    sum_sq = meta[0]
+    sum_sq = all_sum(meta[0], "tensor")
 
     first = lax.axis_index("section") == 0
     row_slot = jnp.where(first, slot_count, meta[1].astype(jnp.int32))
@@ -83,14 +92,14 @@
     gain = norm_gain[0]
     weight = w_kv[0]
     local_width = tok_rows.shape[1]
-    step = local_width // CHUNKS
+    bounds = [local_width * sum(CHUNK_EIGHTHS[:k]) // 8 for k in range(len(CHUNK_EIGHTHS) + 1)]
     tensor = lax.axis_size("tensor")
     me_t = lax.axis_index("tensor")
     levels = tensor.bit_length() - 1
     block = weight.shape[1] // tensor
     partial = None
-    for k in range(CHUNKS):
-        cols = slice(k * step, (k + 1) * step)
+    for k in range(len(CHUNK_EIGHTHS)):
+        cols = slice(bounds[k], bounds[k + 1])
         arrived = shifted(tok_rows[:, cols], "section", 1)
         normed = (arrived.astype(jnp.float32) * gain[cols] * scale[:, None]).astype(jnp.bfloat16)
         terms = []

time: 89.1 us -> 86.1 us (0.966)
  matrix products: 26.1 us -> 15.9 us
  starting transfers between devices: 19.8 us -> 28.5 us
  blocking collectives: 6.33 us -> 0 us
  waiting for transfers between devices: 14.4 us -> 17.3 us
  local copies, waits for them, and re-layouts: 16.4 us -> 17.7 us
    dot_general x16 -> x32, matrix products: 25.8 us -> 15.6 us  [per_device(): lax.dot_general(piece, normed, (((0,), (1,)), ((), ())), preferred_elemen...]
    ppermute x5 -> x9, starting transfers between devices: 17.3 us -> 23.7 us  [shifted(): return lax.ppermute(block, axis, route)]
    psum x1 -> x0, blocking collectives: 6.33 us -> none  [per_device(): sum_sq = lax.psum(jnp.sum(widened * widened, axis=1), 'tensor')]
    ppermute x0 -> x2, waiting for transfers between devices: none -> 3.17 us  [all_sum(): lax.ppermute(value, axis, [(i, i ^ bit) for i in range(size)])]
    ppermute x0 -> x2, starting transfers between devices: none -> 1.59 us  [all_sum(): lax.ppermute(value, axis, [(i, i ^ bit) for i in range(size)])]
    unnamed x14 -> x22, local copies, waits for them, and re-layouts: 0.03 us -> 1.21 us
    slice x1, local copies, waits for them, and re-layouts: 1.84 us -> 2.9 us  [per_device(): arrived = shifted(tok_rows[:, cols], 'section', 1)]
    slice x1, local copies, waits for them, and re-layouts: 12.4 us -> 11.4 us  [per_device(): piece = lax.dynamic_slice_in_dim(weight[cols], column, block, axis=1)]
  transfers between devices with their start and end apart: 8 -> 14, of which waited for: 3 -> 6; matrix products, arithmetic and copies ran while one was open for 38% -> 32% of each run, Pallas kernels for 0% -> 0%
where the time goes in v5:
time: 86.1 us; the launch traced here: 85.5 us
  starting transfers between devices  28.5 us (33%)
  local copies, waits for them, and re-layouts  17.7 us (21%)
  waiting for transfers between devices  17.3 us (20%)
  matrix products  15.9 us (18%)
  other arithmetic  4.23 us (5%)
  between operations  2 us (2%)
    ppermute x9, starting transfers between devices, shifted(): return lax.ppermute(block, axis, route)  23.7 us
    dot_general x32, matrix products, per_device(): lax.dot_general(piece, normed, (((0,), (1,)), ((), ())), preferred_elemen...  15.6 us
    slice x1, local copies, waits for them, and re-layouts, per_device(): piece = lax.dynamic_slice_in_dim(weight[cols], column, block, axis=1)  11.4 us
    ppermute x2, waiting for transfers between devices, scatter_sum(): current = keep + lax.ppermute(send, axis, pairs).astype(jnp.float32)  9.19 us
    ppermute x1, waiting for transfers between devices, per_device(): received[offset] = lax.ppermute(outgoing, 'dp', pairs)  4.58 us
    ppermute x2, waiting for transfers between devices, all_sum(): lax.ppermute(value, axis, [(i, i ^ bit) for i in range(size)])  3.17 us
    slice x1, local copies, waits for them, and re-layouts, per_device(): arrived = shifted(tok_rows[:, cols], 'section', 1)  2.9 us
  transfers between devices with their start and end apart: 14, of which 6 were waited for; matrix products, arithmetic and copies ran while one was open for 32% of the time, Pallas kernels for 0%

profile of v5, /device:TPU:0, one launch (start us, length us, event | category | flops | bytes accessed | tf_op | source)
XLA Modules:
  0.0 85.5 jit_solution(16786581684648258437)
XLA Ops:
  0.0 2.9 %fusion.112 = (bf16[256,512]{1,0:T(8,128)(2,1)S(1)}, bf16[256,512]{1,0:T(8,128)(2,1)}, bf16[256,512]{1,0:T(8,128)(2,1)}, bf16[256,512]{1,0:T(8,128)(2,1)}, bf16[...) fusion(bf16[256,4096]{1,0:T(8,128)(2,1)} %bitcast.222), kind=kLoop, calls=%fused_computation.198 | loop fusion | bytes 4194304 | tf_op jit(solution)/shard_map/slice | solution.py:103
  2.9 5.1 %collective-permute-start.1 = (bf16[256,512]{1,0:T(8,128)(2,1)}, bf16[256,512]{1,0:T(8,128)(2,1)S(1)}, u32[]{:S(2)}, u32[]{:S(2)}) collective-permute-start(bf16[256,512]{1,0:T(8,128)(2,1)} %get-tuple-element.20), channel_id=1, source_target_pairs={{0,8},{8,16},{16,24},{1,9},{9,17},{17,25},{2,10},{10,18},{18,26},{... | collective-permute-start | bytes 786440 | tf_op jit(solution)/shard_map/ppermute | solution.py:18
  8.0 0.5 multiply_reduce_fusion
  9.2 0.6 reduce-window.6
  11.0 3.5 %collective-permute-start = (f32[3,256]{1,0:T(4,128)S(1)}, f32[3,256]{1,0:T(4,128)S(1)}, u32[]{:S(2)}, u32[]{:S(2)}) collective-permute-start(f32[3,256]{1,0:T(4,128)S(1)} %pad_maximum_fusion.2), channel_id=1, source_target_pairs={{0,8},{8,16},{16,24},{1,9},{9,17},{17,25},{2,10},{10,18},{18,26},{... | collective-permute-start | bytes 9224 | tf_op jit(solution)/shard_map/ppermute | solution.py:18
  14.5 3.5 %collective-permute-start.4 = (bf16[256,512]{1,0:T(8,128)(2,1)}, bf16[256,512]{1,0:T(8,128)(2,1)S(1)}, u32[]{:S(2)}, u32[]{:S(2)}) collective-permute-start(bf16[256,512]{1,0:T(8,128)(2,1)} %get-tuple-element.19), channel_id=1, source_target_pairs={{0,8},{8,16},{16,24},{1,9},{9,17},{17,25},{2,10},{10,18},{18,26},{... | collective-permute-start | bytes 786440 | tf_op jit(solution)/shard_map/ppermute | solution.py:18
  18.0 1.9 %collective-permute-start.5 = (bf16[256,512]{1,0:T(8,128)(2,1)}, bf16[256,512]{1,0:T(8,128)(2,1)S(1)}, u32[]{:S(2)}, u32[]{:S(2)}) collective-permute-start(bf16[256,512]{1,0:T(8,128)(2,1)} %get-tuple-element.18), channel_id=1, source_target_pairs={{0,8},{8,16},{16,24},{1,9},{9,17},{17,25},{2,10},{10,18},{18,26},{... | collective-permute-start | bytes 786440 | tf_op jit(solution)/shard_map/ppermute | solution.py:18
  19.9 1.9 %collective-permute-start.6 = (bf16[256,512]{1,0:T(8,128)(2,1)}, bf16[256,512]{1,0:T(8,128)(2,1)S(1)}, u32[]{:S(2)}, u32[]{:S(2)}) collective-permute-start(bf16[256,512]{1,0:T(8,128)(2,1)} %get-tuple-element.17), channel_id=1, source_target_pairs={{0,8},{8,16},{16,24},{1,9},{9,17},{17,25},{2,10},{10,18},{18,26},{... | collective-permute-start | bytes 786440 | tf_op jit(solution)/shard_map/ppermute | solution.py:18
  21.9 11.4 %fusion.111 = (bf16[1,512,2048]{2,1,0:T(8,128)(2,1)S(1)}, bf16[1,512,2048]{2,1,0:T(8,128)(2,1)}, bf16[1,512,2048]{2,1,0:T(8,128)(2,1)}, bf16[1,512,2048]{2,1,0:T...) fusion(bf16[1,4096,2048]{2,1,0:T(8,128)(2,1)} %param.11), kind=kLoop, calls=%fused_computation.197 | loop fusion | bytes 33554432 | tf_op jit(solution)/shard_map/slice | solution.py:108
  33.5 1.1 %collective-permute-done.2 = f32[256]{0:T(256)S(1)} collective-permute-done((f32[256]{0:T(256)S(1)}, f32[256]{0:T(256)S(1)}, u32[]{:S(2)}, u32[]{:S(2)}) %collective-permute-start.2) | collective-permute-done | bytes 1056 | tf_op jit(solution)/shard_map/ppermute | solution.py:40
  34.6 1.5 %collective-permute-start.3 = (f32[256]{0:T(256)S(1)}, f32[256]{0:T(256)S(1)}, u32[]{:S(2)}, u32[]{:S(2)}) collective-permute-start(f32[256]{0:T(256)S(1)} %add.158), channel_id=1, source_target_pairs={{0,2},{1,3},{2,0},{3,1},{4,6},{5,7},{6,4},{7,5},{8,10},{9,11},{10,... | collective-permute-start | bytes 3080 | tf_op jit(solution)/shard_map/ppermute | solution.py:40
  36.1 2.0 %collective-permute-done.3 = f32[256]{0:T(256)S(1)} collective-permute-done((f32[256]{0:T(256)S(1)}, f32[256]{0:T(256)S(1)}, u32[]{:S(2)}, u32[]{:S(2)}) %collective-permute-start.3) | collective-permute-done | bytes 1056 | tf_op jit(solution)/shard_map/ppermute | solution.py:40
  38.1 1.9 %collective-permute-start.7 = (bf16[256,512]{1,0:T(8,128)(2,1)}, bf16[256,512]{1,0:T(8,128)(2,1)S(1)}, u32[]{:S(2)}, u32[]{:S(2)}) collective-permute-start(bf16[256,512]{1,0:T(8,128)(2,1)} %get-tuple-element.16), channel_id=1, source_target_pairs={{0,8},{8,16},{16,24},{1,9},{9,17},{17,25},{2,10},{10,18},{18,26},{... | collective-permute-start | bytes 786440 | tf_op jit(solution)/shard_map/ppermute | solution.py:18
  40.1 1.9 %collective-permute-start.8 = (bf16[256,512]{1,0:T(8,128)(2,1)}, bf16[256,512]{1,0:T(8,128)(2,1)S(1)}, u32[]{:S(2)}, u32[]{:S(2)}) collective-permute-start(bf16[256,512]{1,0:T(8,128)(2,1)} %get-tuple-element.15), channel_id=1, source_target_pairs={{0,8},{8,16},{16,24},{1,9},{9,17},{17,25},{2,10},{10,18},{18,26},{... | collective-permute-start | bytes 786440 | tf_op jit(solution)/shard_map/ppermute | solution.py:18
  42.0 1.5 %convolution_bitcast_fusion.28 = f32[1,512,256]{2,1,0:T(8,128)S(1)} fusion(bf16[1,512,2048]{2,1,0:T(8,128)(2,1)} %get-tuple-element.11, s32[]{:T(128)S(6)} %select_n.126, bf16[256,512]{1,0:T(8,128)(2,1)S(1)} %collective-permute-done.1, f32[256]{0:T(256)S(1)} %add_rsqrt_fusion, f32[512]{0:T(512)S(1)} %bitcast.257), kind=kOutput, calls=%fused_computation.38 | convolution fusion | flops 134742016 | bytes 1313796 | tf_op jit(solution)/shard_map/dot_general | solution.py:110
  43.5 1.6 %convolution_bitcast_fusion.29 = f32[1,512,256]{2,1,0:T(8,128)S(1)} fusion(bf16[1,512,2048]{2,1,0:T(8,128)(2,1)} %get-tuple-element.11, s32[]{:T(128)S(6)} %select_n.125, bf16[256,512]{1,0:T(8,128)(2,1)S(1)} %collective-permute-done.1, f32[256]{0:T(256)S(1)} %add_rsqrt_fusion, f32[512]{0:T(512)S(1)} %bitcast.258), kind=kOutput, calls=%fused_computation.39 | convolution fusion | flops 134742016 | bytes 1313796 | tf_op jit(solution)/shard_map/dot_general | solution.py:110
  45.1 1.9 %collective-permute-start.9 = (bf16[256,512]{1,0:T(8,128)(2,1)S(1)}, bf16[256,512]{1,0:T(8,128)(2,1)S(1)}, u32[]{:S(2)}, u32[]{:S(2)}) collective-permute-start(bf16[256,512]{1,0:T(8,128)(2,1)S(1)} %copy-done.8), channel_id=1, source_target_pairs={{0,8},{8,16},{16,24},{1,9},{9,17},{17,25},{2,10},{10,18},{18,26},{... | collective-permute-start | bytes 786440 | tf_op jit(solution)/shard_map/ppermute | solution.py:18
  47.9 0.4 convolution_bitcast_fusion.30
  48.8 0.4 convolution_bitcast_fusion.31
  49.7 2.1 %collective-permute-start.10 = (bf16[256,512]{1,0:T(8,128)(2,1)S(1)}, bf16[256,512]{1,0:T(8,128)(2,1)S(1)}, u32[]{:S(2)}, u32[]{:S(2)}) collective-permute-start(bf16[256,512]{1,0:T(8,128)(2,1)S(1)} %get-tuple-element.13), channel_id=1, source_target_pairs={{0,8},{8,16},{16,24},{1,9},{9,17},{17,25},{2,10},{10,18},{18,26},{... | collective-permute-start | bytes 786440 | tf_op jit(solution)/shard_map/ppermute | solution.py:18
  56.2 0.4 convolution_bitcast_fusion.13
  56.6 0.4 convolution_bitcast_fusion.14
  57.1 0.4 convolution_bitcast_fusion.15
  63.5 1.3 %fusion.5 = f32[4,512,256]{2,1,0:T(8,128)S(1)} fusion(f32[1,512,256]{2,1,0:T(8,128)S(1)} %convolution_bitcast_fusion.28, f32[1,512,256]{2,1,0:T(8,128)S(1)} %convolution_bitcast_fusion.29, f32[1,512,256]{2,1,0:T(8,128)S(1)} %convolution_bitcast_fusion.30, f32[1,512,256]{2,1,0:T(8,128)S(1)} %convolution_bitcast_fusion.31, ...), kind=kLoop, calls=%fused_computation.8 | loop fusion | flops 16252928 | bytes 18874368 | tf_op jit(solution)/shard_map/add | solution.py:115
  64.8 1.1 %slice.204 = f32[2,512,256]{2,1,0:T(8,128)} slice(f32[4,512,256]{2,1,0:T(8,128)S(1)} %fusion.5), slice={[2:4], [0:512], [0:256]} | slice | bytes 2097152 | tf_op jit(solution)/shard_map/slice | solution.py:27
  66.0 2.7 %collective-permute-done.11 = f32[2,512,256]{2,1,0:T(8,128)S(1)} collective-permute-done((f32[2,512,256]{2,1,0:T(8,128)}, f32[2,512,256]{2,1,0:T(8,128)S(1)}, u32[]{:S(2)}, u32[]{:S(2)}) %collective-permute-start.11) | collective-permute-done | bytes 1048608 | tf_op jit(solution)/shard_map/ppermute | solution.py:31
  68.9 1.6 %collective-permute-start.12 = (bf16[1,512,256]{2,1,0:T(8,128)(2,1)S(1)}, bf16[1,512,256]{2,1,0:T(8,128)(2,1)S(1)}, u32[]{:S(2)}, u32[]{:S(2)}) collective-permute-start(bf16[1,512,256]{2,1,0:T(8,128)(2,1)S(1)} %slice.228), channel_id=1, source_target_pairs={{0,2},{1,3},{2,0},{3,1},{4,6},{5,7},{6,4},{7,5},{8,10},{9,11},{10,... | collective-permute-start | bytes 786440 | tf_op jit(solution)/shard_map/ppermute | solution.py:31
  70.8 6.5 %collective-permute-done.12 = bf16[1,512,256]{2,1,0:T(8,128)(2,1)S(1)} collective-permute-done((bf16[1,512,256]{2,1,0:T(8,128)(2,1)S(1)}, bf16[1,512,256]{2,1,0:T(8,128)(2,1)S(1)}, u32[]{:S(2)}, u32[]{:S(2)}) %collective-permute-start.12) | collective-permute-done | bytes 262176 | tf_op jit(solution)/shard_map/ppermute | solution.py:31
  77.9 1.6 %collective-permute-start.13 = (bf16[192,512]{1,0:T(8,128)(2,1)S(1)}, bf16[192,512]{1,0:T(8,128)(2,1)S(1)}, u32[]{:S(2)}, u32[]{:S(2)}) collective-permute-start(bf16[192,512]{1,0:T(8,128)(2,1)S(1)} %get-tuple-element.22), channel_id=1, source_target_pairs={{0,4},{4,0},{1,5},{5,1},{2,6},{6,2},{3,7},{7,3},{8,12},{12,8},{9,1... | collective-permute-start | bytes 589832 | tf_op jit(solution)/shard_map/ppermute | solution.py:133
  79.4 4.6 %collective-permute-done.13 = bf16[192,512]{1,0:T(8,128)(2,1)S(1)} collective-permute-done((bf16[192,512]{1,0:T(8,128)(2,1)S(1)}, bf16[192,512]{1,0:T(8,128)(2,1)S(1)}, u32[]{:S(2)}, u32[]{:S(2)}) %collective-permute-start.13) | collective-permute-done | bytes 196640 | tf_op jit(solution)/shard_map/ppermute | solution.py:133
  84.1 0.6 gather_fusion
  84.6 0.9 %broadcast_select_fusion = bf16[1,1,384,512]{3,2,1,0:T(8,128)(2,1)} fusion(bf16[1,1,384,512]{3,2,1,0:T(8,128)(2,1)S(1)} %bitcast.226, pred[384]{0:T(512)(128)(4,1)S(1)} %broadcast_in_dim.18), kind=kLoop, calls=%fused_computation.119 | loop fusion | flops 196608 | bytes 786816 | tf_op jit(solution)/shard_map/jit(_take)/select_n | solution.py:135
  (90 shorter events, 13.8 us)
Async XLA Ops:
  0.0 8.0 %copy-start.7 = (bf16[1,1,256,4096]{3,2,1,0:T(8,128)(2,1)S(1)}, bf16[1,1,256,4096]{3,2,1,0:T(8,128)(2,1)}, u32[]{:S(2)}) copy-start(bf16[1,1,256,4096]{3,2,1,0:T(8,128)(2,1)} %param.6) | copy-start | bytes 6291460
  2.9 6.3 %copy-start.10 = (s32[1,1,256,1]{2,3,1,0:T(1,128)S(1)}, s32[1,1,256,1]{2,3,1,0:T(1,128)}, u32[]{:S(2)}) copy-start(s32[1,1,256,1]{2,3,1,0:T(1,128)} %param.7) | copy-start | bytes 3076
  2.9 37.2 %collective-permute-start.1 = (bf16[256,512]{1,0:T(8,128)(2,1)}, bf16[256,512]{1,0:T(8,128)(2,1)S(1)}, u32[]{:S(2)}, u32[]{:S(2)}) collective-permute-start(bf16[256,512]{1,0:T(8,128)(2,1)} %get-tuple-element.20), channel_id=1, source_target_pairs={{0,8},{8,16},{16,24},{1,9},{9,17},{17,25},{2,10},{10,18},{18,26},{... | collective-permute-start | bytes 786440 | tf_op jit(solution)/shard_map/ppermute | solution.py:18
  11.0 22.3 %collective-permute-start = (f32[3,256]{1,0:T(4,128)S(1)}, f32[3,256]{1,0:T(4,128)S(1)}, u32[]{:S(2)}, u32[]{:S(2)}) collective-permute-start(f32[3,256]{1,0:T(4,128)S(1)} %pad_maximum_fusion.2), channel_id=1, source_target_pairs={{0,8},{8,16},{16,24},{1,9},{9,17},{17,25},{2,10},{10,18},{18,26},{... | collective-permute-start | bytes 9224 | tf_op jit(solution)/shard_map/ppermute | solution.py:18
  14.5 30.6 %collective-permute-start.4 = (bf16[256,512]{1,0:T(8,128)(2,1)}, bf16[256,512]{1,0:T(8,128)(2,1)S(1)}, u32[]{:S(2)}, u32[]{:S(2)}) collective-permute-start(bf16[256,512]{1,0:T(8,128)(2,1)} %get-tuple-element.19), channel_id=1, source_target_pairs={{0,8},{8,16},{16,24},{1,9},{9,17},{17,25},{2,10},{10,18},{18,26},{... | collective-permute-start | bytes 786440 | tf_op jit(solution)/shard_map/ppermute | solution.py:18
  18.0 31.6 %collective-permute-start.5 = (bf16[256,512]{1,0:T(8,128)(2,1)}, bf16[256,512]{1,0:T(8,128)(2,1)S(1)}, u32[]{:S(2)}, u32[]{:S(2)}) collective-permute-start(bf16[256,512]{1,0:T(8,128)(2,1)} %get-tuple-element.18), channel_id=1, source_target_pairs={{0,8},{8,16},{16,24},{1,9},{9,17},{17,25},{2,10},{10,18},{18,26},{... | collective-permute-start | bytes 786440 | tf_op jit(solution)/shard_map/ppermute | solution.py:18
  19.9 13.5 %copy-start.9 = (f32[1,4096]{1,0:T(1,128)S(1)}, f32[1,4096]{1,0:T(1,128)}, u32[]{:S(2)}) copy-start(f32[1,4096]{1,0:T(1,128)} %param.10) | copy-start | bytes 49156
  19.9 33.5 %collective-permute-start.6 = (bf16[256,512]{1,0:T(8,128)(2,1)}, bf16[256,512]{1,0:T(8,128)(2,1)S(1)}, u32[]{:S(2)}, u32[]{:S(2)}) collective-permute-start(bf16[256,512]{1,0:T(8,128)(2,1)} %get-tuple-element.17), channel_id=1, source_target_pairs={{0,8},{8,16},{16,24},{1,9},{9,17},{17,25},{2,10},{10,18},{18,26},{... | collective-permute-start | bytes 786440 | tf_op jit(solution)/shard_map/ppermute | solution.py:18
  33.3 1.2 %collective-permute-start.2 = (f32[256]{0:T(256)S(1)}, f32[256]{0:T(256)S(1)}, u32[]{:S(2)}, u32[]{:S(2)}) collective-permute-start(f32[256]{0:T(256)S(1)} %bitcast.267), channel_id=1, source_target_pairs={{0,1},{1,0},{2,3},{3,2},{4,5},{5,4},{6,7},{7,6},{8,9},{9,8},{10,11... | collective-permute-start | bytes 3080 | tf_op jit(solution)/shard_map/ppermute | solution.py:40
  34.6 3.6 %collective-permute-start.3 = (f32[256]{0:T(256)S(1)}, f32[256]{0:T(256)S(1)}, u32[]{:S(2)}, u32[]{:S(2)}) collective-permute-start(f32[256]{0:T(256)S(1)} %add.158), channel_id=1, source_target_pairs={{0,2},{1,3},{2,0},{3,1},{4,6},{5,7},{6,4},{7,5},{8,10},{9,11},{10,... | collective-permute-start | bytes 3080 | tf_op jit(solution)/shard_map/ppermute | solution.py:40
  36.1 9.0 %copy-start.8 = (bf16[256,512]{1,0:T(8,128)(2,1)S(1)}, bf16[256,512]{1,0:T(8,128)(2,1)}, u32[]{:S(2)}) copy-start(bf16[256,512]{1,0:T(8,128)(2,1)} %get-tuple-element.14) | copy-start | bytes 786436
  36.1 11.0 %copy-start.5 = (bf16[1,512,2048]{2,1,0:T(8,128)(2,1)S(1)}, bf16[1,512,2048]{2,1,0:T(8,128)(2,1)}, u32[]{:S(2)}) copy-start(bf16[1,512,2048]{2,1,0:T(8,128)(2,1)} %get-tuple-element.10) | copy-start | bytes 6291460
  38.1 17.3 %collective-permute-start.7 = (bf16[256,512]{1,0:T(8,128)(2,1)}, bf16[256,512]{1,0:T(8,128)(2,1)S(1)}, u32[]{:S(2)}, u32[]{:S(2)}) collective-permute-start(bf16[256,512]{1,0:T(8,128)(2,1)} %get-tuple-element.16), channel_id=1, source_target_pairs={{0,8},{8,16},{16,24},{1,9},{9,17},{17,25},{2,10},{10,18},{18,26},{... | collective-permute-start | bytes 786440 | tf_op jit(solution)/shard_map/ppermute | solution.py:18
  40.1 17.4 %collective-permute-start.8 = (bf16[256,512]{1,0:T(8,128)(2,1)}, bf16[256,512]{1,0:T(8,128)(2,1)S(1)}, u32[]{:S(2)}, u32[]{:S(2)}) collective-permute-start(bf16[256,512]{1,0:T(8,128)(2,1)} %get-tuple-element.15), channel_id=1, source_target_pairs={{0,8},{8,16},{16,24},{1,9},{9,17},{17,25},{2,10},{10,18},{18,26},{... | collective-permute-start | bytes 786440 | tf_op jit(solution)/shard_map/ppermute | solution.py:18
  43.5 4.4 %copy-start.6 = (bf16[1,512,2048]{2,1,0:T(8,128)(2,1)S(1)}, bf16[1,512,2048]{2,1,0:T(8,128)(2,1)}, u32[]{:S(2)}) copy-start(bf16[1,512,2048]{2,1,0:T(8,128)(2,1)} %get-tuple-element.11) | copy-start | bytes 6291460
  45.1 14.4 %collective-permute-start.9 = (bf16[256,512]{1,0:T(8,128)(2,1)S(1)}, bf16[256,512]{1,0:T(8,128)(2,1)S(1)}, u32[]{:S(2)}, u32[]{:S(2)}) collective-permute-start(bf16[256,512]{1,0:T(8,128)(2,1)S(1)} %copy-done.8), channel_id=1, source_target_pairs={{0,8},{8,16},{16,24},{1,9},{9,17},{17,25},{2,10},{10,18},{18,26},{... | collective-permute-start | bytes 786440 | tf_op jit(solution)/shard_map/ppermute | solution.py:18
  48.3 3.4 %copy-start.4 = (bf16[1,512,2048]{2,1,0:T(8,128)(2,1)S(1)}, bf16[1,512,2048]{2,1,0:T(8,128)(2,1)}, u32[]{:S(2)}) copy-start(bf16[1,512,2048]{2,1,0:T(8,128)(2,1)} %get-tuple-element.9) | copy-start | bytes 6291460
  49.7 12.2 %collective-permute-start.10 = (bf16[256,512]{1,0:T(8,128)(2,1)S(1)}, bf16[256,512]{1,0:T(8,128)(2,1)S(1)}, u32[]{:S(2)}, u32[]{:S(2)}) collective-permute-start(bf16[256,512]{1,0:T(8,128)(2,1)S(1)} %get-tuple-element.13), channel_id=1, source_target_pairs={{0,8},{8,16},{16,24},{1,9},{9,17},{17,25},{2,10},{10,18},{18,26},{... | collective-permute-start | bytes 786440 | tf_op jit(solution)/shard_map/ppermute | solution.py:18
  52.2 1.6 %copy-start.3 = (bf16[1,512,2048]{2,1,0:T(8,128)(2,1)S(1)}, bf16[1,512,2048]{2,1,0:T(8,128)(2,1)}, u32[]{:S(2)}) copy-start(bf16[1,512,2048]{2,1,0:T(8,128)(2,1)} %get-tuple-element.8) | copy-start | bytes 6291460
  54.2 1.6 %copy-start.2 = (bf16[1,512,2048]{2,1,0:T(8,128)(2,1)S(1)}, bf16[1,512,2048]{2,1,0:T(8,128)(2,1)}, u32[]{:S(2)}) copy-start(bf16[1,512,2048]{2,1,0:T(8,128)(2,1)} %get-tuple-element.7) | copy-start | bytes 6291460
  56.2 1.6 %copy-start.1 = (bf16[1,512,2048]{2,1,0:T(8,128)(2,1)S(1)}, bf16[1,512,2048]{2,1,0:T(8,128)(2,1)}, u32[]{:S(2)}) copy-start(bf16[1,512,2048]{2,1,0:T(8,128)(2,1)} %get-tuple-element.6) | copy-start | bytes 6291460
  58.2 1.6 %copy-start = (bf16[1,512,2048]{2,1,0:T(8,128)(2,1)S(1)}, bf16[1,512,2048]{2,1,0:T(8,128)(2,1)}, u32[]{:S(2)}) copy-start(bf16[1,512,2048]{2,1,0:T(8,128)(2,1)} %get-tuple-element.12) | copy-start | bytes 6291460
  65.8 2.9 %collective-permute-start.11 = (f32[2,512,256]{2,1,0:T(8,128)}, f32[2,512,256]{2,1,0:T(8,128)S(1)}, u32[]{:S(2)}, u32[]{:S(2)}) collective-permute-start(f32[2,512,256]{2,1,0:T(8,128)} %slice.204), channel_id=1, source_target_pairs={{0,1},{1,0},{2,3},{3,2},{4,5},{5,4},{6,7},{7,6},{8,9},{9,8},{10,11... | collective-permute-start | bytes 3145736 | tf_op jit(solution)/shard_map/ppermute | solution.py:31
  68.9 8.4 %collective-permute-start.12 = (bf16[1,512,256]{2,1,0:T(8,128)(2,1)S(1)}, bf16[1,512,256]{2,1,0:T(8,128)(2,1)S(1)}, u32[]{:S(2)}, u32[]{:S(2)}) collective-permute-start(bf16[1,512,256]{2,1,0:T(8,128)(2,1)S(1)} %slice.228), channel_id=1, source_target_pairs={{0,2},{1,3},{2,0},{3,1},{4,6},{5,7},{6,4},{7,5},{8,10},{9,11},{10,... | collective-permute-start | bytes 786440 | tf_op jit(solution)/shard_map/ppermute | solution.py:31
  77.9 6.2 %collective-permute-start.13 = (bf16[192,512]{1,0:T(8,128)(2,1)S(1)}, bf16[192,512]{1,0:T(8,128)(2,1)S(1)}, u32[]{:S(2)}, u32[]{:S(2)}) collective-permute-start(bf16[192,512]{1,0:T(8,128)(2,1)S(1)} %get-tuple-element.22), channel_id=1, source_target_pairs={{0,4},{4,0},{1,5},{5,1},{2,6},{6,2},{3,7},{7,3},{8,12},{12,8},{9,1... | collective-permute-start | bytes 589832 | tf_op jit(solution)/shard_map/ppermute | solution.py:133

commit v6 on v5

--- a/solution.py
+++ b/solution.py
@@ -102,17 +102,18 @@
         cols = slice(bounds[k], bounds[k + 1])
         arrived = shifted(tok_rows[:, cols], "section", 1)
         normed = (arrived.astype(jnp.float32) * gain[cols] * scale[:, None]).astype(jnp.bfloat16)
-        terms = []
-        for s in range(tensor):
-            column = jnp.bitwise_xor(me_t, bit_reversed(s, levels)) * block
-            piece = lax.dynamic_slice_in_dim(weight[cols], column, block, axis=1)
-            terms.append(
-                lax.dot_general(
-                    piece, normed, (((0,), (1,)), ((), ())), preferred_element_type=jnp.float32
-                )
+        term = jnp.stack([
+            lax.dot_general(
+                weight[cols, j * block:(j + 1) * block], normed, (((0,), (1,)), ((), ())),
+                preferred_element_type=jnp.float32,
             )
-        term = jnp.stack(terms)
+            for j in range(tensor)
+        ])
         partial = term if partial is None else partial + term
+    order = jnp.bitwise_xor(
+        me_t, jnp.array([bit_reversed(s, levels) for s in range(tensor)], dtype=jnp.int32)
+    )
+    partial = jnp.take(partial, order, axis=0)
     summed = scatter_sum(partial, "tensor")
     local_cols = summed.shape[0]
     local_kv = summed.reshape(local_cols // (2 * HD), 2, HD, tok_count)

time: 86.1 us -> 90.9 us (1.056)
  local copies, waits for them, and re-layouts: 17.7 us -> 6.14 us
  matrix products: 15.9 us -> 25.4 us
  other arithmetic: 4.23 us -> 9.39 us
  waiting for transfers between devices: 17.3 us -> 18.3 us
    slice x2, local copies, waits for them, and re-layouts: 11.7 us -> 0.39 us  [the longest x1 11.4 us: per_device(): piece = lax.dynamic_slice_in_dim(weight[cols], column, block, axis=1)]
    dot_general x32, matrix products: 15.6 us -> 25.1 us  [per_device(): lax.dot_general(weight[cols, j * block:(j + 1) * block], normed, (((0,),...]
    gather x0 -> x1, local copies, waits for them, and re-layouts: none -> 2.01 us  [per_device(): partial = jnp.take(partial, order, axis=0)]
    slice x1, local copies, waits for them, and re-layouts: 2.9 us -> 0.96 us  [per_device(): arrived = shifted(tok_rows[:, cols], 'section', 1)]
    select_n x0 -> x1, other arithmetic: none -> 1.93 us  [per_device(): partial = jnp.take(partial, order, axis=0)]
    reduce_sum x1, other arithmetic: 0.49 us -> 2.09 us  [per_device(): part_sq = jnp.sum(widened * widened, axis=1)]
    ppermute x9, waiting for transfers between devices: 0.36 us -> 1.38 us  [shifted(): return lax.ppermute(block, axis, route)]
    unnamed x22 -> x12, local copies, waits for them, and re-layouts: 1.21 us -> 0.29 us
  transfers between devices with their start and end apart: 14 -> 14, of which waited for: 6 -> 6; matrix products, arithmetic and copies ran while one was open for 32% -> 27% of each run, Pallas kernels for 0% -> 0%
where the time goes in v6:
time: 90.9 us; the launch traced here: 90.1 us
  starting transfers between devices  28.7 us (32%)
  matrix products  25.4 us (28%)
  waiting for transfers between devices  18.3 us (20%)
  other arithmetic  9.39 us (10%)
  local copies, waits for them, and re-layouts  6.14 us (7%)
  between operations  2.13 us (2%)
    dot_general x32, matrix products, per_device(): lax.dot_general(weight[cols, j * block:(j + 1) * block], normed, (((0,),...  25.1 us
    ppermute x9, starting transfers between devices, shifted(): return lax.ppermute(block, axis, route)  24 us
    ppermute x2, waiting for transfers between devices, scatter_sum(): current = keep + lax.ppermute(send, axis, pairs).astype(jnp.float32)  9.18 us
    ppermute x1, waiting for transfers between devices, per_device(): received[offset] = lax.ppermute(outgoing, 'dp', pairs)  4.57 us
    ppermute x2, waiting for transfers between devices, all_sum(): lax.ppermute(value, axis, [(i, i ^ bit) for i in range(size)])  3.17 us
    add x1, other arithmetic, per_device(): partial = term if partial is None else partial + term  2.11 us
    reduce_sum x1, other arithmetic, per_device(): part_sq = jnp.sum(widened * widened, axis=1)  2.09 us
    gather x1, local copies, waits for them, and re-layouts, per_device(): partial = jnp.take(partial, order, axis=0)  2.01 us
  transfers between devices with their start and end apart: 14, of which 6 were waited for; matrix products, arithmetic and copies ran while one was open for 27% of the time, Pallas kernels for 0%

profile of v6, /device:TPU:0, one launch (start us, length us, event | category | flops | bytes accessed | tf_op | source)
XLA Modules:
  0.0 90.1 jit_solution(2943020600715520787)
XLA Ops:
  3.2 2.1 %multiply_reduce_fusion = f32[256]{0:T(256)S(1)} fusion(bf16[1,1,256,4096]{3,2,1,0:T(8,128)(2,1)} %param.7), kind=kLoop, calls=%fused_computation.2 | loop fusion | flops 3145472 | bytes 2098176 | tf_op jit(solution)/shard_map/reduce_sum | solution.py:83
  5.4 5.0 %collective-permute-start = (f32[3,256]{1,0:T(4,128)S(1)}, f32[3,256]{1,0:T(4,128)S(1)}, u32[]{:S(2)}, u32[]{:S(2)}) collective-permute-start(f32[3,256]{1,0:T(4,128)S(1)} %pad_maximum_fusion.2), channel_id=1, source_target_pairs={{0,8},{8,16},{16,24},{1,9},{9,17},{17,25},{2,10},{10,18},{18,26},{... | collective-permute-start | bytes 9224 | tf_op jit(solution)/shard_map/ppermute | solution.py:18
  11.4 3.5 %collective-permute-start.10 = (bf16[256,512]{1,0:T(8,128)(2,1)}, bf16[256,512]{1,0:T(8,128)(2,1)S(1)}, u32[]{:S(2)}, u32[]{:S(2)}) collective-permute-start(bf16[256,512]{1,0:T(8,128)(2,1)} %get-tuple-element.7), channel_id=1, source_target_pairs={{0,8},{8,16},{16,24},{1,9},{9,17},{17,25},{2,10},{10,18},{18,26},{... | collective-permute-start | bytes 786440 | tf_op jit(solution)/shard_map/ppermute | solution.py:18
  14.8 3.5 %collective-permute-start.8 = (bf16[256,512]{1,0:T(8,128)(2,1)}, bf16[256,512]{1,0:T(8,128)(2,1)S(1)}, u32[]{:S(2)}, u32[]{:S(2)}) collective-permute-start(bf16[256,512]{1,0:T(8,128)(2,1)} %get-tuple-element.9), channel_id=1, source_target_pairs={{0,8},{8,16},{16,24},{1,9},{9,17},{17,25},{2,10},{10,18},{18,26},{... | collective-permute-start | bytes 786440 | tf_op jit(solution)/shard_map/ppermute | solution.py:18
  18.3 1.9 %collective-permute-start.7 = (bf16[256,512]{1,0:T(8,128)(2,1)}, bf16[256,512]{1,0:T(8,128)(2,1)S(1)}, u32[]{:S(2)}, u32[]{:S(2)}) collective-permute-start(bf16[256,512]{1,0:T(8,128)(2,1)} %get-tuple-element.10), channel_id=1, source_target_pairs={{0,8},{8,16},{16,24},{1,9},{9,17},{17,25},{2,10},{10,18},{18,26},{... | collective-permute-start | bytes 786440 | tf_op jit(solution)/shard_map/ppermute | solution.py:18
  20.3 1.9 %collective-permute-start.6 = (bf16[256,512]{1,0:T(8,128)(2,1)S(1)}, bf16[256,512]{1,0:T(8,128)(2,1)S(1)}, u32[]{:S(2)}, u32[]{:S(2)}) collective-permute-start(bf16[256,512]{1,0:T(8,128)(2,1)S(1)} %get-tuple-element.11), channel_id=1, source_target_pairs={{0,8},{8,16},{16,24},{1,9},{9,17},{17,25},{2,10},{10,18},{18,26},{... | collective-permute-start | bytes 786440 | tf_op jit(solution)/shard_map/ppermute | solution.py:18
  23.5 1.5 %collective-permute-start.3 = (f32[256]{0:T(256)S(1)}, f32[256]{0:T(256)S(1)}, u32[]{:S(2)}, u32[]{:S(2)}) collective-permute-start(f32[256]{0:T(256)S(1)} %add.122), channel_id=1, source_target_pairs={{0,2},{1,3},{2,0},{3,1},{4,6},{5,7},{6,4},{7,5},{8,10},{9,11},{10,... | collective-permute-start | bytes 3080 | tf_op jit(solution)/shard_map/ppermute | solution.py:40
  25.0 2.0 %collective-permute-done.3 = f32[256]{0:T(256)S(1)} collective-permute-done((f32[256]{0:T(256)S(1)}, f32[256]{0:T(256)S(1)}, u32[]{:S(2)}, u32[]{:S(2)}) %collective-permute-start.3) | collective-permute-done | bytes 1056 | tf_op jit(solution)/shard_map/ppermute | solution.py:40
  27.1 1.9 %collective-permute-start.5 = (bf16[256,512]{1,0:T(8,128)(2,1)S(1)}, bf16[256,512]{1,0:T(8,128)(2,1)S(1)}, u32[]{:S(2)}, u32[]{:S(2)}) collective-permute-start(bf16[256,512]{1,0:T(8,128)(2,1)S(1)} %get-tuple-element.12), channel_id=1, source_target_pairs={{0,8},{8,16},{16,24},{1,9},{9,17},{17,25},{2,10},{10,18},{18,26},{... | collective-permute-start | bytes 786440 | tf_op jit(solution)/shard_map/ppermute | solution.py:18
  29.0 1.9 %collective-permute-start.4 = (bf16[256,512]{1,0:T(8,128)(2,1)S(1)}, bf16[256,512]{1,0:T(8,128)(2,1)S(1)}, u32[]{:S(2)}, u32[]{:S(2)}) collective-permute-start(bf16[256,512]{1,0:T(8,128)(2,1)S(1)} %get-tuple-element.13), channel_id=1, source_target_pairs={{0,8},{8,16},{16,24},{1,9},{9,17},{17,25},{2,10},{10,18},{18,26},{... | collective-permute-start | bytes 786440 | tf_op jit(solution)/shard_map/ppermute | solution.py:18
  30.9 1.5 %convolution_bitcast_fusion = f32[1,512,256]{1,2,0:T(8,128)S(1)} fusion(bf16[4096,2048]{1,0:T(8,128)(2,1)} %bitcast.236, bf16[256,512]{1,0:T(8,128)(2,1)S(1)} %collective-permute-done.10, f32[512]{0:T(512)S(1)} %bitcast.216, f32[256]{0:T(256)S(1)} %add_rsqrt_fusion), kind=kOutput, calls=%fused_computation.11 | convolution fusion | flops 134742016 | bytes 1313792 | tf_op jit(solution)/shard_map/dot_general | solution.py:106
  32.5 1.7 %convolution_bitcast_fusion.1 = f32[1,512,256]{1,2,0:T(8,128)S(1)} fusion(bf16[4096,2048]{1,0:T(8,128)(2,1)} %bitcast.237, bf16[256,512]{1,0:T(8,128)(2,1)S(1)} %collective-permute-done.10, f32[512]{0:T(512)S(1)} %bitcast.217, f32[256]{0:T(256)S(1)} %add_rsqrt_fusion), kind=kOutput, calls=%fused_computation.12 | convolution fusion | flops 134742016 | bytes 1313792 | tf_op jit(solution)/shard_map/dot_general | solution.py:106
  34.2 2.3 %collective-permute-start.1 = (bf16[256,512]{1,0:T(8,128)(2,1)S(1)}, bf16[256,512]{1,0:T(8,128)(2,1)S(1)}, u32[]{:S(2)}, u32[]{:S(2)}) collective-permute-start(bf16[256,512]{1,0:T(8,128)(2,1)S(1)} %get-tuple-element.14), channel_id=1, source_target_pairs={{0,8},{8,16},{16,24},{1,9},{9,17},{17,25},{2,10},{10,18},{18,26},{... | collective-permute-start | bytes 786440 | tf_op jit(solution)/shard_map/ppermute | solution.py:18
  37.9 1.4 %convolution_bitcast_fusion.11 = f32[1,512,256]{1,2,0:T(8,128)S(1)} fusion(bf16[4096,2048]{1,0:T(8,128)(2,1)} %bitcast.239, bf16[256,512]{1,0:T(8,128)(2,1)S(1)} %collective-permute-done.8, f32[512]{0:T(512)S(1)} %bitcast.209, f32[256]{0:T(256)S(1)} %add_rsqrt_fusion), kind=kOutput, calls=%fused_computation.22 | convolution fusion | flops 134742016 | bytes 1313792 | tf_op jit(solution)/shard_map/dot_general | solution.py:106
  39.3 2.1 %collective-permute-start.9 = (bf16[256,512]{1,0:T(8,128)(2,1)S(1)}, bf16[256,512]{1,0:T(8,128)(2,1)S(1)}, u32[]{:S(2)}, u32[]{:S(2)}) collective-permute-start(bf16[256,512]{1,0:T(8,128)(2,1)S(1)} %get-tuple-element.8), channel_id=1, source_target_pairs={{0,8},{8,16},{16,24},{1,9},{9,17},{17,25},{2,10},{10,18},{18,26},{... | collective-permute-start | bytes 786440 | tf_op jit(solution)/shard_map/ppermute | solution.py:18
  41.4 1.4 %convolution_bitcast_fusion.12 = f32[1,512,256]{1,2,0:T(8,128)S(1)} fusion(bf16[4096,2048]{1,0:T(8,128)(2,1)} %bitcast.240, bf16[256,512]{1,0:T(8,128)(2,1)S(1)} %collective-permute-done.7, f32[512]{0:T(512)S(1)} %bitcast.232, f32[256]{0:T(256)S(1)} %add_rsqrt_fusion), kind=kOutput, calls=%fused_computation.23 | convolution fusion | flops 134742016 | bytes 1313792 | tf_op jit(solution)/shard_map/dot_general | solution.py:106
  42.8 1.4 %convolution_bitcast_fusion.13 = f32[1,512,256]{1,2,0:T(8,128)S(1)} fusion(bf16[4096,2048]{1,0:T(8,128)(2,1)} %bitcast.241, bf16[256,512]{1,0:T(8,128)(2,1)S(1)} %collective-permute-done.7, f32[512]{0:T(512)S(1)} %bitcast.233, f32[256]{0:T(256)S(1)} %add_rsqrt_fusion), kind=kOutput, calls=%fused_computation.24 | convolution fusion | flops 134742016 | bytes 1313792 | tf_op jit(solution)/shard_map/dot_general | solution.py:106
  44.2 1.4 %convolution_bitcast_fusion.14 = f32[1,512,256]{1,2,0:T(8,128)S(1)} fusion(bf16[4096,2048]{1,0:T(8,128)(2,1)} %bitcast.242, bf16[256,512]{1,0:T(8,128)(2,1)S(1)} %collective-permute-done.7, f32[512]{0:T(512)S(1)} %bitcast.234, f32[256]{0:T(256)S(1)} %add_rsqrt_fusion), kind=kOutput, calls=%fused_computation.25 | convolution fusion | flops 134742016 | bytes 1313792 | tf_op jit(solution)/shard_map/dot_general | solution.py:106
  45.6 1.4 %convolution_bitcast_fusion.15 = f32[1,512,256]{1,2,0:T(8,128)S(1)} fusion(bf16[4096,2048]{1,0:T(8,128)(2,1)} %bitcast.243, bf16[256,512]{1,0:T(8,128)(2,1)S(1)} %collective-permute-done.7, f32[512]{0:T(512)S(1)} %bitcast.235, f32[256]{0:T(256)S(1)} %add_rsqrt_fusion), kind=kOutput, calls=%fused_computation.26 | convolution fusion | flops 134742016 | bytes 1313792 | tf_op jit(solution)/shard_map/dot_general | solution.py:106
  47.0 1.4 %convolution_bitcast_fusion.16 = f32[1,512,256]{1,2,0:T(8,128)S(1)} fusion(bf16[4096,2048]{1,0:T(8,128)(2,1)} %bitcast.244, bf16[256,512]{1,0:T(8,128)(2,1)S(1)} %collective-permute-done.6, f32[512]{0:T(512)S(1)} %bitcast.228, f32[256]{0:T(256)S(1)} %add_rsqrt_fusion), kind=kOutput, calls=%fused_computation.27 | convolution fusion | flops 134742016 | bytes 1313792 | tf_op jit(solution)/shard_map/dot_general | solution.py:106
  48.4 1.4 %convolution_bitcast_fusion.17 = f32[1,512,256]{1,2,0:T(8,128)S(1)} fusion(bf16[4096,2048]{1,0:T(8,128)(2,1)} %bitcast.245, bf16[256,512]{1,0:T(8,128)(2,1)S(1)} %collective-permute-done.6, f32[512]{0:T(512)S(1)} %bitcast.229, f32[256]{0:T(256)S(1)} %add_rsqrt_fusion), kind=kOutput, calls=%fused_computation.28 | convolution fusion | flops 134742016 | bytes 1313792 | tf_op jit(solution)/shard_map/dot_general | solution.py:106
  49.8 1.4 %convolution_bitcast_fusion.18 = f32[1,512,256]{1,2,0:T(8,128)S(1)} fusion(bf16[4096,2048]{1,0:T(8,128)(2,1)} %bitcast.246, bf16[256,512]{1,0:T(8,128)(2,1)S(1)} %collective-permute-done.6, f32[512]{0:T(512)S(1)} %bitcast.230, f32[256]{0:T(256)S(1)} %add_rsqrt_fusion), kind=kOutput, calls=%fused_computation.29 | convolution fusion | flops 134742016 | bytes 1313792 | tf_op jit(solution)/shard_map/dot_general | solution.py:106
  51.2 1.4 %convolution_bitcast_fusion.19 = f32[1,512,256]{1,2,0:T(8,128)S(1)} fusion(bf16[4096,2048]{1,0:T(8,128)(2,1)} %bitcast.247, bf16[256,512]{1,0:T(8,128)(2,1)S(1)} %collective-permute-done.6, f32[512]{0:T(512)S(1)} %bitcast.231, f32[256]{0:T(256)S(1)} %add_rsqrt_fusion), kind=kOutput, calls=%fused_computation.30 | convolution fusion | flops 134742016 | bytes 1313792 | tf_op jit(solution)/shard_map/dot_general | solution.py:106
  52.6 1.4 %convolution_bitcast_fusion.2 = f32[1,512,256]{1,2,0:T(8,128)S(1)} fusion(bf16[4096,2048]{1,0:T(8,128)(2,1)} %bitcast.248, bf16[256,512]{1,0:T(8,128)(2,1)S(1)} %collective-permute-done.10, f32[512]{0:T(512)S(1)} %bitcast.218, f32[256]{0:T(256)S(1)} %add_rsqrt_fusion), kind=kOutput, calls=%fused_computation.13 | convolution fusion | flops 134742016 | bytes 1313792 | tf_op jit(solution)/shard_map/dot_general | solution.py:106
  62.1 2.1 %fusion.5 = f32[4,512,256]{1,2,0:T(8,128)S(1)} fusion(f32[1,512,256]{1,2,0:T(8,128)S(1)} %convolution_bitcast_fusion.28, f32[1,512,256]{1,2,0:T(8,128)S(1)} %convolution_bitcast_fusion.29, f32[1,512,256]{1,2,0:T(8,128)S(1)} %convolution_bitcast_fusion.30, f32[1,512,256]{1,2,0:T(8,128)S(1)} %convolution_bitcast_fusion.31, ...), kind=kLoop, calls=%fused_computation.9 | loop fusion | flops 16252928 | bytes 18874368 | tf_op jit(solution)/shard_map/add | solution.py:112
  64.2 2.0 %gather_fusion = f32[4,512,256]{1,2,0:T(8,128)} fusion(f32[4,512,256]{1,2,0:T(8,128)S(1)} %fusion.5, s32[1024]{0:T(1024)S(1)} %pad_clamp_fusion.1), kind=kCustom, calls=%fused_computation | custom fusion | bytes 4194320 | tf_op jit(solution)/shard_map/jit(_take)/gather | solution.py:116
  66.3 1.9 %broadcast_select_fusion = f32[4,512,256]{1,2,0:T(8,128)S(1)} fusion(f32[4,512,256]{1,2,0:T(8,128)} %gather_fusion, pred[4]{0:T(512)(128)(4,1)S(1)} %get-tuple-element.5), kind=kLoop, calls=%fused_computation.44 | loop fusion | flops 524288 | bytes 4194308 | tf_op jit(solution)/shard_map/jit(_take)/select_n | solution.py:116
  69.4 2.7 %collective-permute-done.11 = f32[2,512,256]{1,2,0:T(8,128)S(1)} collective-permute-done((f32[2,512,256]{1,2,0:T(8,128)}, f32[2,512,256]{1,2,0:T(8,128)S(1)}, u32[]{:S(2)}, u32[]{:S(2)}) %collective-permute-start.11) | collective-permute-done | bytes 1048608 | tf_op jit(solution)/shard_map/ppermute | solution.py:31
  72.4 1.6 %collective-permute-start.12 = (bf16[1,512,256]{1,2,0:T(8,128)(2,1)S(1)}, bf16[1,512,256]{1,2,0:T(8,128)(2,1)S(1)}, u32[]{:S(2)}, u32[]{:S(2)}) collective-permute-start(bf16[1,512,256]{1,2,0:T(8,128)(2,1)S(1)} %slice.388), channel_id=1, source_target_pairs={{0,2},{1,3},{2,0},{3,1},{4,6},{5,7},{6,4},{7,5},{8,10},{9,11},{10,... | collective-permute-start | bytes 786440 | tf_op jit(solution)/shard_map/ppermute | solution.py:31
  74.3 6.5 %collective-permute-done.12 = bf16[1,512,256]{1,2,0:T(8,128)(2,1)S(1)} collective-permute-done((bf16[1,512,256]{1,2,0:T(8,128)(2,1)S(1)}, bf16[1,512,256]{1,2,0:T(8,128)(2,1)S(1)}, u32[]{:S(2)}, u32[]{:S(2)}) %collective-permute-start.12) | collective-permute-done | bytes 262176 | tf_op jit(solution)/shard_map/ppermute | solution.py:31
  82.4 1.6 %collective-permute-start.13 = (bf16[192,512]{1,0:T(8,128)(2,1)S(1)}, bf16[192,512]{1,0:T(8,128)(2,1)S(1)}, u32[]{:S(2)}, u32[]{:S(2)}) collective-permute-start(bf16[192,512]{1,0:T(8,128)(2,1)S(1)} %get-tuple-element.16), channel_id=1, source_target_pairs={{0,4},{4,0},{1,5},{5,1},{2,6},{6,2},{3,7},{7,3},{8,12},{12,8},{9,1... | collective-permute-start | bytes 589832 | tf_op jit(solution)/shard_map/ppermute | solution.py:134
  84.0 4.6 %collective-permute-done.13 = bf16[192,512]{1,0:T(8,128)(2,1)S(1)} collective-permute-done((bf16[192,512]{1,0:T(8,128)(2,1)S(1)}, bf16[192,512]{1,0:T(8,128)(2,1)S(1)}, u32[]{:S(2)}, u32[]{:S(2)}) %collective-permute-start.13) | collective-permute-done | bytes 196640 | tf_op jit(solution)/shard_map/ppermute | solution.py:134
  (85 shorter events, 18.3 us)
Async XLA Ops:
  0.0 5.3 %copy-start.2 = (s32[1,1,256,1]{2,3,1,0:T(1,128)S(1)}, s32[1,1,256,1]{2,3,1,0:T(1,128)}, u32[]{:S(2)}) copy-start(s32[1,1,256,1]{2,3,1,0:T(1,128)} %param.8) | copy-start | bytes 3076
  0.0 10.4 %copy-start = (bf16[1,1,256,4096]{3,2,1,0:T(8,128)(2,1)S(1)}, bf16[1,1,256,4096]{3,2,1,0:T(8,128)(2,1)}, u32[]{:S(2)}) copy-start(bf16[1,1,256,4096]{3,2,1,0:T(8,128)(2,1)} %param.7) | copy-start | bytes 6291460
  5.4 16.8 %collective-permute-start = (f32[3,256]{1,0:T(4,128)S(1)}, f32[3,256]{1,0:T(4,128)S(1)}, u32[]{:S(2)}, u32[]{:S(2)}) collective-permute-start(f32[3,256]{1,0:T(4,128)S(1)} %pad_maximum_fusion.2), channel_id=1, source_target_pairs={{0,8},{8,16},{16,24},{1,9},{9,17},{17,25},{2,10},{10,18},{18,26},{... | collective-permute-start | bytes 9224 | tf_op jit(solution)/shard_map/ppermute | solution.py:18
  10.4 11.8 %copy-start.1 = (f32[1,4096]{1,0:T(1,128)S(1)}, f32[1,4096]{1,0:T(1,128)}, u32[]{:S(2)}) copy-start(f32[1,4096]{1,0:T(1,128)} %param.11) | copy-start | bytes 49156
  10.4 11.9 %copy-start.3 = (s32[4]{0:T(128)S(1)}, s32[4]{0:T(128)}, u32[]{:S(2)}) copy-start(s32[4]{0:T(128)} %constant.97.clone) | copy-start | bytes 52
  11.4 17.6 %collective-permute-start.10 = (bf16[256,512]{1,0:T(8,128)(2,1)}, bf16[256,512]{1,0:T(8,128)(2,1)S(1)}, u32[]{:S(2)}, u32[]{:S(2)}) collective-permute-start(bf16[256,512]{1,0:T(8,128)(2,1)} %get-tuple-element.7), channel_id=1, source_target_pairs={{0,8},{8,16},{16,24},{1,9},{9,17},{17,25},{2,10},{10,18},{18,26},{... | collective-permute-start | bytes 786440 | tf_op jit(solution)/shard_map/ppermute | solution.py:18
  14.8 19.4 %collective-permute-start.8 = (bf16[256,512]{1,0:T(8,128)(2,1)}, bf16[256,512]{1,0:T(8,128)(2,1)S(1)}, u32[]{:S(2)}, u32[]{:S(2)}) collective-permute-start(bf16[256,512]{1,0:T(8,128)(2,1)} %get-tuple-element.9), channel_id=1, source_target_pairs={{0,8},{8,16},{16,24},{1,9},{9,17},{17,25},{2,10},{10,18},{18,26},{... | collective-permute-start | bytes 786440 | tf_op jit(solution)/shard_map/ppermute | solution.py:18
  18.3 21.0 %collective-permute-start.7 = (bf16[256,512]{1,0:T(8,128)(2,1)}, bf16[256,512]{1,0:T(8,128)(2,1)S(1)}, u32[]{:S(2)}, u32[]{:S(2)}) collective-permute-start(bf16[256,512]{1,0:T(8,128)(2,1)} %get-tuple-element.10), channel_id=1, source_target_pairs={{0,8},{8,16},{16,24},{1,9},{9,17},{17,25},{2,10},{10,18},{18,26},{... | collective-permute-start | bytes 786440 | tf_op jit(solution)/shard_map/ppermute | solution.py:18
  20.3 26.7 %collective-permute-start.6 = (bf16[256,512]{1,0:T(8,128)(2,1)S(1)}, bf16[256,512]{1,0:T(8,128)(2,1)S(1)}, u32[]{:S(2)}, u32[]{:S(2)}) collective-permute-start(bf16[256,512]{1,0:T(8,128)(2,1)S(1)} %get-tuple-element.11), channel_id=1, source_target_pairs={{0,8},{8,16},{16,24},{1,9},{9,17},{17,25},{2,10},{10,18},{18,26},{... | collective-permute-start | bytes 786440 | tf_op jit(solution)/shard_map/ppermute | solution.py:18
  22.2 1.2 %collective-permute-start.2 = (f32[256]{0:T(256)S(1)}, f32[256]{0:T(256)S(1)}, u32[]{:S(2)}, u32[]{:S(2)}) collective-permute-start(f32[256]{0:T(256)S(1)} %bitcast.201), channel_id=1, source_target_pairs={{0,1},{1,0},{2,3},{3,2},{4,5},{5,4},{6,7},{7,6},{8,9},{9,8},{10,11... | collective-permute-start | bytes 3080 | tf_op jit(solution)/shard_map/ppermute | solution.py:40
  23.5 3.6 %collective-permute-start.3 = (f32[256]{0:T(256)S(1)}, f32[256]{0:T(256)S(1)}, u32[]{:S(2)}, u32[]{:S(2)}) collective-permute-start(f32[256]{0:T(256)S(1)} %add.122), channel_id=1, source_target_pairs={{0,2},{1,3},{2,0},{3,1},{4,6},{5,7},{6,4},{7,5},{8,10},{9,11},{10,... | collective-permute-start | bytes 3080 | tf_op jit(solution)/shard_map/ppermute | solution.py:40
  27.1 26.9 %collective-permute-start.5 = (bf16[256,512]{1,0:T(8,128)(2,1)S(1)}, bf16[256,512]{1,0:T(8,128)(2,1)S(1)}, u32[]{:S(2)}, u32[]{:S(2)}) collective-permute-start(bf16[256,512]{1,0:T(8,128)(2,1)S(1)} %get-tuple-element.12), channel_id=1, source_target_pairs={{0,8},{8,16},{16,24},{1,9},{9,17},{17,25},{2,10},{10,18},{18,26},{... | collective-permute-start | bytes 786440 | tf_op jit(solution)/shard_map/ppermute | solution.py:18
  29.0 26.4 %collective-permute-start.4 = (bf16[256,512]{1,0:T(8,128)(2,1)S(1)}, bf16[256,512]{1,0:T(8,128)(2,1)S(1)}, u32[]{:S(2)}, u32[]{:S(2)}) collective-permute-start(bf16[256,512]{1,0:T(8,128)(2,1)S(1)} %get-tuple-element.13), channel_id=1, source_target_pairs={{0,8},{8,16},{16,24},{1,9},{9,17},{17,25},{2,10},{10,18},{18,26},{... | collective-permute-start | bytes 786440 | tf_op jit(solution)/shard_map/ppermute | solution.py:18
  30.9 23.0 %copy-start.4 = (bf16[1,4096,2048]{2,1,0:T(8,128)(2,1)S(1)}, bf16[1,4096,2048]{2,1,0:T(8,128)(2,1)}, u32[]{:S(2)}) copy-start(bf16[1,4096,2048]{2,1,0:T(8,128)(2,1)} %param.12) | copy-start | bytes 50331652
  34.2 23.0 %collective-permute-start.1 = (bf16[256,512]{1,0:T(8,128)(2,1)S(1)}, bf16[256,512]{1,0:T(8,128)(2,1)S(1)}, u32[]{:S(2)}, u32[]{:S(2)}) collective-permute-start(bf16[256,512]{1,0:T(8,128)(2,1)S(1)} %get-tuple-element.14), channel_id=1, source_target_pairs={{0,8},{8,16},{16,24},{1,9},{9,17},{17,25},{2,10},{10,18},{18,26},{... | collective-permute-start | bytes 786440 | tf_op jit(solution)/shard_map/ppermute | solution.py:18
  39.3 20.3 %collective-permute-start.9 = (bf16[256,512]{1,0:T(8,128)(2,1)S(1)}, bf16[256,512]{1,0:T(8,128)(2,1)S(1)}, u32[]{:S(2)}, u32[]{:S(2)}) collective-permute-start(bf16[256,512]{1,0:T(8,128)(2,1)S(1)} %get-tuple-element.8), channel_id=1, source_target_pairs={{0,8},{8,16},{16,24},{1,9},{9,17},{17,25},{2,10},{10,18},{18,26},{... | collective-permute-start | bytes 786440 | tf_op jit(solution)/shard_map/ppermute | solution.py:18
  69.2 2.9 %collective-permute-start.11 = (f32[2,512,256]{1,2,0:T(8,128)}, f32[2,512,256]{1,2,0:T(8,128)S(1)}, u32[]{:S(2)}, u32[]{:S(2)}) collective-permute-start(f32[2,512,256]{1,2,0:T(8,128)} %slice.302), channel_id=1, source_target_pairs={{0,1},{1,0},{2,3},{3,2},{4,5},{5,4},{6,7},{7,6},{8,9},{9,8},{10,11... | collective-permute-start | bytes 3145736 | tf_op jit(solution)/shard_map/ppermute | solution.py:31
  72.4 8.4 %collective-permute-start.12 = (bf16[1,512,256]{1,2,0:T(8,128)(2,1)S(1)}, bf16[1,512,256]{1,2,0:T(8,128)(2,1)S(1)}, u32[]{:S(2)}, u32[]{:S(2)}) collective-permute-start(bf16[1,512,256]{1,2,0:T(8,128)(2,1)S(1)} %slice.388), channel_id=1, source_target_pairs={{0,2},{1,3},{2,0},{3,1},{4,6},{5,7},{6,4},{7,5},{8,10},{9,11},{10,... | collective-permute-start | bytes 786440 | tf_op jit(solution)/shard_map/ppermute | solution.py:31
  82.4 6.2 %collective-permute-start.13 = (bf16[192,512]{1,0:T(8,128)(2,1)S(1)}, bf16[192,512]{1,0:T(8,128)(2,1)S(1)}, u32[]{:S(2)}, u32[]{:S(2)}) collective-permute-start(bf16[192,512]{1,0:T(8,128)(2,1)S(1)} %get-tuple-element.16), channel_id=1, source_target_pairs={{0,4},{4,0},{1,5},{5,1},{2,6},{6,2},{3,7},{7,3},{8,12},{12,8},{9,1... | collective-permute-start | bytes 589832 | tf_op jit(solution)/shard_map/ppermute | solution.py:134

commit v7 on v5

--- a/solution.py
+++ b/solution.py
@@ -9,7 +9,7 @@
 
 EPSILON = 1e-05
 ROPE_BASE = 500000.0
-CHUNK_EIGHTHS = (1, 1, 1, 1, 1, 1, 1, 1)
+CHUNK_EIGHTHS = (2, 2, 2, 1, 1)
 
 
 def shifted(block, axis, distance):
@@ -101,6 +101,8 @@
     for k in range(len(CHUNK_EIGHTHS)):
         cols = slice(bounds[k], bounds[k + 1])
         arrived = shifted(tok_rows[:, cols], "section", 1)
+        if partial is not None:
+            partial, arrived = lax.optimization_barrier((partial, arrived))
         normed = (arrived.astype(jnp.float32) * gain[cols] * scale[:, None]).astype(jnp.bfloat16)
         terms = []
         for s in range(tensor):

time: 86.1 us -> 94.8 us (1.10)
  matrix products: 15.9 us -> 24 us
  starting transfers between devices: 28.5 us -> 22.6 us
  local copies, waits for them, and re-layouts: 17.7 us -> 22 us
  other arithmetic: 4.23 us -> 6.46 us
    dot_general x32 -> x20, matrix products: 15.6 us -> 23.7 us  [per_device(): lax.dot_general(piece, normed, (((0,), (1,)), ((), ())), preferred_elemen...]
    ppermute x9 -> x6, starting transfers between devices: 23.7 us -> 17.9 us  [shifted(): return lax.ppermute(block, axis, route)]
    unnamed x22 -> x14, local copies, waits for them, and re-layouts: 1.21 us -> 5.22 us
    reduce_sum x1, other arithmetic: 0.49 us -> 2.09 us  [per_device(): part_sq = jnp.sum(widened * widened, axis=1)]
    slice x1 -> x2, local copies, waits for them, and re-layouts: 11.4 us -> 12.8 us  [per_device(): piece = lax.dynamic_slice_in_dim(weight[cols], column, block, axis=1)]
    slice x1 -> x2, local copies, waits for them, and re-layouts: 2.9 us -> 1.79 us  [per_device(): arrived = shifted(tok_rows[:, cols], 'section', 1)]
  transfers between devices with their start and end apart: 14 -> 11, of which waited for: 6 -> 5; matrix products, arithmetic and copies ran while one was open for 32% -> 41% of each run, Pallas kernels for 0% -> 0%
where the time goes in v7:
time: 94.8 us; the launch traced here: 93.9 us
  matrix products  24 us (25%)
  starting transfers between devices  22.6 us (24%)
  local copies, waits for them, and re-layouts  22 us (23%)
  waiting for transfers between devices  17 us (18%)
  other arithmetic  6.46 us (7%)
  between operations  1.94 us (2%)
    dot_general x20, matrix products, per_device(): lax.dot_general(piece, normed, (((0,), (1,)), ((), ())), preferred_elemen...  23.7 us
    ppermute x6, starting transfers between devices, shifted(): return lax.ppermute(block, axis, route)  17.9 us
    slice x2, local copies, waits for them, and re-layouts, per_device(): piece = lax.dynamic_slice_in_dim(weight[cols], column, block, axis=1)  12.8 us
    ppermute x2, waiting for transfers between devices, scatter_sum(): current = keep + lax.ppermute(send, axis, pairs).astype(jnp.float32)  9.19 us
    unnamed x14, local copies, waits for them, and re-layouts  5.22 us
    ppermute x1, waiting for transfers between devices, per_device(): received[offset] = lax.ppermute(outgoing, 'dp', pairs)  4.57 us
    ppermute x2, waiting for transfers between devices, all_sum(): lax.ppermute(value, axis, [(i, i ^ bit) for i in range(size)])  3.18 us
    reduce_sum x1, other arithmetic, per_device(): part_sq = jnp.sum(widened * widened, axis=1)  2.09 us
  transfers between devices with their start and end apart: 11, of which 5 were waited for; matrix products, arithmetic and copies ran while one was open for 41% of the time, Pallas kernels for 0%

profile of v7, /device:TPU:0, one launch (start us, length us, event | category | flops | bytes accessed | tf_op | source)
XLA Modules:
  0.0 93.9 jit_solution(12382566518507577930)
XLA Ops:
  3.2 2.1 %multiply_reduce_fusion = f32[256]{0:T(256)S(1)} fusion(bf16[1,1,256,4096]{3,2,1,0:T(8,128)(2,1)} %param.6), kind=kLoop, calls=%fused_computation.1 | loop fusion | flops 3145472 | bytes 2098176 | tf_op jit(solution)/shard_map/reduce_sum | solution.py:83
  5.4 5.0 %collective-permute-start = (f32[3,256]{1,0:T(4,128)S(1)}, f32[3,256]{1,0:T(4,128)S(1)}, u32[]{:S(2)}, u32[]{:S(2)}) collective-permute-start(f32[3,256]{1,0:T(4,128)S(1)} %pad_maximum_fusion.3), channel_id=1, source_target_pairs={{0,8},{8,16},{16,24},{1,9},{9,17},{17,25},{2,10},{10,18},{18,26},{... | collective-permute-start | bytes 9224 | tf_op jit(solution)/shard_map/ppermute | solution.py:18
  11.3 4.3 %collective-permute-start.1 = (bf16[256,1024]{1,0:T(8,128)(2,1)}, bf16[256,1024]{1,0:T(8,128)(2,1)}, u32[]{:S(2)}, u32[]{:S(2)}) collective-permute-start(bf16[256,1024]{1,0:T(8,128)(2,1)} %get-tuple-element.30), channel_id=1, source_target_pairs={{0,8},{8,16},{16,24},{1,9},{9,17},{17,25},{2,10},{10,18},{18,26},{... | collective-permute-start | bytes 1572872 | tf_op jit(solution)/shard_map/ppermute | solution.py:18
  15.6 3.5 %collective-permute-start.4 = (bf16[256,1024]{1,0:T(8,128)(2,1)S(1)}, bf16[256,1024]{1,0:T(8,128)(2,1)}, u32[]{:S(2)}, u32[]{:S(2)}) collective-permute-start(bf16[256,1024]{1,0:T(8,128)(2,1)S(1)} %get-tuple-element.29), channel_id=1, source_target_pairs={{0,8},{8,16},{16,24},{1,9},{9,17},{17,25},{2,10},{10,18},{18,26},{... | collective-permute-start | bytes 1572872 | tf_op jit(solution)/shard_map/ppermute | solution.py:18
  19.1 2.1 %collective-permute-start.5 = (bf16[256,1024]{1,0:T(8,128)(2,1)S(1)}, bf16[256,1024]{1,0:T(8,128)(2,1)}, u32[]{:S(2)}, u32[]{:S(2)}) collective-permute-start(bf16[256,1024]{1,0:T(8,128)(2,1)S(1)} %get-tuple-element.28), channel_id=1, source_target_pairs={{0,8},{8,16},{16,24},{1,9},{9,17},{17,25},{2,10},{10,18},{18,26},{... | collective-permute-start | bytes 1572872 | tf_op jit(solution)/shard_map/ppermute | solution.py:18
  22.0 1.3 %collective-permute-start.6 = (bf16[256,512]{1,0:T(8,128)(2,1)}, bf16[256,512]{1,0:T(8,128)(2,1)S(1)}, u32[]{:S(2)}, u32[]{:S(2)}) collective-permute-start(bf16[256,512]{1,0:T(8,128)(2,1)} %get-tuple-element.27), channel_id=1, source_target_pairs={{0,8},{8,16},{16,24},{1,9},{9,17},{17,25},{2,10},{10,18},{18,26},{... | collective-permute-start | bytes 786440 | tf_op jit(solution)/shard_map/ppermute | solution.py:18
  23.3 8.8 %fusion.70 = (bf16[1,1024,2048]{2,1,0:T(8,128)(2,1)}, bf16[1,1024,2048]{2,1,0:T(8,128)(2,1)}, bf16[1,1024,2048]{2,1,0:T(8,128)(2,1)}) fusion(bf16[1,4096,2048]{2,1,0:T(8,128)(2,1)} %param.11), kind=kLoop, calls=%fused_computation.145 | loop fusion | bytes 25165824 | tf_op jit(solution)/shard_map/slice | solution.py:110
  32.2 4.0 %fusion.69 = (bf16[1,512,2048]{2,1,0:T(8,128)(2,1)S(1)}, bf16[1,512,2048]{2,1,0:T(8,128)(2,1)}) fusion(bf16[1,4096,2048]{2,1,0:T(8,128)(2,1)} %param.11), kind=kLoop, calls=%fused_computation.144 | loop fusion | bytes 8388608 | tf_op jit(solution)/shard_map/slice | solution.py:110
  36.3 1.1 %collective-permute-done.2 = f32[256]{0:T(256)S(1)} collective-permute-done((f32[256]{0:T(256)S(1)}, f32[256]{0:T(256)S(1)}, u32[]{:S(2)}, u32[]{:S(2)}) %collective-permute-start.2) | collective-permute-done | bytes 1056 | tf_op jit(solution)/shard_map/ppermute | solution.py:40
  37.4 1.5 %collective-permute-start.3 = (f32[256]{0:T(256)S(1)}, f32[256]{0:T(256)S(1)}, u32[]{:S(2)}, u32[]{:S(2)}) collective-permute-start(f32[256]{0:T(256)S(1)} %add.137), channel_id=1, source_target_pairs={{0,2},{1,3},{2,0},{3,1},{4,6},{5,7},{6,4},{7,5},{8,10},{9,11},{10,... | collective-permute-start | bytes 3080 | tf_op jit(solution)/shard_map/ppermute | solution.py:40
  39.0 2.1 %collective-permute-done.3 = f32[256]{0:T(256)S(1)} collective-permute-done((f32[256]{0:T(256)S(1)}, f32[256]{0:T(256)S(1)}, u32[]{:S(2)}, u32[]{:S(2)}) %collective-permute-start.3) | collective-permute-done | bytes 1056 | tf_op jit(solution)/shard_map/ppermute | solution.py:40
  41.0 1.8 %collective-permute-start.7 = (bf16[256,512]{1,0:T(8,128)(2,1)}, bf16[256,512]{1,0:T(8,128)(2,1)S(1)}, u32[]{:S(2)}, u32[]{:S(2)}) collective-permute-start(bf16[256,512]{1,0:T(8,128)(2,1)} %get-tuple-element.26), channel_id=1, source_target_pairs={{0,8},{8,16},{16,24},{1,9},{9,17},{17,25},{2,10},{10,18},{18,26},{... | collective-permute-start | bytes 786440 | tf_op jit(solution)/shard_map/ppermute | solution.py:18
  42.8 2.1 %convolution_bitcast_fusion.17 = f32[1,512,256]{2,1,0:T(8,128)S(1)} fusion(bf16[1,1024,2048]{2,1,0:T(8,128)(2,1)} %get-tuple-element.25, s32[]{:T(128)S(6)} %select_n.113, bf16[256,1024]{1,0:T(8,128)(2,1)} %collective-permute-done.1, f32[256]{0:T(256)S(1)} %add_rsqrt_fusion, f32[1024]{0:T(1024)S(1)} %bitcast.192), kind=kOutput, calls=%fused_computation.25 | convolution fusion | flops 269484032 | bytes 2102276 | tf_op jit(solution)/shard_map/dot_general | solution.py:112
  44.9 1.9 %convolution_bitcast_fusion.18 = f32[1,512,256]{2,1,0:T(8,128)S(1)} fusion(bf16[1,1024,2048]{2,1,0:T(8,128)(2,1)} %get-tuple-element.25, s32[]{:T(128)S(6)} %select_n.112, bf16[256,1024]{1,0:T(8,128)(2,1)} %collective-permute-done.1, f32[256]{0:T(256)S(1)} %add_rsqrt_fusion, f32[1024]{0:T(1024)S(1)} %bitcast.193), kind=kOutput, calls=%fused_computation.26 | convolution fusion | flops 269484032 | bytes 2102276 | tf_op jit(solution)/shard_map/dot_general | solution.py:112
  46.9 1.6 %convolution_bitcast_fusion.19 = f32[1,512,256]{2,1,0:T(8,128)S(1)} fusion(bf16[1,1024,2048]{2,1,0:T(8,128)(2,1)S(1)} %copy-done.4, s32[]{:T(128)S(6)} %select_n.111, bf16[256,1024]{1,0:T(8,128)(2,1)} %collective-permute-done.1, f32[256]{0:T(256)S(1)} %add_rsqrt_fusion, f32[1024]{0:T(1024)S(1)} %bitcast.194), kind=kOutput, calls=%fused_computation.27 | convolution fusion | flops 269484032 | bytes 2102276 | tf_op jit(solution)/shard_map/dot_general | solution.py:112
  48.5 1.6 %convolution_bitcast_fusion.16 = f32[1,512,256]{2,1,0:T(8,128)S(1)} fusion(bf16[1,1024,2048]{2,1,0:T(8,128)(2,1)S(1)} %copy-done.4, s32[]{:T(128)S(6)} %select_n.114, bf16[256,1024]{1,0:T(8,128)(2,1)} %collective-permute-done.1, f32[256]{0:T(256)S(1)} %add_rsqrt_fusion, f32[1024]{0:T(1024)S(1)} %bitcast.195), kind=kOutput, calls=%fused_computation.24 | convolution fusion | flops 269484032 | bytes 2102276 | tf_op jit(solution)/shard_map/dot_general | solution.py:112
  50.3 2.0 %copy-done.3 = bf16[1,1024,2048]{2,1,0:T(8,128)(2,1)S(1)} copy-done((bf16[1,1024,2048]{2,1,0:T(8,128)(2,1)S(1)}, bf16[1,1024,2048]{2,1,0:T(8,128)(2,1)}, u32[]{:S(2)}) %copy-start.3) | copy-done | bytes 4194328
  52.3 1.6 %convolution_bitcast_fusion.15 = f32[1,512,256]{2,1,0:T(8,128)S(1)} fusion(bf16[1,1024,2048]{2,1,0:T(8,128)(2,1)S(1)} %copy-done.3, s32[]{:T(128)S(6)} %select_n.111, bf16[256,1024]{1,0:T(8,128)(2,1)} %collective-permute-done.4, f32[1024]{0:T(1024)S(1)} %bitcast.188, f32[256]{0:T(256)S(1)} %add_rsqrt_fusion), kind=kOutput, calls=%fused_computation.23 | convolution fusion | flops 269484032 | bytes 2102276 | tf_op jit(solution)/shard_map/dot_general | solution.py:112
  54.0 1.6 %convolution_bitcast_fusion.14 = f32[1,512,256]{2,1,0:T(8,128)S(1)} fusion(bf16[1,1024,2048]{2,1,0:T(8,128)(2,1)S(1)} %copy-done.3, s32[]{:T(128)S(6)} %select_n.112, bf16[256,1024]{1,0:T(8,128)(2,1)} %collective-permute-done.4, f32[1024]{0:T(1024)S(1)} %bitcast.189, f32[256]{0:T(256)S(1)} %add_rsqrt_fusion), kind=kOutput, calls=%fused_computation.22 | convolution fusion | flops 269484032 | bytes 2102276 | tf_op jit(solution)/shard_map/dot_general | solution.py:112
  55.6 1.6 %convolution_bitcast_fusion.13 = f32[1,512,256]{2,1,0:T(8,128)S(1)} fusion(bf16[1,1024,2048]{2,1,0:T(8,128)(2,1)S(1)} %copy-done.3, s32[]{:T(128)S(6)} %select_n.113, bf16[256,1024]{1,0:T(8,128)(2,1)} %collective-permute-done.4, f32[1024]{0:T(1024)S(1)} %bitcast.190, f32[256]{0:T(256)S(1)} %add_rsqrt_fusion), kind=kOutput, calls=%fused_computation.21 | convolution fusion | flops 269484032 | bytes 2102276 | tf_op jit(solution)/shard_map/dot_general | solution.py:112
  57.3 1.6 %convolution_bitcast_fusion.12 = f32[1,512,256]{2,1,0:T(8,128)S(1)} fusion(bf16[1,1024,2048]{2,1,0:T(8,128)(2,1)S(1)} %copy-done.3, s32[]{:T(128)S(6)} %select_n.114, bf16[256,1024]{1,0:T(8,128)(2,1)} %collective-permute-done.4, f32[1024]{0:T(1024)S(1)} %bitcast.191, f32[256]{0:T(256)S(1)} %add_rsqrt_fusion), kind=kOutput, calls=%fused_computation.20 | convolution fusion | flops 269484032 | bytes 2102276 | tf_op jit(solution)/shard_map/dot_general | solution.py:112
  59.2 1.9 %copy-done.2 = bf16[1,1024,2048]{2,1,0:T(8,128)(2,1)S(1)} copy-done((bf16[1,1024,2048]{2,1,0:T(8,128)(2,1)S(1)}, bf16[1,1024,2048]{2,1,0:T(8,128)(2,1)}, u32[]{:S(2)}) %copy-start.2) | copy-done | bytes 4194328
  61.1 1.6 %convolution_bitcast_fusion.11 = f32[1,512,256]{2,1,0:T(8,128)S(1)} fusion(bf16[1,1024,2048]{2,1,0:T(8,128)(2,1)S(1)} %copy-done.2, s32[]{:T(128)S(6)} %select_n.111, bf16[256,1024]{1,0:T(8,128)(2,1)} %collective-permute-done.5, f32[1024]{0:T(1024)S(1)} %bitcast.184, f32[256]{0:T(256)S(1)} %add_rsqrt_fusion), kind=kOutput, calls=%fused_computation.19 | convolution fusion | flops 269484032 | bytes 2102276 | tf_op jit(solution)/shard_map/dot_general | solution.py:112
  62.7 1.6 %convolution_bitcast_fusion.10 = f32[1,512,256]{2,1,0:T(8,128)S(1)} fusion(bf16[1,1024,2048]{2,1,0:T(8,128)(2,1)S(1)} %copy-done.2, s32[]{:T(128)S(6)} %select_n.112, bf16[256,1024]{1,0:T(8,128)(2,1)} %collective-permute-done.5, f32[1024]{0:T(1024)S(1)} %bitcast.185, f32[256]{0:T(256)S(1)} %add_rsqrt_fusion), kind=kOutput, calls=%fused_computation.18 | convolution fusion | flops 269484032 | bytes 2102276 | tf_op jit(solution)/shard_map/dot_general | solution.py:112
  64.4 1.6 %convolution_bitcast_fusion.9 = f32[1,512,256]{2,1,0:T(8,128)S(1)} fusion(bf16[1,1024,2048]{2,1,0:T(8,128)(2,1)S(1)} %copy-done.2, s32[]{:T(128)S(6)} %select_n.113, bf16[256,1024]{1,0:T(8,128)(2,1)} %collective-permute-done.5, f32[1024]{0:T(1024)S(1)} %bitcast.186, f32[256]{0:T(256)S(1)} %add_rsqrt_fusion), kind=kOutput, calls=%fused_computation.17 | convolution fusion | flops 269484032 | bytes 2102276 | tf_op jit(solution)/shard_map/dot_general | solution.py:112
  66.0 1.6 %convolution_bitcast_fusion.8 = f32[1,512,256]{2,1,0:T(8,128)S(1)} fusion(bf16[1,1024,2048]{2,1,0:T(8,128)(2,1)S(1)} %copy-done.2, s32[]{:T(128)S(6)} %select_n.114, bf16[256,1024]{1,0:T(8,128)(2,1)} %collective-permute-done.5, f32[1024]{0:T(1024)S(1)} %bitcast.187, f32[256]{0:T(256)S(1)} %add_rsqrt_fusion), kind=kOutput, calls=%fused_computation.16 | convolution fusion | flops 269484032 | bytes 2102276 | tf_op jit(solution)/shard_map/dot_general | solution.py:112
  68.0 1.3 %copy-done.1 = bf16[1,512,2048]{2,1,0:T(8,128)(2,1)S(1)} copy-done((bf16[1,512,2048]{2,1,0:T(8,128)(2,1)S(1)}, bf16[1,512,2048]{2,1,0:T(8,128)(2,1)}, u32[]{:S(2)}) %copy-start.1) | copy-done | bytes 2097176
  74.4 2.7 %collective-permute-done.8 = f32[2,512,256]{2,1,0:T(8,128)S(1)} collective-permute-done((f32[2,512,256]{2,1,0:T(8,128)}, f32[2,512,256]{2,1,0:T(8,128)S(1)}, u32[]{:S(2)}, u32[]{:S(2)}) %collective-permute-start.8) | collective-permute-done | bytes 1048608 | tf_op jit(solution)/shard_map/ppermute | solution.py:31
  77.3 1.6 %collective-permute-start.9 = (bf16[1,512,256]{2,1,0:T(8,128)(2,1)S(1)}, bf16[1,512,256]{2,1,0:T(8,128)(2,1)S(1)}, u32[]{:S(2)}, u32[]{:S(2)}) collective-permute-start(bf16[1,512,256]{2,1,0:T(8,128)(2,1)S(1)} %slice.174), channel_id=1, source_target_pairs={{0,2},{1,3},{2,0},{3,1},{4,6},{5,7},{6,4},{7,5},{8,10},{9,11},{10,... | collective-permute-start | bytes 786440 | tf_op jit(solution)/shard_map/ppermute | solution.py:31
  79.2 6.5 %collective-permute-done.9 = bf16[1,512,256]{2,1,0:T(8,128)(2,1)S(1)} collective-permute-done((bf16[1,512,256]{2,1,0:T(8,128)(2,1)S(1)}, bf16[1,512,256]{2,1,0:T(8,128)(2,1)S(1)}, u32[]{:S(2)}, u32[]{:S(2)}) %collective-permute-start.9) | collective-permute-done | bytes 262176 | tf_op jit(solution)/shard_map/ppermute | solution.py:31
  86.3 1.6 %collective-permute-start.10 = (bf16[192,512]{1,0:T(8,128)(2,1)S(1)}, bf16[192,512]{1,0:T(8,128)(2,1)S(1)}, u32[]{:S(2)}, u32[]{:S(2)}) collective-permute-start(bf16[192,512]{1,0:T(8,128)(2,1)S(1)} %get-tuple-element.32), channel_id=1, source_target_pairs={{0,4},{4,0},{1,5},{5,1},{2,6},{6,2},{3,7},{7,3},{8,12},{12,8},{9,1... | collective-permute-start | bytes 589832 | tf_op jit(solution)/shard_map/ppermute | solution.py:135
  87.8 4.6 %collective-permute-done.10 = bf16[192,512]{1,0:T(8,128)(2,1)S(1)} collective-permute-done((bf16[192,512]{1,0:T(8,128)(2,1)S(1)}, bf16[192,512]{1,0:T(8,128)(2,1)S(1)}, u32[]{:S(2)}, u32[]{:S(2)}) %collective-permute-start.10) | collective-permute-done | bytes 196640 | tf_op jit(solution)/shard_map/ppermute | solution.py:135
  (71 shorter events, 12.0 us)
Async XLA Ops:
  0.0 5.3 %copy-start.6 = (s32[1,1,256,1]{2,3,1,0:T(1,128)S(1)}, s32[1,1,256,1]{2,3,1,0:T(1,128)}, u32[]{:S(2)}) copy-start(s32[1,1,256,1]{2,3,1,0:T(1,128)} %param.7) | copy-start | bytes 3076
  0.0 10.4 %copy-start = (bf16[1,1,256,4096]{3,2,1,0:T(8,128)(2,1)S(1)}, bf16[1,1,256,4096]{3,2,1,0:T(8,128)(2,1)}, u32[]{:S(2)}) copy-start(bf16[1,1,256,4096]{3,2,1,0:T(8,128)(2,1)} %param.6) | copy-start | bytes 6291460
  5.4 30.8 %collective-permute-start = (f32[3,256]{1,0:T(4,128)S(1)}, f32[3,256]{1,0:T(4,128)S(1)}, u32[]{:S(2)}, u32[]{:S(2)}) collective-permute-start(f32[3,256]{1,0:T(4,128)S(1)} %pad_maximum_fusion.3), channel_id=1, source_target_pairs={{0,8},{8,16},{16,24},{1,9},{9,17},{17,25},{2,10},{10,18},{18,26},{... | collective-permute-start | bytes 9224 | tf_op jit(solution)/shard_map/ppermute | solution.py:18
  11.3 31.5 %collective-permute-start.1 = (bf16[256,1024]{1,0:T(8,128)(2,1)}, bf16[256,1024]{1,0:T(8,128)(2,1)}, u32[]{:S(2)}, u32[]{:S(2)}) collective-permute-start(bf16[256,1024]{1,0:T(8,128)(2,1)} %get-tuple-element.30), channel_id=1, source_target_pairs={{0,8},{8,16},{16,24},{1,9},{9,17},{17,25},{2,10},{10,18},{18,26},{... | collective-permute-start | bytes 1572872 | tf_op jit(solution)/shard_map/ppermute | solution.py:18
  15.6 34.7 %collective-permute-start.4 = (bf16[256,1024]{1,0:T(8,128)(2,1)S(1)}, bf16[256,1024]{1,0:T(8,128)(2,1)}, u32[]{:S(2)}, u32[]{:S(2)}) collective-permute-start(bf16[256,1024]{1,0:T(8,128)(2,1)S(1)} %get-tuple-element.29), channel_id=1, source_target_pairs={{0,8},{8,16},{16,24},{1,9},{9,17},{17,25},{2,10},{10,18},{18,26},{... | collective-permute-start | bytes 1572872 | tf_op jit(solution)/shard_map/ppermute | solution.py:18
  19.1 40.1 %collective-permute-start.5 = (bf16[256,1024]{1,0:T(8,128)(2,1)S(1)}, bf16[256,1024]{1,0:T(8,128)(2,1)}, u32[]{:S(2)}, u32[]{:S(2)}) collective-permute-start(bf16[256,1024]{1,0:T(8,128)(2,1)S(1)} %get-tuple-element.28), channel_id=1, source_target_pairs={{0,8},{8,16},{16,24},{1,9},{9,17},{17,25},{2,10},{10,18},{18,26},{... | collective-permute-start | bytes 1572872 | tf_op jit(solution)/shard_map/ppermute | solution.py:18
  22.0 45.9 %collective-permute-start.6 = (bf16[256,512]{1,0:T(8,128)(2,1)}, bf16[256,512]{1,0:T(8,128)(2,1)S(1)}, u32[]{:S(2)}, u32[]{:S(2)}) collective-permute-start(bf16[256,512]{1,0:T(8,128)(2,1)} %get-tuple-element.27), channel_id=1, source_target_pairs={{0,8},{8,16},{16,24},{1,9},{9,17},{17,25},{2,10},{10,18},{18,26},{... | collective-permute-start | bytes 786440 | tf_op jit(solution)/shard_map/ppermute | solution.py:18
  32.2 4.0 %copy-start.5 = (f32[1,4096]{1,0:T(1,128)S(1)}, f32[1,4096]{1,0:T(1,128)}, u32[]{:S(2)}) copy-start(f32[1,4096]{1,0:T(1,128)} %param.10) | copy-start | bytes 49156
  36.2 1.2 %collective-permute-start.2 = (f32[256]{0:T(256)S(1)}, f32[256]{0:T(256)S(1)}, u32[]{:S(2)}, u32[]{:S(2)}) collective-permute-start(f32[256]{0:T(256)S(1)} %bitcast.181), channel_id=1, source_target_pairs={{0,1},{1,0},{2,3},{3,2},{4,5},{5,4},{6,7},{7,6},{8,9},{9,8},{10,11... | collective-permute-start | bytes 3080 | tf_op jit(solution)/shard_map/ppermute | solution.py:40
  37.4 3.6 %collective-permute-start.3 = (f32[256]{0:T(256)S(1)}, f32[256]{0:T(256)S(1)}, u32[]{:S(2)}, u32[]{:S(2)}) collective-permute-start(f32[256]{0:T(256)S(1)} %add.137), channel_id=1, source_target_pairs={{0,2},{1,3},{2,0},{3,1},{4,6},{5,7},{6,4},{7,5},{8,10},{9,11},{10,... | collective-permute-start | bytes 3080 | tf_op jit(solution)/shard_map/ppermute | solution.py:40
  41.0 30.2 %collective-permute-start.7 = (bf16[256,512]{1,0:T(8,128)(2,1)}, bf16[256,512]{1,0:T(8,128)(2,1)S(1)}, u32[]{:S(2)}, u32[]{:S(2)}) collective-permute-start(bf16[256,512]{1,0:T(8,128)(2,1)} %get-tuple-element.26), channel_id=1, source_target_pairs={{0,8},{8,16},{16,24},{1,9},{9,17},{17,25},{2,10},{10,18},{18,26},{... | collective-permute-start | bytes 786440 | tf_op jit(solution)/shard_map/ppermute | solution.py:18
  42.8 4.1 %copy-start.4 = (bf16[1,1024,2048]{2,1,0:T(8,128)(2,1)S(1)}, bf16[1,1024,2048]{2,1,0:T(8,128)(2,1)}, u32[]{:S(2)}) copy-start(bf16[1,1024,2048]{2,1,0:T(8,128)(2,1)} %get-tuple-element.25) | copy-start | bytes 12582916
  50.1 2.2 %copy-start.3 = (bf16[1,1024,2048]{2,1,0:T(8,128)(2,1)S(1)}, bf16[1,1024,2048]{2,1,0:T(8,128)(2,1)}, u32[]{:S(2)}) copy-start(bf16[1,1024,2048]{2,1,0:T(8,128)(2,1)} %get-tuple-element.24) | copy-start | bytes 12582916
  58.9 2.2 %copy-start.2 = (bf16[1,1024,2048]{2,1,0:T(8,128)(2,1)S(1)}, bf16[1,1024,2048]{2,1,0:T(8,128)(2,1)}, u32[]{:S(2)}) copy-start(bf16[1,1024,2048]{2,1,0:T(8,128)(2,1)} %get-tuple-element.23) | copy-start | bytes 12582916
  67.7 1.6 %copy-start.1 = (bf16[1,512,2048]{2,1,0:T(8,128)(2,1)S(1)}, bf16[1,512,2048]{2,1,0:T(8,128)(2,1)}, u32[]{:S(2)}) copy-start(bf16[1,512,2048]{2,1,0:T(8,128)(2,1)} %get-tuple-element.22) | copy-start | bytes 6291460
  74.3 2.9 %collective-permute-start.8 = (f32[2,512,256]{2,1,0:T(8,128)}, f32[2,512,256]{2,1,0:T(8,128)S(1)}, u32[]{:S(2)}, u32[]{:S(2)}) collective-permute-start(f32[2,512,256]{2,1,0:T(8,128)} %slice.150), channel_id=1, source_target_pairs={{0,1},{1,0},{2,3},{3,2},{4,5},{5,4},{6,7},{7,6},{8,9},{9,8},{10,11... | collective-permute-start | bytes 3145736 | tf_op jit(solution)/shard_map/ppermute | solution.py:31
  77.3 8.4 %collective-permute-start.9 = (bf16[1,512,256]{2,1,0:T(8,128)(2,1)S(1)}, bf16[1,512,256]{2,1,0:T(8,128)(2,1)S(1)}, u32[]{:S(2)}, u32[]{:S(2)}) collective-permute-start(bf16[1,512,256]{2,1,0:T(8,128)(2,1)S(1)} %slice.174), channel_id=1, source_target_pairs={{0,2},{1,3},{2,0},{3,1},{4,6},{5,7},{6,4},{7,5},{8,10},{9,11},{10,... | collective-permute-start | bytes 786440 | tf_op jit(solution)/shard_map/ppermute | solution.py:31
  86.3 6.2 %collective-permute-start.10 = (bf16[192,512]{1,0:T(8,128)(2,1)S(1)}, bf16[192,512]{1,0:T(8,128)(2,1)S(1)}, u32[]{:S(2)}, u32[]{:S(2)}) collective-permute-start(bf16[192,512]{1,0:T(8,128)(2,1)S(1)} %get-tuple-element.32), channel_id=1, source_target_pairs={{0,4},{4,0},{1,5},{5,1},{2,6},{6,2},{3,7},{7,3},{8,12},{12,8},{9,1... | collective-permute-start | bytes 589832 | tf_op jit(solution)/shard_map/ppermute | solution.py:135

commit v8 on v5

--- a/solution.py
+++ b/solution.py
@@ -9,7 +9,7 @@
 
 EPSILON = 1e-05
 ROPE_BASE = 500000.0
-CHUNK_EIGHTHS = (1, 1, 1, 1, 1, 1, 1, 1)
+CHUNK_EIGHTHS = (2, 2, 2, 2)
 
 
 def shifted(block, axis, distance):

time: 86.1 us -> 86.5 us (level)
  matrix products: 15.9 us -> 25.3 us
  starting transfers between devices: 28.5 us -> 21.8 us
  local copies, waits for them, and re-layouts: 17.7 us -> 16.4 us
    dot_general x32 -> x16, matrix products: 15.6 us -> 25 us  [per_device(): lax.dot_general(piece, normed, (((0,), (1,)), ((), ())), preferred_elemen...]
    ppermute x9 -> x5, starting transfers between devices: 23.7 us -> 17.1 us  [shifted(): return lax.ppermute(block, axis, route)]
    unnamed x22 -> x14, local copies, waits for them, and re-layouts: 1.21 us -> 0.03 us
    slice x1, local copies, waits for them, and re-layouts: 2.9 us -> 1.84 us  [per_device(): arrived = shifted(tok_rows[:, cols], 'section', 1)]
    slice x1, local copies, waits for them, and re-layouts: 11.4 us -> 12.4 us  [per_device(): piece = lax.dynamic_slice_in_dim(weight[cols], column, block, axis=1)]
  transfers between devices with their start and end apart: 14 -> 10, of which waited for: 6 -> 5; matrix products, arithmetic and copies ran while one was open for 32% -> 39% of each run, Pallas kernels for 0% -> 0%
where the time goes in v8:
time: 86.5 us; the launch traced here: 85.8 us
  matrix products  25.3 us (29%)
  starting transfers between devices  21.8 us (25%)
  waiting for transfers between devices  16.9 us (20%)
  local copies, waits for them, and re-layouts  16.4 us (19%)
  other arithmetic  3.6 us (4%)
  between operations  1.73 us (2%)
    dot_general x16, matrix products, per_device(): lax.dot_general(piece, normed, (((0,), (1,)), ((), ())), preferred_elemen...  25 us
    ppermute x5, starting transfers between devices, shifted(): return lax.ppermute(block, axis, route)  17.1 us
    slice x1, local copies, waits for them, and re-layouts, per_device(): piece = lax.dynamic_slice_in_dim(weight[cols], column, block, axis=1)  12.4 us
    ppermute x2, waiting for transfers between devices, scatter_sum(): current = keep + lax.ppermute(send, axis, pairs).astype(jnp.float32)  9.17 us
    ppermute x1, waiting for transfers between devices, per_device(): received[offset] = lax.ppermute(outgoing, 'dp', pairs)  4.56 us
    ppermute x2, waiting for transfers between devices, all_sum(): lax.ppermute(value, axis, [(i, i ^ bit) for i in range(size)])  3.17 us
    slice x1, local copies, waits for them, and re-layouts, per_device(): arrived = shifted(tok_rows[:, cols], 'section', 1)  1.84 us
  transfers between devices with their start and end apart: 10, of which 5 were waited for; matrix products, arithmetic and copies ran while one was open for 39% of the time, Pallas kernels for 0%

profile of v8, /device:TPU:0, one launch (start us, length us, event | category | flops | bytes accessed | tf_op | source)
XLA Modules:
  0.0 85.8 jit_solution(6932856370469623351)
XLA Ops:
  0.0 1.8 %fusion.60 = (bf16[256,1024]{1,0:T(8,128)(2,1)S(1)}, bf16[256,1024]{1,0:T(8,128)(2,1)S(1)}, bf16[256,1024]{1,0:T(8,128)(2,1)S(1)}, bf16[256,1024]{1,0:T(8,128)(2,1)S(1)}) fusion(bf16[256,4096]{1,0:T(8,128)(2,1)} %bitcast.138), kind=kLoop, calls=%fused_computation.126 | loop fusion | bytes 4194304 | tf_op jit(solution)/shard_map/slice | solution.py:103
  1.8 5.0 %collective-permute-start.1 = (bf16[256,1024]{1,0:T(8,128)(2,1)S(1)}, bf16[256,1024]{1,0:T(8,128)(2,1)S(1)}, u32[]{:S(2)}, u32[]{:S(2)}) collective-permute-start(bf16[256,1024]{1,0:T(8,128)(2,1)S(1)} %get-tuple-element.12), channel_id=1, source_target_pairs={{0,8},{8,16},{16,24},{1,9},{9,17},{17,25},{2,10},{10,18},{18,26},{... | collective-permute-start | bytes 1572872 | tf_op jit(solution)/shard_map/ppermute | solution.py:18
  9.9 3.5 %collective-permute-start = (f32[3,256]{1,0:T(4,128)S(1)}, f32[3,256]{1,0:T(4,128)S(1)}, u32[]{:S(2)}, u32[]{:S(2)}) collective-permute-start(f32[3,256]{1,0:T(4,128)S(1)} %pad_maximum_fusion.2), channel_id=1, source_target_pairs={{0,8},{8,16},{16,24},{1,9},{9,17},{17,25},{2,10},{10,18},{18,26},{... | collective-permute-start | bytes 9224 | tf_op jit(solution)/shard_map/ppermute | solution.py:18
  13.3 4.3 %collective-permute-start.4 = (bf16[256,1024]{1,0:T(8,128)(2,1)S(1)}, bf16[256,1024]{1,0:T(8,128)(2,1)}, u32[]{:S(2)}, u32[]{:S(2)}) collective-permute-start(bf16[256,1024]{1,0:T(8,128)(2,1)S(1)} %get-tuple-element.11), channel_id=1, source_target_pairs={{0,8},{8,16},{16,24},{1,9},{9,17},{17,25},{2,10},{10,18},{18,26},{... | collective-permute-start | bytes 1572872 | tf_op jit(solution)/shard_map/ppermute | solution.py:18
  17.6 2.1 %collective-permute-start.5 = (bf16[256,1024]{1,0:T(8,128)(2,1)S(1)}, bf16[256,1024]{1,0:T(8,128)(2,1)}, u32[]{:S(2)}, u32[]{:S(2)}) collective-permute-start(bf16[256,1024]{1,0:T(8,128)(2,1)S(1)} %get-tuple-element.10), channel_id=1, source_target_pairs={{0,8},{8,16},{16,24},{1,9},{9,17},{17,25},{2,10},{10,18},{18,26},{... | collective-permute-start | bytes 1572872 | tf_op jit(solution)/shard_map/ppermute | solution.py:18
  19.7 2.2 %collective-permute-start.6 = (bf16[256,1024]{1,0:T(8,128)(2,1)S(1)}, bf16[256,1024]{1,0:T(8,128)(2,1)}, u32[]{:S(2)}, u32[]{:S(2)}) collective-permute-start(bf16[256,1024]{1,0:T(8,128)(2,1)S(1)} %get-tuple-element.9), channel_id=1, source_target_pairs={{0,8},{8,16},{16,24},{1,9},{9,17},{17,25},{2,10},{10,18},{18,26},{... | collective-permute-start | bytes 1572872 | tf_op jit(solution)/shard_map/ppermute | solution.py:18
  21.9 12.4 %fusion.59 = (bf16[1,1024,2048]{2,1,0:T(8,128)(2,1)}, bf16[1,1024,2048]{2,1,0:T(8,128)(2,1)}, bf16[1,1024,2048]{2,1,0:T(8,128)(2,1)}, bf16[1,1024,2048]{2,1,0:T(8,128)(2,1)}) fusion(bf16[1,4096,2048]{2,1,0:T(8,128)(2,1)} %param.11), kind=kLoop, calls=%fused_computation.125 | loop fusion | bytes 33554432 | tf_op jit(solution)/shard_map/slice | solution.py:108
  34.5 1.1 %collective-permute-done.2 = f32[256]{0:T(256)S(1)} collective-permute-done((f32[256]{0:T(256)S(1)}, f32[256]{0:T(256)S(1)}, u32[]{:S(2)}, u32[]{:S(2)}) %collective-permute-start.2) | collective-permute-done | bytes 1056 | tf_op jit(solution)/shard_map/ppermute | solution.py:40
  35.6 1.5 %collective-permute-start.3 = (f32[256]{0:T(256)S(1)}, f32[256]{0:T(256)S(1)}, u32[]{:S(2)}, u32[]{:S(2)}) collective-permute-start(f32[256]{0:T(256)S(1)} %add.130), channel_id=1, source_target_pairs={{0,2},{1,3},{2,0},{3,1},{4,6},{5,7},{6,4},{7,5},{8,10},{9,11},{10,... | collective-permute-start | bytes 3080 | tf_op jit(solution)/shard_map/ppermute | solution.py:40
  37.1 2.1 %collective-permute-done.3 = f32[256]{0:T(256)S(1)} collective-permute-done((f32[256]{0:T(256)S(1)}, f32[256]{0:T(256)S(1)}, u32[]{:S(2)}, u32[]{:S(2)}) %collective-permute-start.3) | collective-permute-done | bytes 1056 | tf_op jit(solution)/shard_map/ppermute | solution.py:40
  39.2 2.0 %convolution_bitcast_fusion.12 = f32[1,512,256]{2,1,0:T(8,128)S(1)} fusion(bf16[1,1024,2048]{2,1,0:T(8,128)(2,1)} %get-tuple-element.7, s32[]{:T(128)S(6)} %select_n.110, bf16[256,1024]{1,0:T(8,128)(2,1)S(1)} %collective-permute-done.1, f32[256]{0:T(256)S(1)} %add_rsqrt_fusion, f32[1024]{0:T(1024)S(1)} %bitcast.166), kind=kOutput, calls=%fused_computation.18 | convolution fusion | flops 269484032 | bytes 2102276 | tf_op jit(solution)/shard_map/dot_general | solution.py:110
  41.2 1.8 %convolution_bitcast_fusion.13 = f32[1,512,256]{2,1,0:T(8,128)S(1)} fusion(bf16[1,1024,2048]{2,1,0:T(8,128)(2,1)} %get-tuple-element.7, s32[]{:T(128)S(6)} %select_n.109, bf16[256,1024]{1,0:T(8,128)(2,1)S(1)} %collective-permute-done.1, f32[256]{0:T(256)S(1)} %add_rsqrt_fusion, f32[1024]{0:T(1024)S(1)} %bitcast.167), kind=kOutput, calls=%fused_computation.19 | convolution fusion | flops 269484032 | bytes 2102276 | tf_op jit(solution)/shard_map/dot_general | solution.py:110
  43.0 1.6 %convolution_bitcast_fusion.8 = f32[1,512,256]{2,1,0:T(8,128)S(1)} fusion(bf16[1,1024,2048]{2,1,0:T(8,128)(2,1)S(1)} %copy-done.3, s32[]{:T(128)S(6)} %select_n.110, bf16[256,1024]{1,0:T(8,128)(2,1)} %collective-permute-done.4, f32[1024]{0:T(1024)S(1)} %bitcast.162, f32[256]{0:T(256)S(1)} %add_rsqrt_fusion), kind=kOutput, calls=%fused_computation.14 | convolution fusion | flops 269484032 | bytes 2102276 | tf_op jit(solution)/shard_map/dot_general | solution.py:110
  44.7 1.6 %convolution_bitcast_fusion.9 = f32[1,512,256]{2,1,0:T(8,128)S(1)} fusion(bf16[1,1024,2048]{2,1,0:T(8,128)(2,1)S(1)} %copy-done.3, s32[]{:T(128)S(6)} %select_n.109, bf16[256,1024]{1,0:T(8,128)(2,1)} %collective-permute-done.4, f32[1024]{0:T(1024)S(1)} %bitcast.163, f32[256]{0:T(256)S(1)} %add_rsqrt_fusion), kind=kOutput, calls=%fused_computation.15 | convolution fusion | flops 269484032 | bytes 2102276 | tf_op jit(solution)/shard_map/dot_general | solution.py:110
  46.9 1.9 %convolution_bitcast_fusion.10 = f32[1,512,256]{2,1,0:T(8,128)S(1)} fusion(bf16[1,1024,2048]{2,1,0:T(8,128)(2,1)S(1)} %copy-done.3, s32[]{:T(128)S(6)} %select_n.108, bf16[256,1024]{1,0:T(8,128)(2,1)} %collective-permute-done.4, f32[1024]{0:T(1024)S(1)} %bitcast.164, f32[256]{0:T(256)S(1)} %add_rsqrt_fusion), kind=kOutput, calls=%fused_computation.16 | convolution fusion | flops 269484032 | bytes 2102276 | tf_op jit(solution)/shard_map/dot_general | solution.py:110
  49.5 1.6 %convolution_bitcast_fusion.11 = f32[1,512,256]{2,1,0:T(8,128)S(1)} fusion(bf16[1,1024,2048]{2,1,0:T(8,128)(2,1)S(1)} %copy-done.3, s32[]{:T(128)S(6)} %select_n.107, bf16[256,1024]{1,0:T(8,128)(2,1)} %collective-permute-done.4, f32[1024]{0:T(1024)S(1)} %bitcast.165, f32[256]{0:T(256)S(1)} %add_rsqrt_fusion), kind=kOutput, calls=%fused_computation.17 | convolution fusion | flops 269484032 | bytes 2102276 | tf_op jit(solution)/shard_map/dot_general | solution.py:110
  51.1 1.8 %convolution_bitcast_fusion.4 = f32[1,512,256]{2,1,0:T(8,128)S(1)} fusion(bf16[1,1024,2048]{2,1,0:T(8,128)(2,1)S(1)} %copy-done.2, s32[]{:T(128)S(6)} %select_n.110, bf16[256,1024]{1,0:T(8,128)(2,1)} %collective-permute-done.5, f32[1024]{0:T(1024)S(1)} %bitcast.158, f32[256]{0:T(256)S(1)} %add_rsqrt_fusion), kind=kOutput, calls=%fused_computation.10 | convolution fusion | flops 269484032 | bytes 2102276 | tf_op jit(solution)/shard_map/dot_general | solution.py:110
  53.0 1.6 %convolution_bitcast_fusion.5 = f32[1,512,256]{2,1,0:T(8,128)S(1)} fusion(bf16[1,1024,2048]{2,1,0:T(8,128)(2,1)S(1)} %copy-done.2, s32[]{:T(128)S(6)} %select_n.109, bf16[256,1024]{1,0:T(8,128)(2,1)} %collective-permute-done.5, f32[1024]{0:T(1024)S(1)} %bitcast.159, f32[256]{0:T(256)S(1)} %add_rsqrt_fusion), kind=kOutput, calls=%fused_computation.11 | convolution fusion | flops 269484032 | bytes 2102276 | tf_op jit(solution)/shard_map/dot_general | solution.py:110
  54.6 1.6 %convolution_bitcast_fusion.6 = f32[1,512,256]{2,1,0:T(8,128)S(1)} fusion(bf16[1,1024,2048]{2,1,0:T(8,128)(2,1)S(1)} %copy-done.2, s32[]{:T(128)S(6)} %select_n.108, bf16[256,1024]{1,0:T(8,128)(2,1)} %collective-permute-done.5, f32[1024]{0:T(1024)S(1)} %bitcast.160, f32[256]{0:T(256)S(1)} %add_rsqrt_fusion), kind=kOutput, calls=%fused_computation.12 | convolution fusion | flops 269484032 | bytes 2102276 | tf_op jit(solution)/shard_map/dot_general | solution.py:110
  56.2 1.6 %convolution_bitcast_fusion.7 = f32[1,512,256]{2,1,0:T(8,128)S(1)} fusion(bf16[1,1024,2048]{2,1,0:T(8,128)(2,1)S(1)} %copy-done.2, s32[]{:T(128)S(6)} %select_n.107, bf16[256,1024]{1,0:T(8,128)(2,1)} %collective-permute-done.5, f32[1024]{0:T(1024)S(1)} %bitcast.161, f32[256]{0:T(256)S(1)} %add_rsqrt_fusion), kind=kOutput, calls=%fused_computation.13 | convolution fusion | flops 269484032 | bytes 2102276 | tf_op jit(solution)/shard_map/dot_general | solution.py:110
  57.9 1.6 %convolution_bitcast_fusion = f32[1,512,256]{2,1,0:T(8,128)S(1)} fusion(bf16[1,1024,2048]{2,1,0:T(8,128)(2,1)S(1)} %copy-done.1, s32[]{:T(128)S(6)} %select_n.110, bf16[256,1024]{1,0:T(8,128)(2,1)} %collective-permute-done.6, f32[1024]{0:T(1024)S(1)} %bitcast.154, f32[256]{0:T(256)S(1)} %add_rsqrt_fusion), kind=kOutput, calls=%fused_computation.6 | convolution fusion | flops 269484032 | bytes 2102276 | tf_op jit(solution)/shard_map/dot_general | solution.py:110
  59.5 1.6 %convolution_bitcast_fusion.1 = f32[1,512,256]{2,1,0:T(8,128)S(1)} fusion(bf16[1,1024,2048]{2,1,0:T(8,128)(2,1)S(1)} %copy-done.1, s32[]{:T(128)S(6)} %select_n.109, bf16[256,1024]{1,0:T(8,128)(2,1)} %collective-permute-done.6, f32[1024]{0:T(1024)S(1)} %bitcast.155, f32[256]{0:T(256)S(1)} %add_rsqrt_fusion), kind=kOutput, calls=%fused_computation.7 | convolution fusion | flops 269484032 | bytes 2102276 | tf_op jit(solution)/shard_map/dot_general | solution.py:110
  61.2 1.6 %convolution_bitcast_fusion.2 = f32[1,512,256]{2,1,0:T(8,128)S(1)} fusion(bf16[1,1024,2048]{2,1,0:T(8,128)(2,1)S(1)} %copy-done.1, s32[]{:T(128)S(6)} %select_n.108, bf16[256,1024]{1,0:T(8,128)(2,1)} %collective-permute-done.6, f32[1024]{0:T(1024)S(1)} %bitcast.156, f32[256]{0:T(256)S(1)} %add_rsqrt_fusion), kind=kOutput, calls=%fused_computation.8 | convolution fusion | flops 269484032 | bytes 2102276 | tf_op jit(solution)/shard_map/dot_general | solution.py:110
  62.8 1.6 %convolution_bitcast_fusion.3 = f32[1,512,256]{2,1,0:T(8,128)S(1)} fusion(bf16[1,1024,2048]{2,1,0:T(8,128)(2,1)S(1)} %copy-done.1, s32[]{:T(128)S(6)} %select_n.107, bf16[256,1024]{1,0:T(8,128)(2,1)} %collective-permute-done.6, f32[1024]{0:T(1024)S(1)} %bitcast.157, f32[256]{0:T(256)S(1)} %add_rsqrt_fusion), kind=kOutput, calls=%fused_computation.9 | convolution fusion | flops 269484032 | bytes 2102276 | tf_op jit(solution)/shard_map/dot_general | solution.py:110
  64.5 0.6 fusion.1
  65.1 1.0 %slice.132 = f32[2,512,256]{2,1,0:T(8,128)} slice(f32[4,512,256]{2,1,0:T(8,128)S(1)} %fusion.1), slice={[2:4], [0:512], [0:256]} | slice | bytes 2097152 | tf_op jit(solution)/shard_map/slice | solution.py:27
  66.3 2.7 %collective-permute-done.7 = f32[2,512,256]{2,1,0:T(8,128)S(1)} collective-permute-done((f32[2,512,256]{2,1,0:T(8,128)}, f32[2,512,256]{2,1,0:T(8,128)S(1)}, u32[]{:S(2)}, u32[]{:S(2)}) %collective-permute-start.7) | collective-permute-done | bytes 1048608 | tf_op jit(solution)/shard_map/ppermute | solution.py:31
  69.2 1.6 %collective-permute-start.8 = (bf16[1,512,256]{2,1,0:T(8,128)(2,1)S(1)}, bf16[1,512,256]{2,1,0:T(8,128)(2,1)S(1)}, u32[]{:S(2)}, u32[]{:S(2)}) collective-permute-start(bf16[1,512,256]{2,1,0:T(8,128)(2,1)S(1)} %slice.156), channel_id=1, source_target_pairs={{0,2},{1,3},{2,0},{3,1},{4,6},{5,7},{6,4},{7,5},{8,10},{9,11},{10,... | collective-permute-start | bytes 786440 | tf_op jit(solution)/shard_map/ppermute | solution.py:31
  71.1 6.5 %collective-permute-done.8 = bf16[1,512,256]{2,1,0:T(8,128)(2,1)S(1)} collective-permute-done((bf16[1,512,256]{2,1,0:T(8,128)(2,1)S(1)}, bf16[1,512,256]{2,1,0:T(8,128)(2,1)S(1)}, u32[]{:S(2)}, u32[]{:S(2)}) %collective-permute-start.8) | collective-permute-done | bytes 262176 | tf_op jit(solution)/shard_map/ppermute | solution.py:31
  78.2 1.6 %collective-permute-start.9 = (bf16[192,512]{1,0:T(8,128)(2,1)S(1)}, bf16[192,512]{1,0:T(8,128)(2,1)S(1)}, u32[]{:S(2)}, u32[]{:S(2)}) collective-permute-start(bf16[192,512]{1,0:T(8,128)(2,1)S(1)} %get-tuple-element.14), channel_id=1, source_target_pairs={{0,4},{4,0},{1,5},{5,1},{2,6},{6,2},{3,7},{7,3},{8,12},{12,8},{9,1... | collective-permute-start | bytes 589832 | tf_op jit(solution)/shard_map/ppermute | solution.py:133
  79.7 4.6 %collective-permute-done.9 = bf16[192,512]{1,0:T(8,128)(2,1)S(1)} collective-permute-done((bf16[192,512]{1,0:T(8,128)(2,1)S(1)}, bf16[192,512]{1,0:T(8,128)(2,1)S(1)}, u32[]{:S(2)}, u32[]{:S(2)}) %collective-permute-start.9) | collective-permute-done | bytes 196640 | tf_op jit(solution)/shard_map/ppermute | solution.py:133
  84.9 0.9 %broadcast_select_fusion = bf16[1,1,384,512]{3,2,1,0:T(8,128)(2,1)} fusion(bf16[1,1,384,512]{3,2,1,0:T(8,128)(2,1)S(1)} %bitcast.142, pred[384]{0:T(512)(128)(4,1)S(1)} %broadcast_in_dim.18), kind=kLoop, calls=%fused_computation.63 | loop fusion | flops 196608 | bytes 786816 | tf_op jit(solution)/shard_map/jit(_take)/select_n | solution.py:135
  (58 shorter events, 4.8 us)
Async XLA Ops:
  0.0 6.8 %copy-start = (bf16[1,1,256,4096]{3,2,1,0:T(8,128)(2,1)S(1)}, bf16[1,1,256,4096]{3,2,1,0:T(8,128)(2,1)}, u32[]{:S(2)}) copy-start(bf16[1,1,256,4096]{3,2,1,0:T(8,128)(2,1)} %param.6) | copy-start | bytes 6291460
  0.0 8.0 %copy-start.6 = (s32[1,1,256,1]{2,3,1,0:T(1,128)S(1)}, s32[1,1,256,1]{2,3,1,0:T(1,128)}, u32[]{:S(2)}) copy-start(s32[1,1,256,1]{2,3,1,0:T(1,128)} %param.7) | copy-start | bytes 3076
  1.8 37.4 %collective-permute-start.1 = (bf16[256,1024]{1,0:T(8,128)(2,1)S(1)}, bf16[256,1024]{1,0:T(8,128)(2,1)S(1)}, u32[]{:S(2)}, u32[]{:S(2)}) collective-permute-start(bf16[256,1024]{1,0:T(8,128)(2,1)S(1)} %get-tuple-element.12), channel_id=1, source_target_pairs={{0,8},{8,16},{16,24},{1,9},{9,17},{17,25},{2,10},{10,18},{18,26},{... | collective-permute-start | bytes 1572872 | tf_op jit(solution)/shard_map/ppermute | solution.py:18
  9.9 24.5 %collective-permute-start = (f32[3,256]{1,0:T(4,128)S(1)}, f32[3,256]{1,0:T(4,128)S(1)}, u32[]{:S(2)}, u32[]{:S(2)}) collective-permute-start(f32[3,256]{1,0:T(4,128)S(1)} %pad_maximum_fusion.2), channel_id=1, source_target_pairs={{0,8},{8,16},{16,24},{1,9},{9,17},{17,25},{2,10},{10,18},{18,26},{... | collective-permute-start | bytes 9224 | tf_op jit(solution)/shard_map/ppermute | solution.py:18
  13.3 29.7 %collective-permute-start.4 = (bf16[256,1024]{1,0:T(8,128)(2,1)S(1)}, bf16[256,1024]{1,0:T(8,128)(2,1)}, u32[]{:S(2)}, u32[]{:S(2)}) collective-permute-start(bf16[256,1024]{1,0:T(8,128)(2,1)S(1)} %get-tuple-element.11), channel_id=1, source_target_pairs={{0,8},{8,16},{16,24},{1,9},{9,17},{17,25},{2,10},{10,18},{18,26},{... | collective-permute-start | bytes 1572872 | tf_op jit(solution)/shard_map/ppermute | solution.py:18
  17.6 33.5 %collective-permute-start.5 = (bf16[256,1024]{1,0:T(8,128)(2,1)S(1)}, bf16[256,1024]{1,0:T(8,128)(2,1)}, u32[]{:S(2)}, u32[]{:S(2)}) collective-permute-start(bf16[256,1024]{1,0:T(8,128)(2,1)S(1)} %get-tuple-element.10), channel_id=1, source_target_pairs={{0,8},{8,16},{16,24},{1,9},{9,17},{17,25},{2,10},{10,18},{18,26},{... | collective-permute-start | bytes 1572872 | tf_op jit(solution)/shard_map/ppermute | solution.py:18
  19.7 14.7 %copy-start.5 = (f32[1,4096]{1,0:T(1,128)S(1)}, f32[1,4096]{1,0:T(1,128)}, u32[]{:S(2)}) copy-start(f32[1,4096]{1,0:T(1,128)} %param.10) | copy-start | bytes 49156
  19.7 38.1 %collective-permute-start.6 = (bf16[256,1024]{1,0:T(8,128)(2,1)S(1)}, bf16[256,1024]{1,0:T(8,128)(2,1)}, u32[]{:S(2)}, u32[]{:S(2)}) collective-permute-start(bf16[256,1024]{1,0:T(8,128)(2,1)S(1)} %get-tuple-element.9), channel_id=1, source_target_pairs={{0,8},{8,16},{16,24},{1,9},{9,17},{17,25},{2,10},{10,18},{18,26},{... | collective-permute-start | bytes 1572872 | tf_op jit(solution)/shard_map/ppermute | solution.py:18
  34.4 1.2 %collective-permute-start.2 = (f32[256]{0:T(256)S(1)}, f32[256]{0:T(256)S(1)}, u32[]{:S(2)}, u32[]{:S(2)}) collective-permute-start(f32[256]{0:T(256)S(1)} %bitcast.151), channel_id=1, source_target_pairs={{0,1},{1,0},{2,3},{3,2},{4,5},{5,4},{6,7},{7,6},{8,9},{9,8},{10,11... | collective-permute-start | bytes 3080 | tf_op jit(solution)/shard_map/ppermute | solution.py:40
  35.6 3.6 %collective-permute-start.3 = (f32[256]{0:T(256)S(1)}, f32[256]{0:T(256)S(1)}, u32[]{:S(2)}, u32[]{:S(2)}) collective-permute-start(f32[256]{0:T(256)S(1)} %add.130), channel_id=1, source_target_pairs={{0,2},{1,3},{2,0},{3,1},{4,6},{5,7},{6,4},{7,5},{8,10},{9,11},{10,... | collective-permute-start | bytes 3080 | tf_op jit(solution)/shard_map/ppermute | solution.py:40
  37.1 5.9 %copy-start.3 = (bf16[1,1024,2048]{2,1,0:T(8,128)(2,1)S(1)}, bf16[1,1024,2048]{2,1,0:T(8,128)(2,1)}, u32[]{:S(2)}) copy-start(bf16[1,1024,2048]{2,1,0:T(8,128)(2,1)} %get-tuple-element.6) | copy-start | bytes 12582916
  39.2 7.1 %copy-start.4 = (bf16[1,1024,2048]{2,1,0:T(8,128)(2,1)S(1)}, bf16[1,1024,2048]{2,1,0:T(8,128)(2,1)}, u32[]{:S(2)}) copy-start(bf16[1,1024,2048]{2,1,0:T(8,128)(2,1)} %get-tuple-element.7) | copy-start | bytes 12582916
  46.3 4.8 %copy-start.2 = (bf16[1,1024,2048]{2,1,0:T(8,128)(2,1)S(1)}, bf16[1,1024,2048]{2,1,0:T(8,128)(2,1)}, u32[]{:S(2)}) copy-start(bf16[1,1024,2048]{2,1,0:T(8,128)(2,1)} %get-tuple-element.8) | copy-start | bytes 12582916
  51.1 6.7 %copy-start.1 = (bf16[1,1024,2048]{2,1,0:T(8,128)(2,1)S(1)}, bf16[1,1024,2048]{2,1,0:T(8,128)(2,1)}, u32[]{:S(2)}) copy-start(bf16[1,1024,2048]{2,1,0:T(8,128)(2,1)} %get-tuple-element.5) | copy-start | bytes 12582916
  66.1 2.9 %collective-permute-start.7 = (f32[2,512,256]{2,1,0:T(8,128)}, f32[2,512,256]{2,1,0:T(8,128)S(1)}, u32[]{:S(2)}, u32[]{:S(2)}) collective-permute-start(f32[2,512,256]{2,1,0:T(8,128)} %slice.132), channel_id=1, source_target_pairs={{0,1},{1,0},{2,3},{3,2},{4,5},{5,4},{6,7},{7,6},{8,9},{9,8},{10,11... | collective-permute-start | bytes 3145736 | tf_op jit(solution)/shard_map/ppermute | solution.py:31
  69.2 8.4 %collective-permute-start.8 = (bf16[1,512,256]{2,1,0:T(8,128)(2,1)S(1)}, bf16[1,512,256]{2,1,0:T(8,128)(2,1)S(1)}, u32[]{:S(2)}, u32[]{:S(2)}) collective-permute-start(bf16[1,512,256]{2,1,0:T(8,128)(2,1)S(1)} %slice.156), channel_id=1, source_target_pairs={{0,2},{1,3},{2,0},{3,1},{4,6},{5,7},{6,4},{7,5},{8,10},{9,11},{10,... | collective-permute-start | bytes 786440 | tf_op jit(solution)/shard_map/ppermute | solution.py:31
  78.2 6.2 %collective-permute-start.9 = (bf16[192,512]{1,0:T(8,128)(2,1)S(1)}, bf16[192,512]{1,0:T(8,128)(2,1)S(1)}, u32[]{:S(2)}, u32[]{:S(2)}) collective-permute-start(bf16[192,512]{1,0:T(8,128)(2,1)S(1)} %get-tuple-element.14), channel_id=1, source_target_pairs={{0,4},{4,0},{1,5},{5,1},{2,6},{6,2},{3,7},{7,3},{8,12},{12,8},{9,1... | collective-permute-start | bytes 589832 | tf_op jit(solution)/shard_map/ppermute | solution.py:133

commit v9 on v8

--- a/solution.py
+++ b/solution.py
@@ -101,17 +101,24 @@
     for k in range(len(CHUNK_EIGHTHS)):
         cols = slice(bounds[k], bounds[k + 1])
         arrived = shifted(tok_rows[:, cols], "section", 1)
-        normed = (arrived.astype(jnp.float32) * gain[cols] * scale[:, None]).astype(jnp.bfloat16)
-        terms = []
-        for s in range(tensor):
-            column = jnp.bitwise_xor(me_t, bit_reversed(s, levels)) * block
-            piece = lax.dynamic_slice_in_dim(weight[cols], column, block, axis=1)
-            terms.append(
-                lax.dot_general(
-                    piece, normed, (((0,), (1,)), ((), ())), preferred_element_type=jnp.float32
+        def project(arrived=arrived, cols=cols):
+            normed = (arrived.astype(jnp.float32) * gain[cols] * scale[:, None]).astype(jnp.bfloat16)
+            terms = []
+            for s in range(tensor):
+                column = jnp.bitwise_xor(me_t, bit_reversed(s, levels)) * block
+                piece = lax.dynamic_slice_in_dim(weight[cols], column, block, axis=1)
+                terms.append(
+                    lax.dot_general(
+                        piece, normed, (((0,), (1,)), ((), ())), preferred_element_type=jnp.float32
+                    )
                 )
-            )
-        term = jnp.stack(terms)
+            return jnp.stack(terms)
+
+        term = lax.cond(
+            first,
+            lambda: jnp.zeros((tensor, block, tok_count), jnp.float32),
+            project,
+        )
         partial = term if partial is None else partial + term
     summed = scatter_sum(partial, "tensor")
     local_cols = summed.shape[0]

time: 86.5 us -> 146 us (1.69)
  the two profiles are of different devices: /device:TPU:0 before, /device:TPU:28 now
where the time goes in v9:
time: 146 us; the launch traced here: 145 us
  waiting for transfers between devices  58.9 us (40%)
  matrix products  36 us (25%)
  local copies, waits for them, and re-layouts  28 us (19%)
  other arithmetic  11 us (8%)
  starting transfers between devices  9.21 us (6%)
  between operations  1.61 us (1%)
    ppermute x5, waiting for transfers between devices, shifted(): return lax.ppermute(block, axis, route)  39.9 us
    dot_general x16, matrix products, project(): lax.dot_general(piece, normed, (((0,), (1,)), ((), ())), preferred_elemen...  35.7 us
    ppermute x2, waiting for transfers between devices, scatter_sum(): current = keep + lax.ppermute(send, axis, pairs).astype(jnp.float32)  10.2 us
    slice x4, local copies, waits for them, and re-layouts, project(): piece = lax.dynamic_slice_in_dim(weight[cols], column, block, axis=1)  9.98 us
    cond x16, local copies, waits for them, and re-layouts  7.73 us
    ppermute x5, starting transfers between devices, shifted(): return lax.ppermute(block, axis, route)  6.58 us
    unnamed x14, local copies, waits for them, and re-layouts  5.39 us
    ppermute x1, waiting for transfers between devices, per_device(): received[offset] = lax.ppermute(outgoing, 'dp', pairs)  4.58 us
  transfers between devices with their start and end apart: 10, of which 6 were waited for; matrix products, arithmetic and copies ran while one was open for 28% of the time, Pallas kernels for 0%

profile of v9, /device:TPU:28, one launch (start us, length us, event | category | flops | bytes accessed | tf_op | source)
XLA Modules:
  0.0 144.9 jit_solution(9657047496508287666)
XLA Ops:
  0.0 2.7 %fusion.41 = (bf16[256,1024]{1,0:T(8,128)(2,1)}, bf16[256,1024]{1,0:T(8,128)(2,1)S(1)}, bf16[256,1024]{1,0:T(8,128)(2,1)S(1)}, bf16[256,1024]{1,0:T(8,128)(2,1)S(1)}) fusion(bf16[256,4096]{1,0:T(8,128)(2,1)} %bitcast.92), kind=kLoop, calls=%fused_computation.111 | loop fusion | bytes 4194304 | tf_op jit(solution)/shard_map/slice | solution.py:103
  12.4 39.9 %collective-permute-done = f32[3,256]{1,0:T(4,128)S(1)} collective-permute-done((f32[3,256]{1,0:T(4,128)S(1)}, f32[3,256]{1,0:T(4,128)S(1)}, u32[]{:S(2)}, u32[]{:S(2)}) %collective-permute-start) | collective-permute-done | bytes 3104 | tf_op jit(solution)/shard_map/ppermute | solution.py:18
  54.0 3.1 %collective-permute-done.3 = f32[256]{0:T(256)S(1)} collective-permute-done((f32[256]{0:T(256)S(1)}, f32[256]{0:T(256)S(1)}, u32[]{:S(2)}, u32[]{:S(2)}) %collective-permute-start.3) | collective-permute-done | bytes 1056 | tf_op jit(solution)/shard_map/ppermute | solution.py:40
  57.0 14.3 %conditional.4 = (f32[4,512,256]{2,1,0:T(8,128)S(1)}) conditional(s32[]{:T(128)} %convert_element_type.92, (bf16[4096,2048]{1,0:T(8,128)(2,1)}, s32[]{:T(128)}, bf16[256,1024]{1,0:T(8,128)(2,1)S(1)}, f32[4096]{0:T(1024)S(1)}, f32[256]{0:T(256)S(1)}) %tuple.57, () %tuple.30), branch_computations={%region_4.5_spmd, %region_5.6_spmd} | conditional | flops 1079508992 | bytes 39874852 | solution.py:117
  57.1 2.5 %slice.30 = bf16[1024,2048]{1,0:T(8,128)(2,1)S(1)} slice(bf16[4096,2048]{1,0:T(8,128)(2,1)} %get-tuple-element.54), slice={[0:1024], [0:2048]} | slice | bytes 8388608 | tf_op jit(solution)/shard_map/cond/branch_0_fun/slice | solution.py:109
  59.6 1.9 %copy-done.5 = bf16[1024,2048]{1,0:T(8,128)(2,1)} copy-done((bf16[1024,2048]{1,0:T(8,128)(2,1)}, bf16[1024,2048]{1,0:T(8,128)(2,1)S(1)}, u32[]{:S(2)}) %copy-start.5) | copy-done | bytes 4194328 | tf_op jit(solution)/shard_map/cond
  62.9 2.6 %convolution_bitcast_fusion.2 = f32[1,512,256]{2,1,0:T(8,128)} fusion(bf16[1024,2048]{1,0:T(8,128)(2,1)} %copy-done.5, s32[]{:T(128)S(6)} %select_n.100, bf16[256,1024]{1,0:T(8,128)(2,1)S(1)} %get-tuple-element.58, f32[256]{0:T(256)S(1)} %get-tuple-element.61, f32[1024]{0:T(1024)S(1)} %slice.50), kind=kOutput, calls=%fused_computation.4 | convolution fusion | flops 269484032 | bytes 2102276 | tf_op jit(solution)/shard_map/cond/branch_0_fun/dot_general | solution.py:111
  65.5 2.6 %convolution_bitcast_fusion.3 = f32[1,512,256]{2,1,0:T(8,128)} fusion(bf16[1024,2048]{1,0:T(8,128)(2,1)} %copy-done.5, s32[]{:T(128)S(6)} %select_n.99, bf16[256,1024]{1,0:T(8,128)(2,1)S(1)} %get-tuple-element.58, f32[256]{0:T(256)S(1)} %get-tuple-element.61, f32[1024]{0:T(1024)S(1)} %slice.50), kind=kOutput, calls=%fused_computation.5 | convolution fusion | flops 269484032 | bytes 2102276 | tf_op jit(solution)/shard_map/cond/branch_0_fun/dot_general | solution.py:111
  68.2 1.9 %convolution_bitcast_fusion = f32[1,512,256]{2,1,0:T(8,128)S(1)} fusion(bf16[1024,2048]{1,0:T(8,128)(2,1)} %copy-done.5, s32[]{:T(128)S(6)} %select_n.102, bf16[256,1024]{1,0:T(8,128)(2,1)S(1)} %get-tuple-element.58, f32[256]{0:T(256)S(1)} %get-tuple-element.61, f32[1024]{0:T(1024)S(1)} %slice.50), kind=kOutput, calls=%fused_computation.2 | convolution fusion | flops 269484032 | bytes 2102276 | tf_op jit(solution)/shard_map/cond/branch_0_fun/dot_general | solution.py:111
  72.7 15.7 %conditional.5 = (f32[4,512,256]{2,1,0:T(8,128)S(1)}) conditional(s32[]{:T(128)} %convert_element_type.92, (bf16[4096,2048]{1,0:T(8,128)(2,1)}, s32[]{:T(128)}, bf16[256,1024]{1,0:T(8,128)(2,1)}, f32[4096]{0:T(1024)S(1)}, f32[256]{0:T(256)S(1)}) %tuple.58, () %tuple.32), branch_computations={%region_6.7_spmd, %region_7.8_spmd} | conditional | flops 1079508992 | bytes 39874852 | solution.py:117
  72.7 2.5 %slice.51 = bf16[1024,2048]{1,0:T(8,128)(2,1)S(1)} slice(bf16[4096,2048]{1,0:T(8,128)(2,1)} %get-tuple-element.62), slice={[1024:2048], [0:2048]} | slice | bytes 8388608 | tf_op jit(solution)/shard_map/cond/branch_0_fun/slice | solution.py:109
  75.2 1.9 %copy-done.6 = bf16[1024,2048]{1,0:T(8,128)(2,1)} copy-done((bf16[1024,2048]{1,0:T(8,128)(2,1)}, bf16[1024,2048]{1,0:T(8,128)(2,1)S(1)}, u32[]{:S(2)}) %copy-start.6) | copy-done | bytes 4194328 | tf_op jit(solution)/shard_map/cond
  77.2 2.4 %convolution_bitcast_fusion.5 = f32[1,512,256]{2,1,0:T(8,128)} fusion(bf16[1024,2048]{1,0:T(8,128)(2,1)S(1)} %slice.51, s32[]{:T(128)S(6)} %select_n.105, bf16[256,1024]{1,0:T(8,128)(2,1)} %get-tuple-element.64, f32[256]{0:T(256)S(1)} %get-tuple-element.66, f32[1024]{0:T(1024)S(1)} %slice.52), kind=kOutput, calls=%fused_computation.17 | convolution fusion | flops 269484032 | bytes 2102276 | tf_op jit(solution)/shard_map/cond/branch_0_fun/dot_general | solution.py:111
  79.6 2.8 %convolution_bitcast_fusion.6 = f32[1,512,256]{2,1,0:T(8,128)} fusion(bf16[1024,2048]{1,0:T(8,128)(2,1)} %copy-done.6, s32[]{:T(128)S(6)} %select_n.104, bf16[256,1024]{1,0:T(8,128)(2,1)} %get-tuple-element.64, f32[256]{0:T(256)S(1)} %get-tuple-element.66, f32[1024]{0:T(1024)S(1)} %slice.52), kind=kOutput, calls=%fused_computation.18 | convolution fusion | flops 269484032 | bytes 2102276 | tf_op jit(solution)/shard_map/cond/branch_0_fun/dot_general | solution.py:111
  82.3 2.7 %convolution_bitcast_fusion.7 = f32[1,512,256]{2,1,0:T(8,128)} fusion(bf16[1024,2048]{1,0:T(8,128)(2,1)} %copy-done.6, s32[]{:T(128)S(6)} %select_n.103, bf16[256,1024]{1,0:T(8,128)(2,1)} %get-tuple-element.64, f32[256]{0:T(256)S(1)} %get-tuple-element.66, f32[1024]{0:T(1024)S(1)} %slice.52), kind=kOutput, calls=%fused_computation.19 | convolution fusion | flops 269484032 | bytes 2102276 | tf_op jit(solution)/shard_map/cond/branch_0_fun/dot_general | solution.py:111
  85.1 2.0 %convolution_bitcast_fusion.4 = f32[1,512,256]{2,1,0:T(8,128)S(1)} fusion(bf16[1024,2048]{1,0:T(8,128)(2,1)} %copy-done.6, s32[]{:T(128)S(6)} %select_n.106, bf16[256,1024]{1,0:T(8,128)(2,1)} %get-tuple-element.64, f32[256]{0:T(256)S(1)} %get-tuple-element.66, f32[1024]{0:T(1024)S(1)} %slice.52), kind=kOutput, calls=%fused_computation.16 | convolution fusion | flops 269484032 | bytes 2102276 | tf_op jit(solution)/shard_map/cond/branch_0_fun/dot_general | solution.py:111
  89.8 14.8 %conditional.6 = (f32[4,512,256]{2,1,0:T(8,128)S(1)}) conditional(s32[]{:T(128)} %convert_element_type.92, (bf16[4096,2048]{1,0:T(8,128)(2,1)}, s32[]{:T(128)}, bf16[256,1024]{1,0:T(8,128)(2,1)}, f32[4096]{0:T(1024)S(1)}, f32[256]{0:T(256)S(1)}) %tuple.59, () %tuple.34), branch_computations={%region_8.9_spmd, %region_9.10_spmd} | conditional | flops 1079508992 | bytes 39874852 | solution.py:117
  89.8 2.5 %slice.53 = bf16[1024,2048]{1,0:T(8,128)(2,1)S(1)} slice(bf16[4096,2048]{1,0:T(8,128)(2,1)} %get-tuple-element.67), slice={[2048:3072], [0:2048]} | slice | bytes 8388608 | tf_op jit(solution)/shard_map/cond/branch_0_fun/slice | solution.py:109
  92.3 1.9 %copy-done.7 = bf16[1024,2048]{1,0:T(8,128)(2,1)} copy-done((bf16[1024,2048]{1,0:T(8,128)(2,1)}, bf16[1024,2048]{1,0:T(8,128)(2,1)S(1)}, u32[]{:S(2)}) %copy-start.7) | copy-done | bytes 4194328 | tf_op jit(solution)/shard_map/cond
  95.9 2.7 %convolution_bitcast_fusion.9 = f32[1,512,256]{2,1,0:T(8,128)} fusion(bf16[1024,2048]{1,0:T(8,128)(2,1)} %copy-done.7, s32[]{:T(128)S(6)} %select_n.109, bf16[256,1024]{1,0:T(8,128)(2,1)} %get-tuple-element.69, f32[256]{0:T(256)S(1)} %get-tuple-element.71, f32[1024]{0:T(1024)S(1)} %slice.54), kind=kOutput, calls=%fused_computation.31 | convolution fusion | flops 269484032 | bytes 2102276 | tf_op jit(solution)/shard_map/cond/branch_0_fun/dot_general | solution.py:111
  98.6 2.7 %convolution_bitcast_fusion.11 = f32[1,512,256]{2,1,0:T(8,128)} fusion(bf16[1024,2048]{1,0:T(8,128)(2,1)} %copy-done.7, s32[]{:T(128)S(6)} %select_n.107, bf16[256,1024]{1,0:T(8,128)(2,1)} %get-tuple-element.69, f32[256]{0:T(256)S(1)} %get-tuple-element.71, f32[1024]{0:T(1024)S(1)} %slice.54), kind=kOutput, calls=%fused_computation.33 | convolution fusion | flops 269484032 | bytes 2102276 | tf_op jit(solution)/shard_map/cond/branch_0_fun/dot_general | solution.py:111
  101.4 2.0 %convolution_bitcast_fusion.8 = f32[1,512,256]{2,1,0:T(8,128)S(1)} fusion(bf16[1024,2048]{1,0:T(8,128)(2,1)} %copy-done.7, s32[]{:T(128)S(6)} %select_n.110, bf16[256,1024]{1,0:T(8,128)(2,1)} %get-tuple-element.69, f32[256]{0:T(256)S(1)} %get-tuple-element.71, f32[1024]{0:T(1024)S(1)} %slice.54), kind=kOutput, calls=%fused_computation.30 | convolution fusion | flops 269484032 | bytes 2102276 | tf_op jit(solution)/shard_map/cond/branch_0_fun/dot_general | solution.py:111
  105.9 12.9 %conditional.7 = (f32[4,512,256]{2,1,0:T(8,128)S(1)}) conditional(s32[]{:T(128)} %convert_element_type.92, (bf16[4096,2048]{1,0:T(8,128)(2,1)}, s32[]{:T(128)}, bf16[256,1024]{1,0:T(8,128)(2,1)}, f32[4096]{0:T(1024)S(1)}, f32[256]{0:T(256)S(1)}) %tuple.60, () %tuple.36), branch_computations={%region_10.11_spmd, %region_11.12_spmd} | conditional | flops 1079508992 | bytes 39874852 | solution.py:117
  105.9 2.5 %slice.70 = bf16[1024,2048]{1,0:T(8,128)(2,1)S(1)} slice(bf16[4096,2048]{1,0:T(8,128)(2,1)} %get-tuple-element.72), slice={[3072:4096], [0:2048]} | slice | bytes 8388608 | tf_op jit(solution)/shard_map/cond/branch_0_fun/slice | solution.py:109
  108.5 1.9 %copy-done.8 = bf16[1024,2048]{1,0:T(8,128)(2,1)} copy-done((bf16[1024,2048]{1,0:T(8,128)(2,1)}, bf16[1024,2048]{1,0:T(8,128)(2,1)S(1)}, u32[]{:S(2)}) %copy-start.8) | copy-done | bytes 4194328 | tf_op jit(solution)/shard_map/cond
  112.0 1.9 %convolution_bitcast_fusion.14 = f32[1,512,256]{2,1,0:T(8,128)S(1)} fusion(bf16[1024,2048]{1,0:T(8,128)(2,1)} %copy-done.8, s32[]{:T(128)S(6)} %select_n.112, bf16[256,1024]{1,0:T(8,128)(2,1)} %get-tuple-element.74, f32[256]{0:T(256)S(1)} %get-tuple-element.76, f32[1024]{0:T(1024)S(1)} %slice.71), kind=kOutput, calls=%fused_computation.46 | convolution fusion | flops 269484032 | bytes 2102276 | tf_op jit(solution)/shard_map/cond/branch_0_fun/dot_general | solution.py:111
  114.0 2.7 %convolution_bitcast_fusion.15 = f32[1,512,256]{2,1,0:T(8,128)} fusion(bf16[1024,2048]{1,0:T(8,128)(2,1)} %copy-done.8, s32[]{:T(128)S(6)} %select_n.111, bf16[256,1024]{1,0:T(8,128)(2,1)} %get-tuple-element.74, f32[256]{0:T(256)S(1)} %get-tuple-element.76, f32[1024]{0:T(1024)S(1)} %slice.71), kind=kOutput, calls=%fused_computation.47 | convolution fusion | flops 269484032 | bytes 2102276 | tf_op jit(solution)/shard_map/cond/branch_0_fun/dot_general | solution.py:111
  116.7 2.0 %convolution_bitcast_fusion.12 = f32[1,512,256]{2,1,0:T(8,128)S(1)} fusion(bf16[1024,2048]{1,0:T(8,128)(2,1)} %copy-done.8, s32[]{:T(128)S(6)} %select_n.114, bf16[256,1024]{1,0:T(8,128)(2,1)} %get-tuple-element.74, f32[256]{0:T(256)S(1)} %get-tuple-element.76, f32[1024]{0:T(1024)S(1)} %slice.71), kind=kOutput, calls=%fused_computation.44 | convolution fusion | flops 269484032 | bytes 2102276 | tf_op jit(solution)/shard_map/cond/branch_0_fun/dot_general | solution.py:111
  120.2 4.0 %add_add_fusion = f32[4,512,256]{2,1,0:T(8,128)S(1)} fusion(f32[4,512,256]{2,1,0:T(8,128)} %copy-done.3, f32[4,512,256]{2,1,0:T(8,128)} %copy-done.2, f32[4,512,256]{2,1,0:T(8,128)} %copy-done, f32[4,512,256]{2,1,0:T(8,128)} %copy-done.1), kind=kLoop, calls=%fused_computation.58 | loop fusion | flops 1572864 | bytes 10485760 | tf_op jit(solution)/shard_map/add | solution.py:122
  125.5 2.7 %collective-permute-done.7 = f32[2,512,256]{2,1,0:T(8,128)S(1)} collective-permute-done((f32[2,512,256]{2,1,0:T(8,128)}, f32[2,512,256]{2,1,0:T(8,128)S(1)}, u32[]{:S(2)}, u32[]{:S(2)}) %collective-permute-start.7) | collective-permute-done | bytes 1048608 | tf_op jit(solution)/shard_map/ppermute | solution.py:31
  129.2 7.5 %collective-permute-done.8 = bf16[1,512,256]{2,1,0:T(8,128)(2,1)S(1)} collective-permute-done((bf16[1,512,256]{2,1,0:T(8,128)(2,1)S(1)}, bf16[1,512,256]{2,1,0:T(8,128)(2,1)S(1)}, u32[]{:S(2)}, u32[]{:S(2)}) %collective-permute-start.8) | collective-permute-done | bytes 262176 | tf_op jit(solution)/shard_map/ppermute | solution.py:31
  138.9 4.6 %collective-permute-done.9 = bf16[192,512]{1,0:T(8,128)(2,1)S(1)} collective-permute-done((bf16[192,512]{1,0:T(8,128)(2,1)S(1)}, bf16[192,512]{1,0:T(8,128)(2,1)S(1)}, u32[]{:S(2)}, u32[]{:S(2)}) %collective-permute-start.9) | collective-permute-done | bytes 196640 | tf_op jit(solution)/shard_map/ppermute | solution.py:140
  (88 shorter events, 29.8 us)
Async XLA Ops:
  0.0 8.1 %copy-start.4 = (bf16[1,1,256,4096]{3,2,1,0:T(8,128)(2,1)S(1)}, bf16[1,1,256,4096]{3,2,1,0:T(8,128)(2,1)}, u32[]{:S(2)}) copy-start(bf16[1,1,256,4096]{3,2,1,0:T(8,128)(2,1)} %param.14) | copy-start | bytes 6291460
  2.7 6.5 %copy-start.14 = (s32[1,1,256,1]{2,3,1,0:T(1,128)S(1)}, s32[1,1,256,1]{2,3,1,0:T(1,128)}, u32[]{:S(2)}) copy-start(s32[1,1,256,1]{2,3,1,0:T(1,128)} %param.15) | copy-start | bytes 3076
  2.7 54.3 %copy-start.13 = (f32[1,4096]{1,0:T(1,128)S(1)}, f32[1,4096]{1,0:T(1,128)}, u32[]{:S(2)}) copy-start(f32[1,4096]{1,0:T(1,128)} %param.18) | copy-start | bytes 49156
  2.7 54.3 %collective-permute-start.1 = (bf16[256,1024]{1,0:T(8,128)(2,1)S(1)}, bf16[256,1024]{1,0:T(8,128)(2,1)S(1)}, u32[]{:S(2)}, u32[]{:S(2)}) collective-permute-start(bf16[256,1024]{1,0:T(8,128)(2,1)S(1)} %get-tuple-element.79), channel_id=1, source_target_pairs={{0,8},{8,16},{16,24},{1,9},{9,17},{17,25},{2,10},{10,18},{18,26},{... | collective-permute-start | bytes 1572872 | tf_op jit(solution)/shard_map/ppermute | solution.py:18
  4.2 67.2 %collective-permute-start.4 = (bf16[256,1024]{1,0:T(8,128)(2,1)}, bf16[256,1024]{1,0:T(8,128)(2,1)}, u32[]{:S(2)}, u32[]{:S(2)}) collective-permute-start(bf16[256,1024]{1,0:T(8,128)(2,1)} %get-tuple-element.77), channel_id=1, source_target_pairs={{0,8},{8,16},{16,24},{1,9},{9,17},{17,25},{2,10},{10,18},{18,26},{... | collective-permute-start | bytes 1572872 | tf_op jit(solution)/shard_map/ppermute | solution.py:18
  5.5 83.0 %collective-permute-start.5 = (bf16[256,1024]{1,0:T(8,128)(2,1)S(1)}, bf16[256,1024]{1,0:T(8,128)(2,1)}, u32[]{:S(2)}, u32[]{:S(2)}) collective-permute-start(bf16[256,1024]{1,0:T(8,128)(2,1)S(1)} %get-tuple-element.78), channel_id=1, source_target_pairs={{0,8},{8,16},{16,24},{1,9},{9,17},{17,25},{2,10},{10,18},{18,26},{... | collective-permute-start | bytes 1572872 | tf_op jit(solution)/shard_map/ppermute | solution.py:18
  6.8 97.8 %collective-permute-start.6 = (bf16[256,1024]{1,0:T(8,128)(2,1)S(1)}, bf16[256,1024]{1,0:T(8,128)(2,1)}, u32[]{:S(2)}, u32[]{:S(2)}) collective-permute-start(bf16[256,1024]{1,0:T(8,128)(2,1)S(1)} %get-tuple-element.80), channel_id=1, source_target_pairs={{0,8},{8,16},{16,24},{1,9},{9,17},{17,25},{2,10},{10,18},{18,26},{... | collective-permute-start | bytes 1572872 | tf_op jit(solution)/shard_map/ppermute | solution.py:18
  11.1 41.2 %collective-permute-start = (f32[3,256]{1,0:T(4,128)S(1)}, f32[3,256]{1,0:T(4,128)S(1)}, u32[]{:S(2)}, u32[]{:S(2)}) collective-permute-start(f32[3,256]{1,0:T(4,128)S(1)} %pad_maximum_fusion.6), channel_id=1, source_target_pairs={{0,8},{8,16},{16,24},{1,9},{9,17},{17,25},{2,10},{10,18},{18,26},{... | collective-permute-start | bytes 9224 | tf_op jit(solution)/shard_map/ppermute | solution.py:18
  52.3 1.2 collective-permute-start.2
  53.4 3.6 %collective-permute-start.3 = (f32[256]{0:T(256)S(1)}, f32[256]{0:T(256)S(1)}, u32[]{:S(2)}, u32[]{:S(2)}) collective-permute-start(f32[256]{0:T(256)S(1)} %add.153), channel_id=1, source_target_pairs={{0,2},{1,3},{2,0},{3,1},{4,6},{5,7},{6,4},{7,5},{8,10},{9,11},{10,... | collective-permute-start | bytes 3080 | tf_op jit(solution)/shard_map/ppermute | solution.py:40
  59.6 1.9 %copy-start.5 = (bf16[1024,2048]{1,0:T(8,128)(2,1)}, bf16[1024,2048]{1,0:T(8,128)(2,1)S(1)}, u32[]{:S(2)}) copy-start(bf16[1024,2048]{1,0:T(8,128)(2,1)S(1)} %slice.30) | copy-start | bytes 12582916 | tf_op jit(solution)/shard_map/cond
  68.1 1.9 %copy-start.9 = (f32[1,512,256]{2,1,0:T(8,128)S(1)}, f32[1,512,256]{2,1,0:T(8,128)}, u32[]{:S(2)}) copy-start(f32[1,512,256]{2,1,0:T(8,128)} %convolution_bitcast_fusion.3) | copy-start | bytes 1572868 | tf_op jit(solution)/shard_map/cond
  71.4 1.3 copy-start
  75.2 1.9 %copy-start.6 = (bf16[1024,2048]{1,0:T(8,128)(2,1)}, bf16[1024,2048]{1,0:T(8,128)(2,1)S(1)}, u32[]{:S(2)}) copy-start(bf16[1024,2048]{1,0:T(8,128)(2,1)S(1)} %slice.51) | copy-start | bytes 12582916 | tf_op jit(solution)/shard_map/cond
  85.1 2.0 %copy-start.10 = (f32[1,512,256]{2,1,0:T(8,128)S(1)}, f32[1,512,256]{2,1,0:T(8,128)}, u32[]{:S(2)}) copy-start(f32[1,512,256]{2,1,0:T(8,128)} %convolution_bitcast_fusion.7) | copy-start | bytes 1572868 | tf_op jit(solution)/shard_map/cond
  88.4 1.4 copy-start.1
  92.3 1.9 %copy-start.7 = (bf16[1024,2048]{1,0:T(8,128)(2,1)}, bf16[1024,2048]{1,0:T(8,128)(2,1)S(1)}, u32[]{:S(2)}) copy-start(bf16[1024,2048]{1,0:T(8,128)(2,1)S(1)} %slice.53) | copy-start | bytes 12582916 | tf_op jit(solution)/shard_map/cond
  101.4 2.0 %copy-start.11 = (f32[1,512,256]{2,1,0:T(8,128)S(1)}, f32[1,512,256]{2,1,0:T(8,128)}, u32[]{:S(2)}) copy-start(f32[1,512,256]{2,1,0:T(8,128)} %convolution_bitcast_fusion.11) | copy-start | bytes 1572868 | tf_op jit(solution)/shard_map/cond
  104.6 1.4 copy-start.2
  108.4 1.9 %copy-start.8 = (bf16[1024,2048]{1,0:T(8,128)(2,1)}, bf16[1024,2048]{1,0:T(8,128)(2,1)S(1)}, u32[]{:S(2)}) copy-start(bf16[1024,2048]{1,0:T(8,128)(2,1)S(1)} %slice.70) | copy-start | bytes 12582916 | tf_op jit(solution)/shard_map/cond
  116.7 2.0 %copy-start.12 = (f32[1,512,256]{2,1,0:T(8,128)S(1)}, f32[1,512,256]{2,1,0:T(8,128)}, u32[]{:S(2)}) copy-start(f32[1,512,256]{2,1,0:T(8,128)} %convolution_bitcast_fusion.15) | copy-start | bytes 1572868 | tf_op jit(solution)/shard_map/cond
  118.9 1.3 copy-start.3
  125.3 2.9 %collective-permute-start.7 = (f32[2,512,256]{2,1,0:T(8,128)}, f32[2,512,256]{2,1,0:T(8,128)S(1)}, u32[]{:S(2)}, u32[]{:S(2)}) collective-permute-start(f32[2,512,256]{2,1,0:T(8,128)} %slice.116), channel_id=1, source_target_pairs={{0,1},{1,0},{2,3},{3,2},{4,5},{5,4},{6,7},{7,6},{8,9},{9,8},{10,11... | collective-permute-start | bytes 3145736 | tf_op jit(solution)/shard_map/ppermute | solution.py:31
  128.3 8.4 %collective-permute-start.8 = (bf16[1,512,256]{2,1,0:T(8,128)(2,1)S(1)}, bf16[1,512,256]{2,1,0:T(8,128)(2,1)S(1)}, u32[]{:S(2)}, u32[]{:S(2)}) collective-permute-start(bf16[1,512,256]{2,1,0:T(8,128)(2,1)S(1)} %slice.140), channel_id=1, source_target_pairs={{0,2},{1,3},{2,0},{3,1},{4,6},{5,7},{6,4},{7,5},{8,10},{9,11},{10,... | collective-permute-start | bytes 786440 | tf_op jit(solution)/shard_map/ppermute | solution.py:31
  137.3 6.2 %collective-permute-start.9 = (bf16[192,512]{1,0:T(8,128)(2,1)S(1)}, bf16[192,512]{1,0:T(8,128)(2,1)S(1)}, u32[]{:S(2)}, u32[]{:S(2)}) collective-permute-start(bf16[192,512]{1,0:T(8,128)(2,1)S(1)} %get-tuple-element.82), channel_id=1, source_target_pairs={{0,4},{4,0},{1,5},{5,1},{2,6},{6,2},{3,7},{7,3},{8,12},{12,8},{9,1... | collective-permute-start | bytes 589832 | tf_op jit(solution)/shard_map/ppermute | solution.py:140

commit v10 on v9

--- a/solution.py
+++ b/solution.py
@@ -101,25 +101,23 @@
     for k in range(len(CHUNK_EIGHTHS)):
         cols = slice(bounds[k], bounds[k + 1])
         arrived = shifted(tok_rows[:, cols], "section", 1)
-        def project(arrived=arrived, cols=cols):
-            normed = (arrived.astype(jnp.float32) * gain[cols] * scale[:, None]).astype(jnp.bfloat16)
+        if partial is not None:
+            partial, arrived = lax.optimization_barrier((partial, arrived))
+        normed = (arrived.astype(jnp.float32) * gain[cols] * scale[:, None]).astype(jnp.bfloat16)
+        for low in range(bounds[k], bounds[k + 1], local_width // 8):
+            part = slice(low, low + local_width // 8)
+            sub = normed[:, low - bounds[k]:low - bounds[k] + local_width // 8]
             terms = []
             for s in range(tensor):
                 column = jnp.bitwise_xor(me_t, bit_reversed(s, levels)) * block
-                piece = lax.dynamic_slice_in_dim(weight[cols], column, block, axis=1)
+                piece = lax.dynamic_slice_in_dim(weight[part], column, block, axis=1)
                 terms.append(
                     lax.dot_general(
-                        piece, normed, (((0,), (1,)), ((), ())), preferred_element_type=jnp.float32
+                        piece, sub, (((0,), (1,)), ((), ())), preferred_element_type=jnp.float32
                     )
                 )
-            return jnp.stack(terms)
-
-        term = lax.cond(
-            first,
-            lambda: jnp.zeros((tensor, block, tok_count), jnp.float32),
-            project,
-        )
-        partial = term if partial is None else partial + term
+            term = jnp.stack(terms)
+            partial = term if partial is None else partial + term
     summed = scatter_sum(partial, "tensor")
     local_cols = summed.shape[0]
     local_kv = summed.reshape(local_cols // (2 * HD), 2, HD, tok_count)

time: 146 us -> 80.9 us (0.55)
  the two profiles are of different devices: /device:TPU:28 before, /device:TPU:0 now
where the time goes in v10:
time: 80.9 us; the launch traced here: 80.3 us
  starting transfers between devices  20.7 us (26%)
  local copies, waits for them, and re-layouts  19.7 us (24%)
  waiting for transfers between devices  16.9 us (21%)
  matrix products  13.8 us (17%)
  other arithmetic  7.37 us (9%)
  between operations  1.9 us (2%)
    ppermute x5, starting transfers between devices, shifted(): return lax.ppermute(block, axis, route)  15.9 us
    dot_general x32, matrix products, per_device(): lax.dot_general(piece, sub, (((0,), (1,)), ((), ())), preferred_element_t...  13.5 us
    slice x1, local copies, waits for them, and re-layouts, per_device(): piece = lax.dynamic_slice_in_dim(weight[part], column, block, axis=1)  11.5 us
    ppermute x2, waiting for transfers between devices, scatter_sum(): current = keep + lax.ppermute(send, axis, pairs).astype(jnp.float32)  9.18 us
    ppermute x1, waiting for transfers between devices, per_device(): received[offset] = lax.ppermute(outgoing, 'dp', pairs)  4.57 us
    ppermute x2, waiting for transfers between devices, all_sum(): lax.ppermute(value, axis, [(i, i ^ bit) for i in range(size)])  3.17 us
    unnamed x20, local copies, waits for them, and re-layouts  3.09 us
    slice x1, local copies, waits for them, and re-layouts, per_device(): arrived = shifted(tok_rows[:, cols], 'section', 1)  3 us
  transfers between devices with their start and end apart: 10, of which 5 were waited for; matrix products, arithmetic and copies ran while one was open for 35% of the time, Pallas kernels for 0%

profile of v10, /device:TPU:0, one launch (start us, length us, event | category | flops | bytes accessed | tf_op | source)
XLA Modules:
  0.0 80.3 jit_solution(14592105698132695483)
XLA Ops:
  0.0 3.0 %fusion.141 = (bf16[256,1024]{1,0:T(8,128)(2,1)}, bf16[256,1024]{1,0:T(8,128)(2,1)}, bf16[256,1024]{1,0:T(8,128)(2,1)}, bf16[256,1024]{1,0:T(8,128)(2,1)}) fusion(bf16[256,4096]{1,0:T(8,128)(2,1)} %bitcast.218), kind=kLoop, calls=%fused_computation.226 | loop fusion | bytes 4194304 | tf_op jit(solution)/shard_map/slice | solution.py:103
  3.0 5.9 %collective-permute-start.1 = (bf16[256,1024]{1,0:T(8,128)(2,1)}, bf16[256,1024]{1,0:T(8,128)(2,1)}, u32[]{:S(2)}, u32[]{:S(2)}) collective-permute-start(bf16[256,1024]{1,0:T(8,128)(2,1)} %get-tuple-element.28), channel_id=1, source_target_pairs={{0,8},{8,16},{16,24},{1,9},{9,17},{17,25},{2,10},{10,18},{18,26},{... | collective-permute-start | bytes 1572872 | tf_op jit(solution)/shard_map/ppermute | solution.py:18
  8.9 0.5 multiply_reduce_fusion
  10.1 0.6 reduce-window.6
  11.9 2.7 %collective-permute-start = (f32[3,256]{1,0:T(4,128)S(1)}, f32[3,256]{1,0:T(4,128)S(1)}, u32[]{:S(2)}, u32[]{:S(2)}) collective-permute-start(f32[3,256]{1,0:T(4,128)S(1)} %pad_maximum_fusion.2), channel_id=1, source_target_pairs={{0,8},{8,16},{16,24},{1,9},{9,17},{17,25},{2,10},{10,18},{18,26},{... | collective-permute-start | bytes 9224 | tf_op jit(solution)/shard_map/ppermute | solution.py:18
  14.6 4.3 %collective-permute-start.4 = (bf16[256,1024]{1,0:T(8,128)(2,1)}, bf16[256,1024]{1,0:T(8,128)(2,1)}, u32[]{:S(2)}, u32[]{:S(2)}) collective-permute-start(bf16[256,1024]{1,0:T(8,128)(2,1)} %get-tuple-element.27), channel_id=1, source_target_pairs={{0,8},{8,16},{16,24},{1,9},{9,17},{17,25},{2,10},{10,18},{18,26},{... | collective-permute-start | bytes 1572872 | tf_op jit(solution)/shard_map/ppermute | solution.py:18
  18.9 1.3 %collective-permute-start.5 = (bf16[256,1024]{1,0:T(8,128)(2,1)}, bf16[256,1024]{1,0:T(8,128)(2,1)S(1)}, u32[]{:S(2)}, u32[]{:S(2)}) collective-permute-start(bf16[256,1024]{1,0:T(8,128)(2,1)} %get-tuple-element.26), channel_id=1, source_target_pairs={{0,8},{8,16},{16,24},{1,9},{9,17},{17,25},{2,10},{10,18},{18,26},{... | collective-permute-start | bytes 1572872 | tf_op jit(solution)/shard_map/ppermute | solution.py:18
  20.2 1.8 %collective-permute-start.6 = (bf16[256,1024]{1,0:T(8,128)(2,1)}, bf16[256,1024]{1,0:T(8,128)(2,1)S(1)}, u32[]{:S(2)}, u32[]{:S(2)}) collective-permute-start(bf16[256,1024]{1,0:T(8,128)(2,1)} %get-tuple-element.25), channel_id=1, source_target_pairs={{0,8},{8,16},{16,24},{1,9},{9,17},{17,25},{2,10},{10,18},{18,26},{... | collective-permute-start | bytes 1572872 | tf_op jit(solution)/shard_map/ppermute | solution.py:18
  22.0 11.5 %fusion.140 = (bf16[1,512,2048]{2,1,0:T(8,128)(2,1)S(1)}, bf16[1,512,2048]{2,1,0:T(8,128)(2,1)}, bf16[1,512,2048]{2,1,0:T(8,128)(2,1)}, bf16[1,512,2048]{2,1,0:T...) fusion(bf16[1,4096,2048]{2,1,0:T(8,128)(2,1)} %param.11), kind=kLoop, calls=%fused_computation.225 | loop fusion | bytes 33554432 | tf_op jit(solution)/shard_map/slice | solution.py:113
  33.6 1.1 %collective-permute-done.2 = f32[256]{0:T(256)S(1)} collective-permute-done((f32[256]{0:T(256)S(1)}, f32[256]{0:T(256)S(1)}, u32[]{:S(2)}, u32[]{:S(2)}) %collective-permute-start.2) | collective-permute-done | bytes 1056 | tf_op jit(solution)/shard_map/ppermute | solution.py:40
  34.7 1.5 %collective-permute-start.3 = (f32[256]{0:T(256)S(1)}, f32[256]{0:T(256)S(1)}, u32[]{:S(2)}, u32[]{:S(2)}) collective-permute-start(f32[256]{0:T(256)S(1)} %add.158), channel_id=1, source_target_pairs={{0,2},{1,3},{2,0},{3,1},{4,6},{5,7},{6,4},{7,5},{8,10},{9,11},{10,... | collective-permute-start | bytes 3080 | tf_op jit(solution)/shard_map/ppermute | solution.py:40
  36.2 2.1 %collective-permute-done.3 = f32[256]{0:T(256)S(1)} collective-permute-done((f32[256]{0:T(256)S(1)}, f32[256]{0:T(256)S(1)}, u32[]{:S(2)}, u32[]{:S(2)}) %collective-permute-start.3) | collective-permute-done | bytes 1056 | tf_op jit(solution)/shard_map/ppermute | solution.py:40
  38.3 1.2 %multiply_convert_fusion.3 = bf16[256,1024]{1,0:T(8,128)(2,1)S(1)} fusion(bf16[256,1024]{1,0:T(8,128)(2,1)} %collective-permute-done.1, f32[256]{0:T(256)S(1)} %add_rsqrt_fusion, f32[1024]{0:T(1024)S(1)} %bitcast.228), kind=kLoop, calls=%fused_computation.46 | loop fusion | flops 1048576 | bytes 1053696 | tf_op jit(solution)/shard_map/convert_element_type | solution.py:106
  39.5 1.4 %convolution_bitcast_fusion.28 = f32[1,512,256]{2,1,0:T(8,128)S(1)} fusion(bf16[1,512,2048]{2,1,0:T(8,128)(2,1)} %get-tuple-element.23, s32[]{:T(128)S(6)} %select_n.126, bf16[256,1024]{1,0:T(8,128)(2,1)S(1)} %multiply_convert_fusion.3), kind=kOutput, calls=%fused_computation.38 | convolution fusion | flops 134217728 | bytes 1310724 | tf_op jit(solution)/shard_map/dot_general | solution.py:115
  40.9 1.5 %convolution_bitcast_fusion.29 = f32[1,512,256]{2,1,0:T(8,128)S(1)} fusion(bf16[1,512,2048]{2,1,0:T(8,128)(2,1)} %get-tuple-element.23, s32[]{:T(128)S(6)} %select_n.125, bf16[256,1024]{1,0:T(8,128)(2,1)S(1)} %multiply_convert_fusion.3), kind=kOutput, calls=%fused_computation.39 | convolution fusion | flops 134217728 | bytes 1310724 | tf_op jit(solution)/shard_map/dot_general | solution.py:115
  44.9 1.3 %multiply_convert_fusion.2 = bf16[256,1024]{1,0:T(8,128)(2,1)S(1)} fusion(bf16[256,1024]{1,0:T(8,128)(2,1)} %collective-permute-done.4, f32[1024]{0:T(1024)S(1)} %bitcast.227, f32[256]{0:T(256)S(1)} %add_rsqrt_fusion), kind=kLoop, calls=%fused_computation.45 | loop fusion | flops 1048576 | bytes 1053696 | tf_op jit(solution)/shard_map/convert_element_type | solution.py:106
  47.8 0.5 copy-done.3
  49.8 0.4 fusion
  50.4 1.0 %copy-done.2 = bf16[1,512,2048]{2,1,0:T(8,128)(2,1)S(1)} copy-done((bf16[1,512,2048]{2,1,0:T(8,128)(2,1)S(1)}, bf16[1,512,2048]{2,1,0:T(8,128)(2,1)}, u32[]{:S(2)}) %copy-start.2) | copy-done | bytes 2097176
  52.8 0.5 copy-done.1
  54.7 0.4 fusion.1
  55.3 1.0 %copy-done = bf16[1,512,2048]{2,1,0:T(8,128)(2,1)S(1)} copy-done((bf16[1,512,2048]{2,1,0:T(8,128)(2,1)S(1)}, bf16[1,512,2048]{2,1,0:T(8,128)(2,1)}, u32[]{:S(2)}) %copy-start) | copy-done | bytes 2097176
  58.1 0.4 convolution_bitcast_fusion.1
  59.2 0.4 fusion.2
  59.6 1.0 %slice.204 = f32[2,512,256]{2,1,0:T(8,128)} slice(f32[4,512,256]{2,1,0:T(8,128)S(1)} %fusion.2), slice={[2:4], [0:512], [0:256]} | slice | bytes 2097152 | tf_op jit(solution)/shard_map/slice | solution.py:27
  60.9 2.7 %collective-permute-done.7 = f32[2,512,256]{2,1,0:T(8,128)S(1)} collective-permute-done((f32[2,512,256]{2,1,0:T(8,128)}, f32[2,512,256]{2,1,0:T(8,128)S(1)}, u32[]{:S(2)}, u32[]{:S(2)}) %collective-permute-start.7) | collective-permute-done | bytes 1048608 | tf_op jit(solution)/shard_map/ppermute | solution.py:31
  63.7 1.6 %collective-permute-start.8 = (bf16[1,512,256]{2,1,0:T(8,128)(2,1)S(1)}, bf16[1,512,256]{2,1,0:T(8,128)(2,1)S(1)}, u32[]{:S(2)}, u32[]{:S(2)}) collective-permute-start(bf16[1,512,256]{2,1,0:T(8,128)(2,1)S(1)} %slice.292), channel_id=1, source_target_pairs={{0,2},{1,3},{2,0},{3,1},{4,6},{5,7},{6,4},{7,5},{8,10},{9,11},{10,... | collective-permute-start | bytes 786440 | tf_op jit(solution)/shard_map/ppermute | solution.py:31
  65.6 6.5 %collective-permute-done.8 = bf16[1,512,256]{2,1,0:T(8,128)(2,1)S(1)} collective-permute-done((bf16[1,512,256]{2,1,0:T(8,128)(2,1)S(1)}, bf16[1,512,256]{2,1,0:T(8,128)(2,1)S(1)}, u32[]{:S(2)}, u32[]{:S(2)}) %collective-permute-start.8) | collective-permute-done | bytes 262176 | tf_op jit(solution)/shard_map/ppermute | solution.py:31
  72.7 1.6 %collective-permute-start.9 = (bf16[192,512]{1,0:T(8,128)(2,1)S(1)}, bf16[192,512]{1,0:T(8,128)(2,1)S(1)}, u32[]{:S(2)}, u32[]{:S(2)}) collective-permute-start(bf16[192,512]{1,0:T(8,128)(2,1)S(1)} %get-tuple-element.30), channel_id=1, source_target_pairs={{0,4},{4,0},{1,5},{5,1},{2,6},{6,2},{3,7},{7,3},{8,12},{12,8},{9,1... | collective-permute-start | bytes 589832 | tf_op jit(solution)/shard_map/ppermute | solution.py:138
  74.3 4.6 %collective-permute-done.9 = bf16[192,512]{1,0:T(8,128)(2,1)S(1)} collective-permute-done((bf16[192,512]{1,0:T(8,128)(2,1)S(1)}, bf16[192,512]{1,0:T(8,128)(2,1)S(1)}, u32[]{:S(2)}, u32[]{:S(2)}) %collective-permute-start.9) | collective-permute-done | bytes 196640 | tf_op jit(solution)/shard_map/ppermute | solution.py:138
  78.9 0.6 gather_fusion
  79.5 0.9 %broadcast_select_fusion = bf16[1,1,384,512]{3,2,1,0:T(8,128)(2,1)} fusion(bf16[1,1,384,512]{3,2,1,0:T(8,128)(2,1)S(1)} %bitcast.222, pred[384]{0:T(512)(128)(4,1)S(1)} %broadcast_in_dim.18), kind=kLoop, calls=%fused_computation.115 | loop fusion | flops 196608 | bytes 786816 | tf_op jit(solution)/shard_map/jit(_take)/select_n | solution.py:140
  (87 shorter events, 12.8 us)
Async XLA Ops:
  0.0 8.9 %copy-start.7 = (bf16[1,1,256,4096]{3,2,1,0:T(8,128)(2,1)S(1)}, bf16[1,1,256,4096]{3,2,1,0:T(8,128)(2,1)}, u32[]{:S(2)}) copy-start(bf16[1,1,256,4096]{3,2,1,0:T(8,128)(2,1)} %param.6) | copy-start | bytes 6291460
  3.0 7.0 %copy-start.9 = (s32[1,1,256,1]{2,3,1,0:T(1,128)S(1)}, s32[1,1,256,1]{2,3,1,0:T(1,128)}, u32[]{:S(2)}) copy-start(s32[1,1,256,1]{2,3,1,0:T(1,128)} %param.7) | copy-start | bytes 3076
  3.0 35.3 %collective-permute-start.1 = (bf16[256,1024]{1,0:T(8,128)(2,1)}, bf16[256,1024]{1,0:T(8,128)(2,1)}, u32[]{:S(2)}, u32[]{:S(2)}) collective-permute-start(bf16[256,1024]{1,0:T(8,128)(2,1)} %get-tuple-element.28), channel_id=1, source_target_pairs={{0,8},{8,16},{16,24},{1,9},{9,17},{17,25},{2,10},{10,18},{18,26},{... | collective-permute-start | bytes 1572872 | tf_op jit(solution)/shard_map/ppermute | solution.py:18
  11.9 21.6 %collective-permute-start = (f32[3,256]{1,0:T(4,128)S(1)}, f32[3,256]{1,0:T(4,128)S(1)}, u32[]{:S(2)}, u32[]{:S(2)}) collective-permute-start(f32[3,256]{1,0:T(4,128)S(1)} %pad_maximum_fusion.2), channel_id=1, source_target_pairs={{0,8},{8,16},{16,24},{1,9},{9,17},{17,25},{2,10},{10,18},{18,26},{... | collective-permute-start | bytes 9224 | tf_op jit(solution)/shard_map/ppermute | solution.py:18
  14.6 30.3 %collective-permute-start.4 = (bf16[256,1024]{1,0:T(8,128)(2,1)}, bf16[256,1024]{1,0:T(8,128)(2,1)}, u32[]{:S(2)}, u32[]{:S(2)}) collective-permute-start(bf16[256,1024]{1,0:T(8,128)(2,1)} %get-tuple-element.27), channel_id=1, source_target_pairs={{0,8},{8,16},{16,24},{1,9},{9,17},{17,25},{2,10},{10,18},{18,26},{... | collective-permute-start | bytes 1572872 | tf_op jit(solution)/shard_map/ppermute | solution.py:18
  18.9 31.3 %collective-permute-start.5 = (bf16[256,1024]{1,0:T(8,128)(2,1)}, bf16[256,1024]{1,0:T(8,128)(2,1)S(1)}, u32[]{:S(2)}, u32[]{:S(2)}) collective-permute-start(bf16[256,1024]{1,0:T(8,128)(2,1)} %get-tuple-element.26), channel_id=1, source_target_pairs={{0,8},{8,16},{16,24},{1,9},{9,17},{17,25},{2,10},{10,18},{18,26},{... | collective-permute-start | bytes 1572872 | tf_op jit(solution)/shard_map/ppermute | solution.py:18
  20.2 13.4 %copy-start.8 = (f32[1,4096]{1,0:T(1,128)S(1)}, f32[1,4096]{1,0:T(1,128)}, u32[]{:S(2)}) copy-start(f32[1,4096]{1,0:T(1,128)} %param.10) | copy-start | bytes 49156
  20.2 34.9 %collective-permute-start.6 = (bf16[256,1024]{1,0:T(8,128)(2,1)}, bf16[256,1024]{1,0:T(8,128)(2,1)S(1)}, u32[]{:S(2)}, u32[]{:S(2)}) collective-permute-start(bf16[256,1024]{1,0:T(8,128)(2,1)} %get-tuple-element.25), channel_id=1, source_target_pairs={{0,8},{8,16},{16,24},{1,9},{9,17},{17,25},{2,10},{10,18},{18,26},{... | collective-permute-start | bytes 1572872 | tf_op jit(solution)/shard_map/ppermute | solution.py:18
  33.5 1.2 %collective-permute-start.2 = (f32[256]{0:T(256)S(1)}, f32[256]{0:T(256)S(1)}, u32[]{:S(2)}, u32[]{:S(2)}) collective-permute-start(f32[256]{0:T(256)S(1)} %bitcast.235), channel_id=1, source_target_pairs={{0,1},{1,0},{2,3},{3,2},{4,5},{5,4},{6,7},{7,6},{8,9},{9,8},{10,11... | collective-permute-start | bytes 3080 | tf_op jit(solution)/shard_map/ppermute | solution.py:40
  34.7 3.6 %collective-permute-start.3 = (f32[256]{0:T(256)S(1)}, f32[256]{0:T(256)S(1)}, u32[]{:S(2)}, u32[]{:S(2)}) collective-permute-start(f32[256]{0:T(256)S(1)} %add.158), channel_id=1, source_target_pairs={{0,2},{1,3},{2,0},{3,1},{4,6},{5,7},{6,4},{7,5},{8,10},{9,11},{10,... | collective-permute-start | bytes 3080 | tf_op jit(solution)/shard_map/ppermute | solution.py:40
  36.2 6.2 %copy-start.5 = (bf16[1,512,2048]{2,1,0:T(8,128)(2,1)S(1)}, bf16[1,512,2048]{2,1,0:T(8,128)(2,1)}, u32[]{:S(2)}) copy-start(bf16[1,512,2048]{2,1,0:T(8,128)(2,1)} %get-tuple-element.22) | copy-start | bytes 6291460
  40.9 2.3 %copy-start.6 = (bf16[1,512,2048]{2,1,0:T(8,128)(2,1)S(1)}, bf16[1,512,2048]{2,1,0:T(8,128)(2,1)}, u32[]{:S(2)}) copy-start(bf16[1,512,2048]{2,1,0:T(8,128)(2,1)} %get-tuple-element.23) | copy-start | bytes 6291460
  44.6 1.7 %copy-start.4 = (bf16[1,512,2048]{2,1,0:T(8,128)(2,1)S(1)}, bf16[1,512,2048]{2,1,0:T(8,128)(2,1)}, u32[]{:S(2)}) copy-start(bf16[1,512,2048]{2,1,0:T(8,128)(2,1)} %get-tuple-element.21) | copy-start | bytes 6291460
  46.7 1.6 %copy-start.3 = (bf16[1,512,2048]{2,1,0:T(8,128)(2,1)S(1)}, bf16[1,512,2048]{2,1,0:T(8,128)(2,1)}, u32[]{:S(2)}) copy-start(bf16[1,512,2048]{2,1,0:T(8,128)(2,1)} %get-tuple-element.20) | copy-start | bytes 6291460
  49.8 1.6 %copy-start.2 = (bf16[1,512,2048]{2,1,0:T(8,128)(2,1)S(1)}, bf16[1,512,2048]{2,1,0:T(8,128)(2,1)}, u32[]{:S(2)}) copy-start(bf16[1,512,2048]{2,1,0:T(8,128)(2,1)} %get-tuple-element.19) | copy-start | bytes 6291460
  51.7 1.6 %copy-start.1 = (bf16[1,512,2048]{2,1,0:T(8,128)(2,1)S(1)}, bf16[1,512,2048]{2,1,0:T(8,128)(2,1)}, u32[]{:S(2)}) copy-start(bf16[1,512,2048]{2,1,0:T(8,128)(2,1)} %get-tuple-element.18) | copy-start | bytes 6291460
  54.7 1.6 %copy-start = (bf16[1,512,2048]{2,1,0:T(8,128)(2,1)S(1)}, bf16[1,512,2048]{2,1,0:T(8,128)(2,1)}, u32[]{:S(2)}) copy-start(bf16[1,512,2048]{2,1,0:T(8,128)(2,1)} %get-tuple-element.24) | copy-start | bytes 6291460
  60.7 2.9 %collective-permute-start.7 = (f32[2,512,256]{2,1,0:T(8,128)}, f32[2,512,256]{2,1,0:T(8,128)S(1)}, u32[]{:S(2)}, u32[]{:S(2)}) collective-permute-start(f32[2,512,256]{2,1,0:T(8,128)} %slice.204), channel_id=1, source_target_pairs={{0,1},{1,0},{2,3},{3,2},{4,5},{5,4},{6,7},{7,6},{8,9},{9,8},{10,11... | collective-permute-start | bytes 3145736 | tf_op jit(solution)/shard_map/ppermute | solution.py:31
  63.7 8.4 %collective-permute-start.8 = (bf16[1,512,256]{2,1,0:T(8,128)(2,1)S(1)}, bf16[1,512,256]{2,1,0:T(8,128)(2,1)S(1)}, u32[]{:S(2)}, u32[]{:S(2)}) collective-permute-start(bf16[1,512,256]{2,1,0:T(8,128)(2,1)S(1)} %slice.292), channel_id=1, source_target_pairs={{0,2},{1,3},{2,0},{3,1},{4,6},{5,7},{6,4},{7,5},{8,10},{9,11},{10,... | collective-permute-start | bytes 786440 | tf_op jit(solution)/shard_map/ppermute | solution.py:31
  72.7 6.2 %collective-permute-start.9 = (bf16[192,512]{1,0:T(8,128)(2,1)S(1)}, bf16[192,512]{1,0:T(8,128)(2,1)S(1)}, u32[]{:S(2)}, u32[]{:S(2)}) collective-permute-start(bf16[192,512]{1,0:T(8,128)(2,1)S(1)} %get-tuple-element.30), channel_id=1, source_target_pairs={{0,4},{4,0},{1,5},{5,1},{2,6},{6,2},{3,7},{7,3},{8,12},{12,8},{9,1... | collective-permute-start | bytes 589832 | tf_op jit(solution)/shard_map/ppermute | solution.py:138

commit v11 on v10

--- a/solution.py
+++ b/solution.py
@@ -110,7 +110,7 @@
             terms = []
             for s in range(tensor):
                 column = jnp.bitwise_xor(me_t, bit_reversed(s, levels)) * block
-                piece = lax.dynamic_slice_in_dim(weight[part], column, block, axis=1)
+                piece = lax.dynamic_slice(weight, (low, column), (local_width // 8, block))
                 terms.append(
                     lax.dot_general(
                         piece, sub, (((0,), (1,)), ((), ())), preferred_element_type=jnp.float32

time: 80.9 us -> 84.5 us (1.044)
  local copies, waits for them, and re-layouts: 19.7 us -> 3.31 us
  waiting for transfers between devices: 16.9 us -> 29.8 us
  matrix products: 13.8 us -> 20.9 us
    ppermute x5, waiting for transfers between devices: 0.01 us -> 12.9 us  [shifted(): return lax.ppermute(block, axis, route)]
    slice x2 -> x1, local copies, waits for them, and re-layouts: 11.7 us -> 0.21 us  [the longest x1 11.5 us: per_device(): piece = lax.dynamic_slice_in_dim(weight[part], column, block, axis=1)]
    dot_general x32, matrix products: 13.5 us -> 20.6 us  [per_device(): lax.dot_general(piece, sub, (((0,), (1,)), ((), ())), preferred_element_t...]
    unnamed x20 -> x8, local copies, waits for them, and re-layouts: 3.09 us -> 0.02 us
    convert_element_type x4, other arithmetic: 2.86 us -> 0.66 us  [per_device(): (arrived.astype(jnp.float32) * gain[cols] * scale[:, None]).astype(jnp.bf...]
    slice x1, local copies, waits for them, and re-layouts: 3 us -> 1.2 us  [per_device(): arrived = shifted(tok_rows[:, cols], 'section', 1)]
    reduce_sum x1, other arithmetic: 0.49 us -> 2.09 us  [per_device(): part_sq = jnp.sum(widened * widened, axis=1)]
  transfers between devices with their start and end apart: 10 -> 10, of which waited for: 5 -> 8; matrix products, arithmetic and copies ran while one was open for 35% -> 25% of each run, Pallas kernels for 0% -> 0%
where the time goes in v11:
time: 84.5 us; the launch traced here: 84 us
  waiting for transfers between devices  29.8 us (35%)
  matrix products  20.9 us (25%)
  starting transfers between devices  20.6 us (24%)
  other arithmetic  7.43 us (9%)
  local copies, waits for them, and re-layouts  3.31 us (4%)
  between operations  1.98 us (2%)
    dot_general x32, matrix products, per_device(): lax.dot_general(piece, sub, (((0,), (1,)), ((), ())), preferred_element_t...  20.6 us
    ppermute x5, starting transfers between devices, shifted(): return lax.ppermute(block, axis, route)  15.8 us
    ppermute x5, waiting for transfers between devices, shifted(): return lax.ppermute(block, axis, route)  12.9 us
    ppermute x2, waiting for transfers between devices, scatter_sum(): current = keep + lax.ppermute(send, axis, pairs).astype(jnp.float32)  9.16 us
    ppermute x1, waiting for transfers between devices, per_device(): received[offset] = lax.ppermute(outgoing, 'dp', pairs)  4.56 us
    ppermute x2, waiting for transfers between devices, all_sum(): lax.ppermute(value, axis, [(i, i ^ bit) for i in range(size)])  3.17 us
    reduce_sum x1, other arithmetic, per_device(): part_sq = jnp.sum(widened * widened, axis=1)  2.09 us
  transfers between devices with their start and end apart: 10, of which 8 were waited for; matrix products, arithmetic and copies ran while one was open for 25% of the time, Pallas kernels for 0%

profile of v11, /device:TPU:0, one launch (start us, length us, event | category | flops | bytes accessed | tf_op | source)
XLA Modules:
  0.0 84.0 jit_solution(14274220431381987373)
XLA Ops:
  0.8 0.7 and_convert_fusion
  1.5 0.6 reduce-window.6
  3.2 2.1 %multiply_reduce_fusion = f32[256]{0:T(256)S(1)} fusion(bf16[1,1,256,4096]{3,2,1,0:T(8,128)(2,1)} %param.6), kind=kLoop, calls=%fused_computation.1 | loop fusion | flops 3145472 | bytes 2098176 | tf_op jit(solution)/shard_map/reduce_sum | solution.py:83
  5.4 5.0 %collective-permute-start = (f32[3,256]{1,0:T(4,128)S(1)}, f32[3,256]{1,0:T(4,128)S(1)}, u32[]{:S(2)}, u32[]{:S(2)}) collective-permute-start(f32[3,256]{1,0:T(4,128)S(1)} %pad_maximum_fusion.2), channel_id=1, source_target_pairs={{0,8},{8,16},{16,24},{1,9},{9,17},{17,25},{2,10},{10,18},{18,26},{... | collective-permute-start | bytes 9224 | tf_op jit(solution)/shard_map/ppermute | solution.py:18
  10.4 1.2 %fusion.168 = (bf16[256,1024]{1,0:T(8,128)(2,1)S(1)}, bf16[256,1024]{1,0:T(8,128)(2,1)S(1)}, bf16[256,1024]{1,0:T(8,128)(2,1)}, bf16[256,1024]{1,0:T(8,128)(2,1)}) fusion(bf16[256,4096]{1,0:T(8,128)(2,1)S(1)} %bitcast.218), kind=kLoop, calls=%fused_computation.253 | loop fusion | bytes 4194304 | tf_op jit(solution)/shard_map/slice | solution.py:103
  11.6 3.5 %collective-permute-start.1 = (bf16[256,1024]{1,0:T(8,128)(2,1)}, bf16[256,1024]{1,0:T(8,128)(2,1)S(1)}, u32[]{:S(2)}, u32[]{:S(2)}) collective-permute-start(bf16[256,1024]{1,0:T(8,128)(2,1)} %get-tuple-element.20), channel_id=1, source_target_pairs={{0,8},{8,16},{16,24},{1,9},{9,17},{17,25},{2,10},{10,18},{18,26},{... | collective-permute-start | bytes 1572872 | tf_op jit(solution)/shard_map/ppermute | solution.py:18
  15.1 3.5 %collective-permute-start.4 = (bf16[256,1024]{1,0:T(8,128)(2,1)}, bf16[256,1024]{1,0:T(8,128)(2,1)S(1)}, u32[]{:S(2)}, u32[]{:S(2)}) collective-permute-start(bf16[256,1024]{1,0:T(8,128)(2,1)} %get-tuple-element.19), channel_id=1, source_target_pairs={{0,8},{8,16},{16,24},{1,9},{9,17},{17,25},{2,10},{10,18},{18,26},{... | collective-permute-start | bytes 1572872 | tf_op jit(solution)/shard_map/ppermute | solution.py:18
  18.6 1.9 %collective-permute-start.5 = (bf16[256,1024]{1,0:T(8,128)(2,1)S(1)}, bf16[256,1024]{1,0:T(8,128)(2,1)S(1)}, u32[]{:S(2)}, u32[]{:S(2)}) collective-permute-start(bf16[256,1024]{1,0:T(8,128)(2,1)S(1)} %get-tuple-element.18), channel_id=1, source_target_pairs={{0,8},{8,16},{16,24},{1,9},{9,17},{17,25},{2,10},{10,18},{18,26},{... | collective-permute-start | bytes 1572872 | tf_op jit(solution)/shard_map/ppermute | solution.py:18
  20.5 1.9 %collective-permute-start.6 = (bf16[256,1024]{1,0:T(8,128)(2,1)S(1)}, bf16[256,1024]{1,0:T(8,128)(2,1)S(1)}, u32[]{:S(2)}, u32[]{:S(2)}) collective-permute-start(bf16[256,1024]{1,0:T(8,128)(2,1)S(1)} %get-tuple-element.17), channel_id=1, source_target_pairs={{0,8},{8,16},{16,24},{1,9},{9,17},{17,25},{2,10},{10,18},{18,26},{... | collective-permute-start | bytes 1572872 | tf_op jit(solution)/shard_map/ppermute | solution.py:18
  22.6 1.1 %collective-permute-done.2 = f32[256]{0:T(256)S(1)} collective-permute-done((f32[256]{0:T(256)S(1)}, f32[256]{0:T(256)S(1)}, u32[]{:S(2)}, u32[]{:S(2)}) %collective-permute-start.2) | collective-permute-done | bytes 1056 | tf_op jit(solution)/shard_map/ppermute | solution.py:40
  23.7 1.5 %collective-permute-start.3 = (f32[256]{0:T(256)S(1)}, f32[256]{0:T(256)S(1)}, u32[]{:S(2)}, u32[]{:S(2)}) collective-permute-start(f32[256]{0:T(256)S(1)} %add.158), channel_id=1, source_target_pairs={{0,2},{1,3},{2,0},{3,1},{4,6},{5,7},{6,4},{7,5},{8,10},{9,11},{10,... | collective-permute-start | bytes 3080 | tf_op jit(solution)/shard_map/ppermute | solution.py:40
  25.2 2.1 %collective-permute-done.3 = f32[256]{0:T(256)S(1)} collective-permute-done((f32[256]{0:T(256)S(1)}, f32[256]{0:T(256)S(1)}, u32[]{:S(2)}, u32[]{:S(2)}) %collective-permute-start.3) | collective-permute-done | bytes 1056 | tf_op jit(solution)/shard_map/ppermute | solution.py:40
  27.9 1.5 %convolution_bitcast_fusion.25 = f32[1,512,256]{2,1,0:T(8,128)S(1)} fusion(bf16[1,4096,2048]{2,1,0:T(8,128)(2,1)} %param.11, s32[]{:T(128)S(6)} %select_n.125, bf16[256,1024]{1,0:T(8,128)(2,1)S(1)} %multiply_convert_fusion.3), kind=kOutput, calls=%fused_computation.35 | convolution fusion | flops 134217728 | bytes 1310724 | tf_op jit(solution)/shard_map/dot_general | solution.py:115
  29.4 1.8 %convolution_bitcast_fusion.29 = f32[1,512,256]{2,1,0:T(8,128)S(1)} fusion(bf16[1,4096,2048]{2,1,0:T(8,128)(2,1)} %param.11, s32[]{:T(128)S(6)} %select_n.125, bf16[256,1024]{1,0:T(8,128)(2,1)S(1)} %multiply_convert_fusion.3), kind=kOutput, calls=%fused_computation.39 | convolution fusion | flops 134217728 | bytes 1310724 | tf_op jit(solution)/shard_map/dot_general | solution.py:115
  31.2 1.9 %convolution_bitcast_fusion.26 = f32[1,512,256]{2,1,0:T(8,128)S(1)} fusion(bf16[1,4096,2048]{2,1,0:T(8,128)(2,1)} %param.11, s32[]{:T(128)S(6)} %select_n.124, bf16[256,1024]{1,0:T(8,128)(2,1)S(1)} %multiply_convert_fusion.3), kind=kOutput, calls=%fused_computation.36 | convolution fusion | flops 134217728 | bytes 1310724 | tf_op jit(solution)/shard_map/dot_general | solution.py:115
  33.1 1.4 %convolution_bitcast_fusion.30 = f32[1,512,256]{2,1,0:T(8,128)S(1)} fusion(bf16[1,4096,2048]{2,1,0:T(8,128)(2,1)} %param.11, s32[]{:T(128)S(6)} %select_n.124, bf16[256,1024]{1,0:T(8,128)(2,1)S(1)} %multiply_convert_fusion.3), kind=kOutput, calls=%fused_computation.40 | convolution fusion | flops 134217728 | bytes 1310724 | tf_op jit(solution)/shard_map/dot_general | solution.py:115
  34.5 1.4 %convolution_bitcast_fusion.27 = f32[1,512,256]{2,1,0:T(8,128)S(1)} fusion(bf16[1,4096,2048]{2,1,0:T(8,128)(2,1)} %param.11, s32[]{:T(128)S(6)} %select_n.123, bf16[256,1024]{1,0:T(8,128)(2,1)S(1)} %multiply_convert_fusion.3), kind=kOutput, calls=%fused_computation.37 | convolution fusion | flops 134217728 | bytes 1310724 | tf_op jit(solution)/shard_map/dot_general | solution.py:115
  35.9 1.4 %convolution_bitcast_fusion.31 = f32[1,512,256]{2,1,0:T(8,128)S(1)} fusion(bf16[1,4096,2048]{2,1,0:T(8,128)(2,1)} %param.11, s32[]{:T(128)S(6)} %select_n.123, bf16[256,1024]{1,0:T(8,128)(2,1)S(1)} %multiply_convert_fusion.3), kind=kOutput, calls=%fused_computation.41 | convolution fusion | flops 134217728 | bytes 1310724 | tf_op jit(solution)/shard_map/dot_general | solution.py:115
  37.3 1.4 %convolution_bitcast_fusion.24 = f32[1,512,256]{2,1,0:T(8,128)S(1)} fusion(bf16[1,4096,2048]{2,1,0:T(8,128)(2,1)} %param.11, s32[]{:T(128)S(6)} %select_n.126, bf16[256,1024]{1,0:T(8,128)(2,1)S(1)} %multiply_convert_fusion.3), kind=kOutput, calls=%fused_computation.34 | convolution fusion | flops 134217728 | bytes 1310724 | tf_op jit(solution)/shard_map/dot_general | solution.py:115
  38.7 1.4 %convolution_bitcast_fusion.28 = f32[1,512,256]{2,1,0:T(8,128)S(1)} fusion(bf16[1,4096,2048]{2,1,0:T(8,128)(2,1)} %param.11, s32[]{:T(128)S(6)} %select_n.126, bf16[256,1024]{1,0:T(8,128)(2,1)S(1)} %multiply_convert_fusion.3), kind=kOutput, calls=%fused_computation.38 | convolution fusion | flops 134217728 | bytes 1310724 | tf_op jit(solution)/shard_map/dot_general | solution.py:115
  43.9 6.2 %collective-permute-done.5 = bf16[256,1024]{1,0:T(8,128)(2,1)S(1)} collective-permute-done((bf16[256,1024]{1,0:T(8,128)(2,1)S(1)}, bf16[256,1024]{1,0:T(8,128)(2,1)S(1)}, u32[]{:S(2)}, u32[]{:S(2)}) %collective-permute-start.5) | collective-permute-done | bytes 524320 | tf_op jit(solution)/shard_map/ppermute | solution.py:18
  53.1 0.4 fusion.1
  53.5 6.4 %collective-permute-done.6 = bf16[256,1024]{1,0:T(8,128)(2,1)S(1)} collective-permute-done((bf16[256,1024]{1,0:T(8,128)(2,1)S(1)}, bf16[256,1024]{1,0:T(8,128)(2,1)S(1)}, u32[]{:S(2)}, u32[]{:S(2)}) %collective-permute-start.6) | collective-permute-done | bytes 524320 | tf_op jit(solution)/shard_map/ppermute | solution.py:18
  62.9 0.4 fusion.2
  63.3 1.0 %slice.140 = f32[2,512,256]{2,1,0:T(8,128)} slice(f32[4,512,256]{2,1,0:T(8,128)S(1)} %fusion.2), slice={[2:4], [0:512], [0:256]} | slice | bytes 2097152 | tf_op jit(solution)/shard_map/slice | solution.py:27
  64.6 2.7 %collective-permute-done.7 = f32[2,512,256]{2,1,0:T(8,128)S(1)} collective-permute-done((f32[2,512,256]{2,1,0:T(8,128)}, f32[2,512,256]{2,1,0:T(8,128)S(1)}, u32[]{:S(2)}, u32[]{:S(2)}) %collective-permute-start.7) | collective-permute-done | bytes 1048608 | tf_op jit(solution)/shard_map/ppermute | solution.py:31
  67.4 1.6 %collective-permute-start.8 = (bf16[1,512,256]{2,1,0:T(8,128)(2,1)S(1)}, bf16[1,512,256]{2,1,0:T(8,128)(2,1)S(1)}, u32[]{:S(2)}, u32[]{:S(2)}) collective-permute-start(bf16[1,512,256]{2,1,0:T(8,128)(2,1)S(1)} %slice.228), channel_id=1, source_target_pairs={{0,2},{1,3},{2,0},{3,1},{4,6},{5,7},{6,4},{7,5},{8,10},{9,11},{10,... | collective-permute-start | bytes 786440 | tf_op jit(solution)/shard_map/ppermute | solution.py:31
  69.3 6.5 %collective-permute-done.8 = bf16[1,512,256]{2,1,0:T(8,128)(2,1)S(1)} collective-permute-done((bf16[1,512,256]{2,1,0:T(8,128)(2,1)S(1)}, bf16[1,512,256]{2,1,0:T(8,128)(2,1)S(1)}, u32[]{:S(2)}, u32[]{:S(2)}) %collective-permute-start.8) | collective-permute-done | bytes 262176 | tf_op jit(solution)/shard_map/ppermute | solution.py:31
  76.4 1.6 %collective-permute-start.9 = (bf16[192,512]{1,0:T(8,128)(2,1)S(1)}, bf16[192,512]{1,0:T(8,128)(2,1)S(1)}, u32[]{:S(2)}, u32[]{:S(2)}) collective-permute-start(bf16[192,512]{1,0:T(8,128)(2,1)S(1)} %get-tuple-element.22), channel_id=1, source_target_pairs={{0,4},{4,0},{1,5},{5,1},{2,6},{6,2},{3,7},{7,3},{8,12},{12,8},{9,1... | collective-permute-start | bytes 589832 | tf_op jit(solution)/shard_map/ppermute | solution.py:138
  78.0 4.6 %collective-permute-done.9 = bf16[192,512]{1,0:T(8,128)(2,1)S(1)} collective-permute-done((bf16[192,512]{1,0:T(8,128)(2,1)S(1)}, bf16[192,512]{1,0:T(8,128)(2,1)S(1)}, u32[]{:S(2)}, u32[]{:S(2)}) %collective-permute-start.9) | collective-permute-done | bytes 196640 | tf_op jit(solution)/shard_map/ppermute | solution.py:138
  82.6 0.6 gather_fusion
  83.2 0.9 %broadcast_select_fusion = bf16[1,1,384,512]{3,2,1,0:T(8,128)(2,1)} fusion(bf16[1,1,384,512]{3,2,1,0:T(8,128)(2,1)S(1)} %bitcast.222, pred[384]{0:T(512)(128)(4,1)S(1)} %broadcast_in_dim.18), kind=kLoop, calls=%fused_computation.115 | loop fusion | flops 196608 | bytes 786816 | tf_op jit(solution)/shard_map/jit(_take)/select_n | solution.py:140
  (74 shorter events, 12.1 us)
Async XLA Ops:
  0.0 5.3 %copy-start.3 = (s32[1,1,256,1]{2,3,1,0:T(1,128)S(1)}, s32[1,1,256,1]{2,3,1,0:T(1,128)}, u32[]{:S(2)}) copy-start(s32[1,1,256,1]{2,3,1,0:T(1,128)} %param.7) | copy-start | bytes 3076
  0.0 10.4 %copy-start.1 = (bf16[1,1,256,4096]{3,2,1,0:T(8,128)(2,1)S(1)}, bf16[1,1,256,4096]{3,2,1,0:T(8,128)(2,1)}, u32[]{:S(2)}) copy-start(bf16[1,1,256,4096]{3,2,1,0:T(8,128)(2,1)} %param.6) | copy-start | bytes 6291460
  5.4 17.0 %collective-permute-start = (f32[3,256]{1,0:T(4,128)S(1)}, f32[3,256]{1,0:T(4,128)S(1)}, u32[]{:S(2)}, u32[]{:S(2)}) collective-permute-start(f32[3,256]{1,0:T(4,128)S(1)} %pad_maximum_fusion.2), channel_id=1, source_target_pairs={{0,8},{8,16},{16,24},{1,9},{9,17},{17,25},{2,10},{10,18},{18,26},{... | collective-permute-start | bytes 9224 | tf_op jit(solution)/shard_map/ppermute | solution.py:18
  10.4 12.2 %copy-start.2 = (f32[1,4096]{1,0:T(1,128)S(1)}, f32[1,4096]{1,0:T(1,128)}, u32[]{:S(2)}) copy-start(f32[1,4096]{1,0:T(1,128)} %param.10) | copy-start | bytes 49156
  11.6 16.1 %collective-permute-start.1 = (bf16[256,1024]{1,0:T(8,128)(2,1)}, bf16[256,1024]{1,0:T(8,128)(2,1)S(1)}, u32[]{:S(2)}, u32[]{:S(2)}) collective-permute-start(bf16[256,1024]{1,0:T(8,128)(2,1)} %get-tuple-element.20), channel_id=1, source_target_pairs={{0,8},{8,16},{16,24},{1,9},{9,17},{17,25},{2,10},{10,18},{18,26},{... | collective-permute-start | bytes 1572872 | tf_op jit(solution)/shard_map/ppermute | solution.py:18
  15.1 25.3 %collective-permute-start.4 = (bf16[256,1024]{1,0:T(8,128)(2,1)}, bf16[256,1024]{1,0:T(8,128)(2,1)S(1)}, u32[]{:S(2)}, u32[]{:S(2)}) collective-permute-start(bf16[256,1024]{1,0:T(8,128)(2,1)} %get-tuple-element.19), channel_id=1, source_target_pairs={{0,8},{8,16},{16,24},{1,9},{9,17},{17,25},{2,10},{10,18},{18,26},{... | collective-permute-start | bytes 1572872 | tf_op jit(solution)/shard_map/ppermute | solution.py:18
  18.6 31.5 %collective-permute-start.5 = (bf16[256,1024]{1,0:T(8,128)(2,1)S(1)}, bf16[256,1024]{1,0:T(8,128)(2,1)S(1)}, u32[]{:S(2)}, u32[]{:S(2)}) collective-permute-start(bf16[256,1024]{1,0:T(8,128)(2,1)S(1)} %get-tuple-element.18), channel_id=1, source_target_pairs={{0,8},{8,16},{16,24},{1,9},{9,17},{17,25},{2,10},{10,18},{18,26},{... | collective-permute-start | bytes 1572872 | tf_op jit(solution)/shard_map/ppermute | solution.py:18
  20.5 39.3 %collective-permute-start.6 = (bf16[256,1024]{1,0:T(8,128)(2,1)S(1)}, bf16[256,1024]{1,0:T(8,128)(2,1)S(1)}, u32[]{:S(2)}, u32[]{:S(2)}) collective-permute-start(bf16[256,1024]{1,0:T(8,128)(2,1)S(1)} %get-tuple-element.17), channel_id=1, source_target_pairs={{0,8},{8,16},{16,24},{1,9},{9,17},{17,25},{2,10},{10,18},{18,26},{... | collective-permute-start | bytes 1572872 | tf_op jit(solution)/shard_map/ppermute | solution.py:18
  22.5 1.2 %collective-permute-start.2 = (f32[256]{0:T(256)S(1)}, f32[256]{0:T(256)S(1)}, u32[]{:S(2)}, u32[]{:S(2)}) collective-permute-start(f32[256]{0:T(256)S(1)} %bitcast.235), channel_id=1, source_target_pairs={{0,1},{1,0},{2,3},{3,2},{4,5},{5,4},{6,7},{7,6},{8,9},{9,8},{10,11... | collective-permute-start | bytes 3080 | tf_op jit(solution)/shard_map/ppermute | solution.py:40
  23.7 3.6 %collective-permute-start.3 = (f32[256]{0:T(256)S(1)}, f32[256]{0:T(256)S(1)}, u32[]{:S(2)}, u32[]{:S(2)}) collective-permute-start(f32[256]{0:T(256)S(1)} %add.158), channel_id=1, source_target_pairs={{0,2},{1,3},{2,0},{3,1},{4,6},{5,7},{6,4},{7,5},{8,10},{9,11},{10,... | collective-permute-start | bytes 3080 | tf_op jit(solution)/shard_map/ppermute | solution.py:40
  27.9 12.7 %copy-start = (bf16[1,4096,2048]{2,1,0:T(8,128)(2,1)S(1)}, bf16[1,4096,2048]{2,1,0:T(8,128)(2,1)}, u32[]{:S(2)}) copy-start(bf16[1,4096,2048]{2,1,0:T(8,128)(2,1)} %param.11) | copy-start | bytes 50331652
  64.4 2.9 %collective-permute-start.7 = (f32[2,512,256]{2,1,0:T(8,128)}, f32[2,512,256]{2,1,0:T(8,128)S(1)}, u32[]{:S(2)}, u32[]{:S(2)}) collective-permute-start(f32[2,512,256]{2,1,0:T(8,128)} %slice.140), channel_id=1, source_target_pairs={{0,1},{1,0},{2,3},{3,2},{4,5},{5,4},{6,7},{7,6},{8,9},{9,8},{10,11... | collective-permute-start | bytes 3145736 | tf_op jit(solution)/shard_map/ppermute | solution.py:31
  67.4 8.4 %collective-permute-start.8 = (bf16[1,512,256]{2,1,0:T(8,128)(2,1)S(1)}, bf16[1,512,256]{2,1,0:T(8,128)(2,1)S(1)}, u32[]{:S(2)}, u32[]{:S(2)}) collective-permute-start(bf16[1,512,256]{2,1,0:T(8,128)(2,1)S(1)} %slice.228), channel_id=1, source_target_pairs={{0,2},{1,3},{2,0},{3,1},{4,6},{5,7},{6,4},{7,5},{8,10},{9,11},{10,... | collective-permute-start | bytes 786440 | tf_op jit(solution)/shard_map/ppermute | solution.py:31
  76.4 6.2 %collective-permute-start.9 = (bf16[192,512]{1,0:T(8,128)(2,1)S(1)}, bf16[192,512]{1,0:T(8,128)(2,1)S(1)}, u32[]{:S(2)}, u32[]{:S(2)}) collective-permute-start(bf16[192,512]{1,0:T(8,128)(2,1)S(1)} %get-tuple-element.22), channel_id=1, source_target_pairs={{0,4},{4,0},{1,5},{5,1},{2,6},{6,2},{3,7},{7,3},{8,12},{12,8},{9,1... | collective-permute-start | bytes 589832 | tf_op jit(solution)/shard_map/ppermute | solution.py:138

commit v12 on v10

--- a/solution.py
+++ b/solution.py
@@ -18,19 +18,19 @@
     return lax.ppermute(block, axis, route)
 
 
-def scatter_sum(blocks, axis):
+def scatter_sum(keep, send, axis):
     size = lax.axis_size(axis)
-    current = blocks
     bit = 1
-    while bit < size:
-        half = current.shape[0] // 2
-        keep, send = current[:half], current[half:]
+    while True:
         if bit >= 2:
             send = send.astype(jnp.bfloat16)
         pairs = [(i, i ^ bit) for i in range(size)]
         current = keep + lax.ppermute(send, axis, pairs).astype(jnp.float32)
         bit *= 2
-    return current[0]
+        if bit >= size:
+            return current[0]
+        half = current.shape[0] // 2
+        keep, send = current[:half], current[half:]
 
 
 def all_sum(value, axis):
@@ -116,9 +116,9 @@
                         piece, sub, (((0,), (1,)), ((), ())), preferred_element_type=jnp.float32
                     )
                 )
-            term = jnp.stack(terms)
-            partial = term if partial is None else partial + term
-    summed = scatter_sum(partial, "tensor")
+            term = (jnp.stack(terms[: tensor // 2]), jnp.stack(terms[tensor // 2:]))
+            partial = term if partial is None else (partial[0] + term[0], partial[1] + term[1])
+    summed = scatter_sum(partial[0], partial[1], "tensor")
     local_cols = summed.shape[0]
     local_kv = summed.reshape(local_cols // (2 * HD), 2, HD, tok_count)
     result = rotate_keys(local_kv, position).reshape(local_cols, tok_count).astype(jnp.bfloat16)
@@ -130,14 +130,15 @@
     ).astype(jnp.bfloat16)
     packed = packed.reshape(groups, capacity, local_cols)
     me = lax.axis_index("dp")
-    received = [None] * groups
-    received[0] = lax.dynamic_index_in_dim(packed, me, 0, keepdims=False)
+    routed = jnp.zeros((groups, capacity, local_cols), jnp.bfloat16)
+    routed = lax.dynamic_update_index_in_dim(
+        routed, lax.dynamic_index_in_dim(packed, me, 0, keepdims=False), me, 0
+    )
     for offset in range(1, groups):
         outgoing = lax.dynamic_index_in_dim(packed, (me + offset) % groups, 0, keepdims=False)
         pairs = [(i, (i + offset) % groups) for i in range(groups)]
-        received[offset] = lax.ppermute(outgoing, "dp", pairs)
-    stacked = jnp.stack(received)
-    routed = jnp.take(stacked, (me - jnp.arange(groups, dtype=jnp.int32)) % groups, axis=0)
+        arrived = lax.ppermute(outgoing, "dp", pairs)
+        routed = lax.dynamic_update_index_in_dim(routed, arrived, (me - offset) % groups, 0)
     return routed.reshape(1, 1, slot_count, local_cols)
 
 

time: 80.9 us -> 104 us (1.29)
  waiting for transfers between devices: 16.9 us -> 35.1 us
  other arithmetic: 7.37 us -> 11.1 us
  matrix products: 13.8 us -> 15.9 us
  local copies, waits for them, and re-layouts: 19.7 us -> 17.7 us
    ppermute x5, waiting for transfers between devices: 0.01 us -> 20.1 us  [shifted(): return lax.ppermute(block, axis, route)]
    ppermute x2, waiting for transfers between devices: 9.18 us -> 6.91 us  [scatter_sum(): current = keep + lax.ppermute(send, axis, pairs).astype(jnp.float32)]
    dot_general x32, matrix products: 13.5 us -> 15.6 us  [per_device(): lax.dot_general(piece, sub, (((0,), (1,)), ((), ())), preferred_element_t...]
    add x4 -> x7, other arithmetic: 1.54 us -> 3.24 us  [the longest x4 1.72 us: per_device(): partial[1] + term[1]]
    slice x1, local copies, waits for them, and re-layouts: 3 us -> 1.37 us  [per_device(): arrived = shifted(tok_rows[:, cols], 'section', 1)]
    reduce_sum x1, other arithmetic: 0.49 us -> 2.09 us  [per_device(): part_sq = jnp.sum(widened * widened, axis=1)]
    add x2, other arithmetic: 0.19 us -> 1.64 us  [scatter_sum(): current = keep + lax.ppermute(send, axis, pairs).astype(jnp.float32)]
    unnamed x20 -> x24, local copies, waits for them, and re-layouts: 3.09 us -> 4.43 us
  transfers between devices with their start and end apart: 10 -> 10, of which waited for: 5 -> 5; matrix products, arithmetic and copies ran while one was open for 35% -> 31% of each run, Pallas kernels for 0% -> 0%
where the time goes in v12:
time: 104 us
  waiting for transfers between devices  35.1 us (34%)
  starting transfers between devices  21.6 us (21%)
  local copies, waits for them, and re-layouts  17.7 us (17%)
  matrix products  15.9 us (15%)
  other arithmetic  11.1 us (11%)
  between operations  2.05 us (2%)
    ppermute x5, waiting for transfers between devices, shifted(): return lax.ppermute(block, axis, route)  20.1 us
    ppermute x5, starting transfers between devices, shifted(): return lax.ppermute(block, axis, route)  16.9 us
    dot_general x32, matrix products, per_device(): lax.dot_general(piece, sub, (((0,), (1,)), ((), ())), preferred_element_t...  15.6 us
    slice x1, local copies, waits for them, and re-layouts, per_device(): piece = lax.dynamic_slice_in_dim(weight[part], column, block, axis=1)  11.6 us
    ppermute x2, waiting for transfers between devices, scatter_sum(): current = keep + lax.ppermute(send, axis, pairs).astype(jnp.float32)  6.91 us
    ppermute x1, waiting for transfers between devices, per_device(): arrived = lax.ppermute(outgoing, 'dp', pairs)  5 us
    unnamed x24, local copies, waits for them, and re-layouts  4.43 us
    ppermute x2, waiting for transfers between devices, all_sum(): lax.ppermute(value, axis, [(i, i ^ bit) for i in range(size)])  3.17 us
  transfers between devices with their start and end apart: 10, of which 5 were waited for; matrix products, arithmetic and copies ran while one was open for 31% of the time, Pallas kernels for 0%

profile of v12, /device:TPU:0, one launch (start us, length us, event | category | flops | bytes accessed | tf_op | source)
XLA Modules:
  0.0 103.6 jit_solution(14375191951592524210)
XLA Ops:
  1.5 2.1 %multiply_reduce_fusion = f32[256]{0:T(256)S(1)} fusion(bf16[1,1,256,4096]{3,2,1,0:T(8,128)(2,1)} %param.6), kind=kLoop, calls=%fused_computation | loop fusion | flops 3145472 | bytes 2098176 | tf_op jit(solution)/shard_map/reduce_sum | solution.py:83
  3.6 0.6 reduce-window.6
  4.8 5.0 %collective-permute-start = (f32[3,256]{1,0:T(4,128)S(1)}, f32[3,256]{1,0:T(4,128)S(1)}, u32[]{:S(2)}, u32[]{:S(2)}) collective-permute-start(f32[3,256]{1,0:T(4,128)S(1)} %pad_maximum_fusion.1), channel_id=1, source_target_pairs={{0,8},{8,16},{16,24},{1,9},{9,17},{17,25},{2,10},{10,18},{18,26},{... | collective-permute-start | bytes 9224 | tf_op jit(solution)/shard_map/ppermute | solution.py:18
  9.7 1.4 %fusion.142 = (bf16[256,1024]{1,0:T(8,128)(2,1)}, bf16[256,1024]{1,0:T(8,128)(2,1)}, bf16[256,1024]{1,0:T(8,128)(2,1)}, bf16[256,1024]{1,0:T(8,128)(2,1)}) fusion(bf16[256,4096]{1,0:T(8,128)(2,1)S(1)} %bitcast.217), kind=kLoop, calls=%fused_computation.218 | loop fusion | bytes 4194304 | tf_op jit(solution)/shard_map/slice | solution.py:103
  11.1 3.5 %collective-permute-start.6 = (bf16[256,1024]{1,0:T(8,128)(2,1)}, bf16[256,1024]{1,0:T(8,128)(2,1)S(1)}, u32[]{:S(2)}, u32[]{:S(2)}) collective-permute-start(bf16[256,1024]{1,0:T(8,128)(2,1)} %get-tuple-element.31), channel_id=1, source_target_pairs={{0,8},{8,16},{16,24},{1,9},{9,17},{17,25},{2,10},{10,18},{18,26},{... | collective-permute-start | bytes 1572872 | tf_op jit(solution)/shard_map/ppermute | solution.py:18
  14.6 3.5 %collective-permute-start.5 = (bf16[256,1024]{1,0:T(8,128)(2,1)}, bf16[256,1024]{1,0:T(8,128)(2,1)S(1)}, u32[]{:S(2)}, u32[]{:S(2)}) collective-permute-start(bf16[256,1024]{1,0:T(8,128)(2,1)} %get-tuple-element.32), channel_id=1, source_target_pairs={{0,8},{8,16},{16,24},{1,9},{9,17},{17,25},{2,10},{10,18},{18,26},{... | collective-permute-start | bytes 1572872 | tf_op jit(solution)/shard_map/ppermute | solution.py:18
  18.1 2.7 %collective-permute-start.4 = (bf16[256,1024]{1,0:T(8,128)(2,1)}, bf16[256,1024]{1,0:T(8,128)(2,1)}, u32[]{:S(2)}, u32[]{:S(2)}) collective-permute-start(bf16[256,1024]{1,0:T(8,128)(2,1)} %get-tuple-element.33), channel_id=1, source_target_pairs={{0,8},{8,16},{16,24},{1,9},{9,17},{17,25},{2,10},{10,18},{18,26},{... | collective-permute-start | bytes 1572872 | tf_op jit(solution)/shard_map/ppermute | solution.py:18
  20.8 2.2 %collective-permute-start.1 = (bf16[256,1024]{1,0:T(8,128)(2,1)}, bf16[256,1024]{1,0:T(8,128)(2,1)}, u32[]{:S(2)}, u32[]{:S(2)}) collective-permute-start(bf16[256,1024]{1,0:T(8,128)(2,1)} %get-tuple-element.34), channel_id=1, source_target_pairs={{0,8},{8,16},{16,24},{1,9},{9,17},{17,25},{2,10},{10,18},{18,26},{... | collective-permute-start | bytes 1572872 | tf_op jit(solution)/shard_map/ppermute | solution.py:18
  23.0 11.6 %fusion.141 = (bf16[1,512,2048]{2,1,0:T(8,128)(2,1)S(1)}, bf16[1,512,2048]{2,1,0:T(8,128)(2,1)}, bf16[1,512,2048]{2,1,0:T(8,128)(2,1)}, bf16[1,512,2048]{2,1,0:T...) fusion(bf16[1,4096,2048]{2,1,0:T(8,128)(2,1)} %param.11), kind=kLoop, calls=%fused_computation.217 | loop fusion | bytes 33554432 | tf_op jit(solution)/shard_map/slice | solution.py:113
  34.7 1.1 %collective-permute-done.2 = f32[256]{0:T(256)S(1)} collective-permute-done((f32[256]{0:T(256)S(1)}, f32[256]{0:T(256)S(1)}, u32[]{:S(2)}, u32[]{:S(2)}) %collective-permute-start.2) | collective-permute-done | bytes 1056 | tf_op jit(solution)/shard_map/ppermute | solution.py:40
  35.8 1.5 %collective-permute-start.3 = (f32[256]{0:T(256)S(1)}, f32[256]{0:T(256)S(1)}, u32[]{:S(2)}, u32[]{:S(2)}) collective-permute-start(f32[256]{0:T(256)S(1)} %add.154), channel_id=1, source_target_pairs={{0,2},{1,3},{2,0},{3,1},{4,6},{5,7},{6,4},{7,5},{8,10},{9,11},{10,... | collective-permute-start | bytes 3080 | tf_op jit(solution)/shard_map/ppermute | solution.py:40
  37.4 2.1 %collective-permute-done.3 = f32[256]{0:T(256)S(1)} collective-permute-done((f32[256]{0:T(256)S(1)}, f32[256]{0:T(256)S(1)}, u32[]{:S(2)}, u32[]{:S(2)}) %collective-permute-start.3) | collective-permute-done | bytes 1056 | tf_op jit(solution)/shard_map/ppermute | solution.py:40
  39.4 20.1 %collective-permute-done.1 = bf16[256,1024]{1,0:T(8,128)(2,1)} collective-permute-done((bf16[256,1024]{1,0:T(8,128)(2,1)}, bf16[256,1024]{1,0:T(8,128)(2,1)}, u32[]{:S(2)}, u32[]{:S(2)}) %collective-permute-start.1) | collective-permute-done | bytes 524320 | tf_op jit(solution)/shard_map/ppermute | solution.py:18
  59.5 1.2 %multiply_convert_fusion.3 = bf16[256,1024]{1,0:T(8,128)(2,1)S(1)} fusion(bf16[256,1024]{1,0:T(8,128)(2,1)} %collective-permute-done.1, f32[256]{0:T(256)S(1)} %add_rsqrt_fusion, f32[1024]{0:T(1024)S(1)} %bitcast.225), kind=kLoop, calls=%fused_computation.52 | loop fusion | flops 1048576 | bytes 1053696 | tf_op jit(solution)/shard_map/convert_element_type | solution.py:106
  60.7 1.4 %convolution_bitcast_fusion.24 = f32[1,512,256]{2,1,0:T(8,128)S(1)} fusion(bf16[1,512,2048]{2,1,0:T(8,128)(2,1)} %get-tuple-element.28, s32[]{:T(128)S(6)} %select_n.89, bf16[256,1024]{1,0:T(8,128)(2,1)S(1)} %multiply_convert_fusion.3), kind=kOutput, calls=%fused_computation.26 | convolution fusion | flops 134217728 | bytes 1310724 | tf_op jit(solution)/shard_map/dot_general | solution.py:115
  62.1 1.5 %convolution_bitcast_fusion.25 = f32[1,512,256]{2,1,0:T(8,128)S(1)} fusion(bf16[1,512,2048]{2,1,0:T(8,128)(2,1)} %get-tuple-element.28, s32[]{:T(128)S(6)} %select_n.88, bf16[256,1024]{1,0:T(8,128)(2,1)S(1)} %multiply_convert_fusion.3), kind=kOutput, calls=%fused_computation.27 | convolution fusion | flops 134217728 | bytes 1310724 | tf_op jit(solution)/shard_map/dot_general | solution.py:115
  66.1 1.3 %multiply_convert_fusion.2 = bf16[256,1024]{1,0:T(8,128)(2,1)S(1)} fusion(bf16[256,1024]{1,0:T(8,128)(2,1)} %collective-permute-done.4, f32[1024]{0:T(1024)S(1)} %bitcast.224, f32[256]{0:T(256)S(1)} %add_rsqrt_fusion), kind=kLoop, calls=%fused_computation.51 | loop fusion | flops 1048576 | bytes 1053696 | tf_op jit(solution)/shard_map/convert_element_type | solution.py:106
  69.1 0.5 copy-done.3
  71.7 1.2 %copy-done.2 = bf16[1,512,2048]{2,1,0:T(8,128)(2,1)S(1)} copy-done((bf16[1,512,2048]{2,1,0:T(8,128)(2,1)S(1)}, bf16[1,512,2048]{2,1,0:T(8,128)(2,1)}, u32[]{:S(2)}) %copy-start.2) | copy-done | bytes 2097176
  73.6 0.4 convolution_bitcast_fusion.10
  74.3 0.5 copy-done.1
  76.2 1.2 %fusion.2 = f32[2,512,256]{2,1,0:T(8,128)} fusion(f32[2,512,256]{2,1,0:T(8,128)S(1)} %fusion, f32[1,512,256]{2,1,0:T(8,128)S(1)} %convolution_bitcast_fusion.14, f32[1,512,256]{2,1,0:T(8,128)S(1)} %convolution_bitcast_fusion.15, f32[1,512,256]{2,1,0:T(8,128)S(1)} %convolution_bitcast_fusion.12, f32[1,512,256]{2,1,0:T(8,128)S(1)} %convolution_bitcast_fusion.13), kind=kLoop, calls=%fused_computation.41 | loop fusion | flops 1048576 | bytes 4194304 | tf_op jit(solution)/shard_map/add | solution.py:120
  77.8 1.2 %copy-done = bf16[1,512,2048]{2,1,0:T(8,128)(2,1)S(1)} copy-done((bf16[1,512,2048]{2,1,0:T(8,128)(2,1)S(1)}, bf16[1,512,2048]{2,1,0:T(8,128)(2,1)}, u32[]{:S(2)}) %copy-start) | copy-done | bytes 2097176
  80.5 1.2 %fusion.6 = f32[2,512,256]{2,1,0:T(8,128)} fusion(f32[2,512,256]{2,1,0:T(8,128)S(1)} %fusion.3, f32[1,512,256]{2,1,0:T(8,128)S(1)} %convolution_bitcast_fusion.2, f32[1,512,256]{2,1,0:T(8,128)S(1)} %convolution_bitcast_fusion.3, f32[1,512,256]{2,1,0:T(8,128)S(1)} %convolution_bitcast_fusion, f32[1,512,256]{2,1,0:T(8,128)S(1)} %convolution_bitcast_fusion.1), kind=kLoop, calls=%fused_computation.48 | loop fusion | flops 1048576 | bytes 4194304 | tf_op jit(solution)/shard_map/add | solution.py:120
  81.7 1.4 %convolution_bitcast_fusion.6 = f32[1,512,256]{2,1,0:T(8,128)S(1)} fusion(bf16[1,512,2048]{2,1,0:T(8,128)(2,1)} %get-tuple-element.30, s32[]{:T(128)S(6)} %select_n.87, bf16[256,1024]{1,0:T(8,128)(2,1)S(1)} %multiply_convert_fusion), kind=kOutput, calls=%fused_computation.8 | convolution fusion | flops 134217728 | bytes 1310724 | tf_op jit(solution)/shard_map/dot_general | solution.py:115
  83.4 1.4 %convolution_bitcast_fusion.7 = f32[1,512,256]{2,1,0:T(8,128)S(1)} fusion(bf16[1,512,2048]{2,1,0:T(8,128)(2,1)} %get-tuple-element.30, s32[]{:T(128)S(6)} %select_n.86, bf16[256,1024]{1,0:T(8,128)(2,1)S(1)} %multiply_convert_fusion), kind=kOutput, calls=%fused_computation.9 | convolution fusion | flops 134217728 | bytes 1310724 | tf_op jit(solution)/shard_map/dot_general | solution.py:115
  85.2 1.6 %fusion.5 = f32[2,512,256]{2,1,0:T(8,128)S(1)} fusion(f32[2,512,256]{2,1,0:T(8,128)} %collective-permute-done.7, f32[2,512,256]{2,1,0:T(8,128)S(1)} %copy-done.8, f32[1,512,256]{2,1,0:T(8,128)S(1)} %convolution_bitcast_fusion.6, f32[1,512,256]{2,1,0:T(8,128)S(1)} %convolution_bitcast_fusion.7, f32[1,512,256]{2,1,0:T(8,128)S(1)} %convolution_bitcast_fusion.4, ...), kind=kLoop, calls=%fused_computation.46 | loop fusion | flops 1310720 | bytes 5242880 | tf_op jit(solution)/shard_map/add | solution.py:28
  86.8 1.6 %collective-permute-start.8 = (bf16[1,512,256]{2,1,0:T(8,128)(2,1)S(1)}, bf16[1,512,256]{2,1,0:T(8,128)(2,1)S(1)}, u32[]{:S(2)}, u32[]{:S(2)}) collective-permute-start(bf16[1,512,256]{2,1,0:T(8,128)(2,1)S(1)} %slice.279), channel_id=1, source_target_pairs={{0,2},{1,3},{2,0},{3,1},{4,6},{5,7},{6,4},{7,5},{8,10},{9,11},{10,... | collective-permute-start | bytes 786440 | tf_op jit(solution)/shard_map/ppermute | solution.py:28
  88.7 6.9 %collective-permute-done.8 = bf16[1,512,256]{2,1,0:T(8,128)(2,1)S(1)} collective-permute-done((bf16[1,512,256]{2,1,0:T(8,128)(2,1)S(1)}, bf16[1,512,256]{2,1,0:T(8,128)(2,1)S(1)}, u32[]{:S(2)}, u32[]{:S(2)}) %collective-permute-start.8) | collective-permute-done | bytes 262176 | tf_op jit(solution)/shard_map/ppermute | solution.py:28
  96.2 1.6 %collective-permute-start.9 = (bf16[192,512]{1,0:T(8,128)(2,1)S(1)}, bf16[192,512]{1,0:T(8,128)(2,1)S(1)}, u32[]{:S(2)}, u32[]{:S(2)}) collective-permute-start(bf16[192,512]{1,0:T(8,128)(2,1)S(1)} %get-tuple-element.35), channel_id=1, source_target_pairs={{0,4},{4,0},{1,5},{5,1},{2,6},{6,2},{3,7},{7,3},{8,12},{12,8},{9,1... | collective-permute-start | bytes 589832 | tf_op jit(solution)/shard_map/ppermute | solution.py:140
  97.8 5.0 %collective-permute-done.9 = bf16[192,512]{1,0:T(8,128)(2,1)S(1)} collective-permute-done((bf16[192,512]{1,0:T(8,128)(2,1)S(1)}, bf16[192,512]{1,0:T(8,128)(2,1)S(1)}, u32[]{:S(2)}, u32[]{:S(2)}) %collective-permute-start.9) | collective-permute-done | bytes 196640 | tf_op jit(solution)/shard_map/ppermute | solution.py:140
  102.8 0.7 copy-done.9
  (87 shorter events, 12.6 us)
Async XLA Ops:
  0.0 9.7 %copy-start.7 = (bf16[1,1,256,4096]{3,2,1,0:T(8,128)(2,1)S(1)}, bf16[1,1,256,4096]{3,2,1,0:T(8,128)(2,1)}, u32[]{:S(2)}) copy-start(bf16[1,1,256,4096]{3,2,1,0:T(8,128)(2,1)} %param.6) | copy-start | bytes 6291460
  0.0 3.6 %copy-start.11 = (s32[1,1,256,1]{2,3,1,0:T(1,128)S(1)}, s32[1,1,256,1]{2,3,1,0:T(1,128)}, u32[]{:S(2)}) copy-start(s32[1,1,256,1]{2,3,1,0:T(1,128)} %param.7) | copy-start | bytes 3076
  4.8 29.8 %collective-permute-start = (f32[3,256]{1,0:T(4,128)S(1)}, f32[3,256]{1,0:T(4,128)S(1)}, u32[]{:S(2)}, u32[]{:S(2)}) collective-permute-start(f32[3,256]{1,0:T(4,128)S(1)} %pad_maximum_fusion.1), channel_id=1, source_target_pairs={{0,8},{8,16},{16,24},{1,9},{9,17},{17,25},{2,10},{10,18},{18,26},{... | collective-permute-start | bytes 9224 | tf_op jit(solution)/shard_map/ppermute | solution.py:18
  11.1 66.5 %collective-permute-start.6 = (bf16[256,1024]{1,0:T(8,128)(2,1)}, bf16[256,1024]{1,0:T(8,128)(2,1)S(1)}, u32[]{:S(2)}, u32[]{:S(2)}) collective-permute-start(bf16[256,1024]{1,0:T(8,128)(2,1)} %get-tuple-element.31), channel_id=1, source_target_pairs={{0,8},{8,16},{16,24},{1,9},{9,17},{17,25},{2,10},{10,18},{18,26},{... | collective-permute-start | bytes 1572872 | tf_op jit(solution)/shard_map/ppermute | solution.py:18
  14.6 56.9 %collective-permute-start.5 = (bf16[256,1024]{1,0:T(8,128)(2,1)}, bf16[256,1024]{1,0:T(8,128)(2,1)S(1)}, u32[]{:S(2)}, u32[]{:S(2)}) collective-permute-start(bf16[256,1024]{1,0:T(8,128)(2,1)} %get-tuple-element.32), channel_id=1, source_target_pairs={{0,8},{8,16},{16,24},{1,9},{9,17},{17,25},{2,10},{10,18},{18,26},{... | collective-permute-start | bytes 1572872 | tf_op jit(solution)/shard_map/ppermute | solution.py:18
  18.1 48.0 %collective-permute-start.4 = (bf16[256,1024]{1,0:T(8,128)(2,1)}, bf16[256,1024]{1,0:T(8,128)(2,1)}, u32[]{:S(2)}, u32[]{:S(2)}) collective-permute-start(bf16[256,1024]{1,0:T(8,128)(2,1)} %get-tuple-element.33), channel_id=1, source_target_pairs={{0,8},{8,16},{16,24},{1,9},{9,17},{17,25},{2,10},{10,18},{18,26},{... | collective-permute-start | bytes 1572872 | tf_op jit(solution)/shard_map/ppermute | solution.py:18
  20.8 13.9 %copy-start.10 = (f32[1,4096]{1,0:T(1,128)S(1)}, f32[1,4096]{1,0:T(1,128)}, u32[]{:S(2)}) copy-start(f32[1,4096]{1,0:T(1,128)} %param.10) | copy-start | bytes 49156
  20.8 38.7 %collective-permute-start.1 = (bf16[256,1024]{1,0:T(8,128)(2,1)}, bf16[256,1024]{1,0:T(8,128)(2,1)}, u32[]{:S(2)}, u32[]{:S(2)}) collective-permute-start(bf16[256,1024]{1,0:T(8,128)(2,1)} %get-tuple-element.34), channel_id=1, source_target_pairs={{0,8},{8,16},{16,24},{1,9},{9,17},{17,25},{2,10},{10,18},{18,26},{... | collective-permute-start | bytes 1572872 | tf_op jit(solution)/shard_map/ppermute | solution.py:18
  34.6 1.2 %collective-permute-start.2 = (f32[256]{0:T(256)S(1)}, f32[256]{0:T(256)S(1)}, u32[]{:S(2)}, u32[]{:S(2)}) collective-permute-start(f32[256]{0:T(256)S(1)} %bitcast.232), channel_id=1, source_target_pairs={{0,1},{1,0},{2,3},{3,2},{4,5},{5,4},{6,7},{7,6},{8,9},{9,8},{10,11... | collective-permute-start | bytes 3080 | tf_op jit(solution)/shard_map/ppermute | solution.py:40
  35.8 3.6 %collective-permute-start.3 = (f32[256]{0:T(256)S(1)}, f32[256]{0:T(256)S(1)}, u32[]{:S(2)}, u32[]{:S(2)}) collective-permute-start(f32[256]{0:T(256)S(1)} %add.154), channel_id=1, source_target_pairs={{0,2},{1,3},{2,0},{3,1},{4,6},{5,7},{6,4},{7,5},{8,10},{9,11},{10,... | collective-permute-start | bytes 3080 | tf_op jit(solution)/shard_map/ppermute | solution.py:40
  37.4 26.3 %copy-start.5 = (bf16[1,512,2048]{2,1,0:T(8,128)(2,1)S(1)}, bf16[1,512,2048]{2,1,0:T(8,128)(2,1)}, u32[]{:S(2)}) copy-start(bf16[1,512,2048]{2,1,0:T(8,128)(2,1)} %get-tuple-element.29) | copy-start | bytes 6291460
  62.1 2.3 %copy-start.6 = (bf16[1,512,2048]{2,1,0:T(8,128)(2,1)S(1)}, bf16[1,512,2048]{2,1,0:T(8,128)(2,1)}, u32[]{:S(2)}) copy-start(bf16[1,512,2048]{2,1,0:T(8,128)(2,1)} %get-tuple-element.28) | copy-start | bytes 6291460
  65.9 1.7 %copy-start.4 = (bf16[1,512,2048]{2,1,0:T(8,128)(2,1)S(1)}, bf16[1,512,2048]{2,1,0:T(8,128)(2,1)}, u32[]{:S(2)}) copy-start(bf16[1,512,2048]{2,1,0:T(8,128)(2,1)} %get-tuple-element.27) | copy-start | bytes 6291460
  68.0 1.6 %copy-start.3 = (bf16[1,512,2048]{2,1,0:T(8,128)(2,1)S(1)}, bf16[1,512,2048]{2,1,0:T(8,128)(2,1)}, u32[]{:S(2)}) copy-start(bf16[1,512,2048]{2,1,0:T(8,128)(2,1)} %get-tuple-element.26) | copy-start | bytes 6291460
  71.3 1.6 %copy-start.2 = (bf16[1,512,2048]{2,1,0:T(8,128)(2,1)S(1)}, bf16[1,512,2048]{2,1,0:T(8,128)(2,1)}, u32[]{:S(2)}) copy-start(bf16[1,512,2048]{2,1,0:T(8,128)(2,1)} %get-tuple-element.25) | copy-start | bytes 6291460
  73.2 1.6 %copy-start.1 = (bf16[1,512,2048]{2,1,0:T(8,128)(2,1)S(1)}, bf16[1,512,2048]{2,1,0:T(8,128)(2,1)}, u32[]{:S(2)}) copy-start(bf16[1,512,2048]{2,1,0:T(8,128)(2,1)} %get-tuple-element.24) | copy-start | bytes 6291460
  77.4 1.6 %copy-start = (bf16[1,512,2048]{2,1,0:T(8,128)(2,1)S(1)}, bf16[1,512,2048]{2,1,0:T(8,128)(2,1)}, u32[]{:S(2)}) copy-start(bf16[1,512,2048]{2,1,0:T(8,128)(2,1)} %get-tuple-element.30) | copy-start | bytes 6291460
  81.7 3.5 %collective-permute-start.7 = (f32[2,512,256]{2,1,0:T(8,128)}, f32[2,512,256]{2,1,0:T(8,128)}, u32[]{:S(2)}, u32[]{:S(2)}) collective-permute-start(f32[2,512,256]{2,1,0:T(8,128)} %fusion.6), channel_id=1, source_target_pairs={{0,1},{1,0},{2,3},{3,2},{4,5},{5,4},{6,7},{7,6},{8,9},{9,8},{10,11... | collective-permute-start | bytes 3145736 | tf_op jit(solution)/shard_map/ppermute | solution.py:28
  83.1 2.1 %copy-start.8 = (f32[2,512,256]{2,1,0:T(8,128)S(1)}, f32[2,512,256]{2,1,0:T(8,128)}, u32[]{:S(2)}) copy-start(f32[2,512,256]{2,1,0:T(8,128)} %fusion.2) | copy-start | bytes 3145732
  86.8 8.8 %collective-permute-start.8 = (bf16[1,512,256]{2,1,0:T(8,128)(2,1)S(1)}, bf16[1,512,256]{2,1,0:T(8,128)(2,1)S(1)}, u32[]{:S(2)}, u32[]{:S(2)}) collective-permute-start(bf16[1,512,256]{2,1,0:T(8,128)(2,1)S(1)} %slice.279), channel_id=1, source_target_pairs={{0,2},{1,3},{2,0},{3,1},{4,6},{5,7},{6,4},{7,5},{8,10},{9,11},{10,... | collective-permute-start | bytes 786440 | tf_op jit(solution)/shard_map/ppermute | solution.py:28
  96.2 6.6 %collective-permute-start.9 = (bf16[192,512]{1,0:T(8,128)(2,1)S(1)}, bf16[192,512]{1,0:T(8,128)(2,1)S(1)}, u32[]{:S(2)}, u32[]{:S(2)}) collective-permute-start(bf16[192,512]{1,0:T(8,128)(2,1)S(1)} %get-tuple-element.35), channel_id=1, source_target_pairs={{0,4},{4,0},{1,5},{5,1},{2,6},{6,2},{3,7},{7,3},{8,12},{12,8},{9,1... | collective-permute-start | bytes 589832 | tf_op jit(solution)/shard_map/ppermute | solution.py:140
  102.8 0.7 copy-start.9

commit v13 on v10

--- a/solution.py
+++ b/solution.py
@@ -130,14 +130,15 @@
     ).astype(jnp.bfloat16)
     packed = packed.reshape(groups, capacity, local_cols)
     me = lax.axis_index("dp")
-    received = [None] * groups
-    received[0] = lax.dynamic_index_in_dim(packed, me, 0, keepdims=False)
+    routed = jnp.zeros((groups, capacity, local_cols), jnp.bfloat16)
+    routed = lax.dynamic_update_index_in_dim(
+        routed, lax.dynamic_index_in_dim(packed, me, 0, keepdims=False), me, 0
+    )
     for offset in range(1, groups):
         outgoing = lax.dynamic_index_in_dim(packed, (me + offset) % groups, 0, keepdims=False)
         pairs = [(i, (i + offset) % groups) for i in range(groups)]
-        received[offset] = lax.ppermute(outgoing, "dp", pairs)
-    stacked = jnp.stack(received)
-    routed = jnp.take(stacked, (me - jnp.arange(groups, dtype=jnp.int32)) % groups, axis=0)
+        arrived = lax.ppermute(outgoing, "dp", pairs)
+        routed = lax.dynamic_update_index_in_dim(routed, arrived, (me - offset) % groups, 0)
     return routed.reshape(1, 1, slot_count, local_cols)
 
 

time: 80.9 us -> 80.3 us (level)
  other arithmetic: 7.37 us -> 6.55 us
    select_n x2 -> x0, other arithmetic: 0.88 us -> none  [per_device(): jnp.take(stacked, (me - jnp.arange(groups, dtype=jnp.int32)) % groups, ax...]
    unnamed x20 -> x22, local copies, waits for them, and re-layouts: 3.09 us -> 3.75 us
where the time goes in v13:
time: 80.3 us; the launch traced here: 79.8 us
  starting transfers between devices  20.7 us (26%)
  local copies, waits for them, and re-layouts  19.7 us (25%)
  waiting for transfers between devices  17.2 us (21%)
  matrix products  13.8 us (17%)
  other arithmetic  6.55 us (8%)
  between operations  1.9 us (2%)
    ppermute x5, starting transfers between devices, shifted(): return lax.ppermute(block, axis, route)  15.9 us
    dot_general x32, matrix products, per_device(): lax.dot_general(piece, sub, (((0,), (1,)), ((), ())), preferred_element_t...  13.5 us
    slice x1, local copies, waits for them, and re-layouts, per_device(): piece = lax.dynamic_slice_in_dim(weight[part], column, block, axis=1)  11.6 us
    ppermute x2, waiting for transfers between devices, scatter_sum(): current = keep + lax.ppermute(send, axis, pairs).astype(jnp.float32)  9.39 us
    ppermute x1, waiting for transfers between devices, per_device(): arrived = lax.ppermute(outgoing, 'dp', pairs)  4.6 us
    unnamed x22, local copies, waits for them, and re-layouts  3.75 us
    ppermute x2, waiting for transfers between devices, all_sum(): lax.ppermute(value, axis, [(i, i ^ bit) for i in range(size)])  3.17 us
    slice x1, local copies, waits for them, and re-layouts, per_device(): arrived = shifted(tok_rows[:, cols], 'section', 1)  3.01 us
  transfers between devices with their start and end apart: 10, of which 5 were waited for; matrix products, arithmetic and copies ran while one was open for 35% of the time, Pallas kernels for 0%

profile of v13, /device:TPU:0, one launch (start us, length us, event | category | flops | bytes accessed | tf_op | source)
XLA Modules:
  0.0 79.8 jit_solution(2328473885667133934)
XLA Ops:
  0.0 3.0 %fusion.138 = (bf16[256,1024]{1,0:T(8,128)(2,1)}, bf16[256,1024]{1,0:T(8,128)(2,1)}, bf16[256,1024]{1,0:T(8,128)(2,1)}, bf16[256,1024]{1,0:T(8,128)(2,1)}) fusion(bf16[256,4096]{1,0:T(8,128)(2,1)} %bitcast.217), kind=kLoop, calls=%fused_computation.211 | loop fusion | bytes 4194304 | tf_op jit(solution)/shard_map/slice | solution.py:103
  3.0 5.9 %collective-permute-start.1 = (bf16[256,1024]{1,0:T(8,128)(2,1)}, bf16[256,1024]{1,0:T(8,128)(2,1)}, u32[]{:S(2)}, u32[]{:S(2)}) collective-permute-start(bf16[256,1024]{1,0:T(8,128)(2,1)} %get-tuple-element.28), channel_id=1, source_target_pairs={{0,8},{8,16},{16,24},{1,9},{9,17},{17,25},{2,10},{10,18},{18,26},{... | collective-permute-start | bytes 1572872 | tf_op jit(solution)/shard_map/ppermute | solution.py:18
  8.9 0.5 multiply_reduce_fusion
  10.1 0.6 reduce-window.6
  11.9 2.7 %collective-permute-start = (f32[3,256]{1,0:T(4,128)S(1)}, f32[3,256]{1,0:T(4,128)S(1)}, u32[]{:S(2)}, u32[]{:S(2)}) collective-permute-start(f32[3,256]{1,0:T(4,128)S(1)} %pad_maximum_fusion.1), channel_id=1, source_target_pairs={{0,8},{8,16},{16,24},{1,9},{9,17},{17,25},{2,10},{10,18},{18,26},{... | collective-permute-start | bytes 9224 | tf_op jit(solution)/shard_map/ppermute | solution.py:18
  14.6 4.3 %collective-permute-start.4 = (bf16[256,1024]{1,0:T(8,128)(2,1)}, bf16[256,1024]{1,0:T(8,128)(2,1)}, u32[]{:S(2)}, u32[]{:S(2)}) collective-permute-start(bf16[256,1024]{1,0:T(8,128)(2,1)} %get-tuple-element.27), channel_id=1, source_target_pairs={{0,8},{8,16},{16,24},{1,9},{9,17},{17,25},{2,10},{10,18},{18,26},{... | collective-permute-start | bytes 1572872 | tf_op jit(solution)/shard_map/ppermute | solution.py:18
  18.9 1.3 %collective-permute-start.5 = (bf16[256,1024]{1,0:T(8,128)(2,1)}, bf16[256,1024]{1,0:T(8,128)(2,1)S(1)}, u32[]{:S(2)}, u32[]{:S(2)}) collective-permute-start(bf16[256,1024]{1,0:T(8,128)(2,1)} %get-tuple-element.26), channel_id=1, source_target_pairs={{0,8},{8,16},{16,24},{1,9},{9,17},{17,25},{2,10},{10,18},{18,26},{... | collective-permute-start | bytes 1572872 | tf_op jit(solution)/shard_map/ppermute | solution.py:18
  20.2 1.8 %collective-permute-start.6 = (bf16[256,1024]{1,0:T(8,128)(2,1)}, bf16[256,1024]{1,0:T(8,128)(2,1)S(1)}, u32[]{:S(2)}, u32[]{:S(2)}) collective-permute-start(bf16[256,1024]{1,0:T(8,128)(2,1)} %get-tuple-element.25), channel_id=1, source_target_pairs={{0,8},{8,16},{16,24},{1,9},{9,17},{17,25},{2,10},{10,18},{18,26},{... | collective-permute-start | bytes 1572872 | tf_op jit(solution)/shard_map/ppermute | solution.py:18
  22.0 11.6 %fusion.137 = (bf16[1,512,2048]{2,1,0:T(8,128)(2,1)S(1)}, bf16[1,512,2048]{2,1,0:T(8,128)(2,1)}, bf16[1,512,2048]{2,1,0:T(8,128)(2,1)}, bf16[1,512,2048]{2,1,0:T...) fusion(bf16[1,4096,2048]{2,1,0:T(8,128)(2,1)} %param.11), kind=kLoop, calls=%fused_computation.210 | loop fusion | bytes 33554432 | tf_op jit(solution)/shard_map/slice | solution.py:113
  33.7 1.1 %collective-permute-done.2 = f32[256]{0:T(256)S(1)} collective-permute-done((f32[256]{0:T(256)S(1)}, f32[256]{0:T(256)S(1)}, u32[]{:S(2)}, u32[]{:S(2)}) %collective-permute-start.2) | collective-permute-done | bytes 1056 | tf_op jit(solution)/shard_map/ppermute | solution.py:40
  34.8 1.5 %collective-permute-start.3 = (f32[256]{0:T(256)S(1)}, f32[256]{0:T(256)S(1)}, u32[]{:S(2)}, u32[]{:S(2)}) collective-permute-start(f32[256]{0:T(256)S(1)} %add.133), channel_id=1, source_target_pairs={{0,2},{1,3},{2,0},{3,1},{4,6},{5,7},{6,4},{7,5},{8,10},{9,11},{10,... | collective-permute-start | bytes 3080 | tf_op jit(solution)/shard_map/ppermute | solution.py:40
  36.3 2.1 %collective-permute-done.3 = f32[256]{0:T(256)S(1)} collective-permute-done((f32[256]{0:T(256)S(1)}, f32[256]{0:T(256)S(1)}, u32[]{:S(2)}, u32[]{:S(2)}) %collective-permute-start.3) | collective-permute-done | bytes 1056 | tf_op jit(solution)/shard_map/ppermute | solution.py:40
  38.4 1.2 %multiply_convert_fusion.3 = bf16[256,1024]{1,0:T(8,128)(2,1)S(1)} fusion(bf16[256,1024]{1,0:T(8,128)(2,1)} %collective-permute-done.1, f32[256]{0:T(256)S(1)} %add_rsqrt_fusion, f32[1024]{0:T(1024)S(1)} %bitcast.225), kind=kLoop, calls=%fused_computation.45 | loop fusion | flops 1048576 | bytes 1053696 | tf_op jit(solution)/shard_map/convert_element_type | solution.py:106
  39.6 1.4 %convolution_bitcast_fusion.28 = f32[1,512,256]{2,1,0:T(8,128)S(1)} fusion(bf16[1,512,2048]{2,1,0:T(8,128)(2,1)} %get-tuple-element.23, s32[]{:T(128)S(6)} %select_n.89, bf16[256,1024]{1,0:T(8,128)(2,1)S(1)} %multiply_convert_fusion.3), kind=kOutput, calls=%fused_computation.37 | convolution fusion | flops 134217728 | bytes 1310724 | tf_op jit(solution)/shard_map/dot_general | solution.py:115
  41.0 1.5 %convolution_bitcast_fusion.29 = f32[1,512,256]{2,1,0:T(8,128)S(1)} fusion(bf16[1,512,2048]{2,1,0:T(8,128)(2,1)} %get-tuple-element.23, s32[]{:T(128)S(6)} %select_n.88, bf16[256,1024]{1,0:T(8,128)(2,1)S(1)} %multiply_convert_fusion.3), kind=kOutput, calls=%fused_computation.38 | convolution fusion | flops 134217728 | bytes 1310724 | tf_op jit(solution)/shard_map/dot_general | solution.py:115
  42.6 0.4 convolution_bitcast_fusion.24
  44.8 0.4 maximum_add_fusion
  45.1 1.4 %multiply_convert_fusion.2 = bf16[256,1024]{1,0:T(8,128)(2,1)S(1)} fusion(bf16[256,1024]{1,0:T(8,128)(2,1)} %collective-permute-done.4, f32[1024]{0:T(1024)S(1)} %bitcast.224, f32[256]{0:T(256)S(1)} %add_rsqrt_fusion), kind=kLoop, calls=%fused_computation.44 | loop fusion | flops 1048576 | bytes 1053696 | tf_op jit(solution)/shard_map/convert_element_type | solution.py:106
  48.0 0.5 copy-done.3
  49.9 0.4 fusion
  50.5 1.0 %copy-done.2 = bf16[1,512,2048]{2,1,0:T(8,128)(2,1)S(1)} copy-done((bf16[1,512,2048]{2,1,0:T(8,128)(2,1)S(1)}, bf16[1,512,2048]{2,1,0:T(8,128)(2,1)}, u32[]{:S(2)}) %copy-start.2) | copy-done | bytes 2097176
  53.0 0.5 copy-done.1
  54.9 0.4 fusion.1
  55.5 1.0 %copy-done = bf16[1,512,2048]{2,1,0:T(8,128)(2,1)S(1)} copy-done((bf16[1,512,2048]{2,1,0:T(8,128)(2,1)S(1)}, bf16[1,512,2048]{2,1,0:T(8,128)(2,1)}, u32[]{:S(2)}) %copy-start) | copy-done | bytes 2097176
  59.3 0.4 fusion.2
  59.8 1.1 %slice.202 = f32[2,512,256]{2,1,0:T(8,128)} slice(f32[4,512,256]{2,1,0:T(8,128)S(1)} %fusion.2), slice={[2:4], [0:512], [0:256]} | slice | bytes 2097152 | tf_op jit(solution)/shard_map/slice | solution.py:27
  60.8 2.9 %collective-permute-done.7 = f32[2,512,256]{2,1,0:T(8,128)S(1)} collective-permute-done((f32[2,512,256]{2,1,0:T(8,128)}, f32[2,512,256]{2,1,0:T(8,128)S(1)}, u32[]{:S(2)}, u32[]{:S(2)}) %collective-permute-start.7) | collective-permute-done | bytes 1048608 | tf_op jit(solution)/shard_map/ppermute | solution.py:31
  63.9 1.6 %collective-permute-start.8 = (bf16[1,512,256]{2,1,0:T(8,128)(2,1)S(1)}, bf16[1,512,256]{2,1,0:T(8,128)(2,1)S(1)}, u32[]{:S(2)}, u32[]{:S(2)}) collective-permute-start(bf16[1,512,256]{2,1,0:T(8,128)(2,1)S(1)} %slice.290), channel_id=1, source_target_pairs={{0,2},{1,3},{2,0},{3,1},{4,6},{5,7},{6,4},{7,5},{8,10},{9,11},{10,... | collective-permute-start | bytes 786440 | tf_op jit(solution)/shard_map/ppermute | solution.py:31
  65.7 6.5 %collective-permute-done.8 = bf16[1,512,256]{2,1,0:T(8,128)(2,1)S(1)} collective-permute-done((bf16[1,512,256]{2,1,0:T(8,128)(2,1)S(1)}, bf16[1,512,256]{2,1,0:T(8,128)(2,1)S(1)}, u32[]{:S(2)}, u32[]{:S(2)}) %collective-permute-start.8) | collective-permute-done | bytes 262176 | tf_op jit(solution)/shard_map/ppermute | solution.py:31
  72.9 1.6 %collective-permute-start.9 = (bf16[192,512]{1,0:T(8,128)(2,1)S(1)}, bf16[192,512]{1,0:T(8,128)(2,1)S(1)}, u32[]{:S(2)}, u32[]{:S(2)}) collective-permute-start(bf16[192,512]{1,0:T(8,128)(2,1)S(1)} %get-tuple-element.29), channel_id=1, source_target_pairs={{0,4},{4,0},{1,5},{5,1},{2,6},{6,2},{3,7},{7,3},{8,12},{12,8},{9,1... | collective-permute-start | bytes 589832 | tf_op jit(solution)/shard_map/ppermute | solution.py:140
  74.4 4.6 %collective-permute-done.9 = bf16[192,512]{1,0:T(8,128)(2,1)S(1)} collective-permute-done((bf16[192,512]{1,0:T(8,128)(2,1)S(1)}, bf16[192,512]{1,0:T(8,128)(2,1)S(1)}, u32[]{:S(2)}, u32[]{:S(2)}) %collective-permute-start.9) | collective-permute-done | bytes 196640 | tf_op jit(solution)/shard_map/ppermute | solution.py:140
  79.1 0.7 copy-done.8
  (83 shorter events, 12.2 us)
Async XLA Ops:
  0.0 8.9 %copy-start.7 = (bf16[1,1,256,4096]{3,2,1,0:T(8,128)(2,1)S(1)}, bf16[1,1,256,4096]{3,2,1,0:T(8,128)(2,1)}, u32[]{:S(2)}) copy-start(bf16[1,1,256,4096]{3,2,1,0:T(8,128)(2,1)} %param.6) | copy-start | bytes 6291460
  3.0 7.1 %copy-start.10 = (s32[1,1,256,1]{2,3,1,0:T(1,128)S(1)}, s32[1,1,256,1]{2,3,1,0:T(1,128)}, u32[]{:S(2)}) copy-start(s32[1,1,256,1]{2,3,1,0:T(1,128)} %param.7) | copy-start | bytes 3076
  3.0 35.4 %collective-permute-start.1 = (bf16[256,1024]{1,0:T(8,128)(2,1)}, bf16[256,1024]{1,0:T(8,128)(2,1)}, u32[]{:S(2)}, u32[]{:S(2)}) collective-permute-start(bf16[256,1024]{1,0:T(8,128)(2,1)} %get-tuple-element.28), channel_id=1, source_target_pairs={{0,8},{8,16},{16,24},{1,9},{9,17},{17,25},{2,10},{10,18},{18,26},{... | collective-permute-start | bytes 1572872 | tf_op jit(solution)/shard_map/ppermute | solution.py:18
  11.9 21.7 %collective-permute-start = (f32[3,256]{1,0:T(4,128)S(1)}, f32[3,256]{1,0:T(4,128)S(1)}, u32[]{:S(2)}, u32[]{:S(2)}) collective-permute-start(f32[3,256]{1,0:T(4,128)S(1)} %pad_maximum_fusion.1), channel_id=1, source_target_pairs={{0,8},{8,16},{16,24},{1,9},{9,17},{17,25},{2,10},{10,18},{18,26},{... | collective-permute-start | bytes 9224 | tf_op jit(solution)/shard_map/ppermute | solution.py:18
  14.6 30.5 %collective-permute-start.4 = (bf16[256,1024]{1,0:T(8,128)(2,1)}, bf16[256,1024]{1,0:T(8,128)(2,1)}, u32[]{:S(2)}, u32[]{:S(2)}) collective-permute-start(bf16[256,1024]{1,0:T(8,128)(2,1)} %get-tuple-element.27), channel_id=1, source_target_pairs={{0,8},{8,16},{16,24},{1,9},{9,17},{17,25},{2,10},{10,18},{18,26},{... | collective-permute-start | bytes 1572872 | tf_op jit(solution)/shard_map/ppermute | solution.py:18
  18.9 31.5 %collective-permute-start.5 = (bf16[256,1024]{1,0:T(8,128)(2,1)}, bf16[256,1024]{1,0:T(8,128)(2,1)S(1)}, u32[]{:S(2)}, u32[]{:S(2)}) collective-permute-start(bf16[256,1024]{1,0:T(8,128)(2,1)} %get-tuple-element.26), channel_id=1, source_target_pairs={{0,8},{8,16},{16,24},{1,9},{9,17},{17,25},{2,10},{10,18},{18,26},{... | collective-permute-start | bytes 1572872 | tf_op jit(solution)/shard_map/ppermute | solution.py:18
  20.2 13.5 %copy-start.9 = (f32[1,4096]{1,0:T(1,128)S(1)}, f32[1,4096]{1,0:T(1,128)}, u32[]{:S(2)}) copy-start(f32[1,4096]{1,0:T(1,128)} %param.10) | copy-start | bytes 49156
  20.2 35.1 %collective-permute-start.6 = (bf16[256,1024]{1,0:T(8,128)(2,1)}, bf16[256,1024]{1,0:T(8,128)(2,1)S(1)}, u32[]{:S(2)}, u32[]{:S(2)}) collective-permute-start(bf16[256,1024]{1,0:T(8,128)(2,1)} %get-tuple-element.25), channel_id=1, source_target_pairs={{0,8},{8,16},{16,24},{1,9},{9,17},{17,25},{2,10},{10,18},{18,26},{... | collective-permute-start | bytes 1572872 | tf_op jit(solution)/shard_map/ppermute | solution.py:18
  33.6 1.2 %collective-permute-start.2 = (f32[256]{0:T(256)S(1)}, f32[256]{0:T(256)S(1)}, u32[]{:S(2)}, u32[]{:S(2)}) collective-permute-start(f32[256]{0:T(256)S(1)} %bitcast.232), channel_id=1, source_target_pairs={{0,1},{1,0},{2,3},{3,2},{4,5},{5,4},{6,7},{7,6},{8,9},{9,8},{10,11... | collective-permute-start | bytes 3080 | tf_op jit(solution)/shard_map/ppermute | solution.py:40
  34.8 3.6 %collective-permute-start.3 = (f32[256]{0:T(256)S(1)}, f32[256]{0:T(256)S(1)}, u32[]{:S(2)}, u32[]{:S(2)}) collective-permute-start(f32[256]{0:T(256)S(1)} %add.133), channel_id=1, source_target_pairs={{0,2},{1,3},{2,0},{3,1},{4,6},{5,7},{6,4},{7,5},{8,10},{9,11},{10,... | collective-permute-start | bytes 3080 | tf_op jit(solution)/shard_map/ppermute | solution.py:40
  36.3 6.2 %copy-start.5 = (bf16[1,512,2048]{2,1,0:T(8,128)(2,1)S(1)}, bf16[1,512,2048]{2,1,0:T(8,128)(2,1)}, u32[]{:S(2)}) copy-start(bf16[1,512,2048]{2,1,0:T(8,128)(2,1)} %get-tuple-element.22) | copy-start | bytes 6291460
  41.0 2.3 %copy-start.6 = (bf16[1,512,2048]{2,1,0:T(8,128)(2,1)S(1)}, bf16[1,512,2048]{2,1,0:T(8,128)(2,1)}, u32[]{:S(2)}) copy-start(bf16[1,512,2048]{2,1,0:T(8,128)(2,1)} %get-tuple-element.23) | copy-start | bytes 6291460
  44.7 1.8 %copy-start.4 = (bf16[1,512,2048]{2,1,0:T(8,128)(2,1)S(1)}, bf16[1,512,2048]{2,1,0:T(8,128)(2,1)}, u32[]{:S(2)}) copy-start(bf16[1,512,2048]{2,1,0:T(8,128)(2,1)} %get-tuple-element.21) | copy-start | bytes 6291460
  46.9 1.6 %copy-start.3 = (bf16[1,512,2048]{2,1,0:T(8,128)(2,1)S(1)}, bf16[1,512,2048]{2,1,0:T(8,128)(2,1)}, u32[]{:S(2)}) copy-start(bf16[1,512,2048]{2,1,0:T(8,128)(2,1)} %get-tuple-element.20) | copy-start | bytes 6291460
  49.9 1.6 %copy-start.2 = (bf16[1,512,2048]{2,1,0:T(8,128)(2,1)S(1)}, bf16[1,512,2048]{2,1,0:T(8,128)(2,1)}, u32[]{:S(2)}) copy-start(bf16[1,512,2048]{2,1,0:T(8,128)(2,1)} %get-tuple-element.19) | copy-start | bytes 6291460
  51.9 1.6 %copy-start.1 = (bf16[1,512,2048]{2,1,0:T(8,128)(2,1)S(1)}, bf16[1,512,2048]{2,1,0:T(8,128)(2,1)}, u32[]{:S(2)}) copy-start(bf16[1,512,2048]{2,1,0:T(8,128)(2,1)} %get-tuple-element.18) | copy-start | bytes 6291460
  54.9 1.6 %copy-start = (bf16[1,512,2048]{2,1,0:T(8,128)(2,1)S(1)}, bf16[1,512,2048]{2,1,0:T(8,128)(2,1)}, u32[]{:S(2)}) copy-start(bf16[1,512,2048]{2,1,0:T(8,128)(2,1)} %get-tuple-element.24) | copy-start | bytes 6291460
  60.8 2.9 %collective-permute-start.7 = (f32[2,512,256]{2,1,0:T(8,128)}, f32[2,512,256]{2,1,0:T(8,128)S(1)}, u32[]{:S(2)}, u32[]{:S(2)}) collective-permute-start(f32[2,512,256]{2,1,0:T(8,128)} %slice.202), channel_id=1, source_target_pairs={{0,1},{1,0},{2,3},{3,2},{4,5},{5,4},{6,7},{7,6},{8,9},{9,8},{10,11... | collective-permute-start | bytes 3145736 | tf_op jit(solution)/shard_map/ppermute | solution.py:31
  63.9 8.4 %collective-permute-start.8 = (bf16[1,512,256]{2,1,0:T(8,128)(2,1)S(1)}, bf16[1,512,256]{2,1,0:T(8,128)(2,1)S(1)}, u32[]{:S(2)}, u32[]{:S(2)}) collective-permute-start(bf16[1,512,256]{2,1,0:T(8,128)(2,1)S(1)} %slice.290), channel_id=1, source_target_pairs={{0,2},{1,3},{2,0},{3,1},{4,6},{5,7},{6,4},{7,5},{8,10},{9,11},{10,... | collective-permute-start | bytes 786440 | tf_op jit(solution)/shard_map/ppermute | solution.py:31
  72.9 6.2 %collective-permute-start.9 = (bf16[192,512]{1,0:T(8,128)(2,1)S(1)}, bf16[192,512]{1,0:T(8,128)(2,1)S(1)}, u32[]{:S(2)}, u32[]{:S(2)}) collective-permute-start(bf16[192,512]{1,0:T(8,128)(2,1)S(1)} %get-tuple-element.29), channel_id=1, source_target_pairs={{0,4},{4,0},{1,5},{5,1},{2,6},{6,2},{3,7},{7,3},{8,12},{12,8},{9,1... | collective-permute-start | bytes 589832 | tf_op jit(solution)/shard_map/ppermute | solution.py:140
  79.0 0.7 copy-start.8

commit v14 on v13

--- a/solution.py
+++ b/solution.py
@@ -9,7 +9,7 @@
 
 EPSILON = 1e-05
 ROPE_BASE = 500000.0
-CHUNK_EIGHTHS = (2, 2, 2, 2)
+CHUNK_EIGHTHS = (3, 3, 2)
 
 
 def shifted(block, axis, distance):

time: 80.3 us -> 77 us (0.959)
  starting transfers between devices: 20.7 us -> 19 us
  matrix products: 13.8 us -> 12.5 us
    ppermute x5 -> x4, starting transfers between devices: 15.9 us -> 14.3 us  [shifted(): return lax.ppermute(block, axis, route)]
    dot_general x32, matrix products: 13.5 us -> 12.2 us  [per_device(): lax.dot_general(piece, sub, (((0,), (1,)), ((), ())), preferred_element_t...]
    unnamed x22, local copies, waits for them, and re-layouts: 3.75 us -> 2.66 us
    slice x1 -> x2, local copies, waits for them, and re-layouts: 3.01 us -> 3.36 us  [per_device(): arrived = shifted(tok_rows[:, cols], 'section', 1)]
    convert_element_type x4 -> x3, other arithmetic: 2.9 us -> 3.17 us  [per_device(): (arrived.astype(jnp.float32) * gain[cols] * scale[:, None]).astype(jnp.bf...]
    add x4 -> x3, other arithmetic: 1.61 us -> 1.78 us  [per_device(): partial = term if partial is None else partial + term]
  transfers between devices with their start and end apart: 10 -> 9, of which waited for: 5 -> 6; matrix products, arithmetic and copies ran while one was open for 35% -> 37% of each run, Pallas kernels for 0% -> 0%
where the time goes in v14:
time: 77 us; the launch traced here: 76.6 us
  local copies, waits for them, and re-layouts  19 us (25%)
  starting transfers between devices  19 us (25%)
  waiting for transfers between devices  17.3 us (22%)
  matrix products  12.5 us (16%)
  other arithmetic  6.98 us (9%)
  between operations  1.86 us (2%)
    ppermute x4, starting transfers between devices, shifted(): return lax.ppermute(block, axis, route)  14.3 us
    dot_general x32, matrix products, per_device(): lax.dot_general(piece, sub, (((0,), (1,)), ((), ())), preferred_element_t...  12.2 us
    slice x1, local copies, waits for them, and re-layouts, per_device(): piece = lax.dynamic_slice_in_dim(weight[part], column, block, axis=1)  11.5 us
    ppermute x2, waiting for transfers between devices, scatter_sum(): current = keep + lax.ppermute(send, axis, pairs).astype(jnp.float32)  9.36 us
    ppermute x1, waiting for transfers between devices, per_device(): arrived = lax.ppermute(outgoing, 'dp', pairs)  4.6 us
    slice x2, local copies, waits for them, and re-layouts, per_device(): arrived = shifted(tok_rows[:, cols], 'section', 1)  3.36 us
    convert_element_type x3, other arithmetic, per_device(): (arrived.astype(jnp.float32) * gain[cols] * scale[:, None]).astype(jnp.bf...  3.17 us
    ppermute x2, waiting for transfers between devices, all_sum(): lax.ppermute(value, axis, [(i, i ^ bit) for i in range(size)])  3.14 us
  transfers between devices with their start and end apart: 9, of which 6 were waited for; matrix products, arithmetic and copies ran while one was open for 37% of the time, Pallas kernels for 0%

profile of v14, /device:TPU:0, one launch (start us, length us, event | category | flops | bytes accessed | tf_op | source)
XLA Modules:
  0.0 76.6 jit_solution(11453734192172635986)
XLA Ops:
  0.0 2.5 %fusion.139 = (bf16[256,1536]{1,0:T(8,128)(2,1)S(1)}, bf16[256,1536]{1,0:T(8,128)(2,1)}) fusion(bf16[256,4096]{1,0:T(8,128)(2,1)} %bitcast.214), kind=kLoop, calls=%fused_computation.212 | loop fusion | bytes 3145728 | tf_op jit(solution)/shard_map/slice | solution.py:103
  2.5 5.8 %collective-permute-start.1 = (bf16[256,1536]{1,0:T(8,128)(2,1)}, bf16[256,1536]{1,0:T(8,128)(2,1)}, u32[]{:S(2)}, u32[]{:S(2)}) collective-permute-start(bf16[256,1536]{1,0:T(8,128)(2,1)} %get-tuple-element.24), channel_id=1, source_target_pairs={{0,8},{8,16},{16,24},{1,9},{9,17},{17,25},{2,10},{10,18},{18,26},{... | collective-permute-start | bytes 2359304 | tf_op jit(solution)/shard_map/ppermute | solution.py:18
  8.4 0.5 multiply_reduce_fusion
  9.5 0.6 reduce-window.6
  11.4 2.6 %collective-permute-start = (f32[3,256]{1,0:T(4,128)S(1)}, f32[3,256]{1,0:T(4,128)S(1)}, u32[]{:S(2)}, u32[]{:S(2)}) collective-permute-start(f32[3,256]{1,0:T(4,128)S(1)} %pad_maximum_fusion.1), channel_id=1, source_target_pairs={{0,8},{8,16},{16,24},{1,9},{9,17},{17,25},{2,10},{10,18},{18,26},{... | collective-permute-start | bytes 9224 | tf_op jit(solution)/shard_map/ppermute | solution.py:18
  14.0 4.4 %collective-permute-start.4 = (bf16[256,1536]{1,0:T(8,128)(2,1)S(1)}, bf16[256,1536]{1,0:T(8,128)(2,1)}, u32[]{:S(2)}, u32[]{:S(2)}) collective-permute-start(bf16[256,1536]{1,0:T(8,128)(2,1)S(1)} %get-tuple-element.23), channel_id=1, source_target_pairs={{0,8},{8,16},{16,24},{1,9},{9,17},{17,25},{2,10},{10,18},{18,26},{... | collective-permute-start | bytes 2359304 | tf_op jit(solution)/shard_map/ppermute | solution.py:18
  18.4 0.8 %slice.188 = bf16[256,1024]{1,0:T(8,128)(2,1)} slice(bf16[256,4096]{1,0:T(8,128)(2,1)S(1)} %bitcast.215), slice={[0:256], [3072:4096]} | slice | bytes 1048576 | tf_op jit(solution)/shard_map/slice | solution.py:103
  19.2 1.4 %collective-permute-start.5 = (bf16[256,1024]{1,0:T(8,128)(2,1)}, bf16[256,1024]{1,0:T(8,128)(2,1)S(1)}, u32[]{:S(2)}, u32[]{:S(2)}) collective-permute-start(bf16[256,1024]{1,0:T(8,128)(2,1)} %slice.188), channel_id=1, source_target_pairs={{0,8},{8,16},{16,24},{1,9},{9,17},{17,25},{2,10},{10,18},{18,26},{... | collective-permute-start | bytes 1572872 | tf_op jit(solution)/shard_map/ppermute | solution.py:18
  20.6 11.5 %fusion.138 = (bf16[1,512,2048]{2,1,0:T(8,128)(2,1)S(1)}, bf16[1,512,2048]{2,1,0:T(8,128)(2,1)}, bf16[1,512,2048]{2,1,0:T(8,128)(2,1)}, bf16[1,512,2048]{2,1,0:T...) fusion(bf16[1,4096,2048]{2,1,0:T(8,128)(2,1)} %param.11), kind=kLoop, calls=%fused_computation.211 | loop fusion | bytes 33554432 | tf_op jit(solution)/shard_map/slice | solution.py:113
  32.3 1.1 %collective-permute-done.2 = f32[256]{0:T(256)S(1)} collective-permute-done((f32[256]{0:T(256)S(1)}, f32[256]{0:T(256)S(1)}, u32[]{:S(2)}, u32[]{:S(2)}) %collective-permute-start.2) | collective-permute-done | bytes 1056 | tf_op jit(solution)/shard_map/ppermute | solution.py:40
  33.4 1.5 %collective-permute-start.3 = (f32[256]{0:T(256)S(1)}, f32[256]{0:T(256)S(1)}, u32[]{:S(2)}, u32[]{:S(2)}) collective-permute-start(f32[256]{0:T(256)S(1)} %add.133), channel_id=1, source_target_pairs={{0,2},{1,3},{2,0},{3,1},{4,6},{5,7},{6,4},{7,5},{8,10},{9,11},{10,... | collective-permute-start | bytes 3080 | tf_op jit(solution)/shard_map/ppermute | solution.py:40
  34.9 2.1 %collective-permute-done.3 = f32[256]{0:T(256)S(1)} collective-permute-done((f32[256]{0:T(256)S(1)}, f32[256]{0:T(256)S(1)}, u32[]{:S(2)}, u32[]{:S(2)}) %collective-permute-start.3) | collective-permute-done | bytes 1056 | tf_op jit(solution)/shard_map/ppermute | solution.py:40
  37.0 1.5 %multiply_convert_fusion.1 = bf16[256,1536]{1,0:T(8,128)(2,1)S(1)} fusion(bf16[256,1536]{1,0:T(8,128)(2,1)} %collective-permute-done.1, f32[256]{0:T(256)S(1)} %add_rsqrt_fusion, f32[1536]{0:T(1024)S(1)} %get-tuple-element.14), kind=kLoop, calls=%fused_computation.9 | loop fusion | flops 1572864 | bytes 1580032 | tf_op jit(solution)/shard_map/convert_element_type | solution.py:106
  38.5 1.4 %convolution_bitcast_fusion.28 = f32[1,512,256]{2,1,0:T(8,128)S(1)} fusion(bf16[1,512,2048]{2,1,0:T(8,128)(2,1)} %get-tuple-element.21, s32[]{:T(128)S(6)} %select_n.89, bf16[256,1536]{1,0:T(8,128)(2,1)S(1)} %multiply_convert_fusion.1), kind=kOutput, calls=%fused_computation.39 | convolution fusion | flops 134217728 | bytes 1310724 | tf_op jit(solution)/shard_map/dot_general | solution.py:115
  42.4 0.5 copy-done.4
  44.3 0.5 fusion
  44.8 1.5 %multiply_convert_fusion = bf16[256,1536]{1,0:T(8,128)(2,1)S(1)} fusion(bf16[256,1536]{1,0:T(8,128)(2,1)} %collective-permute-done.4, f32[1536]{0:T(1024)S(1)} %get-tuple-element.13, f32[256]{0:T(256)S(1)} %add_rsqrt_fusion), kind=kLoop, calls=%fused_computation.8 | loop fusion | flops 1572864 | bytes 1580032 | tf_op jit(solution)/shard_map/convert_element_type | solution.py:106
  47.8 0.5 copy-done.2
  49.7 0.5 copy-done.1
  51.7 0.9 %fusion.2 = f32[4,512,256]{2,1,0:T(8,128)S(1)} fusion(f32[4,512,256]{2,1,0:T(8,128)S(1)} %fusion, f32[1,512,256]{2,1,0:T(8,128)S(1)} %convolution_bitcast_fusion.16, f32[1,512,256]{2,1,0:T(8,128)S(1)} %convolution_bitcast_fusion.17, f32[1,512,256]{2,1,0:T(8,128)S(1)} %convolution_bitcast_fusion.18, f32[1,512,256]{2,1,0:T(8,128)S(1)} %convolution_bitcast_fusion.19, ...), kind=kLoop, calls=%fused_computation.5 | loop fusion | flops 6291456 | bytes 10485760 | tf_op jit(solution)/shard_map/add | solution.py:120
  53.6 0.4 convolution_bitcast_fusion.5
  54.3 0.4 convolution_bitcast_fusion.7
  54.7 0.4 convolution_bitcast_fusion
  55.0 0.4 convolution_bitcast_fusion.1
  56.1 0.4 fusion.3
  56.6 1.0 %slice.192 = f32[2,512,256]{2,1,0:T(8,128)} slice(f32[4,512,256]{2,1,0:T(8,128)S(1)} %fusion.3), slice={[2:4], [0:512], [0:256]} | slice | bytes 2097152 | tf_op jit(solution)/shard_map/slice | solution.py:27
  57.6 2.9 %collective-permute-done.6 = f32[2,512,256]{2,1,0:T(8,128)S(1)} collective-permute-done((f32[2,512,256]{2,1,0:T(8,128)}, f32[2,512,256]{2,1,0:T(8,128)S(1)}, u32[]{:S(2)}, u32[]{:S(2)}) %collective-permute-start.6) | collective-permute-done | bytes 1048608 | tf_op jit(solution)/shard_map/ppermute | solution.py:31
  60.6 1.6 %collective-permute-start.7 = (bf16[1,512,256]{2,1,0:T(8,128)(2,1)S(1)}, bf16[1,512,256]{2,1,0:T(8,128)(2,1)S(1)}, u32[]{:S(2)}, u32[]{:S(2)}) collective-permute-start(bf16[1,512,256]{2,1,0:T(8,128)(2,1)S(1)} %slice.282), channel_id=1, source_target_pairs={{0,2},{1,3},{2,0},{3,1},{4,6},{5,7},{6,4},{7,5},{8,10},{9,11},{10,... | collective-permute-start | bytes 786440 | tf_op jit(solution)/shard_map/ppermute | solution.py:31
  62.5 6.5 %collective-permute-done.7 = bf16[1,512,256]{2,1,0:T(8,128)(2,1)S(1)} collective-permute-done((bf16[1,512,256]{2,1,0:T(8,128)(2,1)S(1)}, bf16[1,512,256]{2,1,0:T(8,128)(2,1)S(1)}, u32[]{:S(2)}, u32[]{:S(2)}) %collective-permute-start.7) | collective-permute-done | bytes 262176 | tf_op jit(solution)/shard_map/ppermute | solution.py:31
  69.7 1.5 %collective-permute-start.8 = (bf16[192,512]{1,0:T(8,128)(2,1)S(1)}, bf16[192,512]{1,0:T(8,128)(2,1)S(1)}, u32[]{:S(2)}, u32[]{:S(2)}) collective-permute-start(bf16[192,512]{1,0:T(8,128)(2,1)S(1)} %get-tuple-element.25), channel_id=1, source_target_pairs={{0,4},{4,0},{1,5},{5,1},{2,6},{6,2},{3,7},{7,3},{8,12},{12,8},{9,1... | collective-permute-start | bytes 589832 | tf_op jit(solution)/shard_map/ppermute | solution.py:140
  71.2 4.6 %collective-permute-done.8 = bf16[192,512]{1,0:T(8,128)(2,1)S(1)} collective-permute-done((bf16[192,512]{1,0:T(8,128)(2,1)S(1)}, bf16[192,512]{1,0:T(8,128)(2,1)S(1)}, u32[]{:S(2)}, u32[]{:S(2)}) %collective-permute-start.8) | collective-permute-done | bytes 196640 | tf_op jit(solution)/shard_map/ppermute | solution.py:140
  75.8 0.7 copy-done.8
  (82 shorter events, 11.8 us)
Async XLA Ops:
  0.0 8.4 %copy-start.7 = (bf16[1,1,256,4096]{3,2,1,0:T(8,128)(2,1)S(1)}, bf16[1,1,256,4096]{3,2,1,0:T(8,128)(2,1)}, u32[]{:S(2)}) copy-start(bf16[1,1,256,4096]{3,2,1,0:T(8,128)(2,1)} %param.6) | copy-start | bytes 6291460
  0.0 9.5 %copy-start.10 = (s32[1,1,256,1]{2,3,1,0:T(1,128)S(1)}, s32[1,1,256,1]{2,3,1,0:T(1,128)}, u32[]{:S(2)}) copy-start(s32[1,1,256,1]{2,3,1,0:T(1,128)} %param.7) | copy-start | bytes 3076
  2.5 34.5 %collective-permute-start.1 = (bf16[256,1536]{1,0:T(8,128)(2,1)}, bf16[256,1536]{1,0:T(8,128)(2,1)}, u32[]{:S(2)}, u32[]{:S(2)}) collective-permute-start(bf16[256,1536]{1,0:T(8,128)(2,1)} %get-tuple-element.24), channel_id=1, source_target_pairs={{0,8},{8,16},{16,24},{1,9},{9,17},{17,25},{2,10},{10,18},{18,26},{... | collective-permute-start | bytes 2359304 | tf_op jit(solution)/shard_map/ppermute | solution.py:18
  11.4 20.8 %collective-permute-start = (f32[3,256]{1,0:T(4,128)S(1)}, f32[3,256]{1,0:T(4,128)S(1)}, u32[]{:S(2)}, u32[]{:S(2)}) collective-permute-start(f32[3,256]{1,0:T(4,128)S(1)} %pad_maximum_fusion.1), channel_id=1, source_target_pairs={{0,8},{8,16},{16,24},{1,9},{9,17},{17,25},{2,10},{10,18},{18,26},{... | collective-permute-start | bytes 9224 | tf_op jit(solution)/shard_map/ppermute | solution.py:18
  14.0 30.8 %collective-permute-start.4 = (bf16[256,1536]{1,0:T(8,128)(2,1)S(1)}, bf16[256,1536]{1,0:T(8,128)(2,1)}, u32[]{:S(2)}, u32[]{:S(2)}) collective-permute-start(bf16[256,1536]{1,0:T(8,128)(2,1)S(1)} %get-tuple-element.23), channel_id=1, source_target_pairs={{0,8},{8,16},{16,24},{1,9},{9,17},{17,25},{2,10},{10,18},{18,26},{... | collective-permute-start | bytes 2359304 | tf_op jit(solution)/shard_map/ppermute | solution.py:18
  19.2 13.1 %copy-start.9 = (f32[1,4096]{1,0:T(1,128)S(1)}, f32[1,4096]{1,0:T(1,128)}, u32[]{:S(2)}) copy-start(f32[1,4096]{1,0:T(1,128)} %param.10) | copy-start | bytes 49156
  19.2 33.6 %collective-permute-start.5 = (bf16[256,1024]{1,0:T(8,128)(2,1)}, bf16[256,1024]{1,0:T(8,128)(2,1)S(1)}, u32[]{:S(2)}, u32[]{:S(2)}) collective-permute-start(bf16[256,1024]{1,0:T(8,128)(2,1)} %slice.188), channel_id=1, source_target_pairs={{0,8},{8,16},{16,24},{1,9},{9,17},{17,25},{2,10},{10,18},{18,26},{... | collective-permute-start | bytes 1572872 | tf_op jit(solution)/shard_map/ppermute | solution.py:18
  32.2 1.2 %collective-permute-start.2 = (f32[256]{0:T(256)S(1)}, f32[256]{0:T(256)S(1)}, u32[]{:S(2)}, u32[]{:S(2)}) collective-permute-start(f32[256]{0:T(256)S(1)} %bitcast.227), channel_id=1, source_target_pairs={{0,1},{1,0},{2,3},{3,2},{4,5},{5,4},{6,7},{7,6},{8,9},{9,8},{10,11... | collective-permute-start | bytes 3080 | tf_op jit(solution)/shard_map/ppermute | solution.py:40
  33.4 3.6 %collective-permute-start.3 = (f32[256]{0:T(256)S(1)}, f32[256]{0:T(256)S(1)}, u32[]{:S(2)}, u32[]{:S(2)}) collective-permute-start(f32[256]{0:T(256)S(1)} %add.133), channel_id=1, source_target_pairs={{0,2},{1,3},{2,0},{3,1},{4,6},{5,7},{6,4},{7,5},{8,10},{9,11},{10,... | collective-permute-start | bytes 3080 | tf_op jit(solution)/shard_map/ppermute | solution.py:40
  34.9 5.0 %copy-start.6 = (bf16[1,512,2048]{2,1,0:T(8,128)(2,1)S(1)}, bf16[1,512,2048]{2,1,0:T(8,128)(2,1)}, u32[]{:S(2)}) copy-start(bf16[1,512,2048]{2,1,0:T(8,128)(2,1)} %get-tuple-element.21) | copy-start | bytes 6291460
  37.0 3.3 %copy-start.5 = (bf16[1,512,2048]{2,1,0:T(8,128)(2,1)S(1)}, bf16[1,512,2048]{2,1,0:T(8,128)(2,1)}, u32[]{:S(2)}) copy-start(bf16[1,512,2048]{2,1,0:T(8,128)(2,1)} %get-tuple-element.20) | copy-start | bytes 6291460
  41.3 1.6 %copy-start.4 = (bf16[1,512,2048]{2,1,0:T(8,128)(2,1)S(1)}, bf16[1,512,2048]{2,1,0:T(8,128)(2,1)}, u32[]{:S(2)}) copy-start(bf16[1,512,2048]{2,1,0:T(8,128)(2,1)} %get-tuple-element.19) | copy-start | bytes 6291460
  44.3 2.0 %copy-start.3 = (bf16[1,512,2048]{2,1,0:T(8,128)(2,1)S(1)}, bf16[1,512,2048]{2,1,0:T(8,128)(2,1)}, u32[]{:S(2)}) copy-start(bf16[1,512,2048]{2,1,0:T(8,128)(2,1)} %get-tuple-element.18) | copy-start | bytes 6291460
  46.7 1.6 %copy-start.2 = (bf16[1,512,2048]{2,1,0:T(8,128)(2,1)S(1)}, bf16[1,512,2048]{2,1,0:T(8,128)(2,1)}, u32[]{:S(2)}) copy-start(bf16[1,512,2048]{2,1,0:T(8,128)(2,1)} %get-tuple-element.17) | copy-start | bytes 6291460
  48.6 1.6 %copy-start.1 = (bf16[1,512,2048]{2,1,0:T(8,128)(2,1)S(1)}, bf16[1,512,2048]{2,1,0:T(8,128)(2,1)}, u32[]{:S(2)}) copy-start(bf16[1,512,2048]{2,1,0:T(8,128)(2,1)} %get-tuple-element.16) | copy-start | bytes 6291460
  51.6 1.1 %slice-start = ((f32[1,4096]{1,0:T(1,128)}), f32[1,1024]{1,0:T(1,128)S(1)}, s32[]{:S(2)}) async-start(f32[1,4096]{1,0:T(1,128)} %param.10), calls=%async_computation | async-start | bytes 8192 | tf_op jit(solution)/shard_map/slice | solution.py:106
  51.7 1.6 %copy-start = (bf16[1,512,2048]{2,1,0:T(8,128)(2,1)S(1)}, bf16[1,512,2048]{2,1,0:T(8,128)(2,1)}, u32[]{:S(2)}) copy-start(bf16[1,512,2048]{2,1,0:T(8,128)(2,1)} %get-tuple-element.22) | copy-start | bytes 6291460
  57.6 2.9 %collective-permute-start.6 = (f32[2,512,256]{2,1,0:T(8,128)}, f32[2,512,256]{2,1,0:T(8,128)S(1)}, u32[]{:S(2)}, u32[]{:S(2)}) collective-permute-start(f32[2,512,256]{2,1,0:T(8,128)} %slice.192), channel_id=1, source_target_pairs={{0,1},{1,0},{2,3},{3,2},{4,5},{5,4},{6,7},{7,6},{8,9},{9,8},{10,11... | collective-permute-start | bytes 3145736 | tf_op jit(solution)/shard_map/ppermute | solution.py:31
  60.6 8.4 %collective-permute-start.7 = (bf16[1,512,256]{2,1,0:T(8,128)(2,1)S(1)}, bf16[1,512,256]{2,1,0:T(8,128)(2,1)S(1)}, u32[]{:S(2)}, u32[]{:S(2)}) collective-permute-start(bf16[1,512,256]{2,1,0:T(8,128)(2,1)S(1)} %slice.282), channel_id=1, source_target_pairs={{0,2},{1,3},{2,0},{3,1},{4,6},{5,7},{6,4},{7,5},{8,10},{9,11},{10,... | collective-permute-start | bytes 786440 | tf_op jit(solution)/shard_map/ppermute | solution.py:31
  69.7 6.1 %collective-permute-start.8 = (bf16[192,512]{1,0:T(8,128)(2,1)S(1)}, bf16[192,512]{1,0:T(8,128)(2,1)S(1)}, u32[]{:S(2)}, u32[]{:S(2)}) collective-permute-start(bf16[192,512]{1,0:T(8,128)(2,1)S(1)} %get-tuple-element.25), channel_id=1, source_target_pairs={{0,4},{4,0},{1,5},{5,1},{2,6},{6,2},{3,7},{7,3},{8,12},{12,8},{9,1... | collective-permute-start | bytes 589832 | tf_op jit(solution)/shard_map/ppermute | solution.py:140
  75.8 0.7 copy-start.8

commit v15 on v14

--- a/solution.py
+++ b/solution.py
@@ -9,7 +9,7 @@
 
 EPSILON = 1e-05
 ROPE_BASE = 500000.0
-CHUNK_EIGHTHS = (3, 3, 2)
+CHUNK_EIGHTHS = (6, 2)
 
 
 def shifted(block, axis, distance):

time: 77 us -> 96.7 us (1.26)
  waiting for transfers between devices: 17.3 us -> 41 us
  starting transfers between devices: 19 us -> 16.7 us
  other arithmetic: 6.98 us -> 5.54 us
    ppermute x4 -> x3, waiting for transfers between devices: 0.19 us -> 25 us  [shifted(): return lax.ppermute(block, axis, route)]
    ppermute x4 -> x3, starting transfers between devices: 14.3 us -> 12 us  [shifted(): return lax.ppermute(block, axis, route)]
    unnamed x22 -> x20, local copies, waits for them, and re-layouts: 2.66 us -> 3.9 us
    convert_element_type x3 -> x2, other arithmetic: 3.17 us -> 2.02 us  [per_device(): (arrived.astype(jnp.float32) * gain[cols] * scale[:, None]).astype(jnp.bf...]
    ppermute x2, waiting for transfers between devices: 3.14 us -> 2.05 us  [all_sum(): lax.ppermute(value, axis, [(i, i ^ bit) for i in range(size)])]
  transfers between devices with their start and end apart: 9 -> 8, of which waited for: 6 -> 5; matrix products, arithmetic and copies ran while one was open for 37% -> 26% of each run, Pallas kernels for 0% -> 0%
where the time goes in v15:
time: 96.7 us; the launch traced here: 96.3 us
  waiting for transfers between devices  41 us (42%)
  local copies, waits for them, and re-layouts  19.6 us (20%)
  starting transfers between devices  16.7 us (17%)
  matrix products  11.6 us (12%)
  other arithmetic  5.54 us (6%)
  between operations  1.86 us (2%)
    ppermute x3, waiting for transfers between devices, shifted(): return lax.ppermute(block, axis, route)  25 us
    ppermute x3, starting transfers between devices, shifted(): return lax.ppermute(block, axis, route)  12 us
    slice x1, local copies, waits for them, and re-layouts, per_device(): piece = lax.dynamic_slice_in_dim(weight[part], column, block, axis=1)  11.4 us
    dot_general x32, matrix products, per_device(): lax.dot_general(piece, sub, (((0,), (1,)), ((), ())), preferred_element_t...  11.3 us
    ppermute x2, waiting for transfers between devices, scatter_sum(): current = keep + lax.ppermute(send, axis, pairs).astype(jnp.float32)  9.38 us
    ppermute x1, waiting for transfers between devices, per_device(): arrived = lax.ppermute(outgoing, 'dp', pairs)  4.61 us
    unnamed x20, local copies, waits for them, and re-layouts  3.9 us
    slice x2, local copies, waits for them, and re-layouts, per_device(): arrived = shifted(tok_rows[:, cols], 'section', 1)  2.87 us
  transfers between devices with their start and end apart: 8, of which 5 were waited for; matrix products, arithmetic and copies ran while one was open for 26% of the time, Pallas kernels for 0%

profile of v15, /device:TPU:0, one launch (start us, length us, event | category | flops | bytes accessed | tf_op | source)
XLA Modules:
  0.0 96.3 jit_solution(2054290443028513047)
XLA Ops:
  0.0 2.8 %slice.170 = bf16[256,3072]{1,0:T(8,128)(2,1)} slice(bf16[256,4096]{1,0:T(8,128)(2,1)} %bitcast.215), slice={[0:256], [0:3072]} | slice | bytes 3145728 | tf_op jit(solution)/shard_map/slice | solution.py:103
  2.8 6.1 %collective-permute-start.1 = (bf16[256,3072]{1,0:T(8,128)(2,1)}, bf16[256,3072]{1,0:T(8,128)(2,1)}, u32[]{:S(2)}, u32[]{:S(2)}) collective-permute-start(bf16[256,3072]{1,0:T(8,128)(2,1)} %slice.170), channel_id=1, source_target_pairs={{0,8},{8,16},{16,24},{1,9},{9,17},{17,25},{2,10},{10,18},{18,26},{... | collective-permute-start | bytes 4718600 | tf_op jit(solution)/shard_map/ppermute | solution.py:18
  8.9 0.5 multiply_reduce_fusion
  10.1 0.6 reduce-window.6
  11.9 2.4 %collective-permute-start = (f32[3,256]{1,0:T(4,128)S(1)}, f32[3,256]{1,0:T(4,128)S(1)}, u32[]{:S(2)}, u32[]{:S(2)}) collective-permute-start(f32[3,256]{1,0:T(4,128)S(1)} %pad_maximum_fusion.1), channel_id=1, source_target_pairs={{0,8},{8,16},{16,24},{1,9},{9,17},{17,25},{2,10},{10,18},{18,26},{... | collective-permute-start | bytes 9224 | tf_op jit(solution)/shard_map/ppermute | solution.py:18
  14.3 3.5 %collective-permute-start.4 = (bf16[256,1024]{1,0:T(8,128)(2,1)S(1)}, bf16[256,1024]{1,0:T(8,128)(2,1)S(1)}, u32[]{:S(2)}, u32[]{:S(2)}) collective-permute-start(bf16[256,1024]{1,0:T(8,128)(2,1)S(1)} %slice.178), channel_id=1, source_target_pairs={{0,8},{8,16},{16,24},{1,9},{9,17},{17,25},{2,10},{10,18},{18,26},{... | collective-permute-start | bytes 1572872 | tf_op jit(solution)/shard_map/ppermute | solution.py:18
  17.9 25.0 %collective-permute-done = f32[3,256]{1,0:T(4,128)S(1)} collective-permute-done((f32[3,256]{1,0:T(4,128)S(1)}, f32[3,256]{1,0:T(4,128)S(1)}, u32[]{:S(2)}, u32[]{:S(2)}) %collective-permute-start) | collective-permute-done | bytes 3104 | tf_op jit(solution)/shard_map/ppermute | solution.py:18
  42.9 11.4 %fusion.139 = (bf16[1,512,2048]{2,1,0:T(8,128)(2,1)S(1)}, bf16[1,512,2048]{2,1,0:T(8,128)(2,1)}, bf16[1,512,2048]{2,1,0:T(8,128)(2,1)}, bf16[1,512,2048]{2,1,0:T...) fusion(bf16[1,4096,2048]{2,1,0:T(8,128)(2,1)} %param.11), kind=kLoop, calls=%fused_computation.208 | loop fusion | bytes 33554432 | tf_op jit(solution)/shard_map/slice | solution.py:113
  54.3 1.6 %collective-permute-start.3 = (f32[256]{0:T(256)S(1)}, f32[256]{0:T(256)S(1)}, u32[]{:S(2)}, u32[]{:S(2)}) collective-permute-start(f32[256]{0:T(256)S(1)} %add.133), channel_id=1, source_target_pairs={{0,2},{1,3},{2,0},{3,1},{4,6},{5,7},{6,4},{7,5},{8,10},{9,11},{10,... | collective-permute-start | bytes 3080 | tf_op jit(solution)/shard_map/ppermute | solution.py:40
  55.9 2.1 %collective-permute-done.3 = f32[256]{0:T(256)S(1)} collective-permute-done((f32[256]{0:T(256)S(1)}, f32[256]{0:T(256)S(1)}, u32[]{:S(2)}, u32[]{:S(2)}) %collective-permute-start.3) | collective-permute-done | bytes 1056 | tf_op jit(solution)/shard_map/ppermute | solution.py:40
  58.0 1.8 %multiply_convert_fusion = bf16[256,3072]{1,0:T(8,128)(2,1)S(1)} fusion(bf16[256,3072]{1,0:T(8,128)(2,1)} %collective-permute-done.1, f32[256]{0:T(256)S(1)} %add_rsqrt_fusion, f32[3072]{0:T(1024)S(1)} %bitcast.221), kind=kLoop, calls=%fused_computation.1 | loop fusion | flops 3145728 | bytes 3159040 | tf_op jit(solution)/shard_map/convert_element_type | solution.py:106
  60.6 0.9 copy-done.5
  63.6 0.5 copy-done.4
  64.1 0.4 convolution_bitcast_fusion.20
  64.5 0.4 convolution_bitcast_fusion.21
  65.6 0.5 copy-done.3
  67.5 0.5 copy-done.2
  68.0 0.4 convolution_bitcast_fusion.12
  68.4 0.4 convolution_bitcast_fusion.13
  69.5 0.5 copy-done.1
  71.4 1.1 %fusion.3 = f32[4,512,256]{2,1,0:T(8,128)S(1)} fusion(f32[1,512,256]{2,1,0:T(8,128)S(1)} %convolution_bitcast_fusion.28, f32[1,512,256]{2,1,0:T(8,128)S(1)} %convolution_bitcast_fusion.29, f32[1,512,256]{2,1,0:T(8,128)S(1)} %convolution_bitcast_fusion.30, f32[1,512,256]{2,1,0:T(8,128)S(1)} %convolution_bitcast_fusion.31, ...), kind=kLoop, calls=%fused_computation.6 | loop fusion | flops 12058624 | bytes 14680064 | tf_op jit(solution)/shard_map/add | solution.py:120
  73.7 0.4 convolution_bitcast_fusion.6
  74.1 0.4 convolution_bitcast_fusion.7
  74.8 0.4 convolution_bitcast_fusion.1
  75.9 0.4 fusion.4
  76.3 1.0 %slice.182 = f32[2,512,256]{2,1,0:T(8,128)} slice(f32[4,512,256]{2,1,0:T(8,128)S(1)} %fusion.4), slice={[2:4], [0:512], [0:256]} | slice | bytes 2097152 | tf_op jit(solution)/shard_map/slice | solution.py:27
  77.4 2.9 %collective-permute-done.5 = f32[2,512,256]{2,1,0:T(8,128)S(1)} collective-permute-done((f32[2,512,256]{2,1,0:T(8,128)}, f32[2,512,256]{2,1,0:T(8,128)S(1)}, u32[]{:S(2)}, u32[]{:S(2)}) %collective-permute-start.5) | collective-permute-done | bytes 1048608 | tf_op jit(solution)/shard_map/ppermute | solution.py:31
  80.4 1.6 %collective-permute-start.6 = (bf16[1,512,256]{2,1,0:T(8,128)(2,1)S(1)}, bf16[1,512,256]{2,1,0:T(8,128)(2,1)S(1)}, u32[]{:S(2)}, u32[]{:S(2)}) collective-permute-start(bf16[1,512,256]{2,1,0:T(8,128)(2,1)S(1)} %slice.270), channel_id=1, source_target_pairs={{0,2},{1,3},{2,0},{3,1},{4,6},{5,7},{6,4},{7,5},{8,10},{9,11},{10,... | collective-permute-start | bytes 786440 | tf_op jit(solution)/shard_map/ppermute | solution.py:31
  82.3 6.5 %collective-permute-done.6 = bf16[1,512,256]{2,1,0:T(8,128)(2,1)S(1)} collective-permute-done((bf16[1,512,256]{2,1,0:T(8,128)(2,1)S(1)}, bf16[1,512,256]{2,1,0:T(8,128)(2,1)S(1)}, u32[]{:S(2)}, u32[]{:S(2)}) %collective-permute-start.6) | collective-permute-done | bytes 262176 | tf_op jit(solution)/shard_map/ppermute | solution.py:31
  89.4 1.5 %collective-permute-start.7 = (bf16[192,512]{1,0:T(8,128)(2,1)S(1)}, bf16[192,512]{1,0:T(8,128)(2,1)S(1)}, u32[]{:S(2)}, u32[]{:S(2)}) collective-permute-start(bf16[192,512]{1,0:T(8,128)(2,1)S(1)} %get-tuple-element.17), channel_id=1, source_target_pairs={{0,4},{4,0},{1,5},{5,1},{2,6},{6,2},{3,7},{7,3},{8,12},{12,8},{9,1... | collective-permute-start | bytes 589832 | tf_op jit(solution)/shard_map/ppermute | solution.py:140
  91.0 4.6 %collective-permute-done.7 = bf16[192,512]{1,0:T(8,128)(2,1)S(1)} collective-permute-done((bf16[192,512]{1,0:T(8,128)(2,1)S(1)}, bf16[192,512]{1,0:T(8,128)(2,1)S(1)}, u32[]{:S(2)}, u32[]{:S(2)}) %collective-permute-start.7) | collective-permute-done | bytes 196640 | tf_op jit(solution)/shard_map/ppermute | solution.py:140
  95.6 0.7 copy-done.8
  (77 shorter events, 10.9 us)
Async XLA Ops:
  0.0 8.9 %copy-start.7 = (bf16[1,1,256,4096]{3,2,1,0:T(8,128)(2,1)S(1)}, bf16[1,1,256,4096]{3,2,1,0:T(8,128)(2,1)}, u32[]{:S(2)}) copy-start(bf16[1,1,256,4096]{3,2,1,0:T(8,128)(2,1)} %param.6) | copy-start | bytes 6291460
  0.0 10.1 %copy-start.9 = (s32[1,1,256,1]{2,3,1,0:T(1,128)S(1)}, s32[1,1,256,1]{2,3,1,0:T(1,128)}, u32[]{:S(2)}) copy-start(s32[1,1,256,1]{2,3,1,0:T(1,128)} %param.7) | copy-start | bytes 3076
  2.8 55.2 %collective-permute-start.1 = (bf16[256,3072]{1,0:T(8,128)(2,1)}, bf16[256,3072]{1,0:T(8,128)(2,1)}, u32[]{:S(2)}, u32[]{:S(2)}) collective-permute-start(bf16[256,3072]{1,0:T(8,128)(2,1)} %slice.170), channel_id=1, source_target_pairs={{0,8},{8,16},{16,24},{1,9},{9,17},{17,25},{2,10},{10,18},{18,26},{... | collective-permute-start | bytes 4718600 | tf_op jit(solution)/shard_map/ppermute | solution.py:18
  11.9 30.9 %collective-permute-start = (f32[3,256]{1,0:T(4,128)S(1)}, f32[3,256]{1,0:T(4,128)S(1)}, u32[]{:S(2)}, u32[]{:S(2)}) collective-permute-start(f32[3,256]{1,0:T(4,128)S(1)} %pad_maximum_fusion.1), channel_id=1, source_target_pairs={{0,8},{8,16},{16,24},{1,9},{9,17},{17,25},{2,10},{10,18},{18,26},{... | collective-permute-start | bytes 9224 | tf_op jit(solution)/shard_map/ppermute | solution.py:18
  14.3 58.2 %collective-permute-start.4 = (bf16[256,1024]{1,0:T(8,128)(2,1)S(1)}, bf16[256,1024]{1,0:T(8,128)(2,1)S(1)}, u32[]{:S(2)}, u32[]{:S(2)}) collective-permute-start(bf16[256,1024]{1,0:T(8,128)(2,1)S(1)} %slice.178), channel_id=1, source_target_pairs={{0,8},{8,16},{16,24},{1,9},{9,17},{17,25},{2,10},{10,18},{18,26},{... | collective-permute-start | bytes 1572872 | tf_op jit(solution)/shard_map/ppermute | solution.py:18
  42.9 15.1 %slice-start = ((f32[1,4096]{1,0:T(1,128)}), f32[1,3072]{1,0:T(1,128)S(1)}, s32[]{:S(2)}) async-start(f32[1,4096]{1,0:T(1,128)} %param.10), calls=%async_computation | async-start | bytes 24576 | tf_op jit(solution)/shard_map/slice | solution.py:106
  42.9 11.4 %collective-permute-start.2 = (f32[256]{0:T(256)S(1)}, f32[256]{0:T(256)S(1)}, u32[]{:S(2)}, u32[]{:S(2)}) collective-permute-start(f32[256]{0:T(256)S(1)} %bitcast.229), channel_id=1, source_target_pairs={{0,1},{1,0},{2,3},{3,2},{4,5},{5,4},{6,7},{7,6},{8,9},{9,8},{10,11... | collective-permute-start | bytes 3080 | tf_op jit(solution)/shard_map/ppermute | solution.py:40
  54.3 3.6 %collective-permute-start.3 = (f32[256]{0:T(256)S(1)}, f32[256]{0:T(256)S(1)}, u32[]{:S(2)}, u32[]{:S(2)}) collective-permute-start(f32[256]{0:T(256)S(1)} %add.133), channel_id=1, source_target_pairs={{0,2},{1,3},{2,0},{3,1},{4,6},{5,7},{6,4},{7,5},{8,10},{9,11},{10,... | collective-permute-start | bytes 3080 | tf_op jit(solution)/shard_map/ppermute | solution.py:40
  55.9 3.9 %copy-start.6 = (bf16[1,512,2048]{2,1,0:T(8,128)(2,1)S(1)}, bf16[1,512,2048]{2,1,0:T(8,128)(2,1)}, u32[]{:S(2)}) copy-start(bf16[1,512,2048]{2,1,0:T(8,128)(2,1)} %get-tuple-element.15) | copy-start | bytes 6291460
  59.8 1.6 %copy-start.5 = (bf16[1,512,2048]{2,1,0:T(8,128)(2,1)S(1)}, bf16[1,512,2048]{2,1,0:T(8,128)(2,1)}, u32[]{:S(2)}) copy-start(bf16[1,512,2048]{2,1,0:T(8,128)(2,1)} %get-tuple-element.14) | copy-start | bytes 6291460
  62.5 1.6 %copy-start.4 = (bf16[1,512,2048]{2,1,0:T(8,128)(2,1)S(1)}, bf16[1,512,2048]{2,1,0:T(8,128)(2,1)}, u32[]{:S(2)}) copy-start(bf16[1,512,2048]{2,1,0:T(8,128)(2,1)} %get-tuple-element.13) | copy-start | bytes 6291460
  64.5 1.6 %copy-start.3 = (bf16[1,512,2048]{2,1,0:T(8,128)(2,1)S(1)}, bf16[1,512,2048]{2,1,0:T(8,128)(2,1)}, u32[]{:S(2)}) copy-start(bf16[1,512,2048]{2,1,0:T(8,128)(2,1)} %get-tuple-element.12) | copy-start | bytes 6291460
  66.4 1.6 %copy-start.2 = (bf16[1,512,2048]{2,1,0:T(8,128)(2,1)S(1)}, bf16[1,512,2048]{2,1,0:T(8,128)(2,1)}, u32[]{:S(2)}) copy-start(bf16[1,512,2048]{2,1,0:T(8,128)(2,1)} %get-tuple-element.11) | copy-start | bytes 6291460
  68.4 1.6 %copy-start.1 = (bf16[1,512,2048]{2,1,0:T(8,128)(2,1)S(1)}, bf16[1,512,2048]{2,1,0:T(8,128)(2,1)}, u32[]{:S(2)}) copy-start(bf16[1,512,2048]{2,1,0:T(8,128)(2,1)} %get-tuple-element.10) | copy-start | bytes 6291460
  71.4 1.1 %slice-start.1 = ((f32[1,4096]{1,0:T(1,128)}), f32[1,1024]{1,0:T(1,128)S(1)}, s32[]{:S(2)}) async-start(f32[1,4096]{1,0:T(1,128)} %param.10), calls=%async_computation.1 | async-start | bytes 8192 | tf_op jit(solution)/shard_map/slice | solution.py:106
  71.4 1.6 %copy-start = (bf16[1,512,2048]{2,1,0:T(8,128)(2,1)S(1)}, bf16[1,512,2048]{2,1,0:T(8,128)(2,1)}, u32[]{:S(2)}) copy-start(bf16[1,512,2048]{2,1,0:T(8,128)(2,1)} %get-tuple-element.16) | copy-start | bytes 6291460
  77.4 2.9 %collective-permute-start.5 = (f32[2,512,256]{2,1,0:T(8,128)}, f32[2,512,256]{2,1,0:T(8,128)S(1)}, u32[]{:S(2)}, u32[]{:S(2)}) collective-permute-start(f32[2,512,256]{2,1,0:T(8,128)} %slice.182), channel_id=1, source_target_pairs={{0,1},{1,0},{2,3},{3,2},{4,5},{5,4},{6,7},{7,6},{8,9},{9,8},{10,11... | collective-permute-start | bytes 3145736 | tf_op jit(solution)/shard_map/ppermute | solution.py:31
  80.4 8.4 %collective-permute-start.6 = (bf16[1,512,256]{2,1,0:T(8,128)(2,1)S(1)}, bf16[1,512,256]{2,1,0:T(8,128)(2,1)S(1)}, u32[]{:S(2)}, u32[]{:S(2)}) collective-permute-start(bf16[1,512,256]{2,1,0:T(8,128)(2,1)S(1)} %slice.270), channel_id=1, source_target_pairs={{0,2},{1,3},{2,0},{3,1},{4,6},{5,7},{6,4},{7,5},{8,10},{9,11},{10,... | collective-permute-start | bytes 786440 | tf_op jit(solution)/shard_map/ppermute | solution.py:31
  89.4 6.2 %collective-permute-start.7 = (bf16[192,512]{1,0:T(8,128)(2,1)S(1)}, bf16[192,512]{1,0:T(8,128)(2,1)S(1)}, u32[]{:S(2)}, u32[]{:S(2)}) collective-permute-start(bf16[192,512]{1,0:T(8,128)(2,1)S(1)} %get-tuple-element.17), channel_id=1, source_target_pairs={{0,4},{4,0},{1,5},{5,1},{2,6},{6,2},{3,7},{7,3},{8,12},{12,8},{9,1... | collective-permute-start | bytes 589832 | tf_op jit(solution)/shard_map/ppermute | solution.py:140
  95.6 0.7 copy-start.8

commit v16 on v15

--- a/solution.py
+++ b/solution.py
@@ -9,7 +9,7 @@
 
 EPSILON = 1e-05
 ROPE_BASE = 500000.0
-CHUNK_EIGHTHS = (6, 2)
+CHUNK_EIGHTHS = (4, 3, 1)
 
 
 def shifted(block, axis, distance):

time: 96.7 us -> 76.9 us (0.80)
  waiting for transfers between devices: 41 us -> 18.2 us
  starting transfers between devices: 16.7 us -> 19 us
  other arithmetic: 5.54 us -> 6.7 us
    ppermute x3 -> x4, waiting for transfers between devices: 25 us -> 1.1 us  [shifted(): return lax.ppermute(block, axis, route)]
    ppermute x3 -> x4, starting transfers between devices: 12 us -> 14.3 us  [shifted(): return lax.ppermute(block, axis, route)]
    ppermute x2, waiting for transfers between devices: 2.05 us -> 3.15 us  [all_sum(): lax.ppermute(value, axis, [(i, i ^ bit) for i in range(size)])]
    unnamed x20 -> x22, local copies, waits for them, and re-layouts: 3.9 us -> 2.87 us
    convert_element_type x2, other arithmetic: 2.02 us -> 3 us  [per_device(): (arrived.astype(jnp.float32) * gain[cols] * scale[:, None]).astype(jnp.bf...]
    slice x2 -> x3, local copies, waits for them, and re-layouts: 2.87 us -> 3.15 us  [per_device(): arrived = shifted(tok_rows[:, cols], 'section', 1)]
  transfers between devices with their start and end apart: 8 -> 9, of which waited for: 5 -> 6; matrix products, arithmetic and copies ran while one was open for 26% -> 38% of each run, Pallas kernels for 0% -> 0%
where the time goes in v16:
time: 76.9 us; the launch traced here: 76.5 us
  starting transfers between devices  19 us (25%)
  local copies, waits for them, and re-layouts  18.9 us (25%)
  waiting for transfers between devices  18.2 us (24%)
  matrix products  11.7 us (15%)
  other arithmetic  6.7 us (9%)
  between operations  1.87 us (2%)
    ppermute x4, starting transfers between devices, shifted(): return lax.ppermute(block, axis, route)  14.3 us
    slice x1, local copies, waits for them, and re-layouts, per_device(): piece = lax.dynamic_slice_in_dim(weight[part], column, block, axis=1)  11.5 us
    dot_general x32, matrix products, per_device(): lax.dot_general(piece, sub, (((0,), (1,)), ((), ())), preferred_element_t...  11.4 us
    ppermute x2, waiting for transfers between devices, scatter_sum(): current = keep + lax.ppermute(send, axis, pairs).astype(jnp.float32)  9.37 us
    ppermute x1, waiting for transfers between devices, per_device(): arrived = lax.ppermute(outgoing, 'dp', pairs)  4.59 us
    ppermute x2, waiting for transfers between devices, all_sum(): lax.ppermute(value, axis, [(i, i ^ bit) for i in range(size)])  3.15 us
    slice x3, local copies, waits for them, and re-layouts, per_device(): arrived = shifted(tok_rows[:, cols], 'section', 1)  3.15 us
    convert_element_type x2, other arithmetic, per_device(): (arrived.astype(jnp.float32) * gain[cols] * scale[:, None]).astype(jnp.bf...  3 us
  transfers between devices with their start and end apart: 9, of which 6 were waited for; matrix products, arithmetic and copies ran while one was open for 38% of the time, Pallas kernels for 0%

profile of v16, /device:TPU:0, one launch (start us, length us, event | category | flops | bytes accessed | tf_op | source)
XLA Modules:
  0.0 76.5 jit_solution(13996506816443958435)
XLA Ops:
  0.0 1.4 %slice.175 = bf16[256,2048]{1,0:T(8,128)(2,1)S(1)} slice(bf16[256,4096]{1,0:T(8,128)(2,1)} %bitcast.215), slice={[0:256], [0:2048]} | slice | bytes 2097152 | tf_op jit(solution)/shard_map/slice | solution.py:103
  1.4 5.9 %collective-permute-start.1 = (bf16[256,2048]{1,0:T(8,128)(2,1)S(1)}, bf16[256,2048]{1,0:T(8,128)(2,1)}, u32[]{:S(2)}, u32[]{:S(2)}) collective-permute-start(bf16[256,2048]{1,0:T(8,128)(2,1)S(1)} %slice.175), channel_id=1, source_target_pairs={{0,8},{8,16},{16,24},{1,9},{9,17},{17,25},{2,10},{10,18},{18,26},{... | collective-permute-start | bytes 3145736 | tf_op jit(solution)/shard_map/ppermute | solution.py:18
  7.4 0.5 multiply_reduce_fusion
  8.6 0.6 reduce-window.6
  10.4 2.5 %collective-permute-start = (f32[3,256]{1,0:T(4,128)S(1)}, f32[3,256]{1,0:T(4,128)S(1)}, u32[]{:S(2)}, u32[]{:S(2)}) collective-permute-start(f32[3,256]{1,0:T(4,128)S(1)} %pad_maximum_fusion.1), channel_id=1, source_target_pairs={{0,8},{8,16},{16,24},{1,9},{9,17},{17,25},{2,10},{10,18},{18,26},{... | collective-permute-start | bytes 9224 | tf_op jit(solution)/shard_map/ppermute | solution.py:18
  12.9 1.0 %slice.181 = bf16[256,1536]{1,0:T(8,128)(2,1)} slice(bf16[256,4096]{1,0:T(8,128)(2,1)S(1)} %bitcast.216), slice={[0:256], [2048:3584]} | slice | bytes 1572864 | tf_op jit(solution)/shard_map/slice | solution.py:103
  13.9 4.4 %collective-permute-start.4 = (bf16[256,1536]{1,0:T(8,128)(2,1)}, bf16[256,1536]{1,0:T(8,128)(2,1)}, u32[]{:S(2)}, u32[]{:S(2)}) collective-permute-start(bf16[256,1536]{1,0:T(8,128)(2,1)} %slice.181), channel_id=1, source_target_pairs={{0,8},{8,16},{16,24},{1,9},{9,17},{17,25},{2,10},{10,18},{18,26},{... | collective-permute-start | bytes 2359304 | tf_op jit(solution)/shard_map/ppermute | solution.py:18
  18.3 0.7 slice.185
  19.0 1.4 %collective-permute-start.5 = (bf16[256,512]{1,0:T(8,128)(2,1)}, bf16[256,512]{1,0:T(8,128)(2,1)S(1)}, u32[]{:S(2)}, u32[]{:S(2)}) collective-permute-start(bf16[256,512]{1,0:T(8,128)(2,1)} %slice.185), channel_id=1, source_target_pairs={{0,8},{8,16},{16,24},{1,9},{9,17},{17,25},{2,10},{10,18},{18,26},{... | collective-permute-start | bytes 786440 | tf_op jit(solution)/shard_map/ppermute | solution.py:18
  20.4 11.5 %fusion.134 = (bf16[1,512,2048]{2,1,0:T(8,128)(2,1)S(1)}, bf16[1,512,2048]{2,1,0:T(8,128)(2,1)}, bf16[1,512,2048]{2,1,0:T(8,128)(2,1)}, bf16[1,512,2048]{2,1,0:T...) fusion(bf16[1,4096,2048]{2,1,0:T(8,128)(2,1)} %param.11), kind=kLoop, calls=%fused_computation.206 | loop fusion | bytes 33554432 | tf_op jit(solution)/shard_map/slice | solution.py:113
  32.1 1.1 %collective-permute-done.2 = f32[256]{0:T(256)S(1)} collective-permute-done((f32[256]{0:T(256)S(1)}, f32[256]{0:T(256)S(1)}, u32[]{:S(2)}, u32[]{:S(2)}) %collective-permute-start.2) | collective-permute-done | bytes 1056 | tf_op jit(solution)/shard_map/ppermute | solution.py:40
  33.2 1.5 %collective-permute-start.3 = (f32[256]{0:T(256)S(1)}, f32[256]{0:T(256)S(1)}, u32[]{:S(2)}, u32[]{:S(2)}) collective-permute-start(f32[256]{0:T(256)S(1)} %add.133), channel_id=1, source_target_pairs={{0,2},{1,3},{2,0},{3,1},{4,6},{5,7},{6,4},{7,5},{8,10},{9,11},{10,... | collective-permute-start | bytes 3080 | tf_op jit(solution)/shard_map/ppermute | solution.py:40
  34.7 2.0 %collective-permute-done.3 = f32[256]{0:T(256)S(1)} collective-permute-done((f32[256]{0:T(256)S(1)}, f32[256]{0:T(256)S(1)}, u32[]{:S(2)}, u32[]{:S(2)}) %collective-permute-start.3) | collective-permute-done | bytes 1056 | tf_op jit(solution)/shard_map/ppermute | solution.py:40
  36.8 1.6 %multiply_convert_fusion = bf16[256,2048]{1,0:T(8,128)(2,1)S(1)} fusion(bf16[256,2048]{1,0:T(8,128)(2,1)} %collective-permute-done.1, f32[256]{0:T(256)S(1)} %add_rsqrt_fusion, f32[2048]{0:T(1024)S(1)} %bitcast.226), kind=kLoop, calls=%fused_computation.8 | loop fusion | flops 2097152 | bytes 2106368 | tf_op jit(solution)/shard_map/convert_element_type | solution.py:106
  41.4 0.5 copy-done.4
  43.3 0.5 copy-done.3
  45.3 0.6 fusion.1
  45.9 1.1 %collective-permute-done.4 = bf16[256,1536]{1,0:T(8,128)(2,1)} collective-permute-done((bf16[256,1536]{1,0:T(8,128)(2,1)}, bf16[256,1536]{1,0:T(8,128)(2,1)}, u32[]{:S(2)}, u32[]{:S(2)}) %collective-permute-start.4) | collective-permute-done | bytes 786464 | tf_op jit(solution)/shard_map/ppermute | solution.py:18
  47.0 1.4 %multiply_convert_fusion.1 = bf16[256,1536]{1,0:T(8,128)(2,1)S(1)} fusion(bf16[256,1536]{1,0:T(8,128)(2,1)} %collective-permute-done.4, f32[256]{0:T(256)S(1)} %add_rsqrt_fusion, f32[1536]{0:T(1024)S(1)} %slice_reduce_fusion), kind=kLoop, calls=%fused_computation.9 | loop fusion | flops 1572864 | bytes 1580032 | tf_op jit(solution)/shard_map/convert_element_type | solution.py:106
  49.8 0.5 copy-done.1
  51.7 0.5 copy-done
  53.7 0.8 %fusion.3 = f32[4,512,256]{2,1,0:T(8,128)S(1)} fusion(f32[4,512,256]{2,1,0:T(8,128)S(1)} %fusion.1, f32[1,512,256]{2,1,0:T(8,128)S(1)} %convolution_bitcast_fusion.12, f32[1,512,256]{2,1,0:T(8,128)S(1)} %convolution_bitcast_fusion.13, f32[1,512,256]{2,1,0:T(8,128)S(1)} %convolution_bitcast_fusion.14, f32[1,512,256]{2,1,0:T(8,128)S(1)} %convolution_bitcast_fusion.15, ...), kind=kLoop, calls=%fused_computation.6 | loop fusion | flops 6291456 | bytes 10485760 | tf_op jit(solution)/shard_map/add | solution.py:120
  54.4 0.4 convolution_bitcast_fusion
  54.9 0.4 convolution_bitcast_fusion.1
  55.3 0.4 convolution_bitcast_fusion.2
  56.4 1.0 %slice.187 = f32[2,512,256]{2,1,0:T(8,128)} slice(f32[4,512,256]{2,1,0:T(8,128)S(1)} %maximum_add_fusion.2), slice={[2:4], [0:512], [0:256]} | slice | bytes 2097152 | tf_op jit(solution)/shard_map/slice | solution.py:27
  57.5 2.9 %collective-permute-done.6 = f32[2,512,256]{2,1,0:T(8,128)S(1)} collective-permute-done((f32[2,512,256]{2,1,0:T(8,128)}, f32[2,512,256]{2,1,0:T(8,128)S(1)}, u32[]{:S(2)}, u32[]{:S(2)}) %collective-permute-start.6) | collective-permute-done | bytes 1048608 | tf_op jit(solution)/shard_map/ppermute | solution.py:31
  60.5 1.6 %collective-permute-start.7 = (bf16[1,512,256]{2,1,0:T(8,128)(2,1)S(1)}, bf16[1,512,256]{2,1,0:T(8,128)(2,1)S(1)}, u32[]{:S(2)}, u32[]{:S(2)}) collective-permute-start(bf16[1,512,256]{2,1,0:T(8,128)(2,1)S(1)} %slice.268), channel_id=1, source_target_pairs={{0,2},{1,3},{2,0},{3,1},{4,6},{5,7},{6,4},{7,5},{8,10},{9,11},{10,... | collective-permute-start | bytes 786440 | tf_op jit(solution)/shard_map/ppermute | solution.py:31
  62.4 6.5 %collective-permute-done.7 = bf16[1,512,256]{2,1,0:T(8,128)(2,1)S(1)} collective-permute-done((bf16[1,512,256]{2,1,0:T(8,128)(2,1)S(1)}, bf16[1,512,256]{2,1,0:T(8,128)(2,1)S(1)}, u32[]{:S(2)}, u32[]{:S(2)}) %collective-permute-start.7) | collective-permute-done | bytes 262176 | tf_op jit(solution)/shard_map/ppermute | solution.py:31
  69.5 1.6 %collective-permute-start.8 = (bf16[192,512]{1,0:T(8,128)(2,1)S(1)}, bf16[192,512]{1,0:T(8,128)(2,1)S(1)}, u32[]{:S(2)}, u32[]{:S(2)}) collective-permute-start(bf16[192,512]{1,0:T(8,128)(2,1)S(1)} %get-tuple-element.21), channel_id=1, source_target_pairs={{0,4},{4,0},{1,5},{5,1},{2,6},{6,2},{3,7},{7,3},{8,12},{12,8},{9,1... | collective-permute-start | bytes 589832 | tf_op jit(solution)/shard_map/ppermute | solution.py:140
  71.1 4.6 %collective-permute-done.8 = bf16[192,512]{1,0:T(8,128)(2,1)S(1)} collective-permute-done((bf16[192,512]{1,0:T(8,128)(2,1)S(1)}, bf16[192,512]{1,0:T(8,128)(2,1)S(1)}, u32[]{:S(2)}, u32[]{:S(2)}) %collective-permute-start.8) | collective-permute-done | bytes 196640 | tf_op jit(solution)/shard_map/ppermute | solution.py:140
  75.7 0.7 copy-done.8
  (83 shorter events, 12.2 us)
Async XLA Ops:
  0.0 7.4 %copy-start.7 = (bf16[1,1,256,4096]{3,2,1,0:T(8,128)(2,1)S(1)}, bf16[1,1,256,4096]{3,2,1,0:T(8,128)(2,1)}, u32[]{:S(2)}) copy-start(bf16[1,1,256,4096]{3,2,1,0:T(8,128)(2,1)} %param.6) | copy-start | bytes 6291460
  0.0 8.6 %copy-start.10 = (s32[1,1,256,1]{2,3,1,0:T(1,128)S(1)}, s32[1,1,256,1]{2,3,1,0:T(1,128)}, u32[]{:S(2)}) copy-start(s32[1,1,256,1]{2,3,1,0:T(1,128)} %param.7) | copy-start | bytes 3076
  1.4 35.3 %collective-permute-start.1 = (bf16[256,2048]{1,0:T(8,128)(2,1)S(1)}, bf16[256,2048]{1,0:T(8,128)(2,1)}, u32[]{:S(2)}, u32[]{:S(2)}) collective-permute-start(bf16[256,2048]{1,0:T(8,128)(2,1)S(1)} %slice.175), channel_id=1, source_target_pairs={{0,8},{8,16},{16,24},{1,9},{9,17},{17,25},{2,10},{10,18},{18,26},{... | collective-permute-start | bytes 3145736 | tf_op jit(solution)/shard_map/ppermute | solution.py:18
  10.4 21.5 %collective-permute-start = (f32[3,256]{1,0:T(4,128)S(1)}, f32[3,256]{1,0:T(4,128)S(1)}, u32[]{:S(2)}, u32[]{:S(2)}) collective-permute-start(f32[3,256]{1,0:T(4,128)S(1)} %pad_maximum_fusion.1), channel_id=1, source_target_pairs={{0,8},{8,16},{16,24},{1,9},{9,17},{17,25},{2,10},{10,18},{18,26},{... | collective-permute-start | bytes 9224 | tf_op jit(solution)/shard_map/ppermute | solution.py:18
  13.9 33.1 %collective-permute-start.4 = (bf16[256,1536]{1,0:T(8,128)(2,1)}, bf16[256,1536]{1,0:T(8,128)(2,1)}, u32[]{:S(2)}, u32[]{:S(2)}) collective-permute-start(bf16[256,1536]{1,0:T(8,128)(2,1)} %slice.181), channel_id=1, source_target_pairs={{0,8},{8,16},{16,24},{1,9},{9,17},{17,25},{2,10},{10,18},{18,26},{... | collective-permute-start | bytes 2359304 | tf_op jit(solution)/shard_map/ppermute | solution.py:18
  19.0 13.0 %copy-start.9 = (f32[1,4096]{1,0:T(1,128)S(1)}, f32[1,4096]{1,0:T(1,128)}, u32[]{:S(2)}) copy-start(f32[1,4096]{1,0:T(1,128)} %param.10) | copy-start | bytes 49156
  19.0 17.8 %slice-start = ((f32[1,4096]{1,0:T(1,128)}), f32[1,2048]{1,0:T(1,128)S(1)}, s32[]{:S(2)}) async-start(f32[1,4096]{1,0:T(1,128)} %param.10), calls=%async_computation | async-start | bytes 16384 | tf_op jit(solution)/shard_map/slice | solution.py:106
  19.0 35.4 %collective-permute-start.5 = (bf16[256,512]{1,0:T(8,128)(2,1)}, bf16[256,512]{1,0:T(8,128)(2,1)S(1)}, u32[]{:S(2)}, u32[]{:S(2)}) collective-permute-start(bf16[256,512]{1,0:T(8,128)(2,1)} %slice.185), channel_id=1, source_target_pairs={{0,8},{8,16},{16,24},{1,9},{9,17},{17,25},{2,10},{10,18},{18,26},{... | collective-permute-start | bytes 786440 | tf_op jit(solution)/shard_map/ppermute | solution.py:18
  32.0 1.2 %collective-permute-start.2 = (f32[256]{0:T(256)S(1)}, f32[256]{0:T(256)S(1)}, u32[]{:S(2)}, u32[]{:S(2)}) collective-permute-start(f32[256]{0:T(256)S(1)} %bitcast.233), channel_id=1, source_target_pairs={{0,1},{1,0},{2,3},{3,2},{4,5},{5,4},{6,7},{7,6},{8,9},{9,8},{10,11... | collective-permute-start | bytes 3080 | tf_op jit(solution)/shard_map/ppermute | solution.py:40
  33.2 3.6 %collective-permute-start.3 = (f32[256]{0:T(256)S(1)}, f32[256]{0:T(256)S(1)}, u32[]{:S(2)}, u32[]{:S(2)}) collective-permute-start(f32[256]{0:T(256)S(1)} %add.133), channel_id=1, source_target_pairs={{0,2},{1,3},{2,0},{3,1},{4,6},{5,7},{6,4},{7,5},{8,10},{9,11},{10,... | collective-permute-start | bytes 3080 | tf_op jit(solution)/shard_map/ppermute | solution.py:40
  34.7 3.7 %copy-start.6 = (bf16[1,512,2048]{2,1,0:T(8,128)(2,1)S(1)}, bf16[1,512,2048]{2,1,0:T(8,128)(2,1)}, u32[]{:S(2)}) copy-start(bf16[1,512,2048]{2,1,0:T(8,128)(2,1)} %get-tuple-element.19) | copy-start | bytes 6291460
  36.8 2.4 %copy-start.5 = (bf16[1,512,2048]{2,1,0:T(8,128)(2,1)S(1)}, bf16[1,512,2048]{2,1,0:T(8,128)(2,1)}, u32[]{:S(2)}) copy-start(bf16[1,512,2048]{2,1,0:T(8,128)(2,1)} %get-tuple-element.18) | copy-start | bytes 6291460
  40.3 1.6 %copy-start.4 = (bf16[1,512,2048]{2,1,0:T(8,128)(2,1)S(1)}, bf16[1,512,2048]{2,1,0:T(8,128)(2,1)}, u32[]{:S(2)}) copy-start(bf16[1,512,2048]{2,1,0:T(8,128)(2,1)} %get-tuple-element.17) | copy-start | bytes 6291460
  42.2 1.6 %copy-start.3 = (bf16[1,512,2048]{2,1,0:T(8,128)(2,1)S(1)}, bf16[1,512,2048]{2,1,0:T(8,128)(2,1)}, u32[]{:S(2)}) copy-start(bf16[1,512,2048]{2,1,0:T(8,128)(2,1)} %get-tuple-element.16) | copy-start | bytes 6291460
  45.3 3.1 %copy-start.2 = (bf16[1,512,2048]{2,1,0:T(8,128)(2,1)S(1)}, bf16[1,512,2048]{2,1,0:T(8,128)(2,1)}, u32[]{:S(2)}) copy-start(bf16[1,512,2048]{2,1,0:T(8,128)(2,1)} %get-tuple-element.15) | copy-start | bytes 6291460
  48.7 1.6 %copy-start.1 = (bf16[1,512,2048]{2,1,0:T(8,128)(2,1)S(1)}, bf16[1,512,2048]{2,1,0:T(8,128)(2,1)}, u32[]{:S(2)}) copy-start(bf16[1,512,2048]{2,1,0:T(8,128)(2,1)} %get-tuple-element.14) | copy-start | bytes 6291460
  50.6 1.6 %copy-start = (bf16[1,512,2048]{2,1,0:T(8,128)(2,1)S(1)}, bf16[1,512,2048]{2,1,0:T(8,128)(2,1)}, u32[]{:S(2)}) copy-start(bf16[1,512,2048]{2,1,0:T(8,128)(2,1)} %get-tuple-element.20) | copy-start | bytes 6291460
  57.5 2.9 %collective-permute-start.6 = (f32[2,512,256]{2,1,0:T(8,128)}, f32[2,512,256]{2,1,0:T(8,128)S(1)}, u32[]{:S(2)}, u32[]{:S(2)}) collective-permute-start(f32[2,512,256]{2,1,0:T(8,128)} %slice.187), channel_id=1, source_target_pairs={{0,1},{1,0},{2,3},{3,2},{4,5},{5,4},{6,7},{7,6},{8,9},{9,8},{10,11... | collective-permute-start | bytes 3145736 | tf_op jit(solution)/shard_map/ppermute | solution.py:31
  60.5 8.4 %collective-permute-start.7 = (bf16[1,512,256]{2,1,0:T(8,128)(2,1)S(1)}, bf16[1,512,256]{2,1,0:T(8,128)(2,1)S(1)}, u32[]{:S(2)}, u32[]{:S(2)}) collective-permute-start(bf16[1,512,256]{2,1,0:T(8,128)(2,1)S(1)} %slice.268), channel_id=1, source_target_pairs={{0,2},{1,3},{2,0},{3,1},{4,6},{5,7},{6,4},{7,5},{8,10},{9,11},{10,... | collective-permute-start | bytes 786440 | tf_op jit(solution)/shard_map/ppermute | solution.py:31
  69.5 6.2 %collective-permute-start.8 = (bf16[192,512]{1,0:T(8,128)(2,1)S(1)}, bf16[192,512]{1,0:T(8,128)(2,1)S(1)}, u32[]{:S(2)}, u32[]{:S(2)}) collective-permute-start(bf16[192,512]{1,0:T(8,128)(2,1)S(1)} %get-tuple-element.21), channel_id=1, source_target_pairs={{0,4},{4,0},{1,5},{5,1},{2,6},{6,2},{3,7},{7,3},{8,12},{12,8},{9,1... | collective-permute-start | bytes 589832 | tf_op jit(solution)/shard_map/ppermute | solution.py:140
  75.7 0.7 copy-start.8

commit v17 on v16

--- a/solution.py
+++ b/solution.py
@@ -9,7 +9,7 @@
 
 EPSILON = 1e-05
 ROPE_BASE = 500000.0
-CHUNK_EIGHTHS = (4, 3, 1)
+CHUNK_EIGHTHS = (5, 2, 1)
 
 
 def shifted(block, axis, distance):

time: 76.9 us -> 80.2 us (1.043)
  waiting for transfers between devices: 18.2 us -> 22.4 us
  other arithmetic: 6.7 us -> 5.71 us
    ppermute x4, waiting for transfers between devices: 1.1 us -> 5.23 us  [shifted(): return lax.ppermute(block, axis, route)]
    convert_element_type x2, other arithmetic: 3 us -> 1.99 us  [per_device(): (arrived.astype(jnp.float32) * gain[cols] * scale[:, None]).astype(jnp.bf...]
  transfers between devices with their start and end apart: 9 -> 9, of which waited for: 6 -> 6; matrix products, arithmetic and copies ran while one was open for 38% -> 34% of each run, Pallas kernels for 0% -> 0%
where the time goes in v17:
time: 80.2 us; the launch traced here: 79.8 us
  waiting for transfers between devices  22.4 us (28%)
  local copies, waits for them, and re-layouts  19.6 us (24%)
  starting transfers between devices  18.6 us (23%)
  matrix products  11.6 us (14%)
  other arithmetic  5.71 us (7%)
  between operations  1.85 us (2%)
    ppermute x4, starting transfers between devices, shifted(): return lax.ppermute(block, axis, route)  14 us
    slice x1, local copies, waits for them, and re-layouts, per_device(): piece = lax.dynamic_slice_in_dim(weight[part], column, block, axis=1)  11.4 us
    dot_general x32, matrix products, per_device(): lax.dot_general(piece, sub, (((0,), (1,)), ((), ())), preferred_element_t...  11.3 us
    ppermute x2, waiting for transfers between devices, scatter_sum(): current = keep + lax.ppermute(send, axis, pairs).astype(jnp.float32)  9.37 us
    ppermute x4, waiting for transfers between devices, shifted(): return lax.ppermute(block, axis, route)  5.23 us
    ppermute x1, waiting for transfers between devices, per_device(): arrived = lax.ppermute(outgoing, 'dp', pairs)  4.61 us
    slice x3, local copies, waits for them, and re-layouts, per_device(): arrived = shifted(tok_rows[:, cols], 'section', 1)  3.41 us
    unnamed x22, local copies, waits for them, and re-layouts  3.32 us
  transfers between devices with their start and end apart: 9, of which 6 were waited for; matrix products, arithmetic and copies ran while one was open for 34% of the time, Pallas kernels for 0%

profile of v17, /device:TPU:0, one launch (start us, length us, event | category | flops | bytes accessed | tf_op | source)
XLA Modules:
  0.0 79.8 jit_solution(17361894233043365418)
XLA Ops:
  0.0 2.7 %slice.175 = bf16[256,2560]{1,0:T(8,128)(2,1)} slice(bf16[256,4096]{1,0:T(8,128)(2,1)} %bitcast.215), slice={[0:256], [0:2560]} | slice | bytes 2621440 | tf_op jit(solution)/shard_map/slice | solution.py:103
  2.7 6.0 %collective-permute-start.1 = (bf16[256,2560]{1,0:T(8,128)(2,1)}, bf16[256,2560]{1,0:T(8,128)(2,1)}, u32[]{:S(2)}, u32[]{:S(2)}) collective-permute-start(bf16[256,2560]{1,0:T(8,128)(2,1)} %slice.175), channel_id=1, source_target_pairs={{0,8},{8,16},{16,24},{1,9},{9,17},{17,25},{2,10},{10,18},{18,26},{... | collective-permute-start | bytes 3932168 | tf_op jit(solution)/shard_map/ppermute | solution.py:18
  8.7 0.5 multiply_reduce_fusion
  9.9 0.6 reduce-window.6
  11.7 2.4 %collective-permute-start = (f32[3,256]{1,0:T(4,128)S(1)}, f32[3,256]{1,0:T(4,128)S(1)}, u32[]{:S(2)}, u32[]{:S(2)}) collective-permute-start(f32[3,256]{1,0:T(4,128)S(1)} %pad_maximum_fusion.1), channel_id=1, source_target_pairs={{0,8},{8,16},{16,24},{1,9},{9,17},{17,25},{2,10},{10,18},{18,26},{... | collective-permute-start | bytes 9224 | tf_op jit(solution)/shard_map/ppermute | solution.py:18
  14.2 3.5 %collective-permute-start.4 = (bf16[256,1024]{1,0:T(8,128)(2,1)S(1)}, bf16[256,1024]{1,0:T(8,128)(2,1)S(1)}, u32[]{:S(2)}, u32[]{:S(2)}) collective-permute-start(bf16[256,1024]{1,0:T(8,128)(2,1)S(1)} %slice.182), channel_id=1, source_target_pairs={{0,8},{8,16},{16,24},{1,9},{9,17},{17,25},{2,10},{10,18},{18,26},{... | collective-permute-start | bytes 1572872 | tf_op jit(solution)/shard_map/ppermute | solution.py:18
  17.7 0.7 slice.185
  18.4 2.0 %collective-permute-start.5 = (bf16[256,512]{1,0:T(8,128)(2,1)}, bf16[256,512]{1,0:T(8,128)(2,1)S(1)}, u32[]{:S(2)}, u32[]{:S(2)}) collective-permute-start(bf16[256,512]{1,0:T(8,128)(2,1)} %slice.185), channel_id=1, source_target_pairs={{0,8},{8,16},{16,24},{1,9},{9,17},{17,25},{2,10},{10,18},{18,26},{... | collective-permute-start | bytes 786440 | tf_op jit(solution)/shard_map/ppermute | solution.py:18
  20.4 11.4 %fusion.134 = (bf16[1,512,2048]{2,1,0:T(8,128)(2,1)S(1)}, bf16[1,512,2048]{2,1,0:T(8,128)(2,1)}, bf16[1,512,2048]{2,1,0:T(8,128)(2,1)}, bf16[1,512,2048]{2,1,0:T...) fusion(bf16[1,4096,2048]{2,1,0:T(8,128)(2,1)} %param.11), kind=kLoop, calls=%fused_computation.206 | loop fusion | bytes 33554432 | tf_op jit(solution)/shard_map/slice | solution.py:113
  31.9 5.2 %collective-permute-done = f32[3,256]{1,0:T(4,128)S(1)} collective-permute-done((f32[3,256]{1,0:T(4,128)S(1)}, f32[3,256]{1,0:T(4,128)S(1)}, u32[]{:S(2)}, u32[]{:S(2)}) %collective-permute-start) | collective-permute-done | bytes 3104 | tf_op jit(solution)/shard_map/ppermute | solution.py:18
  37.1 1.1 %collective-permute-done.2 = f32[256]{0:T(256)S(1)} collective-permute-done((f32[256]{0:T(256)S(1)}, f32[256]{0:T(256)S(1)}, u32[]{:S(2)}, u32[]{:S(2)}) %collective-permute-start.2) | collective-permute-done | bytes 1056 | tf_op jit(solution)/shard_map/ppermute | solution.py:40
  38.3 1.5 %collective-permute-start.3 = (f32[256]{0:T(256)S(1)}, f32[256]{0:T(256)S(1)}, u32[]{:S(2)}, u32[]{:S(2)}) collective-permute-start(f32[256]{0:T(256)S(1)} %add.133), channel_id=1, source_target_pairs={{0,2},{1,3},{2,0},{3,1},{4,6},{5,7},{6,4},{7,5},{8,10},{9,11},{10,... | collective-permute-start | bytes 3080 | tf_op jit(solution)/shard_map/ppermute | solution.py:40
  39.8 2.0 %collective-permute-done.3 = f32[256]{0:T(256)S(1)} collective-permute-done((f32[256]{0:T(256)S(1)}, f32[256]{0:T(256)S(1)}, u32[]{:S(2)}, u32[]{:S(2)}) %collective-permute-start.3) | collective-permute-done | bytes 1056 | tf_op jit(solution)/shard_map/ppermute | solution.py:40
  41.8 1.8 %multiply_convert_fusion = bf16[256,2560]{1,0:T(8,128)(2,1)S(1)} fusion(bf16[256,2560]{1,0:T(8,128)(2,1)} %collective-permute-done.1, f32[256]{0:T(256)S(1)} %add_rsqrt_fusion, f32[2560]{0:T(1024)S(1)} %slice_reduce_fusion), kind=kLoop, calls=%fused_computation.1 | loop fusion | flops 2621440 | bytes 2632704 | tf_op jit(solution)/shard_map/convert_element_type | solution.py:106
  46.5 0.5 copy-done.4
  48.4 0.5 copy-done.3
  50.4 0.5 copy-done.2
  52.3 0.9 %fusion.2 = f32[4,512,256]{2,1,0:T(8,128)S(1)} fusion(f32[1,512,256]{2,1,0:T(8,128)S(1)} %convolution_bitcast_fusion.28, f32[1,512,256]{2,1,0:T(8,128)S(1)} %convolution_bitcast_fusion.29, f32[1,512,256]{2,1,0:T(8,128)S(1)} %convolution_bitcast_fusion.30, f32[1,512,256]{2,1,0:T(8,128)S(1)} %convolution_bitcast_fusion.31, ...), kind=kLoop, calls=%fused_computation.5 | loop fusion | flops 9961472 | bytes 12582912 | tf_op jit(solution)/shard_map/add | solution.py:120
  53.4 0.5 copy-done.1
  55.3 0.5 copy-done
  57.3 0.4 fusion.3
  57.7 0.4 convolution_bitcast_fusion
  58.1 0.4 convolution_bitcast_fusion.1
  58.6 0.4 convolution_bitcast_fusion.2
  59.0 0.4 convolution_bitcast_fusion.3
  59.8 1.0 %slice.187 = f32[2,512,256]{2,1,0:T(8,128)} slice(f32[4,512,256]{2,1,0:T(8,128)S(1)} %maximum_add_fusion.2), slice={[2:4], [0:512], [0:256]} | slice | bytes 2097152 | tf_op jit(solution)/shard_map/slice | solution.py:27
  60.8 2.9 %collective-permute-done.6 = f32[2,512,256]{2,1,0:T(8,128)S(1)} collective-permute-done((f32[2,512,256]{2,1,0:T(8,128)}, f32[2,512,256]{2,1,0:T(8,128)S(1)}, u32[]{:S(2)}, u32[]{:S(2)}) %collective-permute-start.6) | collective-permute-done | bytes 1048608 | tf_op jit(solution)/shard_map/ppermute | solution.py:31
  63.8 1.6 %collective-permute-start.7 = (bf16[1,512,256]{2,1,0:T(8,128)(2,1)S(1)}, bf16[1,512,256]{2,1,0:T(8,128)(2,1)S(1)}, u32[]{:S(2)}, u32[]{:S(2)}) collective-permute-start(bf16[1,512,256]{2,1,0:T(8,128)(2,1)S(1)} %slice.268), channel_id=1, source_target_pairs={{0,2},{1,3},{2,0},{3,1},{4,6},{5,7},{6,4},{7,5},{8,10},{9,11},{10,... | collective-permute-start | bytes 786440 | tf_op jit(solution)/shard_map/ppermute | solution.py:31
  65.7 6.5 %collective-permute-done.7 = bf16[1,512,256]{2,1,0:T(8,128)(2,1)S(1)} collective-permute-done((bf16[1,512,256]{2,1,0:T(8,128)(2,1)S(1)}, bf16[1,512,256]{2,1,0:T(8,128)(2,1)S(1)}, u32[]{:S(2)}, u32[]{:S(2)}) %collective-permute-start.7) | collective-permute-done | bytes 262176 | tf_op jit(solution)/shard_map/ppermute | solution.py:31
  72.9 1.5 %collective-permute-start.8 = (bf16[192,512]{1,0:T(8,128)(2,1)S(1)}, bf16[192,512]{1,0:T(8,128)(2,1)S(1)}, u32[]{:S(2)}, u32[]{:S(2)}) collective-permute-start(bf16[192,512]{1,0:T(8,128)(2,1)S(1)} %get-tuple-element.21), channel_id=1, source_target_pairs={{0,4},{4,0},{1,5},{5,1},{2,6},{6,2},{3,7},{7,3},{8,12},{12,8},{9,1... | collective-permute-start | bytes 589832 | tf_op jit(solution)/shard_map/ppermute | solution.py:140
  74.4 4.6 %collective-permute-done.8 = bf16[192,512]{1,0:T(8,128)(2,1)S(1)} collective-permute-done((bf16[192,512]{1,0:T(8,128)(2,1)S(1)}, bf16[192,512]{1,0:T(8,128)(2,1)S(1)}, u32[]{:S(2)}, u32[]{:S(2)}) %collective-permute-start.8) | collective-permute-done | bytes 196640 | tf_op jit(solution)/shard_map/ppermute | solution.py:140
  79.0 0.7 copy-done.8
  (83 shorter events, 11.9 us)
Async XLA Ops:
  0.0 8.7 %copy-start.7 = (bf16[1,1,256,4096]{3,2,1,0:T(8,128)(2,1)S(1)}, bf16[1,1,256,4096]{3,2,1,0:T(8,128)(2,1)}, u32[]{:S(2)}) copy-start(bf16[1,1,256,4096]{3,2,1,0:T(8,128)(2,1)} %param.6) | copy-start | bytes 6291460
  0.0 9.8 %copy-start.10 = (s32[1,1,256,1]{2,3,1,0:T(1,128)S(1)}, s32[1,1,256,1]{2,3,1,0:T(1,128)}, u32[]{:S(2)}) copy-start(s32[1,1,256,1]{2,3,1,0:T(1,128)} %param.7) | copy-start | bytes 3076
  2.7 39.2 %collective-permute-start.1 = (bf16[256,2560]{1,0:T(8,128)(2,1)}, bf16[256,2560]{1,0:T(8,128)(2,1)}, u32[]{:S(2)}, u32[]{:S(2)}) collective-permute-start(bf16[256,2560]{1,0:T(8,128)(2,1)} %slice.175), channel_id=1, source_target_pairs={{0,8},{8,16},{16,24},{1,9},{9,17},{17,25},{2,10},{10,18},{18,26},{... | collective-permute-start | bytes 3932168 | tf_op jit(solution)/shard_map/ppermute | solution.py:18
  11.7 25.4 %collective-permute-start = (f32[3,256]{1,0:T(4,128)S(1)}, f32[3,256]{1,0:T(4,128)S(1)}, u32[]{:S(2)}, u32[]{:S(2)}) collective-permute-start(f32[3,256]{1,0:T(4,128)S(1)} %pad_maximum_fusion.1), channel_id=1, source_target_pairs={{0,8},{8,16},{16,24},{1,9},{9,17},{17,25},{2,10},{10,18},{18,26},{... | collective-permute-start | bytes 9224 | tf_op jit(solution)/shard_map/ppermute | solution.py:18
  14.2 39.1 %collective-permute-start.4 = (bf16[256,1024]{1,0:T(8,128)(2,1)S(1)}, bf16[256,1024]{1,0:T(8,128)(2,1)S(1)}, u32[]{:S(2)}, u32[]{:S(2)}) collective-permute-start(bf16[256,1024]{1,0:T(8,128)(2,1)S(1)} %slice.182), channel_id=1, source_target_pairs={{0,8},{8,16},{16,24},{1,9},{9,17},{17,25},{2,10},{10,18},{18,26},{... | collective-permute-start | bytes 1572872 | tf_op jit(solution)/shard_map/ppermute | solution.py:18
  18.4 18.7 %copy-start.9 = (f32[1,4096]{1,0:T(1,128)S(1)}, f32[1,4096]{1,0:T(1,128)}, u32[]{:S(2)}) copy-start(f32[1,4096]{1,0:T(1,128)} %param.10) | copy-start | bytes 49156
  18.4 39.3 %collective-permute-start.5 = (bf16[256,512]{1,0:T(8,128)(2,1)}, bf16[256,512]{1,0:T(8,128)(2,1)S(1)}, u32[]{:S(2)}, u32[]{:S(2)}) collective-permute-start(bf16[256,512]{1,0:T(8,128)(2,1)} %slice.185), channel_id=1, source_target_pairs={{0,8},{8,16},{16,24},{1,9},{9,17},{17,25},{2,10},{10,18},{18,26},{... | collective-permute-start | bytes 786440 | tf_op jit(solution)/shard_map/ppermute | solution.py:18
  37.1 1.2 %collective-permute-start.2 = (f32[256]{0:T(256)S(1)}, f32[256]{0:T(256)S(1)}, u32[]{:S(2)}, u32[]{:S(2)}) collective-permute-start(f32[256]{0:T(256)S(1)} %bitcast.233), channel_id=1, source_target_pairs={{0,1},{1,0},{2,3},{3,2},{4,5},{5,4},{6,7},{7,6},{8,9},{9,8},{10,11... | collective-permute-start | bytes 3080 | tf_op jit(solution)/shard_map/ppermute | solution.py:40
  38.3 3.6 %collective-permute-start.3 = (f32[256]{0:T(256)S(1)}, f32[256]{0:T(256)S(1)}, u32[]{:S(2)}, u32[]{:S(2)}) collective-permute-start(f32[256]{0:T(256)S(1)} %add.133), channel_id=1, source_target_pairs={{0,2},{1,3},{2,0},{3,1},{4,6},{5,7},{6,4},{7,5},{8,10},{9,11},{10,... | collective-permute-start | bytes 3080 | tf_op jit(solution)/shard_map/ppermute | solution.py:40
  39.8 3.9 %copy-start.6 = (bf16[1,512,2048]{2,1,0:T(8,128)(2,1)S(1)}, bf16[1,512,2048]{2,1,0:T(8,128)(2,1)}, u32[]{:S(2)}) copy-start(bf16[1,512,2048]{2,1,0:T(8,128)(2,1)} %get-tuple-element.19) | copy-start | bytes 6291460
  41.8 2.5 %copy-start.5 = (bf16[1,512,2048]{2,1,0:T(8,128)(2,1)S(1)}, bf16[1,512,2048]{2,1,0:T(8,128)(2,1)}, u32[]{:S(2)}) copy-start(bf16[1,512,2048]{2,1,0:T(8,128)(2,1)} %get-tuple-element.18) | copy-start | bytes 6291460
  45.4 1.6 %copy-start.4 = (bf16[1,512,2048]{2,1,0:T(8,128)(2,1)S(1)}, bf16[1,512,2048]{2,1,0:T(8,128)(2,1)}, u32[]{:S(2)}) copy-start(bf16[1,512,2048]{2,1,0:T(8,128)(2,1)} %get-tuple-element.17) | copy-start | bytes 6291460
  47.4 1.6 %copy-start.3 = (bf16[1,512,2048]{2,1,0:T(8,128)(2,1)S(1)}, bf16[1,512,2048]{2,1,0:T(8,128)(2,1)}, u32[]{:S(2)}) copy-start(bf16[1,512,2048]{2,1,0:T(8,128)(2,1)} %get-tuple-element.16) | copy-start | bytes 6291460
  49.3 1.6 %copy-start.2 = (bf16[1,512,2048]{2,1,0:T(8,128)(2,1)S(1)}, bf16[1,512,2048]{2,1,0:T(8,128)(2,1)}, u32[]{:S(2)}) copy-start(bf16[1,512,2048]{2,1,0:T(8,128)(2,1)} %get-tuple-element.15) | copy-start | bytes 6291460
  52.3 1.0 %slice-start = ((f32[1,4096]{1,0:T(1,128)}), f32[1,1024]{1,0:T(1,128)S(1)}, s32[]{:S(2)}) async-start(f32[1,4096]{1,0:T(1,128)} %param.10), calls=%async_computation | async-start | bytes 8192 | tf_op jit(solution)/shard_map/slice | solution.py:106
  52.3 1.6 %copy-start.1 = (bf16[1,512,2048]{2,1,0:T(8,128)(2,1)S(1)}, bf16[1,512,2048]{2,1,0:T(8,128)(2,1)}, u32[]{:S(2)}) copy-start(bf16[1,512,2048]{2,1,0:T(8,128)(2,1)} %get-tuple-element.14) | copy-start | bytes 6291460
  54.2 1.6 %copy-start = (bf16[1,512,2048]{2,1,0:T(8,128)(2,1)S(1)}, bf16[1,512,2048]{2,1,0:T(8,128)(2,1)}, u32[]{:S(2)}) copy-start(bf16[1,512,2048]{2,1,0:T(8,128)(2,1)} %get-tuple-element.20) | copy-start | bytes 6291460
  60.8 2.9 %collective-permute-start.6 = (f32[2,512,256]{2,1,0:T(8,128)}, f32[2,512,256]{2,1,0:T(8,128)S(1)}, u32[]{:S(2)}, u32[]{:S(2)}) collective-permute-start(f32[2,512,256]{2,1,0:T(8,128)} %slice.187), channel_id=1, source_target_pairs={{0,1},{1,0},{2,3},{3,2},{4,5},{5,4},{6,7},{7,6},{8,9},{9,8},{10,11... | collective-permute-start | bytes 3145736 | tf_op jit(solution)/shard_map/ppermute | solution.py:31
  63.8 8.4 %collective-permute-start.7 = (bf16[1,512,256]{2,1,0:T(8,128)(2,1)S(1)}, bf16[1,512,256]{2,1,0:T(8,128)(2,1)S(1)}, u32[]{:S(2)}, u32[]{:S(2)}) collective-permute-start(bf16[1,512,256]{2,1,0:T(8,128)(2,1)S(1)} %slice.268), channel_id=1, source_target_pairs={{0,2},{1,3},{2,0},{3,1},{4,6},{5,7},{6,4},{7,5},{8,10},{9,11},{10,... | collective-permute-start | bytes 786440 | tf_op jit(solution)/shard_map/ppermute | solution.py:31
  72.9 6.2 %collective-permute-start.8 = (bf16[192,512]{1,0:T(8,128)(2,1)S(1)}, bf16[192,512]{1,0:T(8,128)(2,1)S(1)}, u32[]{:S(2)}, u32[]{:S(2)}) collective-permute-start(bf16[192,512]{1,0:T(8,128)(2,1)S(1)} %get-tuple-element.21), channel_id=1, source_target_pairs={{0,4},{4,0},{1,5},{5,1},{2,6},{6,2},{3,7},{7,3},{8,12},{12,8},{9,1... | collective-permute-start | bytes 589832 | tf_op jit(solution)/shard_map/ppermute | solution.py:140
  79.0 0.7 copy-start.8

commit v18 on v17

--- a/solution.py
+++ b/solution.py
@@ -9,7 +9,7 @@
 
 EPSILON = 1e-05
 ROPE_BASE = 500000.0
-CHUNK_EIGHTHS = (5, 2, 1)
+CHUNK_EIGHTHS = (4, 2, 2)
 
 
 def shifted(block, axis, distance):

time: 80.2 us -> 76.4 us (0.953)
  waiting for transfers between devices: 22.4 us -> 17.4 us
  other arithmetic: 5.71 us -> 7.74 us
  local copies, waits for them, and re-layouts: 19.6 us -> 17.7 us
  starting transfers between devices: 18.6 us -> 19.7 us
    ppermute x4, waiting for transfers between devices: 5.23 us -> 0.28 us  [shifted(): return lax.ppermute(block, axis, route)]
    convert_element_type x2 -> x3, other arithmetic: 1.99 us -> 4.02 us  [per_device(): (arrived.astype(jnp.float32) * gain[cols] * scale[:, None]).astype(jnp.bf...]
    unnamed x22, local copies, waits for them, and re-layouts: 3.32 us -> 2.31 us
    ppermute x4, starting transfers between devices: 14 us -> 15 us  [shifted(): return lax.ppermute(block, axis, route)]
    slice x3 -> x2, local copies, waits for them, and re-layouts: 3.41 us -> 2.51 us  [per_device(): arrived = shifted(tok_rows[:, cols], 'section', 1)]
  transfers between devices with their start and end apart: 9 -> 9, of which waited for: 6 -> 6; matrix products, arithmetic and copies ran while one was open for 34% -> 36% of each run, Pallas kernels for 0% -> 0%
where the time goes in v18:
time: 76.4 us; the launch traced here: 76 us
  starting transfers between devices  19.7 us (26%)
  local copies, waits for them, and re-layouts  17.7 us (23%)
  waiting for transfers between devices  17.4 us (23%)
  matrix products  11.6 us (15%)
  other arithmetic  7.74 us (10%)
  between operations  1.87 us (2%)
    ppermute x4, starting transfers between devices, shifted(): return lax.ppermute(block, axis, route)  15 us
    slice x1, local copies, waits for them, and re-layouts, per_device(): piece = lax.dynamic_slice_in_dim(weight[part], column, block, axis=1)  11.5 us
    dot_general x32, matrix products, per_device(): lax.dot_general(piece, sub, (((0,), (1,)), ((), ())), preferred_element_t...  11.3 us
    ppermute x2, waiting for transfers between devices, scatter_sum(): current = keep + lax.ppermute(send, axis, pairs).astype(jnp.float32)  9.37 us
    ppermute x1, waiting for transfers between devices, per_device(): arrived = lax.ppermute(outgoing, 'dp', pairs)  4.6 us
    convert_element_type x3, other arithmetic, per_device(): (arrived.astype(jnp.float32) * gain[cols] * scale[:, None]).astype(jnp.bf...  4.02 us
    ppermute x2, waiting for transfers between devices, all_sum(): lax.ppermute(value, axis, [(i, i ^ bit) for i in range(size)])  3.17 us
    slice x2, local copies, waits for them, and re-layouts, per_device(): arrived = shifted(tok_rows[:, cols], 'section', 1)  2.51 us
  transfers between devices with their start and end apart: 9, of which 6 were waited for; matrix products, arithmetic and copies ran while one was open for 36% of the time, Pallas kernels for 0%

profile of v18, /device:TPU:0, one launch (start us, length us, event | category | flops | bytes accessed | tf_op | source)
XLA Modules:
  0.0 76.0 jit_solution(2676141581682937300)
XLA Ops:
  0.0 1.4 %slice.179 = bf16[256,2048]{1,0:T(8,128)(2,1)S(1)} slice(bf16[256,4096]{1,0:T(8,128)(2,1)} %bitcast.216), slice={[0:256], [0:2048]} | slice | bytes 2097152 | tf_op jit(solution)/shard_map/slice | solution.py:103
  1.4 6.0 %collective-permute-start.1 = (bf16[256,2048]{1,0:T(8,128)(2,1)S(1)}, bf16[256,2048]{1,0:T(8,128)(2,1)}, u32[]{:S(2)}, u32[]{:S(2)}) collective-permute-start(bf16[256,2048]{1,0:T(8,128)(2,1)S(1)} %slice.179), channel_id=1, source_target_pairs={{0,8},{8,16},{16,24},{1,9},{9,17},{17,25},{2,10},{10,18},{18,26},{... | collective-permute-start | bytes 3145736 | tf_op jit(solution)/shard_map/ppermute | solution.py:18
  7.4 0.5 multiply_reduce_fusion
  8.6 0.6 reduce-window.6
  10.4 2.5 %collective-permute-start = (f32[3,256]{1,0:T(4,128)S(1)}, f32[3,256]{1,0:T(4,128)S(1)}, u32[]{:S(2)}, u32[]{:S(2)}) collective-permute-start(f32[3,256]{1,0:T(4,128)S(1)} %pad_maximum_fusion.1), channel_id=1, source_target_pairs={{0,8},{8,16},{16,24},{1,9},{9,17},{17,25},{2,10},{10,18},{18,26},{... | collective-permute-start | bytes 9224 | tf_op jit(solution)/shard_map/ppermute | solution.py:18
  12.9 1.1 %fusion.139 = (bf16[256,1024]{1,0:T(8,128)(2,1)}, bf16[256,1024]{1,0:T(8,128)(2,1)}) fusion(bf16[256,4096]{1,0:T(8,128)(2,1)S(1)} %bitcast.217), kind=kLoop, calls=%fused_computation.210 | loop fusion | bytes 2097152 | tf_op jit(solution)/shard_map/slice | solution.py:103
  14.0 4.3 %collective-permute-start.4 = (bf16[256,1024]{1,0:T(8,128)(2,1)}, bf16[256,1024]{1,0:T(8,128)(2,1)}, u32[]{:S(2)}, u32[]{:S(2)}) collective-permute-start(bf16[256,1024]{1,0:T(8,128)(2,1)} %get-tuple-element.22), channel_id=1, source_target_pairs={{0,8},{8,16},{16,24},{1,9},{9,17},{17,25},{2,10},{10,18},{18,26},{... | collective-permute-start | bytes 1572872 | tf_op jit(solution)/shard_map/ppermute | solution.py:18
  18.3 2.2 %collective-permute-start.5 = (bf16[256,1024]{1,0:T(8,128)(2,1)}, bf16[256,1024]{1,0:T(8,128)(2,1)}, u32[]{:S(2)}, u32[]{:S(2)}) collective-permute-start(bf16[256,1024]{1,0:T(8,128)(2,1)} %get-tuple-element.21), channel_id=1, source_target_pairs={{0,8},{8,16},{16,24},{1,9},{9,17},{17,25},{2,10},{10,18},{18,26},{... | collective-permute-start | bytes 1572872 | tf_op jit(solution)/shard_map/ppermute | solution.py:18
  20.5 11.5 %fusion.138 = (bf16[1,512,2048]{2,1,0:T(8,128)(2,1)S(1)}, bf16[1,512,2048]{2,1,0:T(8,128)(2,1)}, bf16[1,512,2048]{2,1,0:T(8,128)(2,1)}, bf16[1,512,2048]{2,1,0:T...) fusion(bf16[1,4096,2048]{2,1,0:T(8,128)(2,1)} %param.11), kind=kLoop, calls=%fused_computation.209 | loop fusion | bytes 33554432 | tf_op jit(solution)/shard_map/slice | solution.py:113
  32.1 1.1 %collective-permute-done.2 = f32[256]{0:T(256)S(1)} collective-permute-done((f32[256]{0:T(256)S(1)}, f32[256]{0:T(256)S(1)}, u32[]{:S(2)}, u32[]{:S(2)}) %collective-permute-start.2) | collective-permute-done | bytes 1056 | tf_op jit(solution)/shard_map/ppermute | solution.py:40
  33.2 1.5 %collective-permute-start.3 = (f32[256]{0:T(256)S(1)}, f32[256]{0:T(256)S(1)}, u32[]{:S(2)}, u32[]{:S(2)}) collective-permute-start(f32[256]{0:T(256)S(1)} %add.133), channel_id=1, source_target_pairs={{0,2},{1,3},{2,0},{3,1},{4,6},{5,7},{6,4},{7,5},{8,10},{9,11},{10,... | collective-permute-start | bytes 3080 | tf_op jit(solution)/shard_map/ppermute | solution.py:40
  34.8 2.1 %collective-permute-done.3 = f32[256]{0:T(256)S(1)} collective-permute-done((f32[256]{0:T(256)S(1)}, f32[256]{0:T(256)S(1)}, u32[]{:S(2)}, u32[]{:S(2)}) %collective-permute-start.3) | collective-permute-done | bytes 1056 | tf_op jit(solution)/shard_map/ppermute | solution.py:40
  36.9 1.6 %multiply_convert_fusion = bf16[256,2048]{1,0:T(8,128)(2,1)S(1)} fusion(bf16[256,2048]{1,0:T(8,128)(2,1)} %collective-permute-done.1, f32[256]{0:T(256)S(1)} %add_rsqrt_fusion, f32[2048]{0:T(1024)S(1)} %bitcast.222), kind=kLoop, calls=%fused_computation.8 | loop fusion | flops 2097152 | bytes 2106368 | tf_op jit(solution)/shard_map/convert_element_type | solution.py:106
  39.2 0.4 convolution_bitcast_fusion.24
  41.4 0.5 copy-done.4
  43.4 0.5 copy-done.3
  44.6 0.4 convolution_bitcast_fusion.18
  44.9 0.4 convolution_bitcast_fusion.19
  45.3 0.8 %fusion.1 = f32[4,512,256]{2,1,0:T(8,128)S(1)} fusion(f32[1,512,256]{2,1,0:T(8,128)S(1)} %convolution_bitcast_fusion.28, f32[1,512,256]{2,1,0:T(8,128)S(1)} %convolution_bitcast_fusion.29, f32[1,512,256]{2,1,0:T(8,128)S(1)} %convolution_bitcast_fusion.30, f32[1,512,256]{2,1,0:T(8,128)S(1)} %convolution_bitcast_fusion.31, ...), kind=kLoop, calls=%fused_computation.3 | loop fusion | flops 7864320 | bytes 10485760 | tf_op jit(solution)/shard_map/add | solution.py:120
  46.2 1.2 %multiply_convert_fusion.2 = bf16[256,1024]{1,0:T(8,128)(2,1)S(1)} fusion(bf16[256,1024]{1,0:T(8,128)(2,1)} %collective-permute-done.4, f32[256]{0:T(256)S(1)} %add_rsqrt_fusion, f32[1024]{0:T(1024)S(1)} %bitcast.224), kind=kLoop, calls=%fused_computation.44 | loop fusion | flops 1048576 | bytes 1053696 | tf_op jit(solution)/shard_map/convert_element_type | solution.py:106
  48.8 0.5 copy-done.1
  49.7 0.4 convolution_bitcast_fusion.9
  50.8 0.4 fusion.2
  51.5 1.2 %multiply_convert_fusion.1 = bf16[256,1024]{1,0:T(8,128)(2,1)S(1)} fusion(bf16[256,1024]{1,0:T(8,128)(2,1)} %collective-permute-done.5, f32[1024]{0:T(1024)S(1)} %bitcast.223, f32[256]{0:T(256)S(1)} %add_rsqrt_fusion), kind=kLoop, calls=%fused_computation.43 | loop fusion | flops 1048576 | bytes 1053696 | tf_op jit(solution)/shard_map/convert_element_type | solution.py:106
  55.6 0.4 fusion.3
  56.0 1.0 %slice.192 = f32[2,512,256]{2,1,0:T(8,128)} slice(f32[4,512,256]{2,1,0:T(8,128)S(1)} %fusion.3), slice={[2:4], [0:512], [0:256]} | slice | bytes 2097152 | tf_op jit(solution)/shard_map/slice | solution.py:27
  57.0 2.9 %collective-permute-done.6 = f32[2,512,256]{2,1,0:T(8,128)S(1)} collective-permute-done((f32[2,512,256]{2,1,0:T(8,128)}, f32[2,512,256]{2,1,0:T(8,128)S(1)}, u32[]{:S(2)}, u32[]{:S(2)}) %collective-permute-start.6) | collective-permute-done | bytes 1048608 | tf_op jit(solution)/shard_map/ppermute | solution.py:31
  60.1 1.6 %collective-permute-start.7 = (bf16[1,512,256]{2,1,0:T(8,128)(2,1)S(1)}, bf16[1,512,256]{2,1,0:T(8,128)(2,1)S(1)}, u32[]{:S(2)}, u32[]{:S(2)}) collective-permute-start(bf16[1,512,256]{2,1,0:T(8,128)(2,1)S(1)} %slice.280), channel_id=1, source_target_pairs={{0,2},{1,3},{2,0},{3,1},{4,6},{5,7},{6,4},{7,5},{8,10},{9,11},{10,... | collective-permute-start | bytes 786440 | tf_op jit(solution)/shard_map/ppermute | solution.py:31
  62.0 6.5 %collective-permute-done.7 = bf16[1,512,256]{2,1,0:T(8,128)(2,1)S(1)} collective-permute-done((bf16[1,512,256]{2,1,0:T(8,128)(2,1)S(1)}, bf16[1,512,256]{2,1,0:T(8,128)(2,1)S(1)}, u32[]{:S(2)}, u32[]{:S(2)}) %collective-permute-start.7) | collective-permute-done | bytes 262176 | tf_op jit(solution)/shard_map/ppermute | solution.py:31
  69.1 1.6 %collective-permute-start.8 = (bf16[192,512]{1,0:T(8,128)(2,1)S(1)}, bf16[192,512]{1,0:T(8,128)(2,1)S(1)}, u32[]{:S(2)}, u32[]{:S(2)}) collective-permute-start(bf16[192,512]{1,0:T(8,128)(2,1)S(1)} %get-tuple-element.23), channel_id=1, source_target_pairs={{0,4},{4,0},{1,5},{5,1},{2,6},{6,2},{3,7},{7,3},{8,12},{12,8},{9,1... | collective-permute-start | bytes 589832 | tf_op jit(solution)/shard_map/ppermute | solution.py:140
  70.6 4.6 %collective-permute-done.8 = bf16[192,512]{1,0:T(8,128)(2,1)S(1)} collective-permute-done((bf16[192,512]{1,0:T(8,128)(2,1)S(1)}, bf16[192,512]{1,0:T(8,128)(2,1)S(1)}, u32[]{:S(2)}, u32[]{:S(2)}) %collective-permute-start.8) | collective-permute-done | bytes 196640 | tf_op jit(solution)/shard_map/ppermute | solution.py:140
  75.3 0.7 copy-done.8
  (82 shorter events, 11.8 us)
Async XLA Ops:
  0.0 7.4 %copy-start.7 = (bf16[1,1,256,4096]{3,2,1,0:T(8,128)(2,1)S(1)}, bf16[1,1,256,4096]{3,2,1,0:T(8,128)(2,1)}, u32[]{:S(2)}) copy-start(bf16[1,1,256,4096]{3,2,1,0:T(8,128)(2,1)} %param.6) | copy-start | bytes 6291460
  0.0 8.6 %copy-start.10 = (s32[1,1,256,1]{2,3,1,0:T(1,128)S(1)}, s32[1,1,256,1]{2,3,1,0:T(1,128)}, u32[]{:S(2)}) copy-start(s32[1,1,256,1]{2,3,1,0:T(1,128)} %param.7) | copy-start | bytes 3076
  1.4 35.4 %collective-permute-start.1 = (bf16[256,2048]{1,0:T(8,128)(2,1)S(1)}, bf16[256,2048]{1,0:T(8,128)(2,1)}, u32[]{:S(2)}, u32[]{:S(2)}) collective-permute-start(bf16[256,2048]{1,0:T(8,128)(2,1)S(1)} %slice.179), channel_id=1, source_target_pairs={{0,8},{8,16},{16,24},{1,9},{9,17},{17,25},{2,10},{10,18},{18,26},{... | collective-permute-start | bytes 3145736 | tf_op jit(solution)/shard_map/ppermute | solution.py:18
  10.4 21.6 %collective-permute-start = (f32[3,256]{1,0:T(4,128)S(1)}, f32[3,256]{1,0:T(4,128)S(1)}, u32[]{:S(2)}, u32[]{:S(2)}) collective-permute-start(f32[3,256]{1,0:T(4,128)S(1)} %pad_maximum_fusion.1), channel_id=1, source_target_pairs={{0,8},{8,16},{16,24},{1,9},{9,17},{17,25},{2,10},{10,18},{18,26},{... | collective-permute-start | bytes 9224 | tf_op jit(solution)/shard_map/ppermute | solution.py:18
  14.0 32.2 %collective-permute-start.4 = (bf16[256,1024]{1,0:T(8,128)(2,1)}, bf16[256,1024]{1,0:T(8,128)(2,1)}, u32[]{:S(2)}, u32[]{:S(2)}) collective-permute-start(bf16[256,1024]{1,0:T(8,128)(2,1)} %get-tuple-element.22), channel_id=1, source_target_pairs={{0,8},{8,16},{16,24},{1,9},{9,17},{17,25},{2,10},{10,18},{18,26},{... | collective-permute-start | bytes 1572872 | tf_op jit(solution)/shard_map/ppermute | solution.py:18
  18.3 13.8 %copy-start.9 = (f32[1,4096]{1,0:T(1,128)S(1)}, f32[1,4096]{1,0:T(1,128)}, u32[]{:S(2)}) copy-start(f32[1,4096]{1,0:T(1,128)} %param.10) | copy-start | bytes 49156
  18.3 18.6 %slice-start = ((f32[1,4096]{1,0:T(1,128)}), f32[1,2048]{1,0:T(1,128)S(1)}, s32[]{:S(2)}) async-start(f32[1,4096]{1,0:T(1,128)} %param.10), calls=%async_computation | async-start | bytes 16384 | tf_op jit(solution)/shard_map/slice | solution.py:106
  18.3 33.2 %collective-permute-start.5 = (bf16[256,1024]{1,0:T(8,128)(2,1)}, bf16[256,1024]{1,0:T(8,128)(2,1)}, u32[]{:S(2)}, u32[]{:S(2)}) collective-permute-start(bf16[256,1024]{1,0:T(8,128)(2,1)} %get-tuple-element.21), channel_id=1, source_target_pairs={{0,8},{8,16},{16,24},{1,9},{9,17},{17,25},{2,10},{10,18},{18,26},{... | collective-permute-start | bytes 1572872 | tf_op jit(solution)/shard_map/ppermute | solution.py:18
  32.0 1.2 %collective-permute-start.2 = (f32[256]{0:T(256)S(1)}, f32[256]{0:T(256)S(1)}, u32[]{:S(2)}, u32[]{:S(2)}) collective-permute-start(f32[256]{0:T(256)S(1)} %bitcast.231), channel_id=1, source_target_pairs={{0,1},{1,0},{2,3},{3,2},{4,5},{5,4},{6,7},{7,6},{8,9},{9,8},{10,11... | collective-permute-start | bytes 3080 | tf_op jit(solution)/shard_map/ppermute | solution.py:40
  33.2 3.6 %collective-permute-start.3 = (f32[256]{0:T(256)S(1)}, f32[256]{0:T(256)S(1)}, u32[]{:S(2)}, u32[]{:S(2)}) collective-permute-start(f32[256]{0:T(256)S(1)} %add.133), channel_id=1, source_target_pairs={{0,2},{1,3},{2,0},{3,1},{4,6},{5,7},{6,4},{7,5},{8,10},{9,11},{10,... | collective-permute-start | bytes 3080 | tf_op jit(solution)/shard_map/ppermute | solution.py:40
  34.8 3.7 %copy-start.6 = (bf16[1,512,2048]{2,1,0:T(8,128)(2,1)S(1)}, bf16[1,512,2048]{2,1,0:T(8,128)(2,1)}, u32[]{:S(2)}) copy-start(bf16[1,512,2048]{2,1,0:T(8,128)(2,1)} %get-tuple-element.19) | copy-start | bytes 6291460
  36.8 2.4 %copy-start.5 = (bf16[1,512,2048]{2,1,0:T(8,128)(2,1)S(1)}, bf16[1,512,2048]{2,1,0:T(8,128)(2,1)}, u32[]{:S(2)}) copy-start(bf16[1,512,2048]{2,1,0:T(8,128)(2,1)} %get-tuple-element.18) | copy-start | bytes 6291460
  40.3 1.6 %copy-start.4 = (bf16[1,512,2048]{2,1,0:T(8,128)(2,1)S(1)}, bf16[1,512,2048]{2,1,0:T(8,128)(2,1)}, u32[]{:S(2)}) copy-start(bf16[1,512,2048]{2,1,0:T(8,128)(2,1)} %get-tuple-element.17) | copy-start | bytes 6291460
  42.3 1.6 %copy-start.3 = (bf16[1,512,2048]{2,1,0:T(8,128)(2,1)S(1)}, bf16[1,512,2048]{2,1,0:T(8,128)(2,1)}, u32[]{:S(2)}) copy-start(bf16[1,512,2048]{2,1,0:T(8,128)(2,1)} %get-tuple-element.16) | copy-start | bytes 6291460
  45.3 2.1 %copy-start.2 = (bf16[1,512,2048]{2,1,0:T(8,128)(2,1)S(1)}, bf16[1,512,2048]{2,1,0:T(8,128)(2,1)}, u32[]{:S(2)}) copy-start(bf16[1,512,2048]{2,1,0:T(8,128)(2,1)} %get-tuple-element.15) | copy-start | bytes 6291460
  47.7 1.6 %copy-start.1 = (bf16[1,512,2048]{2,1,0:T(8,128)(2,1)S(1)}, bf16[1,512,2048]{2,1,0:T(8,128)(2,1)}, u32[]{:S(2)}) copy-start(bf16[1,512,2048]{2,1,0:T(8,128)(2,1)} %get-tuple-element.14) | copy-start | bytes 6291460
  50.8 1.9 %copy-start = (bf16[1,512,2048]{2,1,0:T(8,128)(2,1)S(1)}, bf16[1,512,2048]{2,1,0:T(8,128)(2,1)}, u32[]{:S(2)}) copy-start(bf16[1,512,2048]{2,1,0:T(8,128)(2,1)} %get-tuple-element.20) | copy-start | bytes 6291460
  57.0 2.9 %collective-permute-start.6 = (f32[2,512,256]{2,1,0:T(8,128)}, f32[2,512,256]{2,1,0:T(8,128)S(1)}, u32[]{:S(2)}, u32[]{:S(2)}) collective-permute-start(f32[2,512,256]{2,1,0:T(8,128)} %slice.192), channel_id=1, source_target_pairs={{0,1},{1,0},{2,3},{3,2},{4,5},{5,4},{6,7},{7,6},{8,9},{9,8},{10,11... | collective-permute-start | bytes 3145736 | tf_op jit(solution)/shard_map/ppermute | solution.py:31
  60.1 8.4 %collective-permute-start.7 = (bf16[1,512,256]{2,1,0:T(8,128)(2,1)S(1)}, bf16[1,512,256]{2,1,0:T(8,128)(2,1)S(1)}, u32[]{:S(2)}, u32[]{:S(2)}) collective-permute-start(bf16[1,512,256]{2,1,0:T(8,128)(2,1)S(1)} %slice.280), channel_id=1, source_target_pairs={{0,2},{1,3},{2,0},{3,1},{4,6},{5,7},{6,4},{7,5},{8,10},{9,11},{10,... | collective-permute-start | bytes 786440 | tf_op jit(solution)/shard_map/ppermute | solution.py:31
  69.1 6.2 %collective-permute-start.8 = (bf16[192,512]{1,0:T(8,128)(2,1)S(1)}, bf16[192,512]{1,0:T(8,128)(2,1)S(1)}, u32[]{:S(2)}, u32[]{:S(2)}) collective-permute-start(bf16[192,512]{1,0:T(8,128)(2,1)S(1)} %get-tuple-element.23), channel_id=1, source_target_pairs={{0,4},{4,0},{1,5},{5,1},{2,6},{6,2},{3,7},{7,3},{8,12},{12,8},{9,1... | collective-permute-start | bytes 589832 | tf_op jit(solution)/shard_map/ppermute | solution.py:140
  75.3 0.7 copy-start.8

commit v19 on v18

--- a/solution.py
+++ b/solution.py
@@ -9,7 +9,7 @@
 
 EPSILON = 1e-05
 ROPE_BASE = 500000.0
-CHUNK_EIGHTHS = (4, 2, 2)
+CHUNK_EIGHTHS = (3, 2, 2, 1)
 
 
 def shifted(block, axis, distance):

time: 76.4 us -> 80.3 us (1.051)
  other arithmetic: 7.74 us -> 9.5 us
  matrix products: 11.6 us -> 12.8 us
  starting transfers between devices: 19.7 us -> 20.9 us
    reduce_sum x1, other arithmetic: 0.49 us -> 2.08 us  [per_device(): part_sq = jnp.sum(widened * widened, axis=1)]
    dot_general x32, matrix products: 11.3 us -> 12.5 us  [per_device(): lax.dot_general(piece, sub, (((0,), (1,)), ((), ())), preferred_element_t...]
    ppermute x4 -> x5, starting transfers between devices: 15 us -> 16.1 us  [shifted(): return lax.ppermute(block, axis, route)]
    add x3 -> x4, other arithmetic: 1.69 us -> 1.82 us  [per_device(): partial = term if partial is None else partial + term]
    slice x2 -> x3, local copies, waits for them, and re-layouts: 2.51 us -> 2.4 us  [per_device(): arrived = shifted(tok_rows[:, cols], 'section', 1)]
  transfers between devices with their start and end apart: 9 -> 10, of which waited for: 6 -> 5; matrix products, arithmetic and copies ran while one was open for 36% -> 41% of each run, Pallas kernels for 0% -> 0%
where the time goes in v19:
time: 80.3 us; the launch traced here: 79.8 us
  starting transfers between devices  20.9 us (26%)
  local copies, waits for them, and re-layouts  17.6 us (22%)
  waiting for transfers between devices  17.1 us (21%)
  matrix products  12.8 us (16%)
  other arithmetic  9.5 us (12%)
  between operations  1.91 us (2%)
    ppermute x5, starting transfers between devices, shifted(): return lax.ppermute(block, axis, route)  16.1 us
    dot_general x32, matrix products, per_device(): lax.dot_general(piece, sub, (((0,), (1,)), ((), ())), preferred_element_t...  12.5 us
    slice x1, local copies, waits for them, and re-layouts, per_device(): piece = lax.dynamic_slice_in_dim(weight[part], column, block, axis=1)  11.4 us
    ppermute x2, waiting for transfers between devices, scatter_sum(): current = keep + lax.ppermute(send, axis, pairs).astype(jnp.float32)  9.37 us
    ppermute x1, waiting for transfers between devices, per_device(): arrived = lax.ppermute(outgoing, 'dp', pairs)  4.59 us
    convert_element_type x3, other arithmetic, per_device(): (arrived.astype(jnp.float32) * gain[cols] * scale[:, None]).astype(jnp.bf...  4.06 us
    ppermute x2, waiting for transfers between devices, all_sum(): lax.ppermute(value, axis, [(i, i ^ bit) for i in range(size)])  3.16 us
    slice x3, local copies, waits for them, and re-layouts, per_device(): arrived = shifted(tok_rows[:, cols], 'section', 1)  2.4 us
  transfers between devices with their start and end apart: 10, of which 5 were waited for; matrix products, arithmetic and copies ran while one was open for 41% of the time, Pallas kernels for 0%

profile of v19, /device:TPU:0, one launch (start us, length us, event | category | flops | bytes accessed | tf_op | source)
XLA Modules:
  0.0 79.8 jit_solution(688161555653434648)
XLA Ops:
  0.0 1.3 %slice.184 = bf16[256,1536]{1,0:T(8,128)(2,1)S(1)} slice(bf16[256,4096]{1,0:T(8,128)(2,1)} %bitcast.216), slice={[0:256], [0:1536]} | slice | bytes 1572864 | tf_op jit(solution)/shard_map/slice | solution.py:103
  1.4 5.8 %collective-permute-start.1 = (bf16[256,1536]{1,0:T(8,128)(2,1)S(1)}, bf16[256,1536]{1,0:T(8,128)(2,1)}, u32[]{:S(2)}, u32[]{:S(2)}) collective-permute-start(bf16[256,1536]{1,0:T(8,128)(2,1)S(1)} %slice.184), channel_id=1, source_target_pairs={{0,8},{8,16},{16,24},{1,9},{9,17},{17,25},{2,10},{10,18},{18,26},{... | collective-permute-start | bytes 2359304 | tf_op jit(solution)/shard_map/ppermute | solution.py:18
  7.2 2.1 %multiply_reduce_fusion = f32[256]{0:T(256)S(1)} fusion(bf16[1,1,256,4096]{3,2,1,0:T(8,128)(2,1)} %param.6), kind=kLoop, calls=%fused_computation | loop fusion | flops 3145472 | bytes 2098176 | tf_op jit(solution)/shard_map/reduce_sum | solution.py:83
  10.0 0.6 reduce-window.6
  11.8 2.6 %collective-permute-start = (f32[3,256]{1,0:T(4,128)S(1)}, f32[3,256]{1,0:T(4,128)S(1)}, u32[]{:S(2)}, u32[]{:S(2)}) collective-permute-start(f32[3,256]{1,0:T(4,128)S(1)} %pad_maximum_fusion.1), channel_id=1, source_target_pairs={{0,8},{8,16},{16,24},{1,9},{9,17},{17,25},{2,10},{10,18},{18,26},{... | collective-permute-start | bytes 9224 | tf_op jit(solution)/shard_map/ppermute | solution.py:18
  14.4 1.0 %fusion.134 = (bf16[256,1024]{1,0:T(8,128)(2,1)}, bf16[256,1024]{1,0:T(8,128)(2,1)}) fusion(bf16[256,4096]{1,0:T(8,128)(2,1)S(1)} %bitcast.217), kind=kLoop, calls=%fused_computation.208 | loop fusion | bytes 2097152 | tf_op jit(solution)/shard_map/slice | solution.py:103
  15.5 4.3 %collective-permute-start.4 = (bf16[256,1024]{1,0:T(8,128)(2,1)}, bf16[256,1024]{1,0:T(8,128)(2,1)}, u32[]{:S(2)}, u32[]{:S(2)}) collective-permute-start(bf16[256,1024]{1,0:T(8,128)(2,1)} %get-tuple-element.26), channel_id=1, source_target_pairs={{0,8},{8,16},{16,24},{1,9},{9,17},{17,25},{2,10},{10,18},{18,26},{... | collective-permute-start | bytes 1572872 | tf_op jit(solution)/shard_map/ppermute | solution.py:18
  19.7 2.1 %collective-permute-start.5 = (bf16[256,1024]{1,0:T(8,128)(2,1)}, bf16[256,1024]{1,0:T(8,128)(2,1)}, u32[]{:S(2)}, u32[]{:S(2)}) collective-permute-start(bf16[256,1024]{1,0:T(8,128)(2,1)} %get-tuple-element.25), channel_id=1, source_target_pairs={{0,8},{8,16},{16,24},{1,9},{9,17},{17,25},{2,10},{10,18},{18,26},{... | collective-permute-start | bytes 1572872 | tf_op jit(solution)/shard_map/ppermute | solution.py:18
  21.9 1.3 %collective-permute-start.6 = (bf16[256,512]{1,0:T(8,128)(2,1)S(1)}, bf16[256,512]{1,0:T(8,128)(2,1)S(1)}, u32[]{:S(2)}, u32[]{:S(2)}) collective-permute-start(bf16[256,512]{1,0:T(8,128)(2,1)S(1)} %slice.195), channel_id=1, source_target_pairs={{0,8},{8,16},{16,24},{1,9},{9,17},{17,25},{2,10},{10,18},{18,26},{... | collective-permute-start | bytes 786440 | tf_op jit(solution)/shard_map/ppermute | solution.py:18
  23.2 11.4 %fusion.133 = (bf16[1,512,2048]{2,1,0:T(8,128)(2,1)S(1)}, bf16[1,512,2048]{2,1,0:T(8,128)(2,1)}, bf16[1,512,2048]{2,1,0:T(8,128)(2,1)}, bf16[1,512,2048]{2,1,0:T...) fusion(bf16[1,4096,2048]{2,1,0:T(8,128)(2,1)} %param.11), kind=kLoop, calls=%fused_computation.207 | loop fusion | bytes 33554432 | tf_op jit(solution)/shard_map/slice | solution.py:113
  34.8 1.1 %collective-permute-done.2 = f32[256]{0:T(256)S(1)} collective-permute-done((f32[256]{0:T(256)S(1)}, f32[256]{0:T(256)S(1)}, u32[]{:S(2)}, u32[]{:S(2)}) %collective-permute-start.2) | collective-permute-done | bytes 1056 | tf_op jit(solution)/shard_map/ppermute | solution.py:40
  35.9 1.5 %collective-permute-start.3 = (f32[256]{0:T(256)S(1)}, f32[256]{0:T(256)S(1)}, u32[]{:S(2)}, u32[]{:S(2)}) collective-permute-start(f32[256]{0:T(256)S(1)} %add.133), channel_id=1, source_target_pairs={{0,2},{1,3},{2,0},{3,1},{4,6},{5,7},{6,4},{7,5},{8,10},{9,11},{10,... | collective-permute-start | bytes 3080 | tf_op jit(solution)/shard_map/ppermute | solution.py:40
  37.4 2.0 %collective-permute-done.3 = f32[256]{0:T(256)S(1)} collective-permute-done((f32[256]{0:T(256)S(1)}, f32[256]{0:T(256)S(1)}, u32[]{:S(2)}, u32[]{:S(2)}) %collective-permute-start.3) | collective-permute-done | bytes 1056 | tf_op jit(solution)/shard_map/ppermute | solution.py:40
  39.5 1.5 %multiply_convert_fusion = bf16[256,1536]{1,0:T(8,128)(2,1)S(1)} fusion(bf16[256,1536]{1,0:T(8,128)(2,1)} %collective-permute-done.1, f32[256]{0:T(256)S(1)} %add_rsqrt_fusion, f32[1536]{0:T(1024)S(1)} %slice_reduce_fusion), kind=kLoop, calls=%fused_computation.8 | loop fusion | flops 1572864 | bytes 1580032 | tf_op jit(solution)/shard_map/convert_element_type | solution.py:106
  41.0 1.4 %convolution_bitcast_fusion.28 = f32[1,512,256]{2,1,0:T(8,128)S(1)} fusion(bf16[1,512,2048]{2,1,0:T(8,128)(2,1)} %get-tuple-element.23, s32[]{:T(128)S(6)} %select_n.89, bf16[256,1536]{1,0:T(8,128)(2,1)S(1)} %multiply_convert_fusion), kind=kOutput, calls=%fused_computation.38 | convolution fusion | flops 134217728 | bytes 1310724 | tf_op jit(solution)/shard_map/dot_general | solution.py:115
  44.9 0.5 copy-done.4
  46.8 0.6 fusion
  47.5 1.2 %multiply_convert_fusion.2 = bf16[256,1024]{1,0:T(8,128)(2,1)S(1)} fusion(bf16[256,1024]{1,0:T(8,128)(2,1)} %collective-permute-done.4, f32[256]{0:T(256)S(1)} %add_rsqrt_fusion, f32[1024]{0:T(1024)S(1)} %bitcast.228), kind=kLoop, calls=%fused_computation.44 | loop fusion | flops 1048576 | bytes 1053696 | tf_op jit(solution)/shard_map/convert_element_type | solution.py:106
  50.2 0.5 copy-done.2
  52.1 0.4 fusion.1
  52.5 1.4 %multiply_convert_fusion.1 = bf16[256,1024]{1,0:T(8,128)(2,1)S(1)} fusion(bf16[256,1024]{1,0:T(8,128)(2,1)} %collective-permute-done.5, f32[1024]{0:T(1024)S(1)} %bitcast.227, f32[256]{0:T(256)S(1)} %add_rsqrt_fusion), kind=kLoop, calls=%fused_computation.43 | loop fusion | flops 1048576 | bytes 1053696 | tf_op jit(solution)/shard_map/convert_element_type | solution.py:106
  55.4 0.5 copy-done
  57.3 0.4 fusion.2
  57.7 0.4 convolution_bitcast_fusion
  58.2 0.4 convolution_bitcast_fusion.1
  59.8 1.0 %slice.197 = f32[2,512,256]{2,1,0:T(8,128)} slice(f32[4,512,256]{2,1,0:T(8,128)S(1)} %maximum_add_fusion.3), slice={[2:4], [0:512], [0:256]} | slice | bytes 2097152 | tf_op jit(solution)/shard_map/slice | solution.py:27
  60.8 2.9 %collective-permute-done.7 = f32[2,512,256]{2,1,0:T(8,128)S(1)} collective-permute-done((f32[2,512,256]{2,1,0:T(8,128)}, f32[2,512,256]{2,1,0:T(8,128)S(1)}, u32[]{:S(2)}, u32[]{:S(2)}) %collective-permute-start.7) | collective-permute-done | bytes 1048608 | tf_op jit(solution)/shard_map/ppermute | solution.py:31
  63.9 1.6 %collective-permute-start.8 = (bf16[1,512,256]{2,1,0:T(8,128)(2,1)S(1)}, bf16[1,512,256]{2,1,0:T(8,128)(2,1)S(1)}, u32[]{:S(2)}, u32[]{:S(2)}) collective-permute-start(bf16[1,512,256]{2,1,0:T(8,128)(2,1)S(1)} %slice.278), channel_id=1, source_target_pairs={{0,2},{1,3},{2,0},{3,1},{4,6},{5,7},{6,4},{7,5},{8,10},{9,11},{10,... | collective-permute-start | bytes 786440 | tf_op jit(solution)/shard_map/ppermute | solution.py:31
  65.8 6.5 %collective-permute-done.8 = bf16[1,512,256]{2,1,0:T(8,128)(2,1)S(1)} collective-permute-done((bf16[1,512,256]{2,1,0:T(8,128)(2,1)S(1)}, bf16[1,512,256]{2,1,0:T(8,128)(2,1)S(1)}, u32[]{:S(2)}, u32[]{:S(2)}) %collective-permute-start.8) | collective-permute-done | bytes 262176 | tf_op jit(solution)/shard_map/ppermute | solution.py:31
  72.9 1.6 %collective-permute-start.9 = (bf16[192,512]{1,0:T(8,128)(2,1)S(1)}, bf16[192,512]{1,0:T(8,128)(2,1)S(1)}, u32[]{:S(2)}, u32[]{:S(2)}) collective-permute-start(bf16[192,512]{1,0:T(8,128)(2,1)S(1)} %get-tuple-element.27), channel_id=1, source_target_pairs={{0,4},{4,0},{1,5},{5,1},{2,6},{6,2},{3,7},{7,3},{8,12},{12,8},{9,1... | collective-permute-start | bytes 589832 | tf_op jit(solution)/shard_map/ppermute | solution.py:140
  74.4 4.6 %collective-permute-done.9 = bf16[192,512]{1,0:T(8,128)(2,1)S(1)} collective-permute-done((bf16[192,512]{1,0:T(8,128)(2,1)S(1)}, bf16[192,512]{1,0:T(8,128)(2,1)S(1)}, u32[]{:S(2)}, u32[]{:S(2)}) %collective-permute-start.9) | collective-permute-done | bytes 196640 | tf_op jit(solution)/shard_map/ppermute | solution.py:140
  79.1 0.7 copy-done.8
  (86 shorter events, 12.4 us)
Async XLA Ops:
  0.0 14.4 %copy-start.7 = (bf16[1,1,256,4096]{3,2,1,0:T(8,128)(2,1)S(1)}, bf16[1,1,256,4096]{3,2,1,0:T(8,128)(2,1)}, u32[]{:S(2)}) copy-start(bf16[1,1,256,4096]{3,2,1,0:T(8,128)(2,1)} %param.6) | copy-start | bytes 6291460
  0.0 10.0 %copy-start.10 = (s32[1,1,256,1]{2,3,1,0:T(1,128)S(1)}, s32[1,1,256,1]{2,3,1,0:T(1,128)}, u32[]{:S(2)}) copy-start(s32[1,1,256,1]{2,3,1,0:T(1,128)} %param.7) | copy-start | bytes 3076
  1.4 38.1 %collective-permute-start.1 = (bf16[256,1536]{1,0:T(8,128)(2,1)S(1)}, bf16[256,1536]{1,0:T(8,128)(2,1)}, u32[]{:S(2)}, u32[]{:S(2)}) collective-permute-start(bf16[256,1536]{1,0:T(8,128)(2,1)S(1)} %slice.184), channel_id=1, source_target_pairs={{0,8},{8,16},{16,24},{1,9},{9,17},{17,25},{2,10},{10,18},{18,26},{... | collective-permute-start | bytes 2359304 | tf_op jit(solution)/shard_map/ppermute | solution.py:18
  11.8 22.8 %collective-permute-start = (f32[3,256]{1,0:T(4,128)S(1)}, f32[3,256]{1,0:T(4,128)S(1)}, u32[]{:S(2)}, u32[]{:S(2)}) collective-permute-start(f32[3,256]{1,0:T(4,128)S(1)} %pad_maximum_fusion.1), channel_id=1, source_target_pairs={{0,8},{8,16},{16,24},{1,9},{9,17},{17,25},{2,10},{10,18},{18,26},{... | collective-permute-start | bytes 9224 | tf_op jit(solution)/shard_map/ppermute | solution.py:18
  15.5 32.0 %collective-permute-start.4 = (bf16[256,1024]{1,0:T(8,128)(2,1)}, bf16[256,1024]{1,0:T(8,128)(2,1)}, u32[]{:S(2)}, u32[]{:S(2)}) collective-permute-start(bf16[256,1024]{1,0:T(8,128)(2,1)} %get-tuple-element.26), channel_id=1, source_target_pairs={{0,8},{8,16},{16,24},{1,9},{9,17},{17,25},{2,10},{10,18},{18,26},{... | collective-permute-start | bytes 1572872 | tf_op jit(solution)/shard_map/ppermute | solution.py:18
  19.7 32.8 %collective-permute-start.5 = (bf16[256,1024]{1,0:T(8,128)(2,1)}, bf16[256,1024]{1,0:T(8,128)(2,1)}, u32[]{:S(2)}, u32[]{:S(2)}) collective-permute-start(bf16[256,1024]{1,0:T(8,128)(2,1)} %get-tuple-element.25), channel_id=1, source_target_pairs={{0,8},{8,16},{16,24},{1,9},{9,17},{17,25},{2,10},{10,18},{18,26},{... | collective-permute-start | bytes 1572872 | tf_op jit(solution)/shard_map/ppermute | solution.py:18
  21.9 12.8 %copy-start.9 = (f32[1,4096]{1,0:T(1,128)S(1)}, f32[1,4096]{1,0:T(1,128)}, u32[]{:S(2)}) copy-start(f32[1,4096]{1,0:T(1,128)} %param.10) | copy-start | bytes 49156
  21.9 35.9 %collective-permute-start.6 = (bf16[256,512]{1,0:T(8,128)(2,1)S(1)}, bf16[256,512]{1,0:T(8,128)(2,1)S(1)}, u32[]{:S(2)}, u32[]{:S(2)}) collective-permute-start(bf16[256,512]{1,0:T(8,128)(2,1)S(1)} %slice.195), channel_id=1, source_target_pairs={{0,8},{8,16},{16,24},{1,9},{9,17},{17,25},{2,10},{10,18},{18,26},{... | collective-permute-start | bytes 786440 | tf_op jit(solution)/shard_map/ppermute | solution.py:18
  34.7 1.2 %collective-permute-start.2 = (f32[256]{0:T(256)S(1)}, f32[256]{0:T(256)S(1)}, u32[]{:S(2)}, u32[]{:S(2)}) collective-permute-start(f32[256]{0:T(256)S(1)} %bitcast.235), channel_id=1, source_target_pairs={{0,1},{1,0},{2,3},{3,2},{4,5},{5,4},{6,7},{7,6},{8,9},{9,8},{10,11... | collective-permute-start | bytes 3080 | tf_op jit(solution)/shard_map/ppermute | solution.py:40
  35.9 3.6 %collective-permute-start.3 = (f32[256]{0:T(256)S(1)}, f32[256]{0:T(256)S(1)}, u32[]{:S(2)}, u32[]{:S(2)}) collective-permute-start(f32[256]{0:T(256)S(1)} %add.133), channel_id=1, source_target_pairs={{0,2},{1,3},{2,0},{3,1},{4,6},{5,7},{6,4},{7,5},{8,10},{9,11},{10,... | collective-permute-start | bytes 3080 | tf_op jit(solution)/shard_map/ppermute | solution.py:40
  37.4 5.0 %copy-start.6 = (bf16[1,512,2048]{2,1,0:T(8,128)(2,1)S(1)}, bf16[1,512,2048]{2,1,0:T(8,128)(2,1)}, u32[]{:S(2)}) copy-start(bf16[1,512,2048]{2,1,0:T(8,128)(2,1)} %get-tuple-element.23) | copy-start | bytes 6291460
  39.5 3.3 %copy-start.5 = (bf16[1,512,2048]{2,1,0:T(8,128)(2,1)S(1)}, bf16[1,512,2048]{2,1,0:T(8,128)(2,1)}, u32[]{:S(2)}) copy-start(bf16[1,512,2048]{2,1,0:T(8,128)(2,1)} %get-tuple-element.22) | copy-start | bytes 6291460
  43.8 1.6 %copy-start.4 = (bf16[1,512,2048]{2,1,0:T(8,128)(2,1)S(1)}, bf16[1,512,2048]{2,1,0:T(8,128)(2,1)}, u32[]{:S(2)}) copy-start(bf16[1,512,2048]{2,1,0:T(8,128)(2,1)} %get-tuple-element.21) | copy-start | bytes 6291460
  46.8 1.9 %copy-start.3 = (bf16[1,512,2048]{2,1,0:T(8,128)(2,1)S(1)}, bf16[1,512,2048]{2,1,0:T(8,128)(2,1)}, u32[]{:S(2)}) copy-start(bf16[1,512,2048]{2,1,0:T(8,128)(2,1)} %get-tuple-element.20) | copy-start | bytes 6291460
  49.1 1.6 %copy-start.2 = (bf16[1,512,2048]{2,1,0:T(8,128)(2,1)S(1)}, bf16[1,512,2048]{2,1,0:T(8,128)(2,1)}, u32[]{:S(2)}) copy-start(bf16[1,512,2048]{2,1,0:T(8,128)(2,1)} %get-tuple-element.19) | copy-start | bytes 6291460
  52.1 1.8 %copy-start.1 = (bf16[1,512,2048]{2,1,0:T(8,128)(2,1)S(1)}, bf16[1,512,2048]{2,1,0:T(8,128)(2,1)}, u32[]{:S(2)}) copy-start(bf16[1,512,2048]{2,1,0:T(8,128)(2,1)} %get-tuple-element.18) | copy-start | bytes 6291460
  54.3 1.6 %copy-start = (bf16[1,512,2048]{2,1,0:T(8,128)(2,1)S(1)}, bf16[1,512,2048]{2,1,0:T(8,128)(2,1)}, u32[]{:S(2)}) copy-start(bf16[1,512,2048]{2,1,0:T(8,128)(2,1)} %get-tuple-element.24) | copy-start | bytes 6291460
  60.8 2.9 %collective-permute-start.7 = (f32[2,512,256]{2,1,0:T(8,128)}, f32[2,512,256]{2,1,0:T(8,128)S(1)}, u32[]{:S(2)}, u32[]{:S(2)}) collective-permute-start(f32[2,512,256]{2,1,0:T(8,128)} %slice.197), channel_id=1, source_target_pairs={{0,1},{1,0},{2,3},{3,2},{4,5},{5,4},{6,7},{7,6},{8,9},{9,8},{10,11... | collective-permute-start | bytes 3145736 | tf_op jit(solution)/shard_map/ppermute | solution.py:31
  63.9 8.4 %collective-permute-start.8 = (bf16[1,512,256]{2,1,0:T(8,128)(2,1)S(1)}, bf16[1,512,256]{2,1,0:T(8,128)(2,1)S(1)}, u32[]{:S(2)}, u32[]{:S(2)}) collective-permute-start(bf16[1,512,256]{2,1,0:T(8,128)(2,1)S(1)} %slice.278), channel_id=1, source_target_pairs={{0,2},{1,3},{2,0},{3,1},{4,6},{5,7},{6,4},{7,5},{8,10},{9,11},{10,... | collective-permute-start | bytes 786440 | tf_op jit(solution)/shard_map/ppermute | solution.py:31
  72.9 6.2 %collective-permute-start.9 = (bf16[192,512]{1,0:T(8,128)(2,1)S(1)}, bf16[192,512]{1,0:T(8,128)(2,1)S(1)}, u32[]{:S(2)}, u32[]{:S(2)}) collective-permute-start(bf16[192,512]{1,0:T(8,128)(2,1)S(1)} %get-tuple-element.27), channel_id=1, source_target_pairs={{0,4},{4,0},{1,5},{5,1},{2,6},{6,2},{3,7},{7,3},{8,12},{12,8},{9,1... | collective-permute-start | bytes 589832 | tf_op jit(solution)/shard_map/ppermute | solution.py:140
  79.0 0.7 copy-start.8
